TPU v7x, 32 devices: a whole 2x2x4 slice. The times are simulated.
32 devices in a mesh: side: 4 (over z), slab: 8 (over y, x, core).
Axes of the slice: x: 2, y: 2, z: 4, core: 2. Of those that a mesh axis runs over, the one named last changes fastest.
Arguments:
- flow_force: float32 [4, 64, 64, 512], P('side', 'slab'), may hold values from -6 to 6
- flow_coef: float32 [4, 64, 64, 512], P('side', 'slab'), may hold values from 0.1 to 1.5
- flow_init: float32 [4, 64, 64, 512], P('side', 'slab'), may hold values from -6 to 6
- compliance: float32 [64, 512, 512], P('slab')
- shell_load: float32 [64, 512], P('slab')
- disp_init: float32 [64, 512], P('slab'), may hold values from -3 to 3
- patch_len: int32 [64], P('slab'), may hold values from 256 to 512
- owner: int32 [64, 1], P('slab'), may hold values from 0 to 2; in each aligned block of 8 rows (0 to 7, 8 to 15, ...) at most 4 rows name the same one
- block_row: int32 [64], P('slab'), may hold values from 0 to 7
Outputs:
- disp_next: float32 [4, 64, 512], P('side', 'slab')
- residual: float32 [4, 64, 512], P('side', 'slab')
- flow_final: float32 [4, 64, 64, 512], P('side', 'slab')
Inputs may be any that keep to these rules, and one draw needn't show every extreme that they name: Within the patch blocks of one shell device (aligned blocks of 8), no sector is the owner of more than 4 blocks.
All inputs are finite; a program needn't handle non-finite values.
Results may differ from a plain program's by a relative error of at most 0.0003.
Values sent between devices are 32-bit elements; how exact they have to be, the bound alone decides.
No kernel may reach another device: no remote copies, remote signals or barrier semaphores. Data moves between devices by JAX's collectives and lax.ppermute only.
A program may use at most 128 MiB of HBM per device.

v0:
```python
import jax
import jax.numpy as jnp
from jax import lax
from jax.sharding import PartitionSpec as P

SWEEPS = 4
CAP = 4


RELAX = 0.5
PENALTY = 3.0
HIGH = lax.Precision.HIGHEST


def extended(block, sides, width):
    for axis, dim in sides:
        count = lax.axis_size(axis)
        forward = [(i, i + 1) for i in range(count - 1)]
        backward = [(target, source) for source, target in forward]
        low = lax.ppermute(
            lax.slice_in_dim(block, block.shape[dim] - width, None, axis=dim), axis, forward
        )
        high = lax.ppermute(lax.slice_in_dim(block, 0, width, axis=dim), axis, backward)
        block = jnp.concatenate([low, block, high], axis=dim)
    return block


def neighbours(padded):
    total = padded[2:, 1:-1, 1:-1] + padded[:-2, 1:-1, 1:-1]
    total = total + padded[1:-1, 2:, 1:-1] + padded[1:-1, :-2, 1:-1]
    total = total + padded[1:-1, 1:-1, 2:] + padded[1:-1, 1:-1, :-2]
    return total


def body(
    flow_force, flow_coef, flow_init, compliance, shell_load, disp_init, patch_len, owner, block_row
):
    force_here = flow_force[0]
    coef_here = flow_coef[0]
    start_here = flow_init[0]
    slab_rows, planes, line_cells = force_here.shape
    patches_here = compliance.shape[0]
    side_count = lax.axis_size("side")
    shell_flag = lax.axis_index("side") == side_count - 1
    live_mask = (jnp.arange(line_cells)[None, :] < patch_len[:, None]).astype(jnp.float32)
    sector_of = owner[:, 0]

    def face_rims(state):
        return extended(state, (("slab", 0),), 1)

    def fluid_solve(plane):
        right_side = force_here.at[:, 0, :].add(plane)
        flow_state = start_here
        for sweep_index in range(SWEEPS):
            padded = jnp.pad(face_rims(flow_state), ((0, 0), (1, 1), (1, 1)))
            flow_state = (right_side + neighbours(padded)) / (6.0 + coef_here)
        return flow_state

    patch_ids = jnp.arange(patches_here)
    earlier_same = (sector_of[:, None] == sector_of[None, :]) & (
        patch_ids[None, :] < patch_ids[:, None]
    )
    slot_rank = jnp.sum(earlier_same.astype(jnp.int32), axis=1)
    slot_column = sector_of * CAP + slot_rank
    slot_hits = (slot_column[:, None] == jnp.arange(side_count * CAP)[None, :]) & shell_flag
    slot_table = slot_hits.astype(jnp.float32)
    slot_rows = jnp.sum(slot_hits.astype(jnp.int32) * (block_row + 1)[:, None], axis=0).reshape(
        side_count, CAP
    )

    def interface(disp):
        outgoing = jnp.dot(slot_table.T, disp, precision=HIGH, preferred_element_type=jnp.float32)
        outgoing = outgoing.reshape(side_count, CAP, line_cells)
        arrived, arrived_rows = (
            lax.all_to_all(outgoing, "side", split_axis=0, concat_axis=0, tiled=True),
            lax.all_to_all(slot_rows, "side", split_axis=0, concat_axis=0, tiled=True),
        )
        row_pick = (arrived_rows.reshape(-1)[None, :] - 1 == jnp.arange(slab_rows)[:, None]).astype(
            jnp.float32
        )
        plane = jnp.dot(
            row_pick,
            arrived.reshape(-1, line_cells),
            precision=HIGH,
            preferred_element_type=jnp.float32,
        )
        flow_state = fluid_solve(plane)
        slot_force = PENALTY * jnp.dot(
            row_pick.T, flow_state[:, 0, :], precision=HIGH, preferred_element_type=jnp.float32
        )
        returned = lax.all_to_all(
            slot_force.reshape(side_count, CAP, line_cells),
            "side",
            split_axis=0,
            concat_axis=0,
            tiled=True,
        )
        traction = jnp.dot(
            slot_table,
            returned.reshape(-1, line_cells),
            precision=HIGH,
            preferred_element_type=jnp.float32,
        )
        return (traction, flow_state)

    def evaluate(disp):
        traction, flow_state = interface(disp)
        loaded = live_mask * (shell_load - traction)
        tilde = live_mask * jnp.einsum("pij,pj->pi", compliance, loaded, precision=HIGH)
        return (tilde, flow_state)

    disp_zero = live_mask * disp_init
    tilde_zero, unused_state = evaluate(disp_zero)
    resid_zero = tilde_zero - disp_zero
    disp_one = disp_zero + RELAX * resid_zero
    tilde_one, unused_state = evaluate(disp_one)
    resid_one = tilde_one - disp_one
    diff_one = resid_one - resid_zero
    gram_aa, gram_ab = lax.psum(
        (jnp.sum(diff_one * diff_one), jnp.sum(diff_one * resid_one)), "slab"
    )
    coeff = -gram_ab / (gram_aa + (0.001 * gram_aa + 1e-06))
    disp_two = tilde_one + coeff * (tilde_one - tilde_zero)
    tilde_two, flow_state = evaluate(disp_two)
    resid_two = tilde_two - disp_two
    newer = resid_two - resid_one
    gram_nn, gram_no, proj_new, proj_old = lax.psum(
        (
            jnp.sum(newer * newer),
            jnp.sum(newer * diff_one),
            jnp.sum(newer * resid_two),
            jnp.sum(diff_one * resid_two),
        ),
        "slab",
    )
    shift_two = 0.001 * (gram_nn + gram_aa) + 1e-06
    diag_new = gram_nn + shift_two
    diag_old = gram_aa + shift_two
    determ = diag_new * diag_old - gram_no * gram_no
    coeff_new = (-proj_new * diag_old + proj_old * gram_no) / determ
    coeff_old = (-proj_old * diag_new + proj_new * gram_no) / determ
    disp_three = (
        tilde_two + coeff_new * (tilde_two - tilde_one) + coeff_old * (tilde_one - tilde_zero)
    )
    disp_next = jnp.where(shell_flag, disp_three, 0.0)[None]
    residual = jnp.where(shell_flag, resid_two, 0.0)[None]
    flow_final = jnp.where(shell_flag, 0.0, flow_state)[None]
    return (disp_next, residual, flow_final)


def solution(mesh):
    return jax.shard_map(
        body,
        mesh=mesh,
        in_specs=(
            P("side", "slab", None, None),
            P("side", "slab", None, None),
            P("side", "slab", None, None),
            P("slab", None, None),
            P("slab", None),
            P("slab", None),
            P("slab"),
            P("slab", None),
            P("slab"),
        ),
        out_specs=(P("side", "slab", None), P("side", "slab", None), P("side", "slab", None, None)),
        check_vma=False,
    )
```

profile of v0, /device:TPU:28, one launch (start us, length us, event | category | flops | bytes accessed | tf_op | source)
XLA Modules:
  0.0 237.6 jit_solution(14581723980782719010)
XLA Ops:
  2.9 5.1 %all-to-all-start = ((s32[4,1,4]{2,1,0:T(1,128)}), s32[4,1,4]{2,1,0:T(1,128)S(1)}, u32[]{:S(2)}, u32[]{:S(2)}) async-start(s32[4,1,4]{2,1,0:T(1,128)} %bitcast.3), calls=%async_computation | async-start | bytes 4096 | tf_op jit(solution)/shard_map/all_to_all | solution.py:76
  9.6 2.2 collective-permute-start
  16.0 5.1 %all-to-all-start.1 = ((f32[4,4,512]{2,1,0:T(4,128)}), f32[4,4,512]{2,1,0:T(4,128)S(1)}, u32[]{:S(2)}, u32[]{:S(2)}) async-start(f32[4,4,512]{2,1,0:T(4,128)} %reshape.171), calls=%async_computation.1 | async-start | bytes 65536 | tf_op jit(solution)/shard_map/all_to_all | solution.py:75
  21.2 2.5 %all-to-all-done.1 = f32[4,4,512]{2,1,0:T(4,128)S(1)} async-done(((f32[4,4,512]{2,1,0:T(4,128)}), f32[4,4,512]{2,1,0:T(4,128)S(1)}, u32[]{:S(2)}, u32[]{:S(2)}) %all-to-all-start.1) | async-done | bytes 32800 | tf_op jit(solution)/shard_map/all_to_all | solution.py:75
  27.9 3.2 %collective-permute-start.2 = (f32[1,64,512]{2,1,0:T(8,128)S(1)}, f32[1,64,512]{2,1,0:T(8,128)S(1)}, u32[]{:S(2)}, u32[]{:S(2)}) collective-permute-start(f32[1,64,512]{2,1,0:T(8,128)S(1)} %get-tuple-element.84), channel_id=1, source_target_pairs={{1,0},{2,1},{3,2},{4,3},{5,4},{6,5},{7,6},{9,8},{10,9},{11,10},{12... | collective-permute-start | bytes 393224 | tf_op jit(solution)/shard_map/ppermute | solution.py:23
  33.7 4.7 %collective-permute-done.3 = f32[1,64,512]{2,1,0:T(8,128)S(1)} collective-permute-done((f32[1,64,512]{2,1,0:T(8,128)S(1)}, f32[1,64,512]{2,1,0:T(8,128)S(1)}, u32[]{:S(2)}, u32[]{:S(2)}) %collective-permute-start.3) | collective-permute-done | bytes 131104 | tf_op jit(solution)/shard_map/ppermute | solution.py:20
  41.9 2.4 %collective-permute-start.5 = (f32[1,64,512]{2,1,0:T(8,128)S(1)}, f32[1,64,512]{2,1,0:T(8,128)S(1)}, u32[]{:S(2)}, u32[]{:S(2)}) collective-permute-start(f32[1,64,512]{2,1,0:T(8,128)S(1)} %get-tuple-element.81), channel_id=1, source_target_pairs={{0,1},{1,2},{2,3},{3,4},{4,5},{5,6},{6,7},{8,9},{9,10},{10,11},{11... | collective-permute-start | bytes 393224 | tf_op jit(solution)/shard_map/ppermute | solution.py:20
  44.4 4.7 %collective-permute-done.5 = f32[1,64,512]{2,1,0:T(8,128)S(1)} collective-permute-done((f32[1,64,512]{2,1,0:T(8,128)S(1)}, f32[1,64,512]{2,1,0:T(8,128)S(1)}, u32[]{:S(2)}, u32[]{:S(2)}) %collective-permute-start.5) | collective-permute-done | bytes 131104 | tf_op jit(solution)/shard_map/ppermute | solution.py:20
  52.6 2.4 %collective-permute-start.7 = (f32[1,64,512]{2,1,0:T(8,128)S(1)}, f32[1,64,512]{2,1,0:T(8,128)S(1)}, u32[]{:S(2)}, u32[]{:S(2)}) collective-permute-start(f32[1,64,512]{2,1,0:T(8,128)S(1)} %get-tuple-element.79), channel_id=1, source_target_pairs={{0,1},{1,2},{2,3},{3,4},{4,5},{5,6},{6,7},{8,9},{9,10},{10,11},{11... | collective-permute-start | bytes 393224 | tf_op jit(solution)/shard_map/ppermute | solution.py:20
  55.1 4.6 %collective-permute-done.7 = f32[1,64,512]{2,1,0:T(8,128)S(1)} collective-permute-done((f32[1,64,512]{2,1,0:T(8,128)S(1)}, f32[1,64,512]{2,1,0:T(8,128)S(1)}, u32[]{:S(2)}, u32[]{:S(2)}) %collective-permute-start.7) | collective-permute-done | bytes 131104 | tf_op jit(solution)/shard_map/ppermute | solution.py:20
  61.9 7.7 %all_to_all.41 = f32[4,4,512]{2,1,0:T(4,128)S(1)} all-to-all(f32[4,4,512]{2,1,0:T(4,128)S(1)} %reshape.174), channel_id=1, replica_groups=mesh['side'=4,'slab'=8] {'side'}, dimensions={0} | all-to-all | bytes 65536 | tf_op jit(solution)/shard_map/all_to_all | solution.py:91
  69.8 9.3 %fusion.48 = f32[8,1,512]{2,1,0:T(1,128)S(1)} fusion(f32[8,512,512]{2,1,0:T(8,128)} %param.18, f32[8,512,1]{1,0,2:T(8,128)S(1)} %fusion.10), kind=kOutput, calls=%fused_computation.154 | convolution fusion | flops 25165824 | bytes 8421376 | tf_op jit(solution)/shard_map/pij,pj->pi/dot_general | solution.py:109
  79.4 8.0 %all_to_all.42 = f32[4,4,512]{2,1,0:T(4,128)S(1)} all-to-all(f32[4,4,512]{2,1,0:T(4,128)S(1)} %reshape.176), channel_id=1, replica_groups=mesh['side'=4,'slab'=8] {'side'}, dimensions={0} | all-to-all | bytes 65536 | tf_op jit(solution)/shard_map/all_to_all | solution.py:75
  91.3 2.6 %collective-permute-start.9 = (f32[1,64,512]{2,1,0:T(8,128)S(1)}, f32[1,64,512]{2,1,0:T(8,128)S(1)}, u32[]{:S(2)}, u32[]{:S(2)}) collective-permute-start(f32[1,64,512]{2,1,0:T(8,128)S(1)} %get-tuple-element.77), channel_id=1, source_target_pairs={{0,1},{1,2},{2,3},{3,4},{4,5},{5,6},{6,7},{8,9},{9,10},{10,11},{11... | collective-permute-start | bytes 393224 | tf_op jit(solution)/shard_map/ppermute | solution.py:20
  93.9 4.6 %collective-permute-done.9 = f32[1,64,512]{2,1,0:T(8,128)S(1)} collective-permute-done((f32[1,64,512]{2,1,0:T(8,128)S(1)}, f32[1,64,512]{2,1,0:T(8,128)S(1)}, u32[]{:S(2)}, u32[]{:S(2)}) %collective-permute-start.9) | collective-permute-done | bytes 131104 | tf_op jit(solution)/shard_map/ppermute | solution.py:20
  102.0 2.4 %collective-permute-start.11 = (f32[1,64,512]{2,1,0:T(8,128)S(1)}, f32[1,64,512]{2,1,0:T(8,128)S(1)}, u32[]{:S(2)}, u32[]{:S(2)}) collective-permute-start(f32[1,64,512]{2,1,0:T(8,128)S(1)} %get-tuple-element.75), channel_id=1, source_target_pairs={{0,1},{1,2},{2,3},{3,4},{4,5},{5,6},{6,7},{8,9},{9,10},{10,11},{11... | collective-permute-start | bytes 393224 | tf_op jit(solution)/shard_map/ppermute | solution.py:20
  104.5 4.7 %collective-permute-done.11 = f32[1,64,512]{2,1,0:T(8,128)S(1)} collective-permute-done((f32[1,64,512]{2,1,0:T(8,128)S(1)}, f32[1,64,512]{2,1,0:T(8,128)S(1)}, u32[]{:S(2)}, u32[]{:S(2)}) %collective-permute-start.11) | collective-permute-done | bytes 131104 | tf_op jit(solution)/shard_map/ppermute | solution.py:20
  112.7 2.4 %collective-permute-start.13 = (f32[1,64,512]{2,1,0:T(8,128)S(1)}, f32[1,64,512]{2,1,0:T(8,128)S(1)}, u32[]{:S(2)}, u32[]{:S(2)}) collective-permute-start(f32[1,64,512]{2,1,0:T(8,128)S(1)} %get-tuple-element.73), channel_id=1, source_target_pairs={{0,1},{1,2},{2,3},{3,4},{4,5},{5,6},{6,7},{8,9},{9,10},{10,11},{11... | collective-permute-start | bytes 393224 | tf_op jit(solution)/shard_map/ppermute | solution.py:20
  115.2 4.7 %collective-permute-done.13 = f32[1,64,512]{2,1,0:T(8,128)S(1)} collective-permute-done((f32[1,64,512]{2,1,0:T(8,128)S(1)}, f32[1,64,512]{2,1,0:T(8,128)S(1)}, u32[]{:S(2)}, u32[]{:S(2)}) %collective-permute-start.13) | collective-permute-done | bytes 131104 | tf_op jit(solution)/shard_map/ppermute | solution.py:20
  122.9 8.0 %all_to_all.43 = f32[4,4,512]{2,1,0:T(4,128)S(1)} all-to-all(f32[4,4,512]{2,1,0:T(4,128)S(1)} %reshape.179), channel_id=1, replica_groups=mesh['side'=4,'slab'=8] {'side'}, dimensions={0} | all-to-all | bytes 65536 | tf_op jit(solution)/shard_map/all_to_all | solution.py:91
  131.1 9.3 %fusion.46 = f32[8,1,512]{2,1,0:T(1,128)S(1)} fusion(f32[8,512,512]{2,1,0:T(8,128)} %param.18, f32[8,512,1]{1,0,2:T(8,128)S(1)} %fusion.7), kind=kOutput, calls=%fused_computation.152 | convolution fusion | flops 25165824 | bytes 8421376 | tf_op jit(solution)/shard_map/pij,pj->pi/dot_general | solution.py:109
  141.0 12.4 %all-reduce.11 = (f32[]{:T(128)}, f32[]{:T(128)}) all-reduce(f32[]{:T(128)} %get-tuple-element.44, f32[]{:T(128)} %get-tuple-element.43), channel_id=1, replica_groups=mesh['side'=4,'slab'=8] {'slab'}, use_global_device_ids=true, to_apply=%region_3.4 | all-reduce | flops 2 | bytes 16 | tf_op jit(solution)/shard_map/psum | solution.py:119
  155.7 8.0 %all_to_all.44 = f32[4,4,512]{2,1,0:T(4,128)S(1)} all-to-all(f32[4,4,512]{2,1,0:T(4,128)S(1)} %reshape.181), channel_id=1, replica_groups=mesh['side'=4,'slab'=8] {'side'}, dimensions={0} | all-to-all | bytes 65536 | tf_op jit(solution)/shard_map/all_to_all | solution.py:75
  166.4 2.4 %collective-permute-start.15 = (f32[1,64,512]{2,1,0:T(8,128)S(1)}, f32[1,64,512]{2,1,0:T(8,128)S(1)}, u32[]{:S(2)}, u32[]{:S(2)}) collective-permute-start(f32[1,64,512]{2,1,0:T(8,128)S(1)} %get-tuple-element.71), channel_id=1, source_target_pairs={{0,1},{1,2},{2,3},{3,4},{4,5},{5,6},{6,7},{8,9},{9,10},{10,11},{11... | collective-permute-start | bytes 393224 | tf_op jit(solution)/shard_map/ppermute | solution.py:20
  168.9 4.7 %collective-permute-done.15 = f32[1,64,512]{2,1,0:T(8,128)S(1)} collective-permute-done((f32[1,64,512]{2,1,0:T(8,128)S(1)}, f32[1,64,512]{2,1,0:T(8,128)S(1)}, u32[]{:S(2)}, u32[]{:S(2)}) %collective-permute-start.15) | collective-permute-done | bytes 131104 | tf_op jit(solution)/shard_map/ppermute | solution.py:20
  177.1 2.6 %collective-permute-start.17 = (f32[1,64,512]{2,1,0:T(8,128)S(1)}, f32[1,64,512]{2,1,0:T(8,128)S(1)}, u32[]{:S(2)}, u32[]{:S(2)}) collective-permute-start(f32[1,64,512]{2,1,0:T(8,128)S(1)} %get-tuple-element.69), channel_id=1, source_target_pairs={{0,1},{1,2},{2,3},{3,4},{4,5},{5,6},{6,7},{8,9},{9,10},{10,11},{11... | collective-permute-start | bytes 393224 | tf_op jit(solution)/shard_map/ppermute | solution.py:20
  179.7 4.5 %collective-permute-done.17 = f32[1,64,512]{2,1,0:T(8,128)S(1)} collective-permute-done((f32[1,64,512]{2,1,0:T(8,128)S(1)}, f32[1,64,512]{2,1,0:T(8,128)S(1)}, u32[]{:S(2)}, u32[]{:S(2)}) %collective-permute-start.17) | collective-permute-done | bytes 131104 | tf_op jit(solution)/shard_map/ppermute | solution.py:20
  187.8 2.4 %collective-permute-start.19 = (f32[1,64,512]{2,1,0:T(8,128)S(1)}, f32[1,64,512]{2,1,0:T(8,128)S(1)}, u32[]{:S(2)}, u32[]{:S(2)}) collective-permute-start(f32[1,64,512]{2,1,0:T(8,128)S(1)} %get-tuple-element.67), channel_id=1, source_target_pairs={{0,1},{1,2},{2,3},{3,4},{4,5},{5,6},{6,7},{8,9},{9,10},{10,11},{11... | collective-permute-start | bytes 393224 | tf_op jit(solution)/shard_map/ppermute | solution.py:20
  190.3 4.7 %collective-permute-done.19 = f32[1,64,512]{2,1,0:T(8,128)S(1)} collective-permute-done((f32[1,64,512]{2,1,0:T(8,128)S(1)}, f32[1,64,512]{2,1,0:T(8,128)S(1)}, u32[]{:S(2)}, u32[]{:S(2)}) %collective-permute-start.19) | collective-permute-done | bytes 131104 | tf_op jit(solution)/shard_map/ppermute | solution.py:20
  197.8 8.0 %all_to_all.45 = f32[4,4,512]{2,1,0:T(4,128)S(1)} all-to-all(f32[4,4,512]{2,1,0:T(4,128)S(1)} %reshape.184), channel_id=1, replica_groups=mesh['side'=4,'slab'=8] {'side'}, dimensions={0} | all-to-all | bytes 65536 | tf_op jit(solution)/shard_map/all_to_all | solution.py:91
  206.0 9.2 %fusion.44 = f32[8,1,512]{2,1,0:T(1,128)S(1)} fusion(f32[8,512,512]{2,1,0:T(8,128)} %param.18, f32[8,512,1]{1,0,2:T(8,128)S(1)} %fusion.4), kind=kOutput, calls=%fused_computation.150 | convolution fusion | flops 25165824 | bytes 8421376 | tf_op jit(solution)/shard_map/pij,pj->pi/dot_general | solution.py:109
  216.6 12.5 %all-reduce.10 = (f32[]{:T(128)}, f32[]{:T(128)}, f32[]{:T(128)}, f32[]{:T(128)}) all-reduce(f32[]{:T(128)} %get-tuple-element.42, f32[]{:T(128)} %get-tuple-element.41, f32[]{:T(128)} %get-tuple-element.40, f32[]{:T(128)} %get-tuple-element.39), channel_id=1, replica_groups=mesh['side'=4,'slab'=8] {'slab'}, use_global_device_ids=true, to_apply=%region_11.12 | all-reduce | flops 4 | bytes 32 | tf_op jit(solution)/shard_map/psum | solution.py:127
  (124 shorter events, 54.3 us)
Async XLA Ops:
  0.6 1.3 copy-start.8
  0.6 1.4 copy-start.9
  2.9 13.2 %all-to-all-start = ((s32[4,1,4]{2,1,0:T(1,128)}), s32[4,1,4]{2,1,0:T(1,128)S(1)}, u32[]{:S(2)}, u32[]{:S(2)}) async-start(s32[4,1,4]{2,1,0:T(1,128)} %bitcast.3), calls=%async_computation | async-start | bytes 4096 | tf_op jit(solution)/shard_map/all_to_all | solution.py:76
  9.6 14.4 %collective-permute-start = (f32[1,64,512]{2,1,0:T(8,128)}, f32[1,64,512]{2,1,0:T(8,128)S(1)}, u32[]{:S(2)}, u32[]{:S(2)}) collective-permute-start(f32[1,64,512]{2,1,0:T(8,128)} %get-tuple-element.86), channel_id=1, source_target_pairs={{1,0},{2,1},{3,2},{4,3},{5,4},{6,5},{7,6},{9,8},{10,9},{11,10},{12... | collective-permute-start | bytes 393224 | tf_op jit(solution)/shard_map/ppermute | solution.py:23
  11.8 12.2 %collective-permute-start.1 = (f32[1,64,512]{2,1,0:T(8,128)}, f32[1,64,512]{2,1,0:T(8,128)S(1)}, u32[]{:S(2)}, u32[]{:S(2)}) collective-permute-start(f32[1,64,512]{2,1,0:T(8,128)} %get-tuple-element.85), channel_id=1, source_target_pairs={{0,1},{1,2},{2,3},{3,4},{4,5},{5,6},{6,7},{8,9},{9,10},{10,11},{11... | collective-permute-start | bytes 393224 | tf_op jit(solution)/shard_map/ppermute | solution.py:20
  14.0 1.1 copy-start.5
  14.0 1.1 copy-start.6
  15.1 10.9 %copy-start = (f32[1,8,64,512]{3,2,1,0:T(8,128)S(1)}, f32[1,8,64,512]{3,2,1,0:T(8,128)}, u32[]{:S(2)}) copy-start(f32[1,8,64,512]{3,2,1,0:T(8,128)} %param.16) | copy-start | bytes 3145732
  16.0 7.7 %all-to-all-start.1 = ((f32[4,4,512]{2,1,0:T(4,128)}), f32[4,4,512]{2,1,0:T(4,128)S(1)}, u32[]{:S(2)}, u32[]{:S(2)}) async-start(f32[4,4,512]{2,1,0:T(4,128)} %reshape.171), calls=%async_computation.1 | async-start | bytes 65536 | tf_op jit(solution)/shard_map/all_to_all | solution.py:75
  24.1 1.9 copy-start.3
  27.9 5.7 %collective-permute-start.2 = (f32[1,64,512]{2,1,0:T(8,128)S(1)}, f32[1,64,512]{2,1,0:T(8,128)S(1)}, u32[]{:S(2)}, u32[]{:S(2)}) collective-permute-start(f32[1,64,512]{2,1,0:T(8,128)S(1)} %get-tuple-element.84), channel_id=1, source_target_pairs={{1,0},{2,1},{3,2},{4,3},{5,4},{6,5},{7,6},{9,8},{10,9},{11,10},{12... | collective-permute-start | bytes 393224 | tf_op jit(solution)/shard_map/ppermute | solution.py:23
  31.2 7.2 %collective-permute-start.3 = (f32[1,64,512]{2,1,0:T(8,128)S(1)}, f32[1,64,512]{2,1,0:T(8,128)S(1)}, u32[]{:S(2)}, u32[]{:S(2)}) collective-permute-start(f32[1,64,512]{2,1,0:T(8,128)S(1)} %get-tuple-element.83), channel_id=1, source_target_pairs={{0,1},{1,2},{2,3},{3,4},{4,5},{5,6},{6,7},{8,9},{9,10},{10,11},{11... | collective-permute-start | bytes 393224 | tf_op jit(solution)/shard_map/ppermute | solution.py:20
  40.0 4.4 %collective-permute-start.4 = (f32[1,64,512]{2,1,0:T(8,128)S(1)}, f32[1,64,512]{2,1,0:T(8,128)S(1)}, u32[]{:S(2)}, u32[]{:S(2)}) collective-permute-start(f32[1,64,512]{2,1,0:T(8,128)S(1)} %get-tuple-element.82), channel_id=1, source_target_pairs={{1,0},{2,1},{3,2},{4,3},{5,4},{6,5},{7,6},{9,8},{10,9},{11,10},{12... | collective-permute-start | bytes 393224 | tf_op jit(solution)/shard_map/ppermute | solution.py:23
  41.9 7.2 %collective-permute-start.5 = (f32[1,64,512]{2,1,0:T(8,128)S(1)}, f32[1,64,512]{2,1,0:T(8,128)S(1)}, u32[]{:S(2)}, u32[]{:S(2)}) collective-permute-start(f32[1,64,512]{2,1,0:T(8,128)S(1)} %get-tuple-element.81), channel_id=1, source_target_pairs={{0,1},{1,2},{2,3},{3,4},{4,5},{5,6},{6,7},{8,9},{9,10},{10,11},{11... | collective-permute-start | bytes 393224 | tf_op jit(solution)/shard_map/ppermute | solution.py:20
  50.7 4.5 %collective-permute-start.6 = (f32[1,64,512]{2,1,0:T(8,128)S(1)}, f32[1,64,512]{2,1,0:T(8,128)S(1)}, u32[]{:S(2)}, u32[]{:S(2)}) collective-permute-start(f32[1,64,512]{2,1,0:T(8,128)S(1)} %get-tuple-element.80), channel_id=1, source_target_pairs={{1,0},{2,1},{3,2},{4,3},{5,4},{6,5},{7,6},{9,8},{10,9},{11,10},{12... | collective-permute-start | bytes 393224 | tf_op jit(solution)/shard_map/ppermute | solution.py:23
  52.6 7.2 %collective-permute-start.7 = (f32[1,64,512]{2,1,0:T(8,128)S(1)}, f32[1,64,512]{2,1,0:T(8,128)S(1)}, u32[]{:S(2)}, u32[]{:S(2)}) collective-permute-start(f32[1,64,512]{2,1,0:T(8,128)S(1)} %get-tuple-element.79), channel_id=1, source_target_pairs={{0,1},{1,2},{2,3},{3,4},{4,5},{5,6},{6,7},{8,9},{9,10},{10,11},{11... | collective-permute-start | bytes 393224 | tf_op jit(solution)/shard_map/ppermute | solution.py:20
  55.1 6.4 %copy-start.4 = (f32[8,64,512]{2,1,0:T(8,128)}, f32[8,64,512]{2,1,0:T(8,128)S(1)}, u32[]{:S(2)}) copy-start(f32[8,64,512]{2,1,0:T(8,128)S(1)} %add_bitcast_fusion) | copy-start | bytes 3145732
  60.4 9.2 %copy-start.7 = (f32[8,512]{1,0:T(8,128)S(1)}, f32[8,512]{1,0:T(8,128)}, u32[]{:S(2)}) copy-start(f32[8,512]{1,0:T(8,128)} %param.19) | copy-start | bytes 49156
  69.8 17.8 %copy-start.1 = (f32[8,64,512]{2,1,0:T(8,128)S(1)}, f32[8,64,512]{2,1,0:T(8,128)}, u32[]{:S(2)}) copy-start(f32[8,64,512]{2,1,0:T(8,128)} %copy.102) | copy-start | bytes 3145732
  89.3 4.5 %collective-permute-start.8 = (f32[1,64,512]{2,1,0:T(8,128)S(1)}, f32[1,64,512]{2,1,0:T(8,128)S(1)}, u32[]{:S(2)}, u32[]{:S(2)}) collective-permute-start(f32[1,64,512]{2,1,0:T(8,128)S(1)} %get-tuple-element.78), channel_id=1, source_target_pairs={{1,0},{2,1},{3,2},{4,3},{5,4},{6,5},{7,6},{9,8},{10,9},{11,10},{12... | collective-permute-start | bytes 393224 | tf_op jit(solution)/shard_map/ppermute | solution.py:23
  91.3 7.2 %collective-permute-start.9 = (f32[1,64,512]{2,1,0:T(8,128)S(1)}, f32[1,64,512]{2,1,0:T(8,128)S(1)}, u32[]{:S(2)}, u32[]{:S(2)}) collective-permute-start(f32[1,64,512]{2,1,0:T(8,128)S(1)} %get-tuple-element.77), channel_id=1, source_target_pairs={{0,1},{1,2},{2,3},{3,4},{4,5},{5,6},{6,7},{8,9},{9,10},{10,11},{11... | collective-permute-start | bytes 393224 | tf_op jit(solution)/shard_map/ppermute | solution.py:20
  100.0 4.4 %collective-permute-start.10 = (f32[1,64,512]{2,1,0:T(8,128)S(1)}, f32[1,64,512]{2,1,0:T(8,128)S(1)}, u32[]{:S(2)}, u32[]{:S(2)}) collective-permute-start(f32[1,64,512]{2,1,0:T(8,128)S(1)} %get-tuple-element.76), channel_id=1, source_target_pairs={{1,0},{2,1},{3,2},{4,3},{5,4},{6,5},{7,6},{9,8},{10,9},{11,10},{12... | collective-permute-start | bytes 393224 | tf_op jit(solution)/shard_map/ppermute | solution.py:23
  102.0 7.2 %collective-permute-start.11 = (f32[1,64,512]{2,1,0:T(8,128)S(1)}, f32[1,64,512]{2,1,0:T(8,128)S(1)}, u32[]{:S(2)}, u32[]{:S(2)}) collective-permute-start(f32[1,64,512]{2,1,0:T(8,128)S(1)} %get-tuple-element.75), channel_id=1, source_target_pairs={{0,1},{1,2},{2,3},{3,4},{4,5},{5,6},{6,7},{8,9},{9,10},{10,11},{11... | collective-permute-start | bytes 393224 | tf_op jit(solution)/shard_map/ppermute | solution.py:20
  110.8 4.4 %collective-permute-start.12 = (f32[1,64,512]{2,1,0:T(8,128)S(1)}, f32[1,64,512]{2,1,0:T(8,128)S(1)}, u32[]{:S(2)}, u32[]{:S(2)}) collective-permute-start(f32[1,64,512]{2,1,0:T(8,128)S(1)} %get-tuple-element.74), channel_id=1, source_target_pairs={{1,0},{2,1},{3,2},{4,3},{5,4},{6,5},{7,6},{9,8},{10,9},{11,10},{12... | collective-permute-start | bytes 393224 | tf_op jit(solution)/shard_map/ppermute | solution.py:23
  112.7 7.2 %collective-permute-start.13 = (f32[1,64,512]{2,1,0:T(8,128)S(1)}, f32[1,64,512]{2,1,0:T(8,128)S(1)}, u32[]{:S(2)}, u32[]{:S(2)}) collective-permute-start(f32[1,64,512]{2,1,0:T(8,128)S(1)} %get-tuple-element.73), channel_id=1, source_target_pairs={{0,1},{1,2},{2,3},{3,4},{4,5},{5,6},{6,7},{8,9},{9,10},{10,11},{11... | collective-permute-start | bytes 393224 | tf_op jit(solution)/shard_map/ppermute | solution.py:20
  131.1 33.0 %copy-start.2 = (f32[8,64,512]{2,1,0:T(8,128)S(1)}, f32[8,64,512]{2,1,0:T(8,128)}, u32[]{:S(2)}) copy-start(f32[8,64,512]{2,1,0:T(8,128)} %get-tuple-element.58) | copy-start | bytes 3145732
  164.4 4.4 %collective-permute-start.14 = (f32[1,64,512]{2,1,0:T(8,128)S(1)}, f32[1,64,512]{2,1,0:T(8,128)S(1)}, u32[]{:S(2)}, u32[]{:S(2)}) collective-permute-start(f32[1,64,512]{2,1,0:T(8,128)S(1)} %get-tuple-element.72), channel_id=1, source_target_pairs={{1,0},{2,1},{3,2},{4,3},{5,4},{6,5},{7,6},{9,8},{10,9},{11,10},{12... | collective-permute-start | bytes 393224 | tf_op jit(solution)/shard_map/ppermute | solution.py:23
  166.4 7.2 %collective-permute-start.15 = (f32[1,64,512]{2,1,0:T(8,128)S(1)}, f32[1,64,512]{2,1,0:T(8,128)S(1)}, u32[]{:S(2)}, u32[]{:S(2)}) collective-permute-start(f32[1,64,512]{2,1,0:T(8,128)S(1)} %get-tuple-element.71), channel_id=1, source_target_pairs={{0,1},{1,2},{2,3},{3,4},{4,5},{5,6},{6,7},{8,9},{9,10},{10,11},{11... | collective-permute-start | bytes 393224 | tf_op jit(solution)/shard_map/ppermute | solution.py:20
  175.2 4.6 %collective-permute-start.16 = (f32[1,64,512]{2,1,0:T(8,128)S(1)}, f32[1,64,512]{2,1,0:T(8,128)S(1)}, u32[]{:S(2)}, u32[]{:S(2)}) collective-permute-start(f32[1,64,512]{2,1,0:T(8,128)S(1)} %get-tuple-element.70), channel_id=1, source_target_pairs={{1,0},{2,1},{3,2},{4,3},{5,4},{6,5},{7,6},{9,8},{10,9},{11,10},{12... | collective-permute-start | bytes 393224 | tf_op jit(solution)/shard_map/ppermute | solution.py:23
  177.1 7.2 %collective-permute-start.17 = (f32[1,64,512]{2,1,0:T(8,128)S(1)}, f32[1,64,512]{2,1,0:T(8,128)S(1)}, u32[]{:S(2)}, u32[]{:S(2)}) collective-permute-start(f32[1,64,512]{2,1,0:T(8,128)S(1)} %get-tuple-element.69), channel_id=1, source_target_pairs={{0,1},{1,2},{2,3},{3,4},{4,5},{5,6},{6,7},{8,9},{9,10},{10,11},{11... | collective-permute-start | bytes 393224 | tf_op jit(solution)/shard_map/ppermute | solution.py:20
  185.9 4.4 %collective-permute-start.18 = (f32[1,64,512]{2,1,0:T(8,128)S(1)}, f32[1,64,512]{2,1,0:T(8,128)S(1)}, u32[]{:S(2)}, u32[]{:S(2)}) collective-permute-start(f32[1,64,512]{2,1,0:T(8,128)S(1)} %get-tuple-element.68), channel_id=1, source_target_pairs={{1,0},{2,1},{3,2},{4,3},{5,4},{6,5},{7,6},{9,8},{10,9},{11,10},{12... | collective-permute-start | bytes 393224 | tf_op jit(solution)/shard_map/ppermute | solution.py:23
  187.8 7.2 %collective-permute-start.19 = (f32[1,64,512]{2,1,0:T(8,128)S(1)}, f32[1,64,512]{2,1,0:T(8,128)S(1)}, u32[]{:S(2)}, u32[]{:S(2)}) collective-permute-start(f32[1,64,512]{2,1,0:T(8,128)S(1)} %get-tuple-element.67), channel_id=1, source_target_pairs={{0,1},{1,2},{2,3},{3,4},{4,5},{5,6},{6,7},{8,9},{9,10},{10,11},{11... | collective-permute-start | bytes 393224 | tf_op jit(solution)/shard_map/ppermute | solution.py:20
where the time goes:
time: 242 us; the launch traced here: 238 us
  blocking collectives  64.7 us (27%)
  starting transfers between devices  54.6 us (23%)
  waiting for transfers between devices  45.4 us (19%)
  matrix products  30.1 us (12%)
  other arithmetic  24.3 us (10%)
  between operations  11.2 us (5%)
  local copies, waits for them, and re-layouts  7.21 us (3%)
    ppermute x10, waiting for transfers between devices, extended(): lax.ppermute(lax.slice_in_dim(block, block.shape[dim] - width, None, axis...  41.9 us
    dot_general x3, matrix products, evaluate(): jnp.einsum('pij,pj->pi', compliance, loaded, precision=HIGH)  27.7 us
    all_to_all x3, blocking collectives, interface(): lax.all_to_all(slot_force.reshape(side_count, CAP, line_cells), 'side', s...  23.7 us
    ppermute x10, starting transfers between devices, extended(): lax.ppermute(lax.slice_in_dim(block, block.shape[dim] - width, None, axis...  23.7 us
    ppermute x10, starting transfers between devices, extended(): lax.ppermute(lax.slice_in_dim(block, 0, width, axis=dim), axis, backward)  20.8 us
    all_to_all x2, blocking collectives, interface(): lax.all_to_all(outgoing, 'side', split_axis=0, concat_axis=0, tiled=True)  16 us
    psum x1, blocking collectives, body(): lax.psum((jnp.sum(newer * newer), jnp.sum(newer * diff_one), jnp.sum(newe...  12.5 us
    psum x1, blocking collectives, body(): lax.psum((jnp.sum(diff_one * diff_one), jnp.sum(diff_one * resid_one)), '...  12.4 us
  transfers between devices with their start and end apart: 22, of which 16 were waited for; matrix products, arithmetic and copies ran while one was open for 2% of the time, Pallas kernels for 0%

commit v1 on v0

v1 whole, which is shorter than its diff:
```python
import jax
import jax.numpy as jnp
from jax import lax
from jax.sharding import PartitionSpec as P

SWEEPS = 4
RELAX = 0.5
PENALTY = 3.0
HALO = SWEEPS
BAND = 2 * SWEEPS


def shift_y(a):
    zero = jnp.zeros_like(a[..., :1])
    return (jnp.concatenate([a[..., 1:], zero], axis=-1), jnp.concatenate([zero, a[..., :-1]], axis=-1))


def stencil(rhs, coef, xp, xm, zp, zm, centre):
    yp, ym = shift_y(centre)
    total = ((((xp + xm) + zp) + zm) + yp) + ym
    return (rhs + total) / (6.0 + coef)


def band_solve(q, rhs, coef, row_ok):
    rows, planes = q.shape[0], q.shape[1]
    for k in range(1, SWEEPS + 1):
        centre = q[1:-1, :-1]
        zm = jnp.concatenate([jnp.zeros_like(centre[:, :1]), centre[:, :-1]], axis=1)
        new = stencil(
            rhs[k : rows - k, : planes - k],
            coef[k : rows - k, : planes - k],
            q[2:, :-1],
            q[:-2, :-1],
            q[1:-1, 1:],
            zm,
            centre,
        )
        q = jnp.where(row_ok[k : rows - k], new, 0.0)
    return q


def ring_pairs(count):
    forward = [(i, i + 1) for i in range(count - 1)]
    return forward, [(t, s) for s, t in forward]


def rims(block, width):
    count = lax.axis_size("slab")
    forward, backward = ring_pairs(count)
    low = lax.ppermute(block[block.shape[0] - width :], "slab", forward)
    high = lax.ppermute(block[:width], "slab", backward)
    return jnp.concatenate([low, block, high], axis=0)


def full_solve(q, rhs, coef):
    for k in range(SWEEPS):
        qx = rims(q, 1)
        zero = jnp.zeros_like(q[:, :1])
        q = stencil(
            rhs,
            coef,
            qx[2:],
            qx[:-2],
            jnp.concatenate([q[:, 1:], zero], axis=1),
            jnp.concatenate([zero, q[:, :-1]], axis=1),
            q,
        )
    return q


def allsum(v):
    for axis in ("slab", "side"):
        count = lax.axis_size(axis)
        step = 1
        while step < count:
            v = v + lax.ppermute(v, axis, [(i, i ^ step) for i in range(count)])
            step *= 2
    return v


def body(
    flow_force, flow_coef, flow_init, compliance, shell_load, disp_init, patch_len, owner, block_row
):
    force_here = flow_force[0]
    coef_here = flow_coef[0]
    start_here = flow_init[0]
    slab_rows, planes, line_cells = force_here.shape
    assert slab_rows >= HALO and planes >= BAND
    side_count = lax.axis_size("side")
    side_id = lax.axis_index("side")
    slab_id = lax.axis_index("slab")
    shell_flag = side_id == side_count - 1
    live = (jnp.arange(line_cells)[None, :] < patch_len[:, None]).astype(jnp.float32)
    own = (owner[:, 0] == side_id).astype(jnp.float32)[:, None]
    own_live = own * live
    onehot = (block_row[None, :] == jnp.arange(slab_rows)[:, None]).astype(jnp.float32) * own[:, 0][None, :]

    packed = jnp.stack([start_here[:, :BAND], force_here[:, :BAND], coef_here[:, :BAND]])
    packed = jnp.moveaxis(rims(jnp.moveaxis(packed, 1, 0), HALO), 0, 1)
    init_band, force_band, coef_band = packed[0], packed[1], packed[2]
    global_row = slab_id * slab_rows + jnp.arange(slab_rows + 2 * HALO) - HALO
    total_rows = slab_rows * lax.axis_size("slab")
    row_ok = ((global_row >= 0) & (global_row < total_rows))[:, None, None]

    def evaluate(disp):
        plane = jnp.sum(onehot[:, :, None] * (live * disp)[None], axis=1)
        rhs = force_band.at[:, 0, :].add(rims(plane, HALO))
        band = band_solve(init_band, rhs, coef_band, row_ok)
        traction = PENALTY * band[:, 0, :][block_row]
        loaded = live * (shell_load - traction)
        tilde = own_live * jnp.sum(compliance * loaded[:, None, :], axis=-1)
        return tilde, band

    disp_zero = own_live * disp_init
    tilde_zero, unused = evaluate(disp_zero)
    resid_zero = tilde_zero - disp_zero
    disp_one = disp_zero + RELAX * resid_zero
    tilde_one, unused = evaluate(disp_one)
    resid_one = tilde_one - disp_one
    diff_one = resid_one - resid_zero
    sums = allsum(jnp.stack([jnp.sum(diff_one * diff_one), jnp.sum(diff_one * resid_one)]))
    gram_aa, gram_ab = sums[0], sums[1]
    coeff = -gram_ab / (gram_aa + (0.001 * gram_aa + 1e-06))
    disp_two = tilde_one + coeff * (tilde_one - tilde_zero)
    tilde_two, band_two = evaluate(disp_two)
    resid_two = tilde_two - disp_two
    newer = resid_two - resid_one
    sums = allsum(
        jnp.stack(
            [
                jnp.sum(newer * newer),
                jnp.sum(newer * diff_one),
                jnp.sum(newer * resid_two),
                jnp.sum(diff_one * resid_two),
            ]
        )
    )
    gram_nn, gram_no, proj_new, proj_old = sums[0], sums[1], sums[2], sums[3]

    outgoing = jnp.stack([tilde_two, tilde_one, tilde_zero, resid_two])
    gathered = outgoing
    for source in range(side_count - 1):
        gathered = gathered + lax.ppermute(outgoing, "side", [(source, side_count - 1)])
    tilde_two, tilde_one, tilde_zero, resid_two = gathered[0], gathered[1], gathered[2], gathered[3]

    shift_two = 0.001 * (gram_nn + gram_aa) + 1e-06
    diag_new = gram_nn + shift_two
    diag_old = gram_aa + shift_two
    determ = diag_new * diag_old - gram_no * gram_no
    coeff_new = (-proj_new * diag_old + proj_old * gram_no) / determ
    coeff_old = (-proj_old * diag_new + proj_new * gram_no) / determ
    disp_three = (
        tilde_two + coeff_new * (tilde_two - tilde_one) + coeff_old * (tilde_one - tilde_zero)
    )

    deep = full_solve(start_here, force_here, coef_here)
    flow_state = jnp.concatenate([band_two, deep[:, band_two.shape[1] :]], axis=1)
    disp_next = jnp.where(shell_flag, disp_three, 0.0)[None]
    residual = jnp.where(shell_flag, resid_two, 0.0)[None]
    flow_final = jnp.where(shell_flag, 0.0, flow_state)[None]
    return (disp_next, residual, flow_final)


def solution(mesh):
    return jax.shard_map(
        body,
        mesh=mesh,
        in_specs=(
            P("side", "slab", None, None),
            P("side", "slab", None, None),
            P("side", "slab", None, None),
            P("slab", None, None),
            P("slab", None),
            P("slab", None),
            P("slab"),
            P("slab", None),
            P("slab"),
        ),
        out_specs=(P("side", "slab", None), P("side", "slab", None), P("side", "slab", None, None)),
        check_vma=False,
    )
```

time: 242 us -> 196 us (0.81)
  the two profiles are of different devices: /device:TPU:28 before, /device:TPU:4 now
where the time goes in v1:
time: 196 us; the launch traced here: 194 us
  starting transfers between devices  67.6 us (34%)
  other arithmetic  58.4 us (30%)
  local copies, waits for them, and re-layouts  28.5 us (15%)
  waiting for transfers between devices  28.1 us (14%)
  between operations  11.2 us (6%)
    ppermute x8, starting transfers between devices, rims(): high = lax.ppermute(block[:width], 'slab', backward)  28.7 us
    ppermute x10, waiting for transfers between devices, allsum(): v = v + lax.ppermute(v, axis, [(i, i ^ step) for i in range(count)])  20.4 us
    ppermute x8, starting transfers between devices, rims(): low = lax.ppermute(block[block.shape[0] - width:], 'slab', forward)  17 us
    ppermute x10, starting transfers between devices, allsum(): v = v + lax.ppermute(v, axis, [(i, i ^ step) for i in range(count)])  15.4 us
    reduce_sum x3, other arithmetic, evaluate(): tilde = own_live * jnp.sum(compliance * loaded[:, None, :], axis=-1)  12 us
    div x3, other arithmetic, stencil(): return (rhs + total) / (6.0 + coef)  10.6 us
    unnamed x54, local copies, waits for them, and re-layouts  9.93 us
    ppermute x8, waiting for transfers between devices, rims(): low = lax.ppermute(block[block.shape[0] - width:], 'slab', forward)  7.7 us
  transfers between devices with their start and end apart: 29, of which 12 were waited for; matrix products, arithmetic and copies ran while one was open for 29% of the time, Pallas kernels for 0%

profile of v1, /device:TPU:4, one launch (start us, length us, event | category | flops | bytes accessed | tf_op | source)
XLA Modules:
  0.0 193.8 jit_solution(7761251698764844795)
XLA Ops:
  5.4 4.5 %collective-permute-start.3 = (f32[4,512]{1,0:T(4,128)}, f32[4,512]{1,0:T(4,128)}, u32[]{:S(2)}, u32[]{:S(2)}) collective-permute-start(f32[4,512]{1,0:T(4,128)} %get-tuple-element.117), channel_id=1, source_target_pairs={{1,0},{2,1},{3,2},{4,3},{5,4},{6,5},{7,6},{9,8},{10,9},{11,10},{12... | collective-permute-start | bytes 24584 | tf_op jit(solution)/shard_map/ppermute | solution.py:51
  14.5 4.7 %collective-permute-start.21 = (f32[1,64,512]{2,0,1:T(1,128)}, f32[1,64,512]{2,0,1:T(1,128)}, u32[]{:S(2)}, u32[]{:S(2)}) collective-permute-start(f32[1,64,512]{2,0,1:T(1,128)} %bitcast.95), channel_id=1, source_target_pairs={{1,0},{2,1},{3,2},{4,3},{5,4},{6,5},{7,6},{9,8},{10,9},{11,10},{12... | collective-permute-start | bytes 393224 | tf_op jit(solution)/shard_map/ppermute | solution.py:51
  22.9 2.2 %copy.45 = f32[1,8,64,512]{3,1,2,0:T(8,128)S(1)} copy(f32[1,8,64,512]{3,2,1,0:T(8,128)} %param.16) | data formatting | bytes 2097152 | tf_op args[1]
  34.2 4.5 %collective-permute-start.1 = (f32[4,3,8,512]{3,0,2,1:T(4,128)}, f32[4,3,8,512]{3,0,2,1:T(4,128)S(1)}, u32[]{:S(2)}, u32[]{:S(2)}) collective-permute-start(f32[4,3,8,512]{3,0,2,1:T(4,128)} %get-tuple-element.89), channel_id=1, source_target_pairs={{1,0},{2,1},{3,2},{4,3},{5,4},{6,5},{7,6},{9,8},{10,9},{11,10},{12... | collective-permute-start | bytes 589832 | tf_op jit(solution)/shard_map/ppermute | solution.py:51
  38.8 4.5 %fusion.21 = f32[8,64,512]{2,0,1:T(8,128)S(1)} fusion(f32[8,64,512]{2,0,1:T(8,128)S(1)} %bitcast.99, f32[1,64,512]{2,0,1:T(1,128)} %collective-permute-done.22, f32[1,64,512]{2,0,1:T(1,128)} %collective-permute-done.21, f32[8,64,511]{2,0,1:T(8,128)} %get-tuple-element.82, f32[8,64,511]{2,0,1:T(8,128)} %get-tuple-element.81, ...), kind=kLoop, calls=%fused_computation.34 | loop fusion | flops 2621440 | bytes 8613888 | tf_op jit(solution)/shard_map/div | solution.py:21
  51.2 4.0 %multiply_reduce_fusion.2 = f32[8,512]{1,0:T(8,128)S(1)} fusion(f32[8,512,512]{2,1,0:T(8,128)} %param.18, f32[8,512]{1,0:T(8,128)S(1)} %subtract_select_fusion.2), kind=kLoop, calls=%fused_computation.5 | loop fusion | flops 4190208 | bytes 8421376 | tf_op jit(solution)/shard_map/reduce_sum | solution.py:111
  56.8 1.9 collective-permute-start.4
  58.7 4.5 %collective-permute-start.5 = (f32[4,512]{1,0:T(4,128)S(1)}, f32[4,512]{1,0:T(4,128)S(1)}, u32[]{:S(2)}, u32[]{:S(2)}) collective-permute-start(f32[4,512]{1,0:T(4,128)S(1)} %get-tuple-element.115), channel_id=1, source_target_pairs={{1,0},{2,1},{3,2},{4,3},{5,4},{6,5},{7,6},{9,8},{10,9},{11,10},{12... | collective-permute-start | bytes 24584 | tf_op jit(solution)/shard_map/ppermute | solution.py:51
  68.7 4.0 %multiply_reduce_fusion.1 = f32[8,512]{1,0:T(8,128)S(1)} fusion(f32[8,512,512]{2,1,0:T(8,128)} %param.18, f32[8,512]{1,0:T(8,128)S(1)} %subtract_select_fusion.1), kind=kLoop, calls=%fused_computation.4 | loop fusion | flops 4190208 | bytes 8421376 | tf_op jit(solution)/shard_map/reduce_sum | solution.py:111
  77.9 3.5 %collective-permute-done.7 = f32[2]{0:T(128)S(1)} collective-permute-done((f32[2]{0:T(128)S(1)}, f32[2]{0:T(128)S(1)}, u32[]{:S(2)}, u32[]{:S(2)}) %collective-permute-start.7) | collective-permute-done | bytes 40 | tf_op jit(solution)/shard_map/ppermute | solution.py:76
  83.7 2.6 %collective-permute-done.8 = f32[2]{0:T(128)S(1)} collective-permute-done((f32[2]{0:T(128)S(1)}, f32[2]{0:T(128)S(1)}, u32[]{:S(2)}, u32[]{:S(2)}) %collective-permute-start.8) | collective-permute-done | bytes 40 | tf_op jit(solution)/shard_map/ppermute | solution.py:76
  87.9 2.0 %collective-permute-done.9 = f32[2]{0:T(128)S(1)} collective-permute-done((f32[2]{0:T(128)S(1)}, f32[2]{0:T(128)S(1)}, u32[]{:S(2)}, u32[]{:S(2)}) %collective-permute-start.9) | collective-permute-done | bytes 40 | tf_op jit(solution)/shard_map/ppermute | solution.py:76
  89.8 2.6 %collective-permute-start.10 = (f32[2]{0:T(128)S(1)}, f32[2]{0:T(128)S(1)}, u32[]{:S(2)}, u32[]{:S(2)}) collective-permute-start(f32[2]{0:T(128)S(1)} %add.582), channel_id=1, source_target_pairs={{0,16},{8,24},{16,0},{24,8},{1,17},{9,25},{17,1},{25,9},{2,18},{10... | collective-permute-start | bytes 32 | tf_op jit(solution)/shard_map/ppermute | solution.py:76
  97.1 1.9 collective-permute-start.11
  99.0 4.7 %collective-permute-start.12 = (f32[4,512]{1,0:T(4,128)S(1)}, f32[4,512]{1,0:T(4,128)S(1)}, u32[]{:S(2)}, u32[]{:S(2)}) collective-permute-start(f32[4,512]{1,0:T(4,128)S(1)} %get-tuple-element.113), channel_id=1, source_target_pairs={{1,0},{2,1},{3,2},{4,3},{5,4},{6,5},{7,6},{9,8},{10,9},{11,10},{12... | collective-permute-start | bytes 24584 | tf_op jit(solution)/shard_map/ppermute | solution.py:51
  106.5 2.6 %collective-permute-start.24 = (f32[1,64,512]{2,0,1:T(1,128)}, f32[1,64,512]{2,0,1:T(1,128)}, u32[]{:S(2)}, u32[]{:S(2)}) collective-permute-start(f32[1,64,512]{2,0,1:T(1,128)} %get-tuple-element.78), channel_id=1, source_target_pairs={{0,1},{1,2},{2,3},{3,4},{4,5},{5,6},{6,7},{8,9},{9,10},{10,11},{11... | collective-permute-start | bytes 393224 | tf_op jit(solution)/shard_map/ppermute | solution.py:50
  116.6 4.0 %multiply_reduce_fusion = f32[8,512]{1,0:T(8,128)S(1)} fusion(f32[8,512,512]{2,1,0:T(8,128)} %param.18, f32[8,512]{1,0:T(8,128)S(1)} %subtract_select_fusion), kind=kLoop, calls=%fused_computation.3 | loop fusion | flops 4190208 | bytes 8421376 | tf_op jit(solution)/shard_map/reduce_sum | solution.py:111
  125.4 2.4 %pad_maximum_fusion.10 = f32[4]{0:T(128)S(1)} fusion(f32[1]{0:T(128)} %bitcast.35, f32[1]{0:T(128)} %bitcast.34, f32[1]{0:T(128)} %bitcast.33, f32[1]{0:T(128)} %bitcast.32), kind=kLoop, calls=%fused_computation.204 | loop fusion | flops 12 | bytes 32 | tf_op jit(solution)/shard_map/stack | solution.py:129
  129.0 2.4 %fusion.126 = f32[4]{0:T(128)S(1)} fusion(f32[4]{0:T(128)S(1)} %collective-permute-done.16, f32[1]{0:T(128)} %bitcast.35, f32[1]{0:T(128)} %bitcast.34, f32[1]{0:T(128)} %bitcast.33, f32[1]{0:T(128)} %bitcast.32), kind=kLoop, calls=%fused_computation.233 | loop fusion | flops 16 | bytes 48 | tf_op jit(solution)/shard_map/add | solution.py:76
  132.2 2.8 %collective-permute-done.17 = f32[4]{0:T(128)S(1)} collective-permute-done((f32[4]{0:T(128)S(1)}, f32[4]{0:T(128)S(1)}, u32[]{:S(2)}, u32[]{:S(2)}) %collective-permute-start.17) | collective-permute-done | bytes 48 | tf_op jit(solution)/shard_map/ppermute | solution.py:76
  135.0 2.4 %fusion.128 = f32[4]{0:T(128)S(1)} fusion(f32[4]{0:T(128)S(1)} %collective-permute-done.17, f32[4]{0:T(128)S(1)} %collective-permute-done.16, f32[1]{0:T(128)} %bitcast.35, f32[1]{0:T(128)} %bitcast.34, f32[1]{0:T(128)} %bitcast.33, f32[1]{0:T(128)} %bitcast.32), kind=kLoop, calls=%fused_computation.235 | loop fusion | flops 20 | bytes 64 | tf_op jit(solution)/shard_map/add | solution.py:76
  138.8 2.1 %collective-permute-done.18 = f32[4]{0:T(128)S(1)} collective-permute-done((f32[4]{0:T(128)S(1)}, f32[4]{0:T(128)S(1)}, u32[]{:S(2)}, u32[]{:S(2)}) %collective-permute-start.18) | collective-permute-done | bytes 48 | tf_op jit(solution)/shard_map/ppermute | solution.py:76
  141.0 5.4 %collective-permute-start.19 = (f32[4]{0:T(128)S(1)}, f32[4]{0:T(128)S(1)}, u32[]{:S(2)}, u32[]{:S(2)}) collective-permute-start(f32[4]{0:T(128)S(1)} %add.613), channel_id=1, source_target_pairs={{0,8},{8,0},{16,24},{24,16},{1,9},{9,1},{17,25},{25,17},{2,10},{10... | collective-permute-start | bytes 56 | tf_op jit(solution)/shard_map/ppermute | solution.py:76
  147.9 2.7 %collective-permute-start.20 = (f32[4]{0:T(128)S(1)}, f32[4]{0:T(128)S(1)}, u32[]{:S(2)}, u32[]{:S(2)}) collective-permute-start(f32[4]{0:T(128)S(1)} %add.614), channel_id=1, source_target_pairs={{0,16},{8,24},{16,0},{24,8},{1,17},{9,25},{17,1},{25,9},{2,18},{10... | collective-permute-start | bytes 56 | tf_op jit(solution)/shard_map/ppermute | solution.py:76
  152.3 4.6 %collective-permute-start.13 = (f32[4,8,512]{2,1,0:T(8,128)}, f32[4,8,512]{2,1,0:T(8,128)}, u32[]{:S(2)}, u32[]{:S(2)}) collective-permute-start(f32[4,8,512]{2,1,0:T(8,128)} %pad_maximum_fusion.8), channel_id=1, source_target_pairs={{0,24},{1,25},{2,26},{3,27},{4,28},{5,29},{6,30},{7,31}} | collective-permute-start | bytes 196616 | tf_op jit(solution)/shard_map/ppermute | solution.py:143
  165.2 4.1 %fusion.14 = f32[8,64,512]{2,0,1:T(8,128)S(1)} fusion(f32[8,64,512]{2,0,1:T(8,128)S(1)} %fusion.21, f32[1,64,512]{2,0,1:T(1,128)} %collective-permute-done.24, f32[1,64,512]{2,0,1:T(1,128)} %collective-permute-done.23, f32[8,64,511]{2,0,1:T(8,128)} %get-tuple-element.76, f32[8,64,511]{2,0,1:T(8,128)} %get-tuple-element.75, ...), kind=kLoop, calls=%fused_computation.25 | loop fusion | flops 2621440 | bytes 8613888 | tf_op jit(solution)/shard_map/div | solution.py:21
  170.2 1.9 collective-permute-start.25
  172.1 2.4 %collective-permute-start.26 = (f32[1,64,512]{2,0,1:T(1,128)S(1)}, f32[1,64,512]{2,0,1:T(1,128)S(1)}, u32[]{:S(2)}, u32[]{:S(2)}) collective-permute-start(f32[1,64,512]{2,0,1:T(1,128)S(1)} %get-tuple-element.72), channel_id=1, source_target_pairs={{0,1},{1,2},{2,3},{3,4},{4,5},{5,6},{6,7},{8,9},{9,10},{10,11},{11... | collective-permute-start | bytes 393224 | tf_op jit(solution)/shard_map/ppermute | solution.py:50
  176.1 3.2 %collective-permute-done.26 = f32[1,64,512]{2,0,1:T(1,128)S(1)} collective-permute-done((f32[1,64,512]{2,0,1:T(1,128)S(1)}, f32[1,64,512]{2,0,1:T(1,128)S(1)}, u32[]{:S(2)}, u32[]{:S(2)}) %collective-permute-start.26) | collective-permute-done | bytes 131104 | tf_op jit(solution)/shard_map/ppermute | solution.py:50
  179.3 2.0 %fusion.7 = (f32[8,64,512]{2,0,1:T(8,128)S(1)}, f32[8,64,512]{2,0,1:T(8,128)S(1)}) fusion(f32[8,64,512]{2,0,1:T(8,128)S(1)} %fusion.14, f32[1,64,512]{2,0,1:T(1,128)S(1)} %collective-permute-done.26, f32[1,64,512]{2,0,1:T(1,128)S(1)} %collective-permute-done.25, f32[8,64,511]{2,0,1:T(8,128)S(1)} %get-tuple-element.70, ...), kind=kLoop, calls=%fused_computation.16 | loop fusion | flops 2621440 | bytes 9662464 | tf_op jit(solution)/shard_map/div | solution.py:21
  183.7 2.4 %collective-permute-start.28 = (f32[1,64,512]{2,0,1:T(1,128)S(1)}, f32[1,64,512]{2,0,1:T(1,128)S(1)}, u32[]{:S(2)}, u32[]{:S(2)}) collective-permute-start(f32[1,64,512]{2,0,1:T(1,128)S(1)} %get-tuple-element.60), channel_id=1, source_target_pairs={{0,1},{1,2},{2,3},{3,4},{4,5},{5,6},{6,7},{8,9},{9,10},{10,11},{11... | collective-permute-start | bytes 393224 | tf_op jit(solution)/shard_map/ppermute | solution.py:50
  186.5 4.5 %collective-permute-done.28 = f32[1,64,512]{2,0,1:T(1,128)S(1)} collective-permute-done((f32[1,64,512]{2,0,1:T(1,128)S(1)}, f32[1,64,512]{2,0,1:T(1,128)S(1)}, u32[]{:S(2)}, u32[]{:S(2)}) %collective-permute-start.28) | collective-permute-done | bytes 131104 | tf_op jit(solution)/shard_map/ppermute | solution.py:50
  (192 shorter events, 78.5 us)
Async XLA Ops:
  3.5 43.6 %collective-permute-start.2 = (f32[4,512]{1,0:T(4,128)}, f32[4,512]{1,0:T(4,128)}, u32[]{:S(2)}, u32[]{:S(2)}) collective-permute-start(f32[4,512]{1,0:T(4,128)} %get-tuple-element.116), channel_id=1, source_target_pairs={{0,1},{1,2},{2,3},{3,4},{4,5},{5,6},{6,7},{8,9},{9,10},{10,11},{11... | collective-permute-start | bytes 24584 | tf_op jit(solution)/shard_map/ppermute | solution.py:50
  5.4 41.7 %collective-permute-start.3 = (f32[4,512]{1,0:T(4,128)}, f32[4,512]{1,0:T(4,128)}, u32[]{:S(2)}, u32[]{:S(2)}) collective-permute-start(f32[4,512]{1,0:T(4,128)} %get-tuple-element.117), channel_id=1, source_target_pairs={{1,0},{2,1},{3,2},{4,3},{5,4},{6,5},{7,6},{9,8},{10,9},{11,10},{12... | collective-permute-start | bytes 24584 | tf_op jit(solution)/shard_map/ppermute | solution.py:51
  11.8 22.5 %collective-permute-start.22 = (f32[1,64,512]{2,0,1:T(1,128)}, f32[1,64,512]{2,0,1:T(1,128)}, u32[]{:S(2)}, u32[]{:S(2)}) collective-permute-start(f32[1,64,512]{2,0,1:T(1,128)} %bitcast.94), channel_id=1, source_target_pairs={{0,1},{1,2},{2,3},{3,4},{4,5},{5,6},{6,7},{8,9},{9,10},{10,11},{11... | collective-permute-start | bytes 393224 | tf_op jit(solution)/shard_map/ppermute | solution.py:50
  14.5 24.3 %collective-permute-start.21 = (f32[1,64,512]{2,0,1:T(1,128)}, f32[1,64,512]{2,0,1:T(1,128)}, u32[]{:S(2)}, u32[]{:S(2)}) collective-permute-start(f32[1,64,512]{2,0,1:T(1,128)} %bitcast.95), channel_id=1, source_target_pairs={{1,0},{2,1},{3,2},{4,3},{5,4},{6,5},{7,6},{9,8},{10,9},{11,10},{12... | collective-permute-start | bytes 393224 | tf_op jit(solution)/shard_map/ppermute | solution.py:51
  26.0 19.1 %collective-permute-start = (f32[4,3,8,512]{3,0,2,1:T(4,128)}, f32[4,3,8,512]{3,0,2,1:T(4,128)}, u32[]{:S(2)}, u32[]{:S(2)}) collective-permute-start(f32[4,3,8,512]{3,0,2,1:T(4,128)} %get-tuple-element.88), channel_id=1, source_target_pairs={{0,1},{1,2},{2,3},{3,4},{4,5},{5,6},{6,7},{8,9},{9,10},{10,11},{11... | collective-permute-start | bytes 589832 | tf_op jit(solution)/shard_map/ppermute | solution.py:50
  34.2 10.8 %collective-permute-start.1 = (f32[4,3,8,512]{3,0,2,1:T(4,128)}, f32[4,3,8,512]{3,0,2,1:T(4,128)S(1)}, u32[]{:S(2)}, u32[]{:S(2)}) collective-permute-start(f32[4,3,8,512]{3,0,2,1:T(4,128)} %get-tuple-element.89), channel_id=1, source_target_pairs={{1,0},{2,1},{3,2},{4,3},{5,4},{6,5},{7,6},{9,8},{10,9},{11,10},{12... | collective-permute-start | bytes 589832 | tf_op jit(solution)/shard_map/ppermute | solution.py:51
  56.8 8.1 %collective-permute-start.4 = (f32[4,512]{1,0:T(4,128)S(1)}, f32[4,512]{1,0:T(4,128)S(1)}, u32[]{:S(2)}, u32[]{:S(2)}) collective-permute-start(f32[4,512]{1,0:T(4,128)S(1)} %get-tuple-element.114), channel_id=1, source_target_pairs={{0,1},{1,2},{2,3},{3,4},{4,5},{5,6},{6,7},{8,9},{9,10},{10,11},{11... | collective-permute-start | bytes 24584 | tf_op jit(solution)/shard_map/ppermute | solution.py:50
  58.7 6.1 %collective-permute-start.5 = (f32[4,512]{1,0:T(4,128)S(1)}, f32[4,512]{1,0:T(4,128)S(1)}, u32[]{:S(2)}, u32[]{:S(2)}) collective-permute-start(f32[4,512]{1,0:T(4,128)S(1)} %get-tuple-element.115), channel_id=1, source_target_pairs={{1,0},{2,1},{3,2},{4,3},{5,4},{6,5},{7,6},{9,8},{10,9},{11,10},{12... | collective-permute-start | bytes 24584 | tf_op jit(solution)/shard_map/ppermute | solution.py:51
  64.9 32.1 %copy-start.11 = (f32[8,8]{1,0:T(8,128)S(1)}, f32[8,8]{1,0:T(8,128)}, u32[]{:S(2)}) copy-start(f32[8,8]{1,0:T(8,128)} %copy-done.10) | copy-start | bytes 772
  65.9 45.9 %copy-start.16 = (pred[12]{0:T(512)(128)(4,1)S(1)}, pred[12]{0:T(512)(128)(4,1)}, u32[]{:S(2)}) copy-start(pred[12]{0:T(512)(128)(4,1)} %slice.582) | copy-start | bytes 40
  75.4 1.1 collective-permute-start.6
  77.8 3.5 %collective-permute-start.7 = (f32[2]{0:T(128)S(1)}, f32[2]{0:T(128)S(1)}, u32[]{:S(2)}, u32[]{:S(2)}) collective-permute-start(f32[2]{0:T(128)S(1)} %fusion.127), channel_id=1, source_target_pairs={{0,2},{1,3},{2,0},{3,1},{4,6},{5,7},{6,4},{7,5},{8,10},{9,11},{10,... | collective-permute-start | bytes 32 | tf_op jit(solution)/shard_map/ppermute | solution.py:76
  82.7 3.5 %collective-permute-start.8 = (f32[2]{0:T(128)S(1)}, f32[2]{0:T(128)S(1)}, u32[]{:S(2)}, u32[]{:S(2)}) collective-permute-start(f32[2]{0:T(128)S(1)} %fusion.129), channel_id=1, source_target_pairs={{0,4},{1,5},{2,6},{3,7},{4,0},{5,1},{6,2},{7,3},{8,12},{9,13},{10,... | collective-permute-start | bytes 32 | tf_op jit(solution)/shard_map/ppermute | solution.py:76
  86.3 3.5 %collective-permute-start.9 = (f32[2]{0:T(128)S(1)}, f32[2]{0:T(128)S(1)}, u32[]{:S(2)}, u32[]{:S(2)}) collective-permute-start(f32[2]{0:T(128)S(1)} %add.581), channel_id=1, source_target_pairs={{0,8},{8,0},{16,24},{24,16},{1,9},{9,1},{17,25},{25,17},{2,10},{10... | collective-permute-start | bytes 32 | tf_op jit(solution)/shard_map/ppermute | solution.py:76
  89.8 4.4 %collective-permute-start.10 = (f32[2]{0:T(128)S(1)}, f32[2]{0:T(128)S(1)}, u32[]{:S(2)}, u32[]{:S(2)}) collective-permute-start(f32[2]{0:T(128)S(1)} %add.582), channel_id=1, source_target_pairs={{0,16},{8,24},{16,0},{24,8},{1,17},{9,25},{17,1},{25,9},{2,18},{10... | collective-permute-start | bytes 32 | tf_op jit(solution)/shard_map/ppermute | solution.py:76
  97.1 12.0 %collective-permute-start.11 = (f32[4,512]{1,0:T(4,128)S(1)}, f32[4,512]{1,0:T(4,128)S(1)}, u32[]{:S(2)}, u32[]{:S(2)}) collective-permute-start(f32[4,512]{1,0:T(4,128)S(1)} %get-tuple-element.112), channel_id=1, source_target_pairs={{0,1},{1,2},{2,3},{3,4},{4,5},{5,6},{6,7},{8,9},{9,10},{10,11},{11... | collective-permute-start | bytes 24584 | tf_op jit(solution)/shard_map/ppermute | solution.py:50
  99.0 66.2 %copy-start.1 = (f32[1,8,64,512]{3,2,1,0:T(8,128)S(1)}, f32[1,8,64,512]{3,2,1,0:T(8,128)}, u32[]{:S(2)}) copy-start(f32[1,8,64,512]{3,2,1,0:T(8,128)} %param.15) | copy-start | bytes 3145732
  99.0 10.1 %collective-permute-start.12 = (f32[4,512]{1,0:T(4,128)S(1)}, f32[4,512]{1,0:T(4,128)S(1)}, u32[]{:S(2)}, u32[]{:S(2)}) collective-permute-start(f32[4,512]{1,0:T(4,128)S(1)} %get-tuple-element.113), channel_id=1, source_target_pairs={{1,0},{2,1},{3,2},{4,3},{5,4},{6,5},{7,6},{9,8},{10,9},{11,10},{12... | collective-permute-start | bytes 24584 | tf_op jit(solution)/shard_map/ppermute | solution.py:51
  104.6 60.6 %collective-permute-start.23 = (f32[1,64,512]{2,0,1:T(1,128)}, f32[1,64,512]{2,0,1:T(1,128)}, u32[]{:S(2)}, u32[]{:S(2)}) collective-permute-start(f32[1,64,512]{2,0,1:T(1,128)} %get-tuple-element.77), channel_id=1, source_target_pairs={{1,0},{2,1},{3,2},{4,3},{5,4},{6,5},{7,6},{9,8},{10,9},{11,10},{12... | collective-permute-start | bytes 393224 | tf_op jit(solution)/shard_map/ppermute | solution.py:51
  106.5 58.7 %collective-permute-start.24 = (f32[1,64,512]{2,0,1:T(1,128)}, f32[1,64,512]{2,0,1:T(1,128)}, u32[]{:S(2)}, u32[]{:S(2)}) collective-permute-start(f32[1,64,512]{2,0,1:T(1,128)} %get-tuple-element.78), channel_id=1, source_target_pairs={{0,1},{1,2},{2,3},{3,4},{4,5},{5,6},{6,7},{8,9},{9,10},{10,11},{11... | collective-permute-start | bytes 393224 | tf_op jit(solution)/shard_map/ppermute | solution.py:50
  122.0 52.5 %collective-permute-start.14 = (f32[4,8,512]{2,1,0:T(8,128)}, f32[4,8,512]{2,1,0:T(8,128)S(1)}, u32[]{:S(2)}, u32[]{:S(2)}) collective-permute-start(f32[4,8,512]{2,1,0:T(8,128)} %pad_maximum_fusion.8), channel_id=1, source_target_pairs={{8,24},{9,25},{10,26},{11,27},{12,28},{13,29},{14,30},{15,31}} | collective-permute-start | bytes 196616 | tf_op jit(solution)/shard_map/ppermute | solution.py:143
  122.7 51.8 %collective-permute-start.15 = (f32[4,8,512]{2,1,0:T(8,128)}, f32[4,8,512]{2,1,0:T(8,128)}, u32[]{:S(2)}, u32[]{:S(2)}) collective-permute-start(f32[4,8,512]{2,1,0:T(8,128)} %pad_maximum_fusion.8), channel_id=1, source_target_pairs={{16,24},{17,25},{18,26},{19,27},{20,28},{21,29},{22,30},{23,31}} | collective-permute-start | bytes 196616 | tf_op jit(solution)/shard_map/ppermute | solution.py:143
  127.9 1.1 collective-permute-start.16
  131.4 3.5 %collective-permute-start.17 = (f32[4]{0:T(128)S(1)}, f32[4]{0:T(128)S(1)}, u32[]{:S(2)}, u32[]{:S(2)}) collective-permute-start(f32[4]{0:T(128)S(1)} %fusion.126), channel_id=1, source_target_pairs={{0,2},{1,3},{2,0},{3,1},{4,6},{5,7},{6,4},{7,5},{8,10},{9,11},{10,... | collective-permute-start | bytes 56 | tf_op jit(solution)/shard_map/ppermute | solution.py:76
  137.4 3.5 %collective-permute-start.18 = (f32[4]{0:T(128)S(1)}, f32[4]{0:T(128)S(1)}, u32[]{:S(2)}, u32[]{:S(2)}) collective-permute-start(f32[4]{0:T(128)S(1)} %fusion.128), channel_id=1, source_target_pairs={{0,4},{1,5},{2,6},{3,7},{4,0},{5,1},{6,2},{7,3},{8,12},{9,13},{10,... | collective-permute-start | bytes 56 | tf_op jit(solution)/shard_map/ppermute | solution.py:76
  141.0 6.9 %collective-permute-start.19 = (f32[4]{0:T(128)S(1)}, f32[4]{0:T(128)S(1)}, u32[]{:S(2)}, u32[]{:S(2)}) collective-permute-start(f32[4]{0:T(128)S(1)} %add.613), channel_id=1, source_target_pairs={{0,8},{8,0},{16,24},{24,16},{1,9},{9,1},{17,25},{25,17},{2,10},{10... | collective-permute-start | bytes 56 | tf_op jit(solution)/shard_map/ppermute | solution.py:76
  147.9 4.4 %collective-permute-start.20 = (f32[4]{0:T(128)S(1)}, f32[4]{0:T(128)S(1)}, u32[]{:S(2)}, u32[]{:S(2)}) collective-permute-start(f32[4]{0:T(128)S(1)} %add.614), channel_id=1, source_target_pairs={{0,16},{8,24},{16,0},{24,8},{1,17},{9,25},{17,1},{25,9},{2,18},{10... | collective-permute-start | bytes 56 | tf_op jit(solution)/shard_map/ppermute | solution.py:76
  152.3 22.2 %collective-permute-start.13 = (f32[4,8,512]{2,1,0:T(8,128)}, f32[4,8,512]{2,1,0:T(8,128)}, u32[]{:S(2)}, u32[]{:S(2)}) collective-permute-start(f32[4,8,512]{2,1,0:T(8,128)} %pad_maximum_fusion.8), channel_id=1, source_target_pairs={{0,24},{1,25},{2,26},{3,27},{4,28},{5,29},{6,30},{7,31}} | collective-permute-start | bytes 196616 | tf_op jit(solution)/shard_map/ppermute | solution.py:143
  170.2 5.9 %collective-permute-start.25 = (f32[1,64,512]{2,0,1:T(1,128)S(1)}, f32[1,64,512]{2,0,1:T(1,128)S(1)}, u32[]{:S(2)}, u32[]{:S(2)}) collective-permute-start(f32[1,64,512]{2,0,1:T(1,128)S(1)} %get-tuple-element.71), channel_id=1, source_target_pairs={{1,0},{2,1},{3,2},{4,3},{5,4},{6,5},{7,6},{9,8},{10,9},{11,10},{12... | collective-permute-start | bytes 393224 | tf_op jit(solution)/shard_map/ppermute | solution.py:51
  172.1 7.2 %collective-permute-start.26 = (f32[1,64,512]{2,0,1:T(1,128)S(1)}, f32[1,64,512]{2,0,1:T(1,128)S(1)}, u32[]{:S(2)}, u32[]{:S(2)}) collective-permute-start(f32[1,64,512]{2,0,1:T(1,128)S(1)} %get-tuple-element.72), channel_id=1, source_target_pairs={{0,1},{1,2},{2,3},{3,4},{4,5},{5,6},{6,7},{8,9},{9,10},{10,11},{11... | collective-permute-start | bytes 393224 | tf_op jit(solution)/shard_map/ppermute | solution.py:50
  181.8 4.6 %collective-permute-start.27 = (f32[1,64,512]{2,0,1:T(1,128)S(1)}, f32[1,64,512]{2,0,1:T(1,128)S(1)}, u32[]{:S(2)}, u32[]{:S(2)}) collective-permute-start(f32[1,64,512]{2,0,1:T(1,128)S(1)} %get-tuple-element.59), channel_id=1, source_target_pairs={{1,0},{2,1},{3,2},{4,3},{5,4},{6,5},{7,6},{9,8},{10,9},{11,10},{12... | collective-permute-start | bytes 393224 | tf_op jit(solution)/shard_map/ppermute | solution.py:51
  183.7 7.2 %collective-permute-start.28 = (f32[1,64,512]{2,0,1:T(1,128)S(1)}, f32[1,64,512]{2,0,1:T(1,128)S(1)}, u32[]{:S(2)}, u32[]{:S(2)}) collective-permute-start(f32[1,64,512]{2,0,1:T(1,128)S(1)} %get-tuple-element.60), channel_id=1, source_target_pairs={{0,1},{1,2},{2,3},{3,4},{4,5},{5,6},{6,7},{8,9},{9,10},{10,11},{11... | collective-permute-start | bytes 393224 | tf_op jit(solution)/shard_map/ppermute | solution.py:50
  (20 other events, 216.6 us)

commit v2 on v1

--- a/solution.py
+++ b/solution.py
@@ -68,14 +68,17 @@
     return q
 
 
+def allsum_axis(v, axis):
+    count = lax.axis_size(axis)
+    step = 1
+    while step < count:
+        v = v + lax.ppermute(v, axis, [(i, i ^ step) for i in range(count)])
+        step *= 2
+    return v
+
+
 def allsum(v):
-    for axis in ("slab", "side"):
-        count = lax.axis_size(axis)
-        step = 1
-        while step < count:
-            v = v + lax.ppermute(v, axis, [(i, i ^ step) for i in range(count)])
-            step *= 2
-    return v
+    return allsum_axis(allsum_axis(v, "slab"), "side")
 
 
 def body(
@@ -95,9 +98,14 @@
     own_live = own * live
     onehot = (block_row[None, :] == jnp.arange(slab_rows)[:, None]).astype(jnp.float32) * own[:, 0][None, :]
 
-    packed = jnp.stack([start_here[:, :BAND], force_here[:, :BAND], coef_here[:, :BAND]])
-    packed = jnp.moveaxis(rims(jnp.moveaxis(packed, 1, 0), HALO), 0, 1)
-    init_band, force_band, coef_band = packed[0], packed[1], packed[2]
+    packed = rims(
+        jnp.concatenate([start_here[:, :BAND], force_here[:, :BAND], coef_here[:, :BAND]], axis=1), HALO
+    )
+    init_band, force_band, coef_band = (
+        packed[:, :BAND],
+        packed[:, BAND : 2 * BAND],
+        packed[:, 2 * BAND :],
+    )
     global_row = slab_id * slab_rows + jnp.arange(slab_rows + 2 * HALO) - HALO
     total_rows = slab_rows * lax.axis_size("slab")
     row_ok = ((global_row >= 0) & (global_row < total_rows))[:, None, None]
@@ -125,23 +133,30 @@
     tilde_two, band_two = evaluate(disp_two)
     resid_two = tilde_two - disp_two
     newer = resid_two - resid_one
-    sums = allsum(
-        jnp.stack(
-            [
-                jnp.sum(newer * newer),
-                jnp.sum(newer * diff_one),
-                jnp.sum(newer * resid_two),
-                jnp.sum(diff_one * resid_two),
-            ]
-        )
+    partial = jnp.stack(
+        [
+            jnp.sum(newer * newer),
+            jnp.sum(newer * diff_one),
+            jnp.sum(newer * resid_two),
+            jnp.sum(diff_one * resid_two),
+        ]
     )
-    gram_nn, gram_no, proj_new, proj_old = sums[0], sums[1], sums[2], sums[3]
-
-    outgoing = jnp.stack([tilde_two, tilde_one, tilde_zero, resid_two])
+    patches_here = tilde_two.shape[0]
+    outgoing = jnp.concatenate(
+        [
+            jnp.concatenate([tilde_two, tilde_one, tilde_zero, resid_two], axis=0),
+            jnp.concatenate([partial, jnp.zeros((line_cells - 4,), jnp.float32)])[None],
+        ],
+        axis=0,
+    )
     gathered = outgoing
     for source in range(side_count - 1):
         gathered = gathered + lax.ppermute(outgoing, "side", [(source, side_count - 1)])
-    tilde_two, tilde_one, tilde_zero, resid_two = gathered[0], gathered[1], gathered[2], gathered[3]
+    sums = allsum_axis(gathered[4 * patches_here, :4], "slab")
+    gram_nn, gram_no, proj_new, proj_old = sums[0], sums[1], sums[2], sums[3]
+    tilde_two, tilde_one, tilde_zero, resid_two = (
+        gathered[k * patches_here : (k + 1) * patches_here] for k in range(4)
+    )
 
     shift_two = 0.001 * (gram_nn + gram_aa) + 1e-06
     diag_new = gram_nn + shift_two

time: 196 us -> 180 us (0.918)
  the two profiles are of different devices: /device:TPU:4 before, /device:TPU:1 now
where the time goes in v2:
time: 180 us; the launch traced here: 179 us
  starting transfers between devices  71.2 us (40%)
  other arithmetic  49.2 us (27%)
  local copies, waits for them, and re-layouts  33.8 us (19%)
  waiting for transfers between devices  13.3 us (7%)
  between operations  11.1 us (6%)
    ppermute x8, starting transfers between devices, rims(): low = lax.ppermute(block[block.shape[0] - width:], 'slab', forward)  34.5 us
    ppermute x8, starting transfers between devices, rims(): high = lax.ppermute(block[:width], 'slab', backward)  17.7 us
    div x3, other arithmetic, stencil(): return (rhs + total) / (6.0 + coef)  13.4 us
    reduce_sum x3, other arithmetic, evaluate(): tilde = own_live * jnp.sum(compliance * loaded[:, None, :], axis=-1)  12 us
    ppermute x8, starting transfers between devices, allsum_axis(): v = v + lax.ppermute(v, axis, [(i, i ^ step) for i in range(count)])  11.2 us
    ppermute x8, waiting for transfers between devices, allsum_axis(): v = v + lax.ppermute(v, axis, [(i, i ^ step) for i in range(count)])  10.1 us
    unnamed x59, local copies, waits for them, and re-layouts  9.87 us
    ppermute x3, starting transfers between devices, body(): lax.ppermute(outgoing, 'side', [(source, side_count - 1)])  7.81 us
  transfers between devices with their start and end apart: 27, of which 11 were waited for; matrix products, arithmetic and copies ran while one was open for 28% of the time, Pallas kernels for 0%

profile of v2, /device:TPU:1, one launch (start us, length us, event | category | flops | bytes accessed | tf_op | source)
XLA Modules:
  0.0 178.7 jit_solution(13725872391138403533)
XLA Ops:
  3.5 4.5 %collective-permute-start.2 = (f32[4,512]{1,0:T(4,128)}, f32[4,512]{1,0:T(4,128)}, u32[]{:S(2)}, u32[]{:S(2)}) collective-permute-start(f32[4,512]{1,0:T(4,128)} %get-tuple-element.113), channel_id=1, source_target_pairs={{0,1},{1,2},{2,3},{3,4},{4,5},{5,6},{6,7},{8,9},{9,10},{10,11},{11... | collective-permute-start | bytes 24584 | tf_op jit(solution)/shard_map/ppermute | solution.py:50
  8.0 1.9 %collective-permute-start.3 = (f32[4,512]{1,0:T(4,128)}, f32[4,512]{1,0:T(4,128)}, u32[]{:S(2)}, u32[]{:S(2)}) collective-permute-start(f32[4,512]{1,0:T(4,128)} %get-tuple-element.114), channel_id=1, source_target_pairs={{1,0},{2,1},{3,2},{4,3},{5,4},{6,5},{7,6},{9,8},{10,9},{11,10},{12... | collective-permute-start | bytes 24584 | tf_op jit(solution)/shard_map/ppermute | solution.py:51
  11.7 3.6 %collective-permute-start.20 = (f32[1,64,512]{2,0,1:T(1,128)}, f32[1,64,512]{2,0,1:T(1,128)}, u32[]{:S(2)}, u32[]{:S(2)}) collective-permute-start(f32[1,64,512]{2,0,1:T(1,128)} %bitcast.79), channel_id=1, source_target_pairs={{0,1},{1,2},{2,3},{3,4},{4,5},{5,6},{6,7},{8,9},{9,10},{10,11},{11... | collective-permute-start | bytes 393224 | tf_op jit(solution)/shard_map/ppermute | solution.py:50
  16.2 2.0 %collective-permute-start.19 = (f32[1,64,512]{2,0,1:T(1,128)}, f32[1,64,512]{2,0,1:T(1,128)}, u32[]{:S(2)}, u32[]{:S(2)}) collective-permute-start(f32[1,64,512]{2,0,1:T(1,128)} %bitcast.80), channel_id=1, source_target_pairs={{1,0},{2,1},{3,2},{4,3},{5,4},{6,5},{7,6},{9,8},{10,9},{11,10},{12... | collective-permute-start | bytes 393224 | tf_op jit(solution)/shard_map/ppermute | solution.py:51
  18.2 1.8 %copy.47 = f32[1,8,64,512]{3,1,2,0:T(8,128)S(1)} copy(f32[1,8,64,512]{3,2,1,0:T(8,128)} %param.17) | data formatting | bytes 2097152 | tf_op args[2]
  20.1 1.8 %copy.46 = f32[1,8,64,512]{3,1,2,0:T(8,128)S(1)} copy(f32[1,8,64,512]{3,2,1,0:T(8,128)} %param.15) | data formatting | bytes 2097152 | tf_op args[0]
  21.9 2.2 %copy.45 = f32[1,8,64,512]{3,1,2,0:T(8,128)S(1)} copy(f32[1,8,64,512]{3,2,1,0:T(8,128)} %param.16) | data formatting | bytes 2097152 | tf_op args[1]
  25.2 3.6 %collective-permute-start = (f32[4,24,512]{2,0,1:T(4,128)}, f32[4,24,512]{2,0,1:T(4,128)}, u32[]{:S(2)}, u32[]{:S(2)}) collective-permute-start(f32[4,24,512]{2,0,1:T(4,128)} %get-tuple-element.86), channel_id=1, source_target_pairs={{0,1},{1,2},{2,3},{3,4},{4,5},{5,6},{6,7},{8,9},{9,10},{10,11},{11... | collective-permute-start | bytes 589832 | tf_op jit(solution)/shard_map/ppermute | solution.py:50
  37.1 1.9 %collective-permute-start.1 = (f32[4,24,512]{2,0,1:T(4,128)}, f32[4,24,512]{2,0,1:T(4,128)S(1)}, u32[]{:S(2)}, u32[]{:S(2)}) collective-permute-start(f32[4,24,512]{2,0,1:T(4,128)} %get-tuple-element.87), channel_id=1, source_target_pairs={{1,0},{2,1},{3,2},{4,3},{5,4},{6,5},{7,6},{9,8},{10,9},{11,10},{12... | collective-permute-start | bytes 589832 | tf_op jit(solution)/shard_map/ppermute | solution.py:51
  39.0 4.5 %fusion.21 = f32[8,64,512]{2,0,1:T(8,128)S(1)} fusion(f32[8,64,512]{2,0,1:T(8,128)S(1)} %bitcast.84, f32[1,64,512]{2,0,1:T(1,128)} %collective-permute-done.20, f32[1,64,512]{2,0,1:T(1,128)} %collective-permute-done.19, f32[8,64,511]{2,0,1:T(8,128)} %get-tuple-element.81, f32[8,64,511]{2,0,1:T(8,128)} %get-tuple-element.80, ...), kind=kLoop, calls=%fused_computation.34 | loop fusion | flops 2621440 | bytes 8613888 | tf_op jit(solution)/shard_map/div | solution.py:21
  52.1 4.0 %multiply_reduce_fusion.2 = f32[8,512]{1,0:T(8,128)S(1)} fusion(f32[8,512,512]{2,1,0:T(8,128)} %param.18, f32[8,512]{1,0:T(8,128)S(1)} %subtract_select_fusion.2), kind=kLoop, calls=%fused_computation.5 | loop fusion | flops 4190208 | bytes 8421376 | tf_op jit(solution)/shard_map/reduce_sum | solution.py:119
  56.3 3.6 %collective-permute-start.4 = (f32[4,512]{1,0:T(4,128)S(1)}, f32[4,512]{1,0:T(4,128)S(1)}, u32[]{:S(2)}, u32[]{:S(2)}) collective-permute-start(f32[4,512]{1,0:T(4,128)S(1)} %get-tuple-element.111), channel_id=1, source_target_pairs={{0,1},{1,2},{2,3},{3,4},{4,5},{5,6},{6,7},{8,9},{9,10},{10,11},{11... | collective-permute-start | bytes 24584 | tf_op jit(solution)/shard_map/ppermute | solution.py:50
  60.0 1.9 %collective-permute-start.5 = (f32[4,512]{1,0:T(4,128)S(1)}, f32[4,512]{1,0:T(4,128)S(1)}, u32[]{:S(2)}, u32[]{:S(2)}) collective-permute-start(f32[4,512]{1,0:T(4,128)S(1)} %get-tuple-element.112), channel_id=1, source_target_pairs={{1,0},{2,1},{3,2},{4,3},{5,4},{6,5},{7,6},{9,8},{10,9},{11,10},{12... | collective-permute-start | bytes 24584 | tf_op jit(solution)/shard_map/ppermute | solution.py:51
  68.2 4.0 %multiply_reduce_fusion.1 = f32[8,512]{1,0:T(8,128)S(1)} fusion(f32[8,512,512]{2,1,0:T(8,128)} %param.18, f32[8,512]{1,0:T(8,128)S(1)} %subtract_select_fusion.1), kind=kLoop, calls=%fused_computation.4 | loop fusion | flops 4190208 | bytes 8421376 | tf_op jit(solution)/shard_map/reduce_sum | solution.py:119
  76.8 4.8 %collective-permute-start.7 = (f32[2]{0:T(128)S(1)}, f32[2]{0:T(128)S(1)}, u32[]{:S(2)}, u32[]{:S(2)}) collective-permute-start(f32[2]{0:T(128)S(1)} %fusion.135), channel_id=1, source_target_pairs={{0,2},{1,3},{2,0},{3,1},{4,6},{5,7},{6,4},{7,5},{8,10},{9,11},{10,... | collective-permute-start | bytes 32 | tf_op jit(solution)/shard_map/ppermute | solution.py:75
  84.2 2.0 %collective-permute-done.8 = f32[2]{0:T(128)S(1)} collective-permute-done((f32[2]{0:T(128)S(1)}, f32[2]{0:T(128)S(1)}, u32[]{:S(2)}, u32[]{:S(2)}) %collective-permute-start.8) | collective-permute-done | bytes 40 | tf_op jit(solution)/shard_map/ppermute | solution.py:75
  88.6 2.3 %collective-permute-start.10 = (f32[2]{0:T(128)S(1)}, f32[2]{0:T(128)S(1)}, u32[]{:S(2)}, u32[]{:S(2)}) collective-permute-start(f32[2]{0:T(128)S(1)} %add.548), channel_id=1, source_target_pairs={{0,16},{8,24},{16,0},{24,8},{1,17},{9,25},{17,1},{25,9},{2,18},{10... | collective-permute-start | bytes 32 | tf_op jit(solution)/shard_map/ppermute | solution.py:75
  94.7 8.1 %collective-permute-start.11 = (f32[4,512]{1,0:T(4,128)S(1)}, f32[4,512]{1,0:T(4,128)S(1)}, u32[]{:S(2)}, u32[]{:S(2)}) collective-permute-start(f32[4,512]{1,0:T(4,128)S(1)} %get-tuple-element.109), channel_id=1, source_target_pairs={{0,1},{1,2},{2,3},{3,4},{4,5},{5,6},{6,7},{8,9},{9,10},{10,11},{11... | collective-permute-start | bytes 24584 | tf_op jit(solution)/shard_map/ppermute | solution.py:50
  102.8 1.9 %collective-permute-start.12 = (f32[4,512]{1,0:T(4,128)S(1)}, f32[4,512]{1,0:T(4,128)S(1)}, u32[]{:S(2)}, u32[]{:S(2)}) collective-permute-start(f32[4,512]{1,0:T(4,128)S(1)} %get-tuple-element.110), channel_id=1, source_target_pairs={{1,0},{2,1},{3,2},{4,3},{5,4},{6,5},{7,6},{9,8},{10,9},{11,10},{12... | collective-permute-start | bytes 24584 | tf_op jit(solution)/shard_map/ppermute | solution.py:51
  105.6 1.9 %collective-permute-start.21 = (f32[1,64,512]{2,0,1:T(1,128)}, f32[1,64,512]{2,0,1:T(1,128)}, u32[]{:S(2)}, u32[]{:S(2)}) collective-permute-start(f32[1,64,512]{2,0,1:T(1,128)} %get-tuple-element.76), channel_id=1, source_target_pairs={{1,0},{2,1},{3,2},{4,3},{5,4},{6,5},{7,6},{9,8},{10,9},{11,10},{12... | collective-permute-start | bytes 393224 | tf_op jit(solution)/shard_map/ppermute | solution.py:51
  107.5 3.8 %collective-permute-start.22 = (f32[1,64,512]{2,0,1:T(1,128)}, f32[1,64,512]{2,0,1:T(1,128)}, u32[]{:S(2)}, u32[]{:S(2)}) collective-permute-start(f32[1,64,512]{2,0,1:T(1,128)} %get-tuple-element.77), channel_id=1, source_target_pairs={{0,1},{1,2},{2,3},{3,4},{4,5},{5,6},{6,7},{8,9},{9,10},{10,11},{11... | collective-permute-start | bytes 393224 | tf_op jit(solution)/shard_map/ppermute | solution.py:50
  115.4 4.0 %multiply_reduce_fusion = f32[8,512]{1,0:T(8,128)S(1)} fusion(f32[8,512,512]{2,1,0:T(8,128)} %param.18, f32[8,512]{1,0:T(8,128)S(1)} %subtract_select_fusion), kind=kLoop, calls=%fused_computation.3 | loop fusion | flops 4190208 | bytes 8421376 | tf_op jit(solution)/shard_map/reduce_sum | solution.py:119
  120.3 2.6 %concatenate.248 = f32[512]{0:T(512)S(1)} concatenate(f32[1]{0:T(128)} %bitcast.14, f32[1]{0:T(128)} %bitcast.15, f32[1]{0:T(128)} %bitcast.16, f32[1]{0:T(128)} %bitcast.17, f32[508]{0:T(512)S(1)} %broadcast_in_dim.129), dimensions={0} | concatenate | bytes 4096 | tf_op jit(solution)/shard_map/concatenate | solution.py:148
  124.3 6.5 %collective-permute-start.13 = (f32[33,512]{1,0:T(8,128)S(1)}, f32[33,512]{1,0:T(8,128)S(1)}, u32[]{:S(2)}, u32[]{:S(2)}) collective-permute-start(f32[33,512]{1,0:T(8,128)S(1)} %dynamic-update-slice.13), channel_id=1, source_target_pairs={{0,24},{1,25},{2,26},{3,27},{4,28},{5,29},{6,30},{7,31}} | collective-permute-start | bytes 202760 | tf_op jit(solution)/shard_map/ppermute | solution.py:154
  130.8 4.5 %fusion.14 = f32[8,64,512]{2,0,1:T(8,128)S(1)} fusion(f32[8,64,512]{2,0,1:T(8,128)S(1)} %fusion.21, f32[1,64,512]{2,0,1:T(1,128)} %collective-permute-done.22, f32[1,64,512]{2,0,1:T(1,128)} %collective-permute-done.21, f32[8,64,511]{2,0,1:T(8,128)} %get-tuple-element.75, f32[8,64,511]{2,0,1:T(8,128)} %get-tuple-element.74, ...), kind=kLoop, calls=%fused_computation.25 | loop fusion | flops 2621440 | bytes 8613888 | tf_op jit(solution)/shard_map/div | solution.py:21
  138.7 1.9 %collective-permute-start.23 = (f32[1,64,512]{2,0,1:T(1,128)S(1)}, f32[1,64,512]{2,0,1:T(1,128)S(1)}, u32[]{:S(2)}, u32[]{:S(2)}) collective-permute-start(f32[1,64,512]{2,0,1:T(1,128)S(1)} %get-tuple-element.70), channel_id=1, source_target_pairs={{1,0},{2,1},{3,2},{4,3},{5,4},{6,5},{7,6},{9,8},{10,9},{11,10},{12... | collective-permute-start | bytes 393224 | tf_op jit(solution)/shard_map/ppermute | solution.py:51
  140.7 3.6 %collective-permute-start.24 = (f32[1,64,512]{2,0,1:T(1,128)S(1)}, f32[1,64,512]{2,0,1:T(1,128)S(1)}, u32[]{:S(2)}, u32[]{:S(2)}) collective-permute-start(f32[1,64,512]{2,0,1:T(1,128)S(1)} %get-tuple-element.71), channel_id=1, source_target_pairs={{0,1},{1,2},{2,3},{3,4},{4,5},{5,6},{6,7},{8,9},{9,10},{10,11},{11... | collective-permute-start | bytes 393224 | tf_op jit(solution)/shard_map/ppermute | solution.py:50
  146.4 2.0 %collective-permute-start.17 = (f32[4]{0:T(128)S(1)}, f32[4]{0:T(128)S(1)}, u32[]{:S(2)}, u32[]{:S(2)}) collective-permute-start(f32[4]{0:T(128)S(1)} %fusion.102), channel_id=1, source_target_pairs={{0,2},{1,3},{2,0},{3,1},{4,6},{5,7},{6,4},{7,5},{8,10},{9,11},{10,... | collective-permute-start | bytes 56 | tf_op jit(solution)/shard_map/ppermute | solution.py:75
  149.8 2.0 %collective-permute-done.18 = f32[4]{0:T(128)S(1)} collective-permute-done((f32[4]{0:T(128)S(1)}, f32[4]{0:T(128)S(1)}, u32[]{:S(2)}, u32[]{:S(2)}) %collective-permute-start.18) | collective-permute-done | bytes 48 | tf_op jit(solution)/shard_map/ppermute | solution.py:75
  161.2 4.5 %fusion.7 = (f32[8,64,512]{2,0,1:T(8,128)S(1)}, f32[8,64,512]{2,0,1:T(8,128)S(1)}) fusion(f32[8,64,512]{2,0,1:T(8,128)S(1)} %fusion.14, f32[1,64,512]{2,0,1:T(1,128)} %copy-done.10, f32[1,64,512]{2,0,1:T(1,128)S(1)} %collective-permute-done.23, f32[8,64,511]{2,0,1:T(8,128)} %get-tuple-element.69, f32[8,64,511]{2,0,1:T(8,128)} %get-tuple-element.68, ...), kind=kLoop, calls=%fused_computation.16 | loop fusion | flops 2621440 | bytes 9662464 | tf_op jit(solution)/shard_map/div | solution.py:21
  166.2 4.1 %collective-permute-start.25 = (f32[1,64,512]{2,0,1:T(1,128)S(1)}, f32[1,64,512]{2,0,1:T(1,128)S(1)}, u32[]{:S(2)}, u32[]{:S(2)}) collective-permute-start(f32[1,64,512]{2,0,1:T(1,128)S(1)} %get-tuple-element.58), channel_id=1, source_target_pairs={{1,0},{2,1},{3,2},{4,3},{5,4},{6,5},{7,6},{9,8},{10,9},{11,10},{12... | collective-permute-start | bytes 393224 | tf_op jit(solution)/shard_map/ppermute | solution.py:51
  170.3 3.5 %collective-permute-start.26 = (f32[1,64,512]{2,0,1:T(1,128)S(1)}, f32[1,64,512]{2,0,1:T(1,128)S(1)}, u32[]{:S(2)}, u32[]{:S(2)}) collective-permute-start(f32[1,64,512]{2,0,1:T(1,128)S(1)} %get-tuple-element.59), channel_id=1, source_target_pairs={{0,1},{1,2},{2,3},{3,4},{4,5},{5,6},{6,7},{8,9},{9,10},{10,11},{11... | collective-permute-start | bytes 393224 | tf_op jit(solution)/shard_map/ppermute | solution.py:50
  (195 shorter events, 61.9 us)
Async XLA Ops:
  0.6 28.2 %copy-start.24 = (s32[8]{0:T(128)S(1)}, s32[8]{0:T(128)}, u32[]{:S(2)}) copy-start(s32[8]{0:T(128)} %param.23) | copy-start | bytes 100
  3.5 43.1 %collective-permute-start.2 = (f32[4,512]{1,0:T(4,128)}, f32[4,512]{1,0:T(4,128)}, u32[]{:S(2)}, u32[]{:S(2)}) collective-permute-start(f32[4,512]{1,0:T(4,128)} %get-tuple-element.113), channel_id=1, source_target_pairs={{0,1},{1,2},{2,3},{3,4},{4,5},{5,6},{6,7},{8,9},{9,10},{10,11},{11... | collective-permute-start | bytes 24584 | tf_op jit(solution)/shard_map/ppermute | solution.py:50
  8.0 38.6 %collective-permute-start.3 = (f32[4,512]{1,0:T(4,128)}, f32[4,512]{1,0:T(4,128)}, u32[]{:S(2)}, u32[]{:S(2)}) collective-permute-start(f32[4,512]{1,0:T(4,128)} %get-tuple-element.114), channel_id=1, source_target_pairs={{1,0},{2,1},{3,2},{4,3},{5,4},{6,5},{7,6},{9,8},{10,9},{11,10},{12... | collective-permute-start | bytes 24584 | tf_op jit(solution)/shard_map/ppermute | solution.py:51
  11.7 25.4 %collective-permute-start.20 = (f32[1,64,512]{2,0,1:T(1,128)}, f32[1,64,512]{2,0,1:T(1,128)}, u32[]{:S(2)}, u32[]{:S(2)}) collective-permute-start(f32[1,64,512]{2,0,1:T(1,128)} %bitcast.79), channel_id=1, source_target_pairs={{0,1},{1,2},{2,3},{3,4},{4,5},{5,6},{6,7},{8,9},{9,10},{10,11},{11... | collective-permute-start | bytes 393224 | tf_op jit(solution)/shard_map/ppermute | solution.py:50
  16.2 22.9 %copy-start = (f32[1,8,64,512]{3,2,1,0:T(8,128)S(1)}, f32[1,8,64,512]{3,2,1,0:T(8,128)}, u32[]{:S(2)}) copy-start(f32[1,8,64,512]{3,2,1,0:T(8,128)} %param.16) | copy-start | bytes 3145732
  16.2 22.9 %collective-permute-start.19 = (f32[1,64,512]{2,0,1:T(1,128)}, f32[1,64,512]{2,0,1:T(1,128)}, u32[]{:S(2)}, u32[]{:S(2)}) collective-permute-start(f32[1,64,512]{2,0,1:T(1,128)} %bitcast.80), channel_id=1, source_target_pairs={{1,0},{2,1},{3,2},{4,3},{5,4},{6,5},{7,6},{9,8},{10,9},{11,10},{12... | collective-permute-start | bytes 393224 | tf_op jit(solution)/shard_map/ppermute | solution.py:51
  21.9 17.1 %copy-start.1 = (f32[1,8,64,512]{3,1,2,0:T(8,128)}, f32[1,8,64,512]{3,1,2,0:T(8,128)S(1)}, u32[]{:S(2)}) copy-start(f32[1,8,64,512]{3,1,2,0:T(8,128)S(1)} %copy.46) | copy-start | bytes 3145732
  21.9 23.3 %copy-start.3 = (f32[8,8,512]{2,0,1:T(8,128)}, f32[8,8,512]{2,0,1:T(8,128)S(1)}, u32[]{:S(2)}) copy-start(f32[8,8,512]{2,0,1:T(8,128)S(1)} %slice.728) | copy-start | bytes 393220
  24.2 21.0 %copy-start.4 = (f32[8,8,512]{2,0,1:T(8,128)}, f32[8,8,512]{2,0,1:T(8,128)S(1)}, u32[]{:S(2)}) copy-start(f32[8,8,512]{2,0,1:T(8,128)S(1)} %slice.729) | copy-start | bytes 393220
  25.2 20.0 %collective-permute-start = (f32[4,24,512]{2,0,1:T(4,128)}, f32[4,24,512]{2,0,1:T(4,128)}, u32[]{:S(2)}, u32[]{:S(2)}) collective-permute-start(f32[4,24,512]{2,0,1:T(4,128)} %get-tuple-element.86), channel_id=1, source_target_pairs={{0,1},{1,2},{2,3},{3,4},{4,5},{5,6},{6,7},{8,9},{9,10},{10,11},{11... | collective-permute-start | bytes 589832 | tf_op jit(solution)/shard_map/ppermute | solution.py:50
  37.1 8.2 %collective-permute-start.1 = (f32[4,24,512]{2,0,1:T(4,128)}, f32[4,24,512]{2,0,1:T(4,128)S(1)}, u32[]{:S(2)}, u32[]{:S(2)}) collective-permute-start(f32[4,24,512]{2,0,1:T(4,128)} %get-tuple-element.87), channel_id=1, source_target_pairs={{1,0},{2,1},{3,2},{4,3},{5,4},{6,5},{7,6},{9,8},{10,9},{11,10},{12... | collective-permute-start | bytes 589832 | tf_op jit(solution)/shard_map/ppermute | solution.py:51
  56.3 7.2 %collective-permute-start.4 = (f32[4,512]{1,0:T(4,128)S(1)}, f32[4,512]{1,0:T(4,128)S(1)}, u32[]{:S(2)}, u32[]{:S(2)}) collective-permute-start(f32[4,512]{1,0:T(4,128)S(1)} %get-tuple-element.111), channel_id=1, source_target_pairs={{0,1},{1,2},{2,3},{3,4},{4,5},{5,6},{6,7},{8,9},{9,10},{10,11},{11... | collective-permute-start | bytes 24584 | tf_op jit(solution)/shard_map/ppermute | solution.py:50
  60.0 5.0 %collective-permute-start.5 = (f32[4,512]{1,0:T(4,128)S(1)}, f32[4,512]{1,0:T(4,128)S(1)}, u32[]{:S(2)}, u32[]{:S(2)}) collective-permute-start(f32[4,512]{1,0:T(4,128)S(1)} %get-tuple-element.112), channel_id=1, source_target_pairs={{1,0},{2,1},{3,2},{4,3},{5,4},{6,5},{7,6},{9,8},{10,9},{11,10},{12... | collective-permute-start | bytes 24584 | tf_op jit(solution)/shard_map/ppermute | solution.py:51
  74.3 1.1 collective-permute-start.6
  76.8 5.7 %collective-permute-start.7 = (f32[2]{0:T(128)S(1)}, f32[2]{0:T(128)S(1)}, u32[]{:S(2)}, u32[]{:S(2)}) collective-permute-start(f32[2]{0:T(128)S(1)} %fusion.135), channel_id=1, source_target_pairs={{0,2},{1,3},{2,0},{3,1},{4,6},{5,7},{6,4},{7,5},{8,10},{9,11},{10,... | collective-permute-start | bytes 32 | tf_op jit(solution)/shard_map/ppermute | solution.py:75
  83.8 2.4 %collective-permute-start.8 = (f32[2]{0:T(128)S(1)}, f32[2]{0:T(128)S(1)}, u32[]{:S(2)}, u32[]{:S(2)}) collective-permute-start(f32[2]{0:T(128)S(1)} %fusion.136), channel_id=1, source_target_pairs={{0,4},{1,5},{2,6},{3,7},{4,0},{5,1},{6,2},{7,3},{8,12},{9,13},{10,... | collective-permute-start | bytes 32 | tf_op jit(solution)/shard_map/ppermute | solution.py:75
  86.2 2.4 %collective-permute-start.9 = (f32[2]{0:T(128)S(1)}, f32[2]{0:T(128)S(1)}, u32[]{:S(2)}, u32[]{:S(2)}) collective-permute-start(f32[2]{0:T(128)S(1)} %add.547), channel_id=1, source_target_pairs={{0,8},{8,0},{16,24},{24,16},{1,9},{9,1},{17,25},{25,17},{2,10},{10... | collective-permute-start | bytes 32 | tf_op jit(solution)/shard_map/ppermute | solution.py:75
  88.6 3.3 %collective-permute-start.10 = (f32[2]{0:T(128)S(1)}, f32[2]{0:T(128)S(1)}, u32[]{:S(2)}, u32[]{:S(2)}) collective-permute-start(f32[2]{0:T(128)S(1)} %add.548), channel_id=1, source_target_pairs={{0,16},{8,24},{16,0},{24,8},{1,17},{9,25},{17,1},{25,9},{2,18},{10... | collective-permute-start | bytes 32 | tf_op jit(solution)/shard_map/ppermute | solution.py:75
  94.7 16.6 %collective-permute-start.11 = (f32[4,512]{1,0:T(4,128)S(1)}, f32[4,512]{1,0:T(4,128)S(1)}, u32[]{:S(2)}, u32[]{:S(2)}) collective-permute-start(f32[4,512]{1,0:T(4,128)S(1)} %get-tuple-element.109), channel_id=1, source_target_pairs={{0,1},{1,2},{2,3},{3,4},{4,5},{5,6},{6,7},{8,9},{9,10},{10,11},{11... | collective-permute-start | bytes 24584 | tf_op jit(solution)/shard_map/ppermute | solution.py:50
  102.8 8.5 %collective-permute-start.12 = (f32[4,512]{1,0:T(4,128)S(1)}, f32[4,512]{1,0:T(4,128)S(1)}, u32[]{:S(2)}, u32[]{:S(2)}) collective-permute-start(f32[4,512]{1,0:T(4,128)S(1)} %get-tuple-element.110), channel_id=1, source_target_pairs={{1,0},{2,1},{3,2},{4,3},{5,4},{6,5},{7,6},{9,8},{10,9},{11,10},{12... | collective-permute-start | bytes 24584 | tf_op jit(solution)/shard_map/ppermute | solution.py:51
  105.6 25.2 %collective-permute-start.21 = (f32[1,64,512]{2,0,1:T(1,128)}, f32[1,64,512]{2,0,1:T(1,128)}, u32[]{:S(2)}, u32[]{:S(2)}) collective-permute-start(f32[1,64,512]{2,0,1:T(1,128)} %get-tuple-element.76), channel_id=1, source_target_pairs={{1,0},{2,1},{3,2},{4,3},{5,4},{6,5},{7,6},{9,8},{10,9},{11,10},{12... | collective-permute-start | bytes 393224 | tf_op jit(solution)/shard_map/ppermute | solution.py:51
  107.5 23.3 %collective-permute-start.22 = (f32[1,64,512]{2,0,1:T(1,128)}, f32[1,64,512]{2,0,1:T(1,128)}, u32[]{:S(2)}, u32[]{:S(2)}) collective-permute-start(f32[1,64,512]{2,0,1:T(1,128)} %get-tuple-element.77), channel_id=1, source_target_pairs={{0,1},{1,2},{2,3},{3,4},{4,5},{5,6},{6,7},{8,9},{9,10},{10,11},{11... | collective-permute-start | bytes 393224 | tf_op jit(solution)/shard_map/ppermute | solution.py:50
  122.9 21.4 %collective-permute-start.15 = (f32[33,512]{1,0:T(8,128)S(1)}, f32[33,512]{1,0:T(8,128)S(1)}, u32[]{:S(2)}, u32[]{:S(2)}) collective-permute-start(f32[33,512]{1,0:T(8,128)S(1)} %dynamic-update-slice.13), channel_id=1, source_target_pairs={{16,24},{17,25},{18,26},{19,27},{20,28},{21,29},{22,30},{23,31}} | collective-permute-start | bytes 202760 | tf_op jit(solution)/shard_map/ppermute | solution.py:154
  123.6 20.7 %collective-permute-start.14 = (f32[33,512]{1,0:T(8,128)S(1)}, f32[33,512]{1,0:T(8,128)S(1)}, u32[]{:S(2)}, u32[]{:S(2)}) collective-permute-start(f32[33,512]{1,0:T(8,128)S(1)} %dynamic-update-slice.13), channel_id=1, source_target_pairs={{8,24},{9,25},{10,26},{11,27},{12,28},{13,29},{14,30},{15,31}} | collective-permute-start | bytes 202760 | tf_op jit(solution)/shard_map/ppermute | solution.py:154
  124.3 20.1 %collective-permute-start.13 = (f32[33,512]{1,0:T(8,128)S(1)}, f32[33,512]{1,0:T(8,128)S(1)}, u32[]{:S(2)}, u32[]{:S(2)}) collective-permute-start(f32[33,512]{1,0:T(8,128)S(1)} %dynamic-update-slice.13), channel_id=1, source_target_pairs={{0,24},{1,25},{2,26},{3,27},{4,28},{5,29},{6,30},{7,31}} | collective-permute-start | bytes 202760 | tf_op jit(solution)/shard_map/ppermute | solution.py:154
  138.7 21.8 %collective-permute-start.23 = (f32[1,64,512]{2,0,1:T(1,128)S(1)}, f32[1,64,512]{2,0,1:T(1,128)S(1)}, u32[]{:S(2)}, u32[]{:S(2)}) collective-permute-start(f32[1,64,512]{2,0,1:T(1,128)S(1)} %get-tuple-element.70), channel_id=1, source_target_pairs={{1,0},{2,1},{3,2},{4,3},{5,4},{6,5},{7,6},{9,8},{10,9},{11,10},{12... | collective-permute-start | bytes 393224 | tf_op jit(solution)/shard_map/ppermute | solution.py:51
  140.7 19.8 %collective-permute-start.24 = (f32[1,64,512]{2,0,1:T(1,128)S(1)}, f32[1,64,512]{2,0,1:T(1,128)S(1)}, u32[]{:S(2)}, u32[]{:S(2)}) collective-permute-start(f32[1,64,512]{2,0,1:T(1,128)S(1)} %get-tuple-element.71), channel_id=1, source_target_pairs={{0,1},{1,2},{2,3},{3,4},{4,5},{5,6},{6,7},{8,9},{9,10},{10,11},{11... | collective-permute-start | bytes 393224 | tf_op jit(solution)/shard_map/ppermute | solution.py:50
  145.3 1.2 collective-permute-start.16
  146.4 2.9 %collective-permute-start.17 = (f32[4]{0:T(128)S(1)}, f32[4]{0:T(128)S(1)}, u32[]{:S(2)}, u32[]{:S(2)}) collective-permute-start(f32[4]{0:T(128)S(1)} %fusion.102), channel_id=1, source_target_pairs={{0,2},{1,3},{2,0},{3,1},{4,6},{5,7},{6,4},{7,5},{8,10},{9,11},{10,... | collective-permute-start | bytes 56 | tf_op jit(solution)/shard_map/ppermute | solution.py:75
  149.4 2.4 %collective-permute-start.18 = (f32[4]{0:T(128)S(1)}, f32[4]{0:T(128)S(1)}, u32[]{:S(2)}, u32[]{:S(2)}) collective-permute-start(f32[4]{0:T(128)S(1)} %add.577), channel_id=1, source_target_pairs={{0,4},{1,5},{2,6},{3,7},{4,0},{5,1},{6,2},{7,3},{8,12},{9,13},{10,... | collective-permute-start | bytes 56 | tf_op jit(solution)/shard_map/ppermute | solution.py:75
  166.2 8.4 %collective-permute-start.25 = (f32[1,64,512]{2,0,1:T(1,128)S(1)}, f32[1,64,512]{2,0,1:T(1,128)S(1)}, u32[]{:S(2)}, u32[]{:S(2)}) collective-permute-start(f32[1,64,512]{2,0,1:T(1,128)S(1)} %get-tuple-element.58), channel_id=1, source_target_pairs={{1,0},{2,1},{3,2},{4,3},{5,4},{6,5},{7,6},{9,8},{10,9},{11,10},{12... | collective-permute-start | bytes 393224 | tf_op jit(solution)/shard_map/ppermute | solution.py:51
  170.3 5.5 %collective-permute-start.26 = (f32[1,64,512]{2,0,1:T(1,128)S(1)}, f32[1,64,512]{2,0,1:T(1,128)S(1)}, u32[]{:S(2)}, u32[]{:S(2)}) collective-permute-start(f32[1,64,512]{2,0,1:T(1,128)S(1)} %get-tuple-element.59), channel_id=1, source_target_pairs={{0,1},{1,2},{2,3},{3,4},{4,5},{5,6},{6,7},{8,9},{9,10},{10,11},{11... | collective-permute-start | bytes 393224 | tf_op jit(solution)/shard_map/ppermute | solution.py:50
  (20 other events, 199.5 us)

commit v3 on v2

--- a/solution.py
+++ b/solution.py
@@ -52,20 +52,18 @@
     return jnp.concatenate([low, block, high], axis=0)
 
 
-def full_solve(q, rhs, coef):
-    for k in range(SWEEPS):
-        qx = rims(q, 1)
-        zero = jnp.zeros_like(q[:, :1])
-        q = stencil(
-            rhs,
-            coef,
-            qx[2:],
-            qx[:-2],
-            jnp.concatenate([q[:, 1:], zero], axis=1),
-            jnp.concatenate([zero, q[:, :-1]], axis=1),
-            q,
-        )
-    return q
+def full_sweep(q, rhs, coef):
+    qx = rims(q, 1)
+    zero = jnp.zeros_like(q[:, :1])
+    return stencil(
+        rhs,
+        coef,
+        qx[2:],
+        qx[:-2],
+        jnp.concatenate([q[:, 1:], zero], axis=1),
+        jnp.concatenate([zero, q[:, :-1]], axis=1),
+        q,
+    )
 
 
 def allsum_axis(v, axis):
@@ -97,6 +95,7 @@
     own = (owner[:, 0] == side_id).astype(jnp.float32)[:, None]
     own_live = own * live
     onehot = (block_row[None, :] == jnp.arange(slab_rows)[:, None]).astype(jnp.float32) * own[:, 0][None, :]
+    pick = (block_row[:, None] == jnp.arange(slab_rows)[None, :]).astype(jnp.float32)
 
     packed = rims(
         jnp.concatenate([start_here[:, :BAND], force_here[:, :BAND], coef_here[:, :BAND]], axis=1), HALO
@@ -114,7 +113,7 @@
         plane = jnp.sum(onehot[:, :, None] * (live * disp)[None], axis=1)
         rhs = force_band.at[:, 0, :].add(rims(plane, HALO))
         band = band_solve(init_band, rhs, coef_band, row_ok)
-        traction = PENALTY * band[:, 0, :][block_row]
+        traction = PENALTY * jnp.sum(pick[:, :, None] * band[:, 0, :][None], axis=1)
         loaded = live * (shell_load - traction)
         tilde = own_live * jnp.sum(compliance * loaded[:, None, :], axis=-1)
         return tilde, band
@@ -123,12 +122,19 @@
     tilde_zero, unused = evaluate(disp_zero)
     resid_zero = tilde_zero - disp_zero
     disp_one = disp_zero + RELAX * resid_zero
+    deep = start_here
+    for k in range(SWEEPS // 2):
+        deep = full_sweep(deep, force_here, coef_here)
+    disp_one, deep = lax.optimization_barrier((disp_one, deep))
     tilde_one, unused = evaluate(disp_one)
     resid_one = tilde_one - disp_one
     diff_one = resid_one - resid_zero
     sums = allsum(jnp.stack([jnp.sum(diff_one * diff_one), jnp.sum(diff_one * resid_one)]))
     gram_aa, gram_ab = sums[0], sums[1]
     coeff = -gram_ab / (gram_aa + (0.001 * gram_aa + 1e-06))
+    for k in range(SWEEPS // 2, SWEEPS):
+        deep = full_sweep(deep, force_here, coef_here)
+    coeff, deep = lax.optimization_barrier((coeff, deep))
     disp_two = tilde_one + coeff * (tilde_one - tilde_zero)
     tilde_two, band_two = evaluate(disp_two)
     resid_two = tilde_two - disp_two
@@ -145,7 +151,9 @@
     outgoing = jnp.concatenate(
         [
             jnp.concatenate([tilde_two, tilde_one, tilde_zero, resid_two], axis=0),
-            jnp.concatenate([partial, jnp.zeros((line_cells - 4,), jnp.float32)])[None],
+            sum(
+                jnp.where(jnp.arange(line_cells) == k, partial[k], 0.0) for k in range(4)
+            )[None],
         ],
         axis=0,
     )
@@ -168,7 +176,6 @@
         tilde_two + coeff_new * (tilde_two - tilde_one) + coeff_old * (tilde_one - tilde_zero)
     )
 
-    deep = full_solve(start_here, force_here, coef_here)
     flow_state = jnp.concatenate([band_two, deep[:, band_two.shape[1] :]], axis=1)
     disp_next = jnp.where(shell_flag, disp_three, 0.0)[None]
     residual = jnp.where(shell_flag, resid_two, 0.0)[None]

time: 180 us -> 159 us (0.88)
  the two profiles are of different devices: /device:TPU:1 before, /device:TPU:28 now
where the time goes in v3:
time: 159 us; the launch traced here: 157 us
  starting transfers between devices  51.8 us (33%)
  waiting for transfers between devices  33.9 us (21%)
  other arithmetic  33 us (21%)
  local copies, waits for them, and re-layouts  26.6 us (17%)
  between operations  11.7 us (7%)
    ppermute x8, starting transfers between devices, rims(): high = lax.ppermute(block[:width], 'slab', backward)  29.2 us
    ppermute x8, waiting for transfers between devices, allsum_axis(): v = v + lax.ppermute(v, axis, [(i, i ^ step) for i in range(count)])  22.7 us
    ppermute x8, starting transfers between devices, rims(): low = lax.ppermute(block[block.shape[0] - width:], 'slab', forward)  17 us
    div x4, other arithmetic, stencil(): return (rhs + total) / (6.0 + coef)  12.1 us
    unnamed x79, local copies, waits for them, and re-layouts  9.92 us
    slice x14, local copies, waits for them, and re-layouts, shift_y(): a[..., 1:]  5.24 us
    ppermute x3, waiting for transfers between devices, body(): lax.ppermute(outgoing, 'side', [(source, side_count - 1)])  5.15 us
    ppermute x8, waiting for transfers between devices, rims(): low = lax.ppermute(block[block.shape[0] - width:], 'slab', forward)  4.81 us
  transfers between devices with their start and end apart: 27, of which 14 were waited for; matrix products, arithmetic and copies ran while one was open for 23% of the time, Pallas kernels for 0%

profile of v3, /device:TPU:28, one launch (start us, length us, event | category | flops | bytes accessed | tf_op | source)
XLA Modules:
  0.0 157.0 jit_solution(11715785260289348769)
XLA Ops:
  3.5 1.9 %collective-permute-start.2 = (f32[4,512]{1,0:T(4,128)}, f32[4,512]{1,0:T(4,128)}, u32[]{:S(2)}, u32[]{:S(2)}) collective-permute-start(f32[4,512]{1,0:T(4,128)} %get-tuple-element.116), channel_id=1, source_target_pairs={{0,1},{1,2},{2,3},{3,4},{4,5},{5,6},{6,7},{8,9},{9,10},{10,11},{11... | collective-permute-start | bytes 24584 | tf_op jit(solution)/shard_map/ppermute | solution.py:50
  5.4 4.5 %collective-permute-start.3 = (f32[4,512]{1,0:T(4,128)}, f32[4,512]{1,0:T(4,128)}, u32[]{:S(2)}, u32[]{:S(2)}) collective-permute-start(f32[4,512]{1,0:T(4,128)} %get-tuple-element.117), channel_id=1, source_target_pairs={{1,0},{2,1},{3,2},{4,3},{5,4},{6,5},{7,6},{9,8},{10,9},{11,10},{12... | collective-permute-start | bytes 24584 | tf_op jit(solution)/shard_map/ppermute | solution.py:51
  11.7 1.9 %collective-permute-start.5 = (f32[1,64,512]{2,0,1:T(1,128)}, f32[1,64,512]{2,0,1:T(1,128)}, u32[]{:S(2)}, u32[]{:S(2)}) collective-permute-start(f32[1,64,512]{2,0,1:T(1,128)} %bitcast.76), channel_id=1, source_target_pairs={{0,1},{1,2},{2,3},{3,4},{4,5},{5,6},{6,7},{8,9},{9,10},{10,11},{11... | collective-permute-start | bytes 393224 | tf_op jit(solution)/shard_map/ppermute | solution.py:50
  14.5 4.7 %collective-permute-start.4 = (f32[1,64,512]{2,0,1:T(1,128)}, f32[1,64,512]{2,0,1:T(1,128)}, u32[]{:S(2)}, u32[]{:S(2)}) collective-permute-start(f32[1,64,512]{2,0,1:T(1,128)} %bitcast.77), channel_id=1, source_target_pairs={{1,0},{2,1},{3,2},{4,3},{5,4},{6,5},{7,6},{9,8},{10,9},{11,10},{12... | collective-permute-start | bytes 393224 | tf_op jit(solution)/shard_map/ppermute | solution.py:51
  19.1 1.8 %copy.43 = f32[1,8,64,512]{3,1,2,0:T(8,128)S(1)} copy(f32[1,8,64,512]{3,2,1,0:T(8,128)} %param.17) | data formatting | bytes 2097152 | tf_op args[2]
  21.0 1.8 %copy.42 = f32[1,8,64,512]{3,1,2,0:T(8,128)S(1)} copy(f32[1,8,64,512]{3,2,1,0:T(8,128)} %param.15) | data formatting | bytes 2097152 | tf_op args[0]
  22.9 1.9 %copy.41 = f32[1,8,64,512]{3,1,2,0:T(8,128)S(1)} copy(f32[1,8,64,512]{3,2,1,0:T(8,128)} %param.16) | data formatting | bytes 2097152 | tf_op args[1]
  26.6 1.9 %collective-permute-start = (f32[4,24,512]{2,0,1:T(4,128)}, f32[4,24,512]{2,0,1:T(4,128)}, u32[]{:S(2)}, u32[]{:S(2)}) collective-permute-start(f32[4,24,512]{2,0,1:T(4,128)} %get-tuple-element.89), channel_id=1, source_target_pairs={{0,1},{1,2},{2,3},{3,4},{4,5},{5,6},{6,7},{8,9},{9,10},{10,11},{11... | collective-permute-start | bytes 589832 | tf_op jit(solution)/shard_map/ppermute | solution.py:50
  36.6 4.5 %collective-permute-start.1 = (f32[4,24,512]{2,0,1:T(4,128)}, f32[4,24,512]{2,0,1:T(4,128)S(1)}, u32[]{:S(2)}, u32[]{:S(2)}) collective-permute-start(f32[4,24,512]{2,0,1:T(4,128)} %get-tuple-element.90), channel_id=1, source_target_pairs={{1,0},{2,1},{3,2},{4,3},{5,4},{6,5},{7,6},{9,8},{10,9},{11,10},{12... | collective-permute-start | bytes 589832 | tf_op jit(solution)/shard_map/ppermute | solution.py:51
  41.1 4.1 %fusion.27 = f32[8,64,512]{2,0,1:T(8,128)S(1)} fusion(f32[8,64,512]{2,0,1:T(8,128)S(1)} %bitcast.85, f32[1,64,512]{2,0,1:T(1,128)} %collective-permute-done.5, f32[1,64,512]{2,0,1:T(1,128)} %collective-permute-done.4, f32[8,64,511]{2,0,1:T(8,128)} %get-tuple-element.84, f32[8,64,511]{2,0,1:T(8,128)} %get-tuple-element.83, ...), kind=kLoop, calls=%fused_computation.37 | loop fusion | flops 2621440 | bytes 8613888 | tf_op jit(solution)/shard_map/div | solution.py:21
  45.9 2.2 %collective-permute-start.6 = (f32[1,64,512]{2,0,1:T(1,128)S(1)}, f32[1,64,512]{2,0,1:T(1,128)S(1)}, u32[]{:S(2)}, u32[]{:S(2)}) collective-permute-start(f32[1,64,512]{2,0,1:T(1,128)S(1)} %get-tuple-element.79), channel_id=1, source_target_pairs={{1,0},{2,1},{3,2},{4,3},{5,4},{6,5},{7,6},{9,8},{10,9},{11,10},{12... | collective-permute-start | bytes 393224 | tf_op jit(solution)/shard_map/ppermute | solution.py:51
  48.4 2.4 %collective-permute-start.7 = (f32[1,64,512]{2,0,1:T(1,128)S(1)}, f32[1,64,512]{2,0,1:T(1,128)S(1)}, u32[]{:S(2)}, u32[]{:S(2)}) collective-permute-start(f32[1,64,512]{2,0,1:T(1,128)S(1)} %get-tuple-element.80), channel_id=1, source_target_pairs={{0,1},{1,2},{2,3},{3,4},{4,5},{5,6},{6,7},{8,9},{9,10},{10,11},{11... | collective-permute-start | bytes 393224 | tf_op jit(solution)/shard_map/ppermute | solution.py:50
  55.6 1.9 %fusion.20 = f32[8,64,512]{2,0,1:T(8,128)S(1)} fusion(f32[8,64,512]{2,0,1:T(8,128)S(1)} %fusion.27, f32[1,64,512]{2,0,1:T(1,128)S(1)} %collective-permute-done.7, f32[1,64,512]{2,0,1:T(1,128)S(1)} %collective-permute-done.6, f32[8,64,511]{2,0,1:T(8,128)S(1)} %get-tuple-element.78, f32[8,64,511]{2,0,1:T(8,128)S(1)} %get-tuple-element.77, ...), kind=kLoop, calls=%fused_computation.28 | loop fusion | flops 2621440 | bytes 8613888 | tf_op jit(solution)/shard_map/div | solution.py:21
  61.0 1.9 %collective-permute-start.8 = (f32[4,512]{1,0:T(4,128)S(1)}, f32[4,512]{1,0:T(4,128)S(1)}, u32[]{:S(2)}, u32[]{:S(2)}) collective-permute-start(f32[4,512]{1,0:T(4,128)S(1)} %get-tuple-element.114), channel_id=1, source_target_pairs={{0,1},{1,2},{2,3},{3,4},{4,5},{5,6},{6,7},{8,9},{9,10},{10,11},{11... | collective-permute-start | bytes 24584 | tf_op jit(solution)/shard_map/ppermute | solution.py:50
  62.9 4.5 %collective-permute-start.9 = (f32[4,512]{1,0:T(4,128)S(1)}, f32[4,512]{1,0:T(4,128)S(1)}, u32[]{:S(2)}, u32[]{:S(2)}) collective-permute-start(f32[4,512]{1,0:T(4,128)S(1)} %get-tuple-element.115), channel_id=1, source_target_pairs={{1,0},{2,1},{3,2},{4,3},{5,4},{6,5},{7,6},{9,8},{10,9},{11,10},{12... | collective-permute-start | bytes 24584 | tf_op jit(solution)/shard_map/ppermute | solution.py:51
  68.4 1.9 %collective-permute-start.15 = (f32[1,64,512]{2,0,1:T(1,128)}, f32[1,64,512]{2,0,1:T(1,128)}, u32[]{:S(2)}, u32[]{:S(2)}) collective-permute-start(f32[1,64,512]{2,0,1:T(1,128)} %get-tuple-element.73), channel_id=1, source_target_pairs={{1,0},{2,1},{3,2},{4,3},{5,4},{6,5},{7,6},{9,8},{10,9},{11,10},{12... | collective-permute-start | bytes 393224 | tf_op jit(solution)/shard_map/ppermute | solution.py:51
  70.3 2.6 %collective-permute-start.16 = (f32[1,64,512]{2,0,1:T(1,128)}, f32[1,64,512]{2,0,1:T(1,128)}, u32[]{:S(2)}, u32[]{:S(2)}) collective-permute-start(f32[1,64,512]{2,0,1:T(1,128)} %get-tuple-element.74), channel_id=1, source_target_pairs={{0,1},{1,2},{2,3},{3,4},{4,5},{5,6},{6,7},{8,9},{9,10},{10,11},{11... | collective-permute-start | bytes 393224 | tf_op jit(solution)/shard_map/ppermute | solution.py:50
  79.3 3.5 %collective-permute-done.11 = f32[2]{0:T(128)S(1)} collective-permute-done((f32[2]{0:T(128)S(1)}, f32[2]{0:T(128)S(1)}, u32[]{:S(2)}, u32[]{:S(2)}) %collective-permute-start.11) | collective-permute-done | bytes 40 | tf_op jit(solution)/shard_map/ppermute | solution.py:73
  85.0 2.8 %collective-permute-done.12 = f32[2]{0:T(128)S(1)} collective-permute-done((f32[2]{0:T(128)S(1)}, f32[2]{0:T(128)S(1)}, u32[]{:S(2)}, u32[]{:S(2)}) %collective-permute-start.12) | collective-permute-done | bytes 40 | tf_op jit(solution)/shard_map/ppermute | solution.py:73
  88.2 3.1 %collective-permute-done.13 = f32[2]{0:T(128)S(1)} collective-permute-done((f32[2]{0:T(128)S(1)}, f32[2]{0:T(128)S(1)}, u32[]{:S(2)}, u32[]{:S(2)}) %collective-permute-start.13) | collective-permute-done | bytes 40 | tf_op jit(solution)/shard_map/ppermute | solution.py:73
  91.6 4.1 %collective-permute-done.14 = f32[2]{0:T(128)S(1)} collective-permute-done((f32[2]{0:T(128)S(1)}, f32[2]{0:T(128)S(1)}, u32[]{:S(2)}, u32[]{:S(2)}) %collective-permute-start.14) | collective-permute-done | bytes 40 | tf_op jit(solution)/shard_map/ppermute | solution.py:73
  98.3 4.1 %fusion.13 = f32[8,64,512]{2,0,1:T(8,128)S(1)} fusion(f32[8,64,512]{2,0,1:T(8,128)S(1)} %fusion.20, f32[1,64,512]{2,0,1:T(1,128)} %collective-permute-done.16, f32[1,64,512]{2,0,1:T(1,128)} %collective-permute-done.15, f32[8,64,511]{2,0,1:T(8,128)} %get-tuple-element.72, f32[8,64,511]{2,0,1:T(8,128)} %get-tuple-element.71, ...), kind=kLoop, calls=%fused_computation.19 | loop fusion | flops 2621440 | bytes 8613888 | tf_op jit(solution)/shard_map/div | solution.py:21
  103.1 2.1 %collective-permute-start.17 = (f32[1,64,512]{2,0,1:T(1,128)S(1)}, f32[1,64,512]{2,0,1:T(1,128)S(1)}, u32[]{:S(2)}, u32[]{:S(2)}) collective-permute-start(f32[1,64,512]{2,0,1:T(1,128)S(1)} %get-tuple-element.67), channel_id=1, source_target_pairs={{1,0},{2,1},{3,2},{4,3},{5,4},{6,5},{7,6},{9,8},{10,9},{11,10},{12... | collective-permute-start | bytes 393224 | tf_op jit(solution)/shard_map/ppermute | solution.py:51
  105.1 2.4 %collective-permute-start.18 = (f32[1,64,512]{2,0,1:T(1,128)S(1)}, f32[1,64,512]{2,0,1:T(1,128)S(1)}, u32[]{:S(2)}, u32[]{:S(2)}) collective-permute-start(f32[1,64,512]{2,0,1:T(1,128)S(1)} %get-tuple-element.68), channel_id=1, source_target_pairs={{0,1},{1,2},{2,3},{3,4},{4,5},{5,6},{6,7},{8,9},{9,10},{10,11},{11... | collective-permute-start | bytes 393224 | tf_op jit(solution)/shard_map/ppermute | solution.py:50
  107.8 4.5 %collective-permute-done.18 = f32[1,64,512]{2,0,1:T(1,128)S(1)} collective-permute-done((f32[1,64,512]{2,0,1:T(1,128)S(1)}, f32[1,64,512]{2,0,1:T(1,128)S(1)}, u32[]{:S(2)}, u32[]{:S(2)}) %collective-permute-start.18) | collective-permute-done | bytes 131104 | tf_op jit(solution)/shard_map/ppermute | solution.py:50
  112.3 1.9 %fusion.6 = f32[8,64,512]{2,0,1:T(8,128)S(1)} fusion(f32[8,64,512]{2,0,1:T(8,128)S(1)} %fusion.13, f32[1,64,512]{2,0,1:T(1,128)S(1)} %collective-permute-done.18, f32[1,64,512]{2,0,1:T(1,128)S(1)} %collective-permute-done.17, f32[8,64,511]{2,0,1:T(8,128)S(1)} %get-tuple-element.66, f32[8,64,511]{2,0,1:T(8,128)S(1)} %get-tuple-element.65, ...), kind=kLoop, calls=%fused_computation.10 | loop fusion | flops 2621440 | bytes 8613888 | tf_op jit(solution)/shard_map/div | solution.py:21
  114.5 1.9 %collective-permute-start.19 = (f32[4,512]{1,0:T(4,128)S(1)}, f32[4,512]{1,0:T(4,128)S(1)}, u32[]{:S(2)}, u32[]{:S(2)}) collective-permute-start(f32[4,512]{1,0:T(4,128)S(1)} %get-tuple-element.112), channel_id=1, source_target_pairs={{0,1},{1,2},{2,3},{3,4},{4,5},{5,6},{6,7},{8,9},{9,10},{10,11},{11... | collective-permute-start | bytes 24584 | tf_op jit(solution)/shard_map/ppermute | solution.py:50
  116.4 4.8 %collective-permute-start.20 = (f32[4,512]{1,0:T(4,128)S(1)}, f32[4,512]{1,0:T(4,128)S(1)}, u32[]{:S(2)}, u32[]{:S(2)}) collective-permute-start(f32[4,512]{1,0:T(4,128)S(1)} %get-tuple-element.113), channel_id=1, source_target_pairs={{1,0},{2,1},{3,2},{4,3},{5,4},{6,5},{7,6},{9,8},{10,9},{11,10},{12... | collective-permute-start | bytes 24584 | tf_op jit(solution)/shard_map/ppermute | solution.py:51
  126.2 2.6 %fusion.109 = f32[1,512]{1,0:T(1,128)S(1)} fusion(f32[]{:T(128)} %get-tuple-element.52, f32[]{:T(128)} %get-tuple-element.53, f32[]{:T(128)} %get-tuple-element.51, f32[]{:T(128)} %get-tuple-element.50), kind=kLoop, calls=%fused_computation.202 | loop fusion | flops 5632 | bytes 2064 | tf_op jit(solution)/shard_map/add | solution.py:154
  136.1 2.2 %collective-permute-done.22 = f32[33,512]{1,0:T(8,128)S(1)} collective-permute-done((f32[33,512]{1,0:T(8,128)S(1)}, f32[33,512]{1,0:T(8,128)S(1)}, u32[]{:S(2)}, u32[]{:S(2)}) %collective-permute-start.22) | collective-permute-done | bytes 67616 | tf_op jit(solution)/shard_map/ppermute | solution.py:162
  140.8 3.5 %collective-permute-done.25 = f32[4]{0:T(128)S(1)} collective-permute-done((f32[4]{0:T(128)S(1)}, f32[4]{0:T(128)S(1)}, u32[]{:S(2)}, u32[]{:S(2)}) %collective-permute-start.25) | collective-permute-done | bytes 48 | tf_op jit(solution)/shard_map/ppermute | solution.py:73
  144.5 3.4 %collective-permute-done.26 = f32[4]{0:T(128)S(1)} collective-permute-done((f32[4]{0:T(128)S(1)}, f32[4]{0:T(128)S(1)}, u32[]{:S(2)}, u32[]{:S(2)}) %collective-permute-start.26) | collective-permute-done | bytes 48 | tf_op jit(solution)/shard_map/ppermute | solution.py:73
  (216 shorter events, 51.7 us)
Async XLA Ops:
  3.5 48.7 %collective-permute-start.2 = (f32[4,512]{1,0:T(4,128)}, f32[4,512]{1,0:T(4,128)}, u32[]{:S(2)}, u32[]{:S(2)}) collective-permute-start(f32[4,512]{1,0:T(4,128)} %get-tuple-element.116), channel_id=1, source_target_pairs={{0,1},{1,2},{2,3},{3,4},{4,5},{5,6},{6,7},{8,9},{9,10},{10,11},{11... | collective-permute-start | bytes 24584 | tf_op jit(solution)/shard_map/ppermute | solution.py:50
  5.4 46.8 %collective-permute-start.3 = (f32[4,512]{1,0:T(4,128)}, f32[4,512]{1,0:T(4,128)}, u32[]{:S(2)}, u32[]{:S(2)}) collective-permute-start(f32[4,512]{1,0:T(4,128)} %get-tuple-element.117), channel_id=1, source_target_pairs={{1,0},{2,1},{3,2},{4,3},{5,4},{6,5},{7,6},{9,8},{10,9},{11,10},{12... | collective-permute-start | bytes 24584 | tf_op jit(solution)/shard_map/ppermute | solution.py:51
  11.7 24.8 %collective-permute-start.5 = (f32[1,64,512]{2,0,1:T(1,128)}, f32[1,64,512]{2,0,1:T(1,128)}, u32[]{:S(2)}, u32[]{:S(2)}) collective-permute-start(f32[1,64,512]{2,0,1:T(1,128)} %bitcast.76), channel_id=1, source_target_pairs={{0,1},{1,2},{2,3},{3,4},{4,5},{5,6},{6,7},{8,9},{9,10},{10,11},{11... | collective-permute-start | bytes 393224 | tf_op jit(solution)/shard_map/ppermute | solution.py:50
  14.5 26.7 %copy-start = (f32[1,8,64,512]{3,2,1,0:T(8,128)S(1)}, f32[1,8,64,512]{3,2,1,0:T(8,128)}, u32[]{:S(2)}) copy-start(f32[1,8,64,512]{3,2,1,0:T(8,128)} %param.16) | copy-start | bytes 3145732
  14.5 26.7 %copy-start.1 = (f32[1,8,64,512]{3,2,1,0:T(8,128)S(1)}, f32[1,8,64,512]{3,2,1,0:T(8,128)}, u32[]{:S(2)}) copy-start(f32[1,8,64,512]{3,2,1,0:T(8,128)} %param.15) | copy-start | bytes 3145732
  14.5 26.6 %collective-permute-start.4 = (f32[1,64,512]{2,0,1:T(1,128)}, f32[1,64,512]{2,0,1:T(1,128)}, u32[]{:S(2)}, u32[]{:S(2)}) collective-permute-start(f32[1,64,512]{2,0,1:T(1,128)} %bitcast.77), channel_id=1, source_target_pairs={{1,0},{2,1},{3,2},{4,3},{5,4},{6,5},{7,6},{9,8},{10,9},{11,10},{12... | collective-permute-start | bytes 393224 | tf_op jit(solution)/shard_map/ppermute | solution.py:51
  22.8 28.0 %copy-start.4 = (f32[8,8,512]{2,0,1:T(8,128)}, f32[8,8,512]{2,0,1:T(8,128)S(1)}, u32[]{:S(2)}) copy-start(f32[8,8,512]{2,0,1:T(8,128)S(1)} %slice.722) | copy-start | bytes 393220
  25.7 25.1 %copy-start.5 = (f32[8,8,512]{2,0,1:T(8,128)}, f32[8,8,512]{2,0,1:T(8,128)S(1)}, u32[]{:S(2)}) copy-start(f32[8,8,512]{2,0,1:T(8,128)S(1)} %slice.723) | copy-start | bytes 393220
  26.6 21.8 %collective-permute-start = (f32[4,24,512]{2,0,1:T(4,128)}, f32[4,24,512]{2,0,1:T(4,128)}, u32[]{:S(2)}, u32[]{:S(2)}) collective-permute-start(f32[4,24,512]{2,0,1:T(4,128)} %get-tuple-element.89), channel_id=1, source_target_pairs={{0,1},{1,2},{2,3},{3,4},{4,5},{5,6},{6,7},{8,9},{9,10},{10,11},{11... | collective-permute-start | bytes 589832 | tf_op jit(solution)/shard_map/ppermute | solution.py:50
  36.6 37.3 %copy-start.17 = (f32[8,8]{1,0:T(8,128)}, f32[8,8]{1,0:T(8,128)S(1)}, u32[]{:S(2)}) copy-start(f32[8,8]{1,0:T(8,128)S(1)} %fusion.105) | copy-start | bytes 772
  36.6 14.2 %collective-permute-start.1 = (f32[4,24,512]{2,0,1:T(4,128)}, f32[4,24,512]{2,0,1:T(4,128)S(1)}, u32[]{:S(2)}, u32[]{:S(2)}) collective-permute-start(f32[4,24,512]{2,0,1:T(4,128)} %get-tuple-element.90), channel_id=1, source_target_pairs={{1,0},{2,1},{3,2},{4,3},{5,4},{6,5},{7,6},{9,8},{10,9},{11,10},{12... | collective-permute-start | bytes 589832 | tf_op jit(solution)/shard_map/ppermute | solution.py:51
  45.9 9.3 %collective-permute-start.6 = (f32[1,64,512]{2,0,1:T(1,128)S(1)}, f32[1,64,512]{2,0,1:T(1,128)S(1)}, u32[]{:S(2)}, u32[]{:S(2)}) collective-permute-start(f32[1,64,512]{2,0,1:T(1,128)S(1)} %get-tuple-element.79), channel_id=1, source_target_pairs={{1,0},{2,1},{3,2},{4,3},{5,4},{6,5},{7,6},{9,8},{10,9},{11,10},{12... | collective-permute-start | bytes 393224 | tf_op jit(solution)/shard_map/ppermute | solution.py:51
  48.4 7.2 %collective-permute-start.7 = (f32[1,64,512]{2,0,1:T(1,128)S(1)}, f32[1,64,512]{2,0,1:T(1,128)S(1)}, u32[]{:S(2)}, u32[]{:S(2)}) collective-permute-start(f32[1,64,512]{2,0,1:T(1,128)S(1)} %get-tuple-element.80), channel_id=1, source_target_pairs={{0,1},{1,2},{2,3},{3,4},{4,5},{5,6},{6,7},{8,9},{9,10},{10,11},{11... | collective-permute-start | bytes 393224 | tf_op jit(solution)/shard_map/ppermute | solution.py:50
  61.0 11.9 %collective-permute-start.8 = (f32[4,512]{1,0:T(4,128)S(1)}, f32[4,512]{1,0:T(4,128)S(1)}, u32[]{:S(2)}, u32[]{:S(2)}) collective-permute-start(f32[4,512]{1,0:T(4,128)S(1)} %get-tuple-element.114), channel_id=1, source_target_pairs={{0,1},{1,2},{2,3},{3,4},{4,5},{5,6},{6,7},{8,9},{9,10},{10,11},{11... | collective-permute-start | bytes 24584 | tf_op jit(solution)/shard_map/ppermute | solution.py:50
  62.9 9.9 %collective-permute-start.9 = (f32[4,512]{1,0:T(4,128)S(1)}, f32[4,512]{1,0:T(4,128)S(1)}, u32[]{:S(2)}, u32[]{:S(2)}) collective-permute-start(f32[4,512]{1,0:T(4,128)S(1)} %get-tuple-element.115), channel_id=1, source_target_pairs={{1,0},{2,1},{3,2},{4,3},{5,4},{6,5},{7,6},{9,8},{10,9},{11,10},{12... | collective-permute-start | bytes 24584 | tf_op jit(solution)/shard_map/ppermute | solution.py:51
  68.4 29.9 %collective-permute-start.15 = (f32[1,64,512]{2,0,1:T(1,128)}, f32[1,64,512]{2,0,1:T(1,128)}, u32[]{:S(2)}, u32[]{:S(2)}) collective-permute-start(f32[1,64,512]{2,0,1:T(1,128)} %get-tuple-element.73), channel_id=1, source_target_pairs={{1,0},{2,1},{3,2},{4,3},{5,4},{6,5},{7,6},{9,8},{10,9},{11,10},{12... | collective-permute-start | bytes 393224 | tf_op jit(solution)/shard_map/ppermute | solution.py:51
  70.3 28.0 %collective-permute-start.16 = (f32[1,64,512]{2,0,1:T(1,128)}, f32[1,64,512]{2,0,1:T(1,128)}, u32[]{:S(2)}, u32[]{:S(2)}) collective-permute-start(f32[1,64,512]{2,0,1:T(1,128)} %get-tuple-element.74), channel_id=1, source_target_pairs={{0,1},{1,2},{2,3},{3,4},{4,5},{5,6},{6,7},{8,9},{9,10},{10,11},{11... | collective-permute-start | bytes 393224 | tf_op jit(solution)/shard_map/ppermute | solution.py:50
  76.8 1.1 collective-permute-start.10
  79.3 3.5 %collective-permute-start.11 = (f32[2]{0:T(128)S(1)}, f32[2]{0:T(128)S(1)}, u32[]{:S(2)}, u32[]{:S(2)}) collective-permute-start(f32[2]{0:T(128)S(1)} %fusion.144), channel_id=1, source_target_pairs={{0,2},{1,3},{2,0},{3,1},{4,6},{5,7},{6,4},{7,5},{8,10},{9,11},{10,... | collective-permute-start | bytes 32 | tf_op jit(solution)/shard_map/ppermute | solution.py:73
  84.2 3.5 %collective-permute-start.12 = (f32[2]{0:T(128)S(1)}, f32[2]{0:T(128)S(1)}, u32[]{:S(2)}, u32[]{:S(2)}) collective-permute-start(f32[2]{0:T(128)S(1)} %fusion.145), channel_id=1, source_target_pairs={{0,4},{1,5},{2,6},{3,7},{4,0},{5,1},{6,2},{7,3},{8,12},{9,13},{10,... | collective-permute-start | bytes 32 | tf_op jit(solution)/shard_map/ppermute | solution.py:73
  87.7 3.5 %collective-permute-start.13 = (f32[2]{0:T(128)S(1)}, f32[2]{0:T(128)S(1)}, u32[]{:S(2)}, u32[]{:S(2)}) collective-permute-start(f32[2]{0:T(128)S(1)} %add.584), channel_id=1, source_target_pairs={{0,8},{8,0},{16,24},{24,16},{1,9},{9,1},{17,25},{25,17},{2,10},{10... | collective-permute-start | bytes 32 | tf_op jit(solution)/shard_map/ppermute | solution.py:73
  91.3 4.4 %collective-permute-start.14 = (f32[2]{0:T(128)S(1)}, f32[2]{0:T(128)S(1)}, u32[]{:S(2)}, u32[]{:S(2)}) collective-permute-start(f32[2]{0:T(128)S(1)} %add.585), channel_id=1, source_target_pairs={{0,16},{8,24},{16,0},{24,8},{1,17},{9,25},{17,1},{25,9},{2,18},{10... | collective-permute-start | bytes 32 | tf_op jit(solution)/shard_map/ppermute | solution.py:73
  103.1 4.8 %collective-permute-start.17 = (f32[1,64,512]{2,0,1:T(1,128)S(1)}, f32[1,64,512]{2,0,1:T(1,128)S(1)}, u32[]{:S(2)}, u32[]{:S(2)}) collective-permute-start(f32[1,64,512]{2,0,1:T(1,128)S(1)} %get-tuple-element.67), channel_id=1, source_target_pairs={{1,0},{2,1},{3,2},{4,3},{5,4},{6,5},{7,6},{9,8},{10,9},{11,10},{12... | collective-permute-start | bytes 393224 | tf_op jit(solution)/shard_map/ppermute | solution.py:51
  105.1 7.2 %collective-permute-start.18 = (f32[1,64,512]{2,0,1:T(1,128)S(1)}, f32[1,64,512]{2,0,1:T(1,128)S(1)}, u32[]{:S(2)}, u32[]{:S(2)}) collective-permute-start(f32[1,64,512]{2,0,1:T(1,128)S(1)} %get-tuple-element.68), channel_id=1, source_target_pairs={{0,1},{1,2},{2,3},{3,4},{4,5},{5,6},{6,7},{8,9},{9,10},{10,11},{11... | collective-permute-start | bytes 393224 | tf_op jit(solution)/shard_map/ppermute | solution.py:50
  114.5 6.8 %collective-permute-start.19 = (f32[4,512]{1,0:T(4,128)S(1)}, f32[4,512]{1,0:T(4,128)S(1)}, u32[]{:S(2)}, u32[]{:S(2)}) collective-permute-start(f32[4,512]{1,0:T(4,128)S(1)} %get-tuple-element.112), channel_id=1, source_target_pairs={{0,1},{1,2},{2,3},{3,4},{4,5},{5,6},{6,7},{8,9},{9,10},{10,11},{11... | collective-permute-start | bytes 24584 | tf_op jit(solution)/shard_map/ppermute | solution.py:50
  116.4 6.2 %collective-permute-start.20 = (f32[4,512]{1,0:T(4,128)S(1)}, f32[4,512]{1,0:T(4,128)S(1)}, u32[]{:S(2)}, u32[]{:S(2)}) collective-permute-start(f32[4,512]{1,0:T(4,128)S(1)} %get-tuple-element.113), channel_id=1, source_target_pairs={{1,0},{2,1},{3,2},{4,3},{5,4},{6,5},{7,6},{9,8},{10,9},{11,10},{12... | collective-permute-start | bytes 24584 | tf_op jit(solution)/shard_map/ppermute | solution.py:51
  128.9 7.2 %collective-permute-start.23 = (f32[33,512]{1,0:T(8,128)S(1)}, f32[33,512]{1,0:T(8,128)S(1)}, u32[]{:S(2)}, u32[]{:S(2)}) collective-permute-start(f32[33,512]{1,0:T(8,128)S(1)} %dynamic-update-slice.13), channel_id=1, source_target_pairs={{16,24},{17,25},{18,26},{19,27},{20,28},{21,29},{22,30},{23,31}} | collective-permute-start | bytes 202760 | tf_op jit(solution)/shard_map/ppermute | solution.py:162
  130.2 8.1 %collective-permute-start.22 = (f32[33,512]{1,0:T(8,128)S(1)}, f32[33,512]{1,0:T(8,128)S(1)}, u32[]{:S(2)}, u32[]{:S(2)}) collective-permute-start(f32[33,512]{1,0:T(8,128)S(1)} %dynamic-update-slice.13), channel_id=1, source_target_pairs={{8,24},{9,25},{10,26},{11,27},{12,28},{13,29},{14,30},{15,31}} | collective-permute-start | bytes 202760 | tf_op jit(solution)/shard_map/ppermute | solution.py:162
  131.5 8.1 %collective-permute-start.21 = (f32[33,512]{1,0:T(8,128)S(1)}, f32[33,512]{1,0:T(8,128)S(1)}, u32[]{:S(2)}, u32[]{:S(2)}) collective-permute-start(f32[33,512]{1,0:T(8,128)S(1)} %dynamic-update-slice.13), channel_id=1, source_target_pairs={{0,24},{1,25},{2,26},{3,27},{4,28},{5,29},{6,30},{7,31}} | collective-permute-start | bytes 202760 | tf_op jit(solution)/shard_map/ppermute | solution.py:162
  139.6 1.2 collective-permute-start.24
  140.8 3.5 %collective-permute-start.25 = (f32[4]{0:T(128)S(1)}, f32[4]{0:T(128)S(1)}, u32[]{:S(2)}, u32[]{:S(2)}) collective-permute-start(f32[4]{0:T(128)S(1)} %fusion.111), channel_id=1, source_target_pairs={{0,2},{1,3},{2,0},{3,1},{4,6},{5,7},{6,4},{7,5},{8,10},{9,11},{10,... | collective-permute-start | bytes 56 | tf_op jit(solution)/shard_map/ppermute | solution.py:73
  144.4 3.5 %collective-permute-start.26 = (f32[4]{0:T(128)S(1)}, f32[4]{0:T(128)S(1)}, u32[]{:S(2)}, u32[]{:S(2)}) collective-permute-start(f32[4]{0:T(128)S(1)} %add.629), channel_id=1, source_target_pairs={{0,4},{1,5},{2,6},{3,7},{4,0},{5,1},{6,2},{7,3},{8,12},{9,13},{10,... | collective-permute-start | bytes 56 | tf_op jit(solution)/shard_map/ppermute | solution.py:73
  (30 other events, 326.6 us)

commit v4 on v3

--- a/solution.py
+++ b/solution.py
@@ -52,18 +52,22 @@
     return jnp.concatenate([low, block, high], axis=0)
 
 
-def full_sweep(q, rhs, coef):
-    qx = rims(q, 1)
-    zero = jnp.zeros_like(q[:, :1])
-    return stencil(
-        rhs,
-        coef,
-        qx[2:],
-        qx[:-2],
-        jnp.concatenate([q[:, 1:], zero], axis=1),
-        jnp.concatenate([zero, q[:, :-1]], axis=1),
-        q,
-    )
+def deep_solve(q, rhs, coef, row_ok):
+    rows = q.shape[0]
+    for k in range(1, SWEEPS + 1):
+        centre = q[1:-1]
+        zero = jnp.zeros_like(centre[:, :1])
+        new = stencil(
+            rhs[k : rows - k],
+            coef[k : rows - k],
+            q[2:],
+            q[:-2],
+            jnp.concatenate([centre[:, 1:], zero], axis=1),
+            jnp.concatenate([zero, centre[:, :-1]], axis=1),
+            centre,
+        )
+        q = jnp.where(row_ok[k : rows - k], new, 0.0)
+    return q
 
 
 def allsum_axis(v, axis):
@@ -122,18 +126,22 @@
     tilde_zero, unused = evaluate(disp_zero)
     resid_zero = tilde_zero - disp_zero
     disp_one = disp_zero + RELAX * resid_zero
-    deep = start_here
-    for k in range(SWEEPS // 2):
-        deep = full_sweep(deep, force_here, coef_here)
-    disp_one, deep = lax.optimization_barrier((disp_one, deep))
     tilde_one, unused = evaluate(disp_one)
     resid_one = tilde_one - disp_one
     diff_one = resid_one - resid_zero
     sums = allsum(jnp.stack([jnp.sum(diff_one * diff_one), jnp.sum(diff_one * resid_one)]))
     gram_aa, gram_ab = sums[0], sums[1]
     coeff = -gram_ab / (gram_aa + (0.001 * gram_aa + 1e-06))
-    for k in range(SWEEPS // 2, SWEEPS):
-        deep = full_sweep(deep, force_here, coef_here)
+    deep_rims = rims(
+        jnp.concatenate([start_here[:, BAND:], force_here[:, BAND:], coef_here[:, BAND:]], axis=1), HALO
+    )
+    rest = planes - BAND
+    deep = deep_solve(
+        jnp.concatenate([init_band, deep_rims[:, :rest]], axis=1),
+        jnp.concatenate([force_band, deep_rims[:, rest : 2 * rest]], axis=1),
+        jnp.concatenate([coef_band, deep_rims[:, 2 * rest :]], axis=1),
+        row_ok,
+    )
     coeff, deep = lax.optimization_barrier((coeff, deep))
     disp_two = tilde_one + coeff * (tilde_one - tilde_zero)
     tilde_two, band_two = evaluate(disp_two)

time: 159 us -> 155 us (0.975)
  waiting for transfers between devices: 33.9 us -> 46.7 us
  starting transfers between devices: 51.8 us -> 39.4 us
  local copies, waits for them, and re-layouts: 26.6 us -> 17.7 us
  other arithmetic: 33 us -> 38.4 us
    div x4 -> x0, other arithmetic: 12.1 us -> none  [stencil(): return (rhs + total) / (6.0 + coef)]
    ppermute x8 -> x5, waiting for transfers between devices: 4.81 us -> 16.2 us  [rims(): low = lax.ppermute(block[block.shape[0] - width:], 'slab', forward)]
    select_n x0 -> x4, other arithmetic: none -> 9.31 us  [deep_solve(): q = jnp.where(row_ok[k:rows - k], new, 0.0)]
    ppermute x8 -> x5, starting transfers between devices: 17 us -> 9.57 us  [rims(): low = lax.ppermute(block[block.shape[0] - width:], 'slab', forward)]
    reduce_sum x3, other arithmetic: 1.9 us -> 8.67 us  [evaluate(): tilde = own_live * jnp.sum(compliance * loaded[:, None, :], axis=-1)]
    ppermute x8 -> x5, starting transfers between devices: 29.2 us -> 22.9 us  [rims(): high = lax.ppermute(block[:width], 'slab', backward)]
    slice x9 -> x8, local copies, waits for them, and re-layouts: 5.92 us -> 2.21 us  [the longest x3 1.35 us: deep_solve(): centre[:, 1:]]
    unnamed x79, local copies, waits for them, and re-layouts: 9.92 us -> 6.51 us
  transfers between devices with their start and end apart: 27 -> 21, of which waited for: 14 -> 14; matrix products, arithmetic and copies ran while one was open for 23% -> 17% of each run, Pallas kernels for 0% -> 0%
where the time goes in v4:
time: 155 us; the launch traced here: 153 us
  waiting for transfers between devices  46.7 us (30%)
  starting transfers between devices  39.4 us (25%)
  other arithmetic  38.4 us (25%)
  local copies, waits for them, and re-layouts  17.7 us (11%)
  between operations  11.2 us (7%)
    ppermute x5, starting transfers between devices, rims(): high = lax.ppermute(block[:width], 'slab', backward)  22.9 us
    ppermute x8, waiting for transfers between devices, allsum_axis(): v = v + lax.ppermute(v, axis, [(i, i ^ step) for i in range(count)])  21.4 us
    ppermute x5, waiting for transfers between devices, rims(): low = lax.ppermute(block[block.shape[0] - width:], 'slab', forward)  16.2 us
    ppermute x5, starting transfers between devices, rims(): low = lax.ppermute(block[block.shape[0] - width:], 'slab', forward)  9.57 us
    select_n x4, other arithmetic, deep_solve(): q = jnp.where(row_ok[k:rows - k], new, 0.0)  9.31 us
    reduce_sum x3, other arithmetic, evaluate(): tilde = own_live * jnp.sum(compliance * loaded[:, None, :], axis=-1)  8.67 us
    unnamed x79, local copies, waits for them, and re-layouts  6.51 us
    ppermute x3, waiting for transfers between devices, body(): lax.ppermute(outgoing, 'side', [(source, side_count - 1)])  6.41 us
  transfers between devices with their start and end apart: 21, of which 14 were waited for; matrix products, arithmetic and copies ran while one was open for 17% of the time, Pallas kernels for 0%

profile of v4, /device:TPU:28, one launch (start us, length us, event | category | flops | bytes accessed | tf_op | source)
XLA Modules:
  0.0 153.4 jit_solution(4104692725819775636)
XLA Ops:
  0.7 2.0 %copy.19 = f32[1,8,64,512]{3,1,2,0:T(8,128)S(1)} copy(f32[1,8,64,512]{3,2,1,0:T(8,128)} %param.16) | data formatting | bytes 2097152 | tf_op args[1]
  4.9 1.9 %collective-permute-start = (f32[4,24,512]{2,0,1:T(4,128)}, f32[4,24,512]{2,0,1:T(4,128)S(1)}, u32[]{:S(2)}, u32[]{:S(2)}) collective-permute-start(f32[4,24,512]{2,0,1:T(4,128)} %get-tuple-element.83), channel_id=1, source_target_pairs={{0,1},{1,2},{2,3},{3,4},{4,5},{5,6},{6,7},{8,9},{9,10},{10,11},{11... | collective-permute-start | bytes 589832 | tf_op jit(solution)/shard_map/ppermute | solution.py:50
  6.8 4.5 %collective-permute-start.1 = (f32[4,24,512]{2,0,1:T(4,128)}, f32[4,24,512]{2,0,1:T(4,128)}, u32[]{:S(2)}, u32[]{:S(2)}) collective-permute-start(f32[4,24,512]{2,0,1:T(4,128)} %get-tuple-element.84), channel_id=1, source_target_pairs={{1,0},{2,1},{3,2},{4,3},{5,4},{6,5},{7,6},{9,8},{10,9},{11,10},{12... | collective-permute-start | bytes 589832 | tf_op jit(solution)/shard_map/ppermute | solution.py:51
  11.9 2.0 %fusion.133 = (f32[4,168,512]{2,0,1:T(4,128)}, f32[4,168,512]{2,0,1:T(4,128)}) fusion(f32[8,168,512]{2,0,1:T(8,128)S(1)} %pad_maximum_fusion.1), kind=kLoop, calls=%fused_computation.247 | loop fusion | bytes 5505024 | tf_op jit(solution)/shard_map/slice | solution.py:50
  13.8 1.9 %collective-permute-start.11 = (f32[4,168,512]{2,0,1:T(4,128)}, f32[4,168,512]{2,0,1:T(4,128)}, u32[]{:S(2)}, u32[]{:S(2)}) collective-permute-start(f32[4,168,512]{2,0,1:T(4,128)} %get-tuple-element.62), channel_id=1, source_target_pairs={{0,1},{1,2},{2,3},{3,4},{4,5},{5,6},{6,7},{8,9},{9,10},{10,11},{11... | collective-permute-start | bytes 4128776 | tf_op jit(solution)/shard_map/ppermute | solution.py:50
  15.8 4.5 %collective-permute-start.12 = (f32[4,168,512]{2,0,1:T(4,128)}, f32[4,168,512]{2,0,1:T(4,128)}, u32[]{:S(2)}, u32[]{:S(2)}) collective-permute-start(f32[4,168,512]{2,0,1:T(4,128)} %get-tuple-element.63), channel_id=1, source_target_pairs={{1,0},{2,1},{3,2},{4,3},{5,4},{6,5},{7,6},{9,8},{10,9},{11,10},{12... | collective-permute-start | bytes 4128776 | tf_op jit(solution)/shard_map/ppermute | solution.py:51
  21.2 1.9 %collective-permute-start.2 = (f32[4,512]{1,0:T(4,128)}, f32[4,512]{1,0:T(4,128)}, u32[]{:S(2)}, u32[]{:S(2)}) collective-permute-start(f32[4,512]{1,0:T(4,128)} %get-tuple-element.110), channel_id=1, source_target_pairs={{0,1},{1,2},{2,3},{3,4},{4,5},{5,6},{6,7},{8,9},{9,10},{10,11},{11... | collective-permute-start | bytes 24584 | tf_op jit(solution)/shard_map/ppermute | solution.py:50
  23.5 4.7 %collective-permute-start.3 = (f32[4,512]{1,0:T(4,128)}, f32[4,512]{1,0:T(4,128)S(1)}, u32[]{:S(2)}, u32[]{:S(2)}) collective-permute-start(f32[4,512]{1,0:T(4,128)} %get-tuple-element.111), channel_id=1, source_target_pairs={{1,0},{2,1},{3,2},{4,3},{5,4},{6,5},{7,6},{9,8},{10,9},{11,10},{12... | collective-permute-start | bytes 24584 | tf_op jit(solution)/shard_map/ppermute | solution.py:51
  31.3 16.2 %collective-permute-done.11 = f32[4,168,512]{2,0,1:T(4,128)} collective-permute-done((f32[4,168,512]{2,0,1:T(4,128)}, f32[4,168,512]{2,0,1:T(4,128)}, u32[]{:S(2)}, u32[]{:S(2)}) %collective-permute-start.11) | collective-permute-done | bytes 1376288 | tf_op jit(solution)/shard_map/ppermute | solution.py:50
  47.5 2.6 %pad_maximum_fusion = f32[16,168,512]{2,0,1:T(8,128)S(1)} fusion(f32[4,168,512]{2,0,1:T(4,128)} %collective-permute-done.12, f32[8,56,512]{2,0,1:T(8,128)S(1)} %slice.839, f32[8,56,512]{2,0,1:T(8,128)S(1)} %slice.838, f32[8,56,512]{2,0,1:T(8,128)S(1)} %slice.837, f32[4,168,512]{2,0,1:T(4,128)} %collective-permute-done.11), kind=kLoop, calls=%fused_computation.3 | loop fusion | flops 5505024 | bytes 11010048 | tf_op jit(solution)/shard_map/concatenate | solution.py:52
  52.0 2.6 %fusion.7 = f32[14,64,512]{2,0,1:T(8,128)S(1)} fusion(f32[16,56,512]{2,0,1:T(8,128)S(1)} %get-tuple-element.60, f32[16,56,512]{2,0,1:T(8,128)S(1)} %get-tuple-element.59, f32[16,8,512]{2,0,1:T(8,128)S(1)} %get-tuple-element.79, f32[16,8,512]{2,0,1:T(8,128)S(1)} %get-tuple-element.78, f32[16,56,512]{2,0,1:T(8,128)S(1)} %get-tuple-element.61, ...), kind=kLoop, calls=%fused_computation.34 | loop fusion | flops 7798784 | bytes 13570574 | tf_op jit(solution)/shard_map/jit(_where)/select_n | solution.py:69
  56.2 2.6 %fusion.11 = f32[12,64,512]{2,0,1:T(8,128)S(1)} fusion(f32[16,56,512]{2,0,1:T(8,128)S(1)} %get-tuple-element.60, f32[16,56,512]{2,0,1:T(8,128)S(1)} %get-tuple-element.61, f32[16,8,512]{2,0,1:T(8,128)S(1)} %get-tuple-element.79, f32[16,8,512]{2,0,1:T(8,128)S(1)} %get-tuple-element.80, f32[14,64,512]{2,0,1:T(8,128)S(1)} %fusion.7, ...), kind=kLoop, calls=%fused_computation.38 | loop fusion | flops 4325376 | bytes 15149068 | tf_op jit(solution)/shard_map/jit(_where)/select_n | solution.py:69
  60.4 2.7 %fusion.3 = f32[10,64,512]{2,0,1:T(8,128)S(1)} fusion(f32[16,56,512]{2,0,1:T(8,128)S(1)} %get-tuple-element.60, f32[16,56,512]{2,0,1:T(8,128)S(1)} %get-tuple-element.61, f32[16,8,512]{2,0,1:T(8,128)S(1)} %get-tuple-element.79, f32[16,8,512]{2,0,1:T(8,128)S(1)} %get-tuple-element.80, f32[12,64,512]{2,0,1:T(8,128)S(1)} %fusion.11, ...), kind=kLoop, calls=%fused_computation.30 | loop fusion | flops 3604480 | bytes 13323274 | tf_op jit(solution)/shard_map/jit(_where)/select_n | solution.py:69
  64.0 1.4 fusion.38
  65.5 1.5 fusion.96
  70.1 1.9 %collective-permute-start.4 = (f32[4,512]{1,0:T(4,128)S(1)}, f32[4,512]{1,0:T(4,128)S(1)}, u32[]{:S(2)}, u32[]{:S(2)}) collective-permute-start(f32[4,512]{1,0:T(4,128)S(1)} %get-tuple-element.108), channel_id=1, source_target_pairs={{0,1},{1,2},{2,3},{3,4},{4,5},{5,6},{6,7},{8,9},{9,10},{10,11},{11... | collective-permute-start | bytes 24584 | tf_op jit(solution)/shard_map/ppermute | solution.py:50
  72.0 4.5 %collective-permute-start.5 = (f32[4,512]{1,0:T(4,128)S(1)}, f32[4,512]{1,0:T(4,128)S(1)}, u32[]{:S(2)}, u32[]{:S(2)}) collective-permute-start(f32[4,512]{1,0:T(4,128)S(1)} %get-tuple-element.109), channel_id=1, source_target_pairs={{1,0},{2,1},{3,2},{4,3},{5,4},{6,5},{7,6},{9,8},{10,9},{11,10},{12... | collective-permute-start | bytes 24584 | tf_op jit(solution)/shard_map/ppermute | solution.py:51
  79.3 4.0 %multiply_reduce_fusion.1 = f32[8,512]{1,0:T(8,128)S(1)} fusion(f32[8,512,512]{2,1,0:T(8,128)} %param.18, f32[8,512]{1,0:T(8,128)S(1)} %subtract_select_fusion.1), kind=kLoop, calls=%fused_computation.1 | loop fusion | flops 4190208 | bytes 8421376 | tf_op jit(solution)/shard_map/reduce_sum | solution.py:122
  87.9 3.5 %collective-permute-done.7 = f32[2]{0:T(128)S(1)} collective-permute-done((f32[2]{0:T(128)S(1)}, f32[2]{0:T(128)S(1)}, u32[]{:S(2)}, u32[]{:S(2)}) %collective-permute-start.7) | collective-permute-done | bytes 40 | tf_op jit(solution)/shard_map/ppermute | solution.py:77
  94.0 2.3 %collective-permute-done.8 = f32[2]{0:T(128)S(1)} collective-permute-done((f32[2]{0:T(128)S(1)}, f32[2]{0:T(128)S(1)}, u32[]{:S(2)}, u32[]{:S(2)}) %collective-permute-start.8) | collective-permute-done | bytes 40 | tf_op jit(solution)/shard_map/ppermute | solution.py:77
  96.8 3.1 %collective-permute-done.9 = f32[2]{0:T(128)S(1)} collective-permute-done((f32[2]{0:T(128)S(1)}, f32[2]{0:T(128)S(1)}, u32[]{:S(2)}, u32[]{:S(2)}) %collective-permute-start.9) | collective-permute-done | bytes 40 | tf_op jit(solution)/shard_map/ppermute | solution.py:77
  100.2 4.1 %collective-permute-done.10 = f32[2]{0:T(128)S(1)} collective-permute-done((f32[2]{0:T(128)S(1)}, f32[2]{0:T(128)S(1)}, u32[]{:S(2)}, u32[]{:S(2)}) %collective-permute-start.10) | collective-permute-done | bytes 40 | tf_op jit(solution)/shard_map/ppermute | solution.py:77
  107.1 1.9 %collective-permute-start.13 = (f32[4,512]{1,0:T(4,128)S(1)}, f32[4,512]{1,0:T(4,128)S(1)}, u32[]{:S(2)}, u32[]{:S(2)}) collective-permute-start(f32[4,512]{1,0:T(4,128)S(1)} %get-tuple-element.106), channel_id=1, source_target_pairs={{0,1},{1,2},{2,3},{3,4},{4,5},{5,6},{6,7},{8,9},{9,10},{10,11},{11... | collective-permute-start | bytes 24584 | tf_op jit(solution)/shard_map/ppermute | solution.py:50
  109.0 4.5 %collective-permute-start.14 = (f32[4,512]{1,0:T(4,128)S(1)}, f32[4,512]{1,0:T(4,128)S(1)}, u32[]{:S(2)}, u32[]{:S(2)}) collective-permute-start(f32[4,512]{1,0:T(4,128)S(1)} %get-tuple-element.107), channel_id=1, source_target_pairs={{1,0},{2,1},{3,2},{4,3},{5,4},{6,5},{7,6},{9,8},{10,9},{11,10},{12... | collective-permute-start | bytes 24584 | tf_op jit(solution)/shard_map/ppermute | solution.py:51
  116.9 4.0 %multiply_reduce_fusion = f32[8,512]{1,0:T(8,128)S(1)} fusion(f32[8,512,512]{2,1,0:T(8,128)} %param.18, f32[8,512]{1,0:T(8,128)S(1)} %subtract_select_fusion), kind=kLoop, calls=%fused_computation | loop fusion | flops 4190208 | bytes 8421376 | tf_op jit(solution)/shard_map/reduce_sum | solution.py:122
  121.8 2.5 %fusion.125 = f32[1,512]{1,0:T(1,128)S(1)} fusion(f32[]{:T(128)} %get-tuple-element.48, f32[]{:T(128)} %get-tuple-element.49, f32[]{:T(128)} %get-tuple-element.47, f32[]{:T(128)} %get-tuple-element.46), kind=kLoop, calls=%fused_computation.239 | loop fusion | flops 5632 | bytes 2064 | tf_op jit(solution)/shard_map/add | solution.py:162
  128.4 1.6 %copy.15 = f32[1,8,64,512]{3,2,1,0:T(8,128)} copy(f32[1,8,64,512]{3,1,2,0:T(8,128)S(1)} %maximum_select_fusion) | data formatting | bytes 2097152
  129.9 3.1 %collective-permute-done.15 = f32[33,512]{1,0:T(8,128)S(1)} collective-permute-done((f32[33,512]{1,0:T(8,128)S(1)}, f32[33,512]{1,0:T(8,128)S(1)}, u32[]{:S(2)}, u32[]{:S(2)}) %collective-permute-start.15) | collective-permute-done | bytes 67616 | tf_op jit(solution)/shard_map/ppermute | solution.py:170
  133.0 1.7 %collective-permute-done.16 = f32[33,512]{1,0:T(8,128)S(1)} collective-permute-done((f32[33,512]{1,0:T(8,128)S(1)}, f32[33,512]{1,0:T(8,128)S(1)}, u32[]{:S(2)}, u32[]{:S(2)}) %collective-permute-start.16) | collective-permute-done | bytes 67616 | tf_op jit(solution)/shard_map/ppermute | solution.py:170
  134.7 1.7 %collective-permute-done.17 = f32[33,512]{1,0:T(8,128)S(1)} collective-permute-done((f32[33,512]{1,0:T(8,128)S(1)}, f32[33,512]{1,0:T(8,128)S(1)}, u32[]{:S(2)}, u32[]{:S(2)}) %collective-permute-start.17) | collective-permute-done | bytes 67616 | tf_op jit(solution)/shard_map/ppermute | solution.py:170
  137.6 3.5 %collective-permute-done.19 = f32[4]{0:T(128)S(1)} collective-permute-done((f32[4]{0:T(128)S(1)}, f32[4]{0:T(128)S(1)}, u32[]{:S(2)}, u32[]{:S(2)}) %collective-permute-start.19) | collective-permute-done | bytes 48 | tf_op jit(solution)/shard_map/ppermute | solution.py:77
  142.0 2.7 %collective-permute-done.20 = f32[4]{0:T(128)S(1)} collective-permute-done((f32[4]{0:T(128)S(1)}, f32[4]{0:T(128)S(1)}, u32[]{:S(2)}, u32[]{:S(2)}) %collective-permute-start.20) | collective-permute-done | bytes 48 | tf_op jit(solution)/shard_map/ppermute | solution.py:77
  (204 shorter events, 38.4 us)
Async XLA Ops:
  2.6 8.7 %copy-start = (f32[1,8,64,512]{3,1,2,0:T(8,128)}, f32[1,8,64,512]{3,1,2,0:T(8,128)S(1)}, u32[]{:S(2)}) copy-start(f32[1,8,64,512]{3,1,2,0:T(8,128)S(1)} %copy.19) | copy-start | bytes 3145732
  4.9 18.7 %collective-permute-start = (f32[4,24,512]{2,0,1:T(4,128)}, f32[4,24,512]{2,0,1:T(4,128)S(1)}, u32[]{:S(2)}, u32[]{:S(2)}) collective-permute-start(f32[4,24,512]{2,0,1:T(4,128)} %get-tuple-element.83), channel_id=1, source_target_pairs={{0,1},{1,2},{2,3},{3,4},{4,5},{5,6},{6,7},{8,9},{9,10},{10,11},{11... | collective-permute-start | bytes 589832 | tf_op jit(solution)/shard_map/ppermute | solution.py:50
  6.8 21.5 %collective-permute-start.1 = (f32[4,24,512]{2,0,1:T(4,128)}, f32[4,24,512]{2,0,1:T(4,128)}, u32[]{:S(2)}, u32[]{:S(2)}) collective-permute-start(f32[4,24,512]{2,0,1:T(4,128)} %get-tuple-element.84), channel_id=1, source_target_pairs={{1,0},{2,1},{3,2},{4,3},{5,4},{6,5},{7,6},{9,8},{10,9},{11,10},{12... | collective-permute-start | bytes 589832 | tf_op jit(solution)/shard_map/ppermute | solution.py:51
  11.8 8.5 %copy-start.14 = (f32[8,512]{1,0:T(8,128)S(1)}, f32[8,512]{1,0:T(8,128)}, u32[]{:S(2)}) copy-start(f32[8,512]{1,0:T(8,128)} %param.20) | copy-start | bytes 49156
  11.9 8.6 %copy-start.32 = (s32[8]{0:T(128)S(1)}, s32[8]{0:T(128)}, u32[]{:S(2)}) copy-start(s32[8]{0:T(128)} %param.23) | copy-start | bytes 100
  13.8 33.7 %collective-permute-start.11 = (f32[4,168,512]{2,0,1:T(4,128)}, f32[4,168,512]{2,0,1:T(4,128)}, u32[]{:S(2)}, u32[]{:S(2)}) collective-permute-start(f32[4,168,512]{2,0,1:T(4,128)} %get-tuple-element.62), channel_id=1, source_target_pairs={{0,1},{1,2},{2,3},{3,4},{4,5},{5,6},{6,7},{8,9},{9,10},{10,11},{11... | collective-permute-start | bytes 4128776 | tf_op jit(solution)/shard_map/ppermute | solution.py:50
  15.8 31.8 %collective-permute-start.12 = (f32[4,168,512]{2,0,1:T(4,128)}, f32[4,168,512]{2,0,1:T(4,128)}, u32[]{:S(2)}, u32[]{:S(2)}) collective-permute-start(f32[4,168,512]{2,0,1:T(4,128)} %get-tuple-element.63), channel_id=1, source_target_pairs={{1,0},{2,1},{3,2},{4,3},{5,4},{6,5},{7,6},{9,8},{10,9},{11,10},{12... | collective-permute-start | bytes 4128776 | tf_op jit(solution)/shard_map/ppermute | solution.py:51
  21.2 44.2 %collective-permute-start.2 = (f32[4,512]{1,0:T(4,128)}, f32[4,512]{1,0:T(4,128)}, u32[]{:S(2)}, u32[]{:S(2)}) collective-permute-start(f32[4,512]{1,0:T(4,128)} %get-tuple-element.110), channel_id=1, source_target_pairs={{0,1},{1,2},{2,3},{3,4},{4,5},{5,6},{6,7},{8,9},{9,10},{10,11},{11... | collective-permute-start | bytes 24584 | tf_op jit(solution)/shard_map/ppermute | solution.py:50
  23.2 43.8 %copy-start.28 = (pred[14]{0:T(512)(128)(4,1)}, pred[14]{0:T(512)(128)(4,1)S(1)}, u32[]{:S(2)}) copy-start(pred[14]{0:T(512)(128)(4,1)S(1)} %slice.632) | copy-start | bytes 46
  23.3 44.1 %copy-start.24 = (pred[12]{0:T(512)(128)(4,1)}, pred[12]{0:T(512)(128)(4,1)S(1)}, u32[]{:S(2)}) copy-start(pred[12]{0:T(512)(128)(4,1)S(1)} %slice.630) | copy-start | bytes 40
  23.4 44.4 %copy-start.26 = (pred[10]{0:T(512)(128)(4,1)}, pred[10]{0:T(512)(128)(4,1)S(1)}, u32[]{:S(2)}) copy-start(pred[10]{0:T(512)(128)(4,1)S(1)} %slice.628) | copy-start | bytes 34
  23.4 45.4 %copy-start.30 = (pred[8]{0:T(512)(128)(4,1)}, pred[8]{0:T(512)(128)(4,1)S(1)}, u32[]{:S(2)}) copy-start(pred[8]{0:T(512)(128)(4,1)S(1)} %slice.617) | copy-start | bytes 28
  23.5 45.5 %copy-start.18 = (f32[8,8]{1,0:T(8,128)}, f32[8,8]{1,0:T(8,128)S(1)}, u32[]{:S(2)}) copy-start(f32[8,8]{1,0:T(8,128)S(1)} %fusion.121) | copy-start | bytes 772
  23.5 41.9 %collective-permute-start.3 = (f32[4,512]{1,0:T(4,128)}, f32[4,512]{1,0:T(4,128)S(1)}, u32[]{:S(2)}, u32[]{:S(2)}) collective-permute-start(f32[4,512]{1,0:T(4,128)} %get-tuple-element.111), channel_id=1, source_target_pairs={{1,0},{2,1},{3,2},{4,3},{5,4},{6,5},{7,6},{9,8},{10,9},{11,10},{12... | collective-permute-start | bytes 24584 | tf_op jit(solution)/shard_map/ppermute | solution.py:51
  69.2 8.7 %copy-start.1 = (f32[16,8,512]{2,0,1:T(8,128)S(1)}, f32[16,8,512]{2,0,1:T(8,128)}, u32[]{:S(2)}) copy-start(f32[16,8,512]{2,0,1:T(8,128)} %copy.23) | copy-start | bytes 786436
  69.2 8.7 %copy-start.29 = (pred[14]{0:T(512)(128)(4,1)S(1)}, pred[14]{0:T(512)(128)(4,1)}, u32[]{:S(2)}) copy-start(pred[14]{0:T(512)(128)(4,1)} %copy-done.28) | copy-start | bytes 46
  70.1 6.5 %collective-permute-start.4 = (f32[4,512]{1,0:T(4,128)S(1)}, f32[4,512]{1,0:T(4,128)S(1)}, u32[]{:S(2)}, u32[]{:S(2)}) collective-permute-start(f32[4,512]{1,0:T(4,128)S(1)} %get-tuple-element.108), channel_id=1, source_target_pairs={{0,1},{1,2},{2,3},{3,4},{4,5},{5,6},{6,7},{8,9},{9,10},{10,11},{11... | collective-permute-start | bytes 24584 | tf_op jit(solution)/shard_map/ppermute | solution.py:50
  72.0 5.9 %collective-permute-start.5 = (f32[4,512]{1,0:T(4,128)S(1)}, f32[4,512]{1,0:T(4,128)S(1)}, u32[]{:S(2)}, u32[]{:S(2)}) collective-permute-start(f32[4,512]{1,0:T(4,128)S(1)} %get-tuple-element.109), channel_id=1, source_target_pairs={{1,0},{2,1},{3,2},{4,3},{5,4},{6,5},{7,6},{9,8},{10,9},{11,10},{12... | collective-permute-start | bytes 24584 | tf_op jit(solution)/shard_map/ppermute | solution.py:51
  83.3 31.6 %copy-start.2 = (f32[16,8,512]{2,0,1:T(8,128)S(1)}, f32[16,8,512]{2,0,1:T(8,128)}, u32[]{:S(2)}) copy-start(f32[16,8,512]{2,0,1:T(8,128)} %copy.24) | copy-start | bytes 786436
  85.4 1.1 collective-permute-start.6
  87.8 3.5 %collective-permute-start.7 = (f32[2]{0:T(128)S(1)}, f32[2]{0:T(128)S(1)}, u32[]{:S(2)}, u32[]{:S(2)}) collective-permute-start(f32[2]{0:T(128)S(1)} %fusion.157), channel_id=1, source_target_pairs={{0,2},{1,3},{2,0},{3,1},{4,6},{5,7},{6,4},{7,5},{8,10},{9,11},{10,... | collective-permute-start | bytes 32 | tf_op jit(solution)/shard_map/ppermute | solution.py:77
  92.8 3.5 %collective-permute-start.8 = (f32[2]{0:T(128)S(1)}, f32[2]{0:T(128)S(1)}, u32[]{:S(2)}, u32[]{:S(2)}) collective-permute-start(f32[2]{0:T(128)S(1)} %fusion.158), channel_id=1, source_target_pairs={{0,4},{1,5},{2,6},{3,7},{4,0},{5,1},{6,2},{7,3},{8,12},{9,13},{10,... | collective-permute-start | bytes 32 | tf_op jit(solution)/shard_map/ppermute | solution.py:77
  96.3 3.5 %collective-permute-start.9 = (f32[2]{0:T(128)S(1)}, f32[2]{0:T(128)S(1)}, u32[]{:S(2)}, u32[]{:S(2)}) collective-permute-start(f32[2]{0:T(128)S(1)} %add.589), channel_id=1, source_target_pairs={{0,8},{8,0},{16,24},{24,16},{1,9},{9,1},{17,25},{25,17},{2,10},{10... | collective-permute-start | bytes 32 | tf_op jit(solution)/shard_map/ppermute | solution.py:77
  99.9 4.4 %collective-permute-start.10 = (f32[2]{0:T(128)S(1)}, f32[2]{0:T(128)S(1)}, u32[]{:S(2)}, u32[]{:S(2)}) collective-permute-start(f32[2]{0:T(128)S(1)} %add.590), channel_id=1, source_target_pairs={{0,16},{8,24},{16,0},{24,8},{1,17},{9,25},{17,1},{25,9},{2,18},{10... | collective-permute-start | bytes 32 | tf_op jit(solution)/shard_map/ppermute | solution.py:77
  107.1 6.6 %collective-permute-start.13 = (f32[4,512]{1,0:T(4,128)S(1)}, f32[4,512]{1,0:T(4,128)S(1)}, u32[]{:S(2)}, u32[]{:S(2)}) collective-permute-start(f32[4,512]{1,0:T(4,128)S(1)} %get-tuple-element.106), channel_id=1, source_target_pairs={{0,1},{1,2},{2,3},{3,4},{4,5},{5,6},{6,7},{8,9},{9,10},{10,11},{11... | collective-permute-start | bytes 24584 | tf_op jit(solution)/shard_map/ppermute | solution.py:50
  109.0 5.9 %collective-permute-start.14 = (f32[4,512]{1,0:T(4,128)S(1)}, f32[4,512]{1,0:T(4,128)S(1)}, u32[]{:S(2)}, u32[]{:S(2)}) collective-permute-start(f32[4,512]{1,0:T(4,128)S(1)} %get-tuple-element.107), channel_id=1, source_target_pairs={{1,0},{2,1},{3,2},{4,3},{5,4},{6,5},{7,6},{9,8},{10,9},{11,10},{12... | collective-permute-start | bytes 24584 | tf_op jit(solution)/shard_map/ppermute | solution.py:51
  124.4 8.7 %collective-permute-start.15 = (f32[33,512]{1,0:T(8,128)S(1)}, f32[33,512]{1,0:T(8,128)S(1)}, u32[]{:S(2)}, u32[]{:S(2)}) collective-permute-start(f32[33,512]{1,0:T(8,128)S(1)} %dynamic-update-slice.13), channel_id=1, source_target_pairs={{0,24},{1,25},{2,26},{3,27},{4,28},{5,29},{6,30},{7,31}} | collective-permute-start | bytes 202760 | tf_op jit(solution)/shard_map/ppermute | solution.py:170
  125.7 9.0 %collective-permute-start.16 = (f32[33,512]{1,0:T(8,128)S(1)}, f32[33,512]{1,0:T(8,128)S(1)}, u32[]{:S(2)}, u32[]{:S(2)}) collective-permute-start(f32[33,512]{1,0:T(8,128)S(1)} %dynamic-update-slice.13), channel_id=1, source_target_pairs={{8,24},{9,25},{10,26},{11,27},{12,28},{13,29},{14,30},{15,31}} | collective-permute-start | bytes 202760 | tf_op jit(solution)/shard_map/ppermute | solution.py:170
  127.0 9.4 %collective-permute-start.17 = (f32[33,512]{1,0:T(8,128)S(1)}, f32[33,512]{1,0:T(8,128)S(1)}, u32[]{:S(2)}, u32[]{:S(2)}) collective-permute-start(f32[33,512]{1,0:T(8,128)S(1)} %dynamic-update-slice.13), channel_id=1, source_target_pairs={{16,24},{17,25},{18,26},{19,27},{20,28},{21,29},{22,30},{23,31}} | collective-permute-start | bytes 202760 | tf_op jit(solution)/shard_map/ppermute | solution.py:170
  136.4 1.2 collective-permute-start.18
  137.6 3.5 %collective-permute-start.19 = (f32[4]{0:T(128)S(1)}, f32[4]{0:T(128)S(1)}, u32[]{:S(2)}, u32[]{:S(2)}) collective-permute-start(f32[4]{0:T(128)S(1)} %fusion.127), channel_id=1, source_target_pairs={{0,2},{1,3},{2,0},{3,1},{4,6},{5,7},{6,4},{7,5},{8,10},{9,11},{10,... | collective-permute-start | bytes 56 | tf_op jit(solution)/shard_map/ppermute | solution.py:77
  141.1 3.5 %collective-permute-start.20 = (f32[4]{0:T(128)S(1)}, f32[4]{0:T(128)S(1)}, u32[]{:S(2)}, u32[]{:S(2)}) collective-permute-start(f32[4]{0:T(128)S(1)} %add.654), channel_id=1, source_target_pairs={{0,4},{1,5},{2,6},{3,7},{4,0},{5,1},{6,2},{7,3},{8,12},{9,13},{10,... | collective-permute-start | bytes 56 | tf_op jit(solution)/shard_map/ppermute | solution.py:77
  (25 other events, 91.0 us)

commit v5 on v4

--- a/solution.py
+++ b/solution.py
@@ -136,6 +136,7 @@
         jnp.concatenate([start_here[:, BAND:], force_here[:, BAND:], coef_here[:, BAND:]], axis=1), HALO
     )
     rest = planes - BAND
+    deep_rims, tilde_one = lax.optimization_barrier((deep_rims, tilde_one))
     deep = deep_solve(
         jnp.concatenate([init_band, deep_rims[:, :rest]], axis=1),
         jnp.concatenate([force_band, deep_rims[:, rest : 2 * rest]], axis=1),

time: 155 us -> 156 us (level)
  waiting for transfers between devices: 46.7 us -> 37.2 us
  local copies, waits for them, and re-layouts: 17.7 us -> 22 us
  starting transfers between devices: 39.4 us -> 42.8 us
  other arithmetic: 38.4 us -> 40.8 us
    ppermute x5, waiting for transfers between devices: 16.2 us -> 0.01 us  [rims(): low = lax.ppermute(block[block.shape[0] - width:], 'slab', forward)]
    ppermute x8, waiting for transfers between devices: 21.4 us -> 30.8 us  [allsum_axis(): v = v + lax.ppermute(v, axis, [(i, i ^ step) for i in range(count)])]
    reduce_sum x3, other arithmetic: 8.67 us -> 5.28 us  [evaluate(): tilde = own_live * jnp.sum(compliance * loaded[:, None, :], axis=-1)]
    ppermute x8, starting transfers between devices: 3.04 us -> 6 us  [allsum_axis(): v = v + lax.ppermute(v, axis, [(i, i ^ step) for i in range(count)])]
    select_n x10, other arithmetic: 2.3 us -> 3.96 us  [band_solve(): q = jnp.where(row_ok[k:rows - k], new, 0.0)]
    unnamed x79 -> x80, local copies, waits for them, and re-layouts: 6.51 us -> 7.79 us
  transfers between devices with their start and end apart: 21 -> 21, of which waited for: 14 -> 13; matrix products, arithmetic and copies ran while one was open for 17% -> 17% of each run, Pallas kernels for 0% -> 0%
where the time goes in v5:
time: 156 us; the launch traced here: 154 us
  starting transfers between devices  42.8 us (27%)
  other arithmetic  40.8 us (26%)
  waiting for transfers between devices  37.2 us (24%)
  local copies, waits for them, and re-layouts  22 us (14%)
  between operations  11.3 us (7%)
    ppermute x8, waiting for transfers between devices, allsum_axis(): v = v + lax.ppermute(v, axis, [(i, i ^ step) for i in range(count)])  30.8 us
    ppermute x5, starting transfers between devices, rims(): high = lax.ppermute(block[:width], 'slab', backward)  23.1 us
    ppermute x5, starting transfers between devices, rims(): low = lax.ppermute(block[block.shape[0] - width:], 'slab', forward)  9.82 us
    select_n x4, other arithmetic, deep_solve(): q = jnp.where(row_ok[k:rows - k], new, 0.0)  9.15 us
    unnamed x80, local copies, waits for them, and re-layouts  7.79 us
    ppermute x8, starting transfers between devices, allsum_axis(): v = v + lax.ppermute(v, axis, [(i, i ^ step) for i in range(count)])  6 us
    reduce_sum x3, other arithmetic, evaluate(): tilde = own_live * jnp.sum(compliance * loaded[:, None, :], axis=-1)  5.28 us
    ppermute x3, waiting for transfers between devices, body(): lax.ppermute(outgoing, 'side', [(source, side_count - 1)])  5.15 us
  transfers between devices with their start and end apart: 21, of which 13 were waited for; matrix products, arithmetic and copies ran while one was open for 17% of the time, Pallas kernels for 0%

profile of v5, /device:TPU:28, one launch (start us, length us, event | category | flops | bytes accessed | tf_op | source)
XLA Modules:
  0.0 153.9 jit_solution(11646752916057453016)
XLA Ops:
  3.6 1.9 %collective-permute-start.4 = (f32[4,512]{1,0:T(4,128)}, f32[4,512]{1,0:T(4,128)}, u32[]{:S(2)}, u32[]{:S(2)}) collective-permute-start(f32[4,512]{1,0:T(4,128)} %get-tuple-element.115), channel_id=1, source_target_pairs={{0,1},{1,2},{2,3},{3,4},{4,5},{5,6},{6,7},{8,9},{9,10},{10,11},{11... | collective-permute-start | bytes 24584 | tf_op jit(solution)/shard_map/ppermute | solution.py:50
  5.5 4.7 %collective-permute-start.5 = (f32[4,512]{1,0:T(4,128)}, f32[4,512]{1,0:T(4,128)}, u32[]{:S(2)}, u32[]{:S(2)}) collective-permute-start(f32[4,512]{1,0:T(4,128)} %get-tuple-element.116), channel_id=1, source_target_pairs={{1,0},{2,1},{3,2},{4,3},{5,4},{6,5},{7,6},{9,8},{10,9},{11,10},{12... | collective-permute-start | bytes 24584 | tf_op jit(solution)/shard_map/ppermute | solution.py:51
  10.2 1.8 %copy.20 = f32[1,8,64,512]{3,1,2,0:T(8,128)S(1)} copy(f32[1,8,64,512]{3,2,1,0:T(8,128)} %param.15) | data formatting | bytes 2097152 | tf_op args[0]
  12.8 1.6 %copy.21 = f32[1,8,64,512]{3,1,2,0:T(8,128)} copy(f32[1,8,64,512]{3,2,1,0:T(8,128)S(1)} %copy-done.8) | data formatting | bytes 2097152 | tf_op args[2]
  16.1 1.9 %collective-permute-start = (f32[4,24,512]{2,0,1:T(4,128)}, f32[4,24,512]{2,0,1:T(4,128)}, u32[]{:S(2)}, u32[]{:S(2)}) collective-permute-start(f32[4,24,512]{2,0,1:T(4,128)} %get-tuple-element.88), channel_id=1, source_target_pairs={{0,1},{1,2},{2,3},{3,4},{4,5},{5,6},{6,7},{8,9},{9,10},{10,11},{11... | collective-permute-start | bytes 589832 | tf_op jit(solution)/shard_map/ppermute | solution.py:50
  18.0 4.5 %collective-permute-start.1 = (f32[4,24,512]{2,0,1:T(4,128)}, f32[4,24,512]{2,0,1:T(4,128)}, u32[]{:S(2)}, u32[]{:S(2)}) collective-permute-start(f32[4,24,512]{2,0,1:T(4,128)} %get-tuple-element.89), channel_id=1, source_target_pairs={{1,0},{2,1},{3,2},{4,3},{5,4},{6,5},{7,6},{9,8},{10,9},{11,10},{12... | collective-permute-start | bytes 589832 | tf_op jit(solution)/shard_map/ppermute | solution.py:51
  26.1 1.7 %pad_maximum_fusion.4 = f32[16,24,512]{2,0,1:T(8,128)S(1)} fusion(f32[4,24,512]{2,0,1:T(4,128)} %collective-permute-done.1, f32[8,8,512]{2,0,1:T(8,128)S(1)} %slice.769, f32[8,8,512]{2,0,1:T(8,128)S(1)} %slice.768, f32[8,8,512]{2,0,1:T(8,128)S(1)} %slice.767, f32[4,24,512]{2,0,1:T(4,128)} %collective-permute-done), kind=kLoop, calls=%fused_computation.83 | loop fusion | flops 786432 | bytes 1572864 | tf_op jit(solution)/shard_map/concatenate | solution.py:52
  28.7 1.7 %fusion.96 = (f32[16,8,512]{2,0,1:T(8,128)S(1)}, f32[16,1,512]{2,0,1:T(8,128)}) fusion(f32[16,8,512]{2,0,1:T(8,128)S(1)} %copy.22, f32[4,512]{1,0:T(4,128)} %collective-permute-done.5, f32[8,512]{1,0:T(8,128)S(1)} %multiply_reduce_fusion.8, f32[4,512]{1,0:T(4,128)} %collective-permute-done.4, f32[4,24,512]{2,0,1:T(4,128)} %collective-permute-done.1, ...), kind=kLoop, calls=%fused_computation.173 | loop fusion | flops 57344 | bytes 884736 | tf_op jit(solution)/shard_map/scatter-add | solution.py:118
  35.2 1.9 %collective-permute-start.6 = (f32[4,512]{1,0:T(4,128)}, f32[4,512]{1,0:T(4,128)S(1)}, u32[]{:S(2)}, u32[]{:S(2)}) collective-permute-start(f32[4,512]{1,0:T(4,128)} %get-tuple-element.113), channel_id=1, source_target_pairs={{0,1},{1,2},{2,3},{3,4},{4,5},{5,6},{6,7},{8,9},{9,10},{10,11},{11... | collective-permute-start | bytes 24584 | tf_op jit(solution)/shard_map/ppermute | solution.py:50
  37.1 4.5 %collective-permute-start.7 = (f32[4,512]{1,0:T(4,128)S(1)}, f32[4,512]{1,0:T(4,128)S(1)}, u32[]{:S(2)}, u32[]{:S(2)}) collective-permute-start(f32[4,512]{1,0:T(4,128)S(1)} %get-tuple-element.114), channel_id=1, source_target_pairs={{1,0},{2,1},{3,2},{4,3},{5,4},{6,5},{7,6},{9,8},{10,9},{11,10},{12... | collective-permute-start | bytes 24584 | tf_op jit(solution)/shard_map/ppermute | solution.py:51
  41.6 2.0 %fusion.132 = (f32[4,168,512]{2,0,1:T(4,128)}, f32[4,168,512]{2,0,1:T(4,128)}) fusion(f32[8,168,512]{2,0,1:T(8,128)S(1)} %pad_maximum_fusion.1), kind=kLoop, calls=%fused_computation.247 | loop fusion | bytes 5505024 | tf_op jit(solution)/shard_map/slice | solution.py:50
  43.6 2.0 %collective-permute-start.2 = (f32[4,168,512]{2,0,1:T(4,128)}, f32[4,168,512]{2,0,1:T(4,128)}, u32[]{:S(2)}, u32[]{:S(2)}) collective-permute-start(f32[4,168,512]{2,0,1:T(4,128)} %get-tuple-element.67), channel_id=1, source_target_pairs={{0,1},{1,2},{2,3},{3,4},{4,5},{5,6},{6,7},{8,9},{9,10},{10,11},{11... | collective-permute-start | bytes 4128776 | tf_op jit(solution)/shard_map/ppermute | solution.py:50
  45.7 4.5 %collective-permute-start.3 = (f32[4,168,512]{2,0,1:T(4,128)}, f32[4,168,512]{2,0,1:T(4,128)}, u32[]{:S(2)}, u32[]{:S(2)}) collective-permute-start(f32[4,168,512]{2,0,1:T(4,128)} %get-tuple-element.68), channel_id=1, source_target_pairs={{1,0},{2,1},{3,2},{4,3},{5,4},{6,5},{7,6},{9,8},{10,9},{11,10},{12... | collective-permute-start | bytes 4128776 | tf_op jit(solution)/shard_map/ppermute | solution.py:51
  53.3 4.0 %multiply_reduce_fusion.1 = f32[8,512]{1,0:T(8,128)S(1)} fusion(f32[8,512,512]{2,1,0:T(8,128)} %param.18, f32[8,512]{1,0:T(8,128)S(1)} %subtract_select_fusion.1), kind=kLoop, calls=%fused_computation.1 | loop fusion | flops 4190208 | bytes 8421376 | tf_op jit(solution)/shard_map/reduce_sum | solution.py:122
  61.9 12.9 %collective-permute-done.9 = f32[2]{0:T(128)S(1)} collective-permute-done((f32[2]{0:T(128)S(1)}, f32[2]{0:T(128)S(1)}, u32[]{:S(2)}, u32[]{:S(2)}) %collective-permute-start.9) | collective-permute-done | bytes 40 | tf_op jit(solution)/shard_map/ppermute | solution.py:77
  76.1 5.0 %collective-permute-start.10 = (f32[2]{0:T(128)S(1)}, f32[2]{0:T(128)S(1)}, u32[]{:S(2)}, u32[]{:S(2)}) collective-permute-start(f32[2]{0:T(128)S(1)} %fusion.157), channel_id=1, source_target_pairs={{0,4},{1,5},{2,6},{3,7},{4,0},{5,1},{6,2},{7,3},{8,12},{9,13},{10,... | collective-permute-start | bytes 32 | tf_op jit(solution)/shard_map/ppermute | solution.py:77
  81.1 1.5 collective-permute-done.10
  83.1 3.1 %collective-permute-done.11 = f32[2]{0:T(128)S(1)} collective-permute-done((f32[2]{0:T(128)S(1)}, f32[2]{0:T(128)S(1)}, u32[]{:S(2)}, u32[]{:S(2)}) %collective-permute-start.11) | collective-permute-done | bytes 40 | tf_op jit(solution)/shard_map/ppermute | solution.py:77
  86.5 4.1 %collective-permute-done.12 = f32[2]{0:T(128)S(1)} collective-permute-done((f32[2]{0:T(128)S(1)}, f32[2]{0:T(128)S(1)}, u32[]{:S(2)}, u32[]{:S(2)}) %collective-permute-start.12) | collective-permute-done | bytes 40 | tf_op jit(solution)/shard_map/ppermute | solution.py:77
  93.2 2.9 %pad_maximum_fusion = f32[16,168,512]{2,0,1:T(8,128)S(1)} fusion(f32[4,168,512]{2,0,1:T(4,128)} %collective-permute-done.3, f32[8,56,512]{2,0,1:T(8,128)S(1)} %slice.775, f32[8,56,512]{2,0,1:T(8,128)S(1)} %slice.774, f32[8,56,512]{2,0,1:T(8,128)} %copy-done, f32[4,168,512]{2,0,1:T(4,128)} %collective-permute-done.2), kind=kLoop, calls=%fused_computation.3 | loop fusion | flops 5505024 | bytes 11010048 | tf_op jit(solution)/shard_map/concatenate | solution.py:52
  98.3 2.6 %fusion.7 = f32[14,64,512]{2,0,1:T(8,128)S(1)} fusion(f32[16,56,512]{2,0,1:T(8,128)S(1)} %get-tuple-element.65, f32[16,56,512]{2,0,1:T(8,128)S(1)} %get-tuple-element.64, f32[16,8,512]{2,0,1:T(8,128)S(1)} %get-tuple-element.84, f32[16,8,512]{2,0,1:T(8,128)S(1)} %get-tuple-element.83, f32[16,56,512]{2,0,1:T(8,128)S(1)} %get-tuple-element.66, ...), kind=kLoop, calls=%fused_computation.34 | loop fusion | flops 7798784 | bytes 13570574 | tf_op jit(solution)/shard_map/jit(_where)/select_n | solution.py:69
  102.7 2.5 %fusion.11 = f32[12,64,512]{2,0,1:T(8,128)S(1)} fusion(f32[16,56,512]{2,0,1:T(8,128)S(1)} %get-tuple-element.65, f32[16,56,512]{2,0,1:T(8,128)S(1)} %get-tuple-element.66, f32[16,8,512]{2,0,1:T(8,128)S(1)} %get-tuple-element.84, f32[16,8,512]{2,0,1:T(8,128)S(1)} %get-tuple-element.85, f32[14,64,512]{2,0,1:T(8,128)S(1)} %fusion.7, ...), kind=kLoop, calls=%fused_computation.38 | loop fusion | flops 4325376 | bytes 15149068 | tf_op jit(solution)/shard_map/jit(_where)/select_n | solution.py:69
  106.9 2.5 %fusion.3 = f32[10,64,512]{2,0,1:T(8,128)S(1)} fusion(f32[16,56,512]{2,0,1:T(8,128)S(1)} %get-tuple-element.65, f32[16,56,512]{2,0,1:T(8,128)S(1)} %get-tuple-element.66, f32[16,8,512]{2,0,1:T(8,128)S(1)} %get-tuple-element.84, f32[16,8,512]{2,0,1:T(8,128)S(1)} %get-tuple-element.85, f32[12,64,512]{2,0,1:T(8,128)S(1)} %fusion.11, ...), kind=kLoop, calls=%fused_computation.30 | loop fusion | flops 3604480 | bytes 13323274 | tf_op jit(solution)/shard_map/jit(_where)/select_n | solution.py:69
  110.4 1.4 fusion.38
  112.1 2.1 %collective-permute-start.13 = (f32[4,512]{1,0:T(4,128)S(1)}, f32[4,512]{1,0:T(4,128)S(1)}, u32[]{:S(2)}, u32[]{:S(2)}) collective-permute-start(f32[4,512]{1,0:T(4,128)S(1)} %get-tuple-element.111), channel_id=1, source_target_pairs={{0,1},{1,2},{2,3},{3,4},{4,5},{5,6},{6,7},{8,9},{9,10},{10,11},{11... | collective-permute-start | bytes 24584 | tf_op jit(solution)/shard_map/ppermute | solution.py:50
  114.1 4.8 %collective-permute-start.14 = (f32[4,512]{1,0:T(4,128)S(1)}, f32[4,512]{1,0:T(4,128)S(1)}, u32[]{:S(2)}, u32[]{:S(2)}) collective-permute-start(f32[4,512]{1,0:T(4,128)S(1)} %get-tuple-element.112), channel_id=1, source_target_pairs={{1,0},{2,1},{3,2},{4,3},{5,4},{6,5},{7,6},{9,8},{10,9},{11,10},{12... | collective-permute-start | bytes 24584 | tf_op jit(solution)/shard_map/ppermute | solution.py:51
  123.5 2.5 %fusion.123 = f32[1,512]{1,0:T(1,128)S(1)} fusion(f32[]{:T(128)} %get-tuple-element.52, f32[]{:T(128)} %get-tuple-element.53, f32[]{:T(128)} %get-tuple-element.51, f32[]{:T(128)} %get-tuple-element.50), kind=kLoop, calls=%fused_computation.238 | loop fusion | flops 5632 | bytes 2064 | tf_op jit(solution)/shard_map/add | solution.py:163
  130.0 1.6 %copy.15 = f32[1,8,64,512]{3,2,1,0:T(8,128)} copy(f32[1,8,64,512]{3,1,2,0:T(8,128)S(1)} %maximum_select_fusion) | data formatting | bytes 2097152
  131.6 1.6 %collective-permute-done.17 = f32[33,512]{1,0:T(8,128)S(1)} collective-permute-done((f32[33,512]{1,0:T(8,128)S(1)}, f32[33,512]{1,0:T(8,128)S(1)}, u32[]{:S(2)}, u32[]{:S(2)}) %collective-permute-start.17) | collective-permute-done | bytes 67616 | tf_op jit(solution)/shard_map/ppermute | solution.py:171
  133.3 2.2 %collective-permute-done.16 = f32[33,512]{1,0:T(8,128)S(1)} collective-permute-done((f32[33,512]{1,0:T(8,128)S(1)}, f32[33,512]{1,0:T(8,128)S(1)}, u32[]{:S(2)}, u32[]{:S(2)}) %collective-permute-start.16) | collective-permute-done | bytes 67616 | tf_op jit(solution)/shard_map/ppermute | solution.py:171
  138.0 3.5 %collective-permute-done.19 = f32[4]{0:T(128)S(1)} collective-permute-done((f32[4]{0:T(128)S(1)}, f32[4]{0:T(128)S(1)}, u32[]{:S(2)}, u32[]{:S(2)}) %collective-permute-start.19) | collective-permute-done | bytes 48 | tf_op jit(solution)/shard_map/ppermute | solution.py:77
  141.6 3.4 %collective-permute-done.20 = f32[4]{0:T(128)S(1)} collective-permute-done((f32[4]{0:T(128)S(1)}, f32[4]{0:T(128)S(1)}, u32[]{:S(2)}, u32[]{:S(2)}) %collective-permute-start.20) | collective-permute-done | bytes 48 | tf_op jit(solution)/shard_map/ppermute | solution.py:77
  (205 shorter events, 43.5 us)
Async XLA Ops:
  0.6 11.4 %copy-start.7 = (f32[1,8,64,512]{3,2,1,0:T(8,128)S(1)}, f32[1,8,64,512]{3,2,1,0:T(8,128)}, u32[]{:S(2)}) copy-start(f32[1,8,64,512]{3,2,1,0:T(8,128)} %param.16) | copy-start | bytes 3145732
  1.4 10.6 %copy-start.17 = (f32[8]{0:T(128)}, f32[8]{0:T(128)S(1)}, u32[]{:S(2)}) copy-start(f32[8]{0:T(128)S(1)} %fusion.124) | copy-start | bytes 100
  2.1 10.0 %copy-start.13 = (f32[8,8]{1,0:T(8,128)}, f32[8,8]{1,0:T(8,128)S(1)}, u32[]{:S(2)}) copy-start(f32[8,8]{1,0:T(8,128)S(1)} %fusion.120) | copy-start | bytes 772
  3.6 24.5 %collective-permute-start.4 = (f32[4,512]{1,0:T(4,128)}, f32[4,512]{1,0:T(4,128)}, u32[]{:S(2)}, u32[]{:S(2)}) collective-permute-start(f32[4,512]{1,0:T(4,128)} %get-tuple-element.115), channel_id=1, source_target_pairs={{0,1},{1,2},{2,3},{3,4},{4,5},{5,6},{6,7},{8,9},{9,10},{10,11},{11... | collective-permute-start | bytes 24584 | tf_op jit(solution)/shard_map/ppermute | solution.py:50
  5.5 22.5 %collective-permute-start.5 = (f32[4,512]{1,0:T(4,128)}, f32[4,512]{1,0:T(4,128)}, u32[]{:S(2)}, u32[]{:S(2)}) collective-permute-start(f32[4,512]{1,0:T(4,128)} %get-tuple-element.116), channel_id=1, source_target_pairs={{1,0},{2,1},{3,2},{4,3},{5,4},{6,5},{7,6},{9,8},{10,9},{11,10},{12... | collective-permute-start | bytes 24584 | tf_op jit(solution)/shard_map/ppermute | solution.py:51
  12.7 10.9 %copy-start.1 = (f32[1,8,64,512]{3,1,2,0:T(8,128)}, f32[1,8,64,512]{3,1,2,0:T(8,128)S(1)}, u32[]{:S(2)}) copy-start(f32[1,8,64,512]{3,1,2,0:T(8,128)S(1)} %copy.19) | copy-start | bytes 3145732
  12.7 9.9 %copy-start.31 = (s32[8]{0:T(128)S(1)}, s32[8]{0:T(128)}, u32[]{:S(2)}) copy-start(s32[8]{0:T(128)} %param.23) | copy-start | bytes 100
  12.7 13.3 %copy-start.2 = (f32[8,8,512]{2,0,1:T(8,128)}, f32[8,8,512]{2,0,1:T(8,128)S(1)}, u32[]{:S(2)}) copy-start(f32[8,8,512]{2,0,1:T(8,128)S(1)} %slice.769) | copy-start | bytes 393220
  15.3 10.8 %copy-start.4 = (f32[8,8,512]{2,0,1:T(8,128)}, f32[8,8,512]{2,0,1:T(8,128)S(1)}, u32[]{:S(2)}) copy-start(f32[8,8,512]{2,0,1:T(8,128)S(1)} %slice.767) | copy-start | bytes 393220
  16.1 9.8 %collective-permute-start = (f32[4,24,512]{2,0,1:T(4,128)}, f32[4,24,512]{2,0,1:T(4,128)}, u32[]{:S(2)}, u32[]{:S(2)}) collective-permute-start(f32[4,24,512]{2,0,1:T(4,128)} %get-tuple-element.88), channel_id=1, source_target_pairs={{0,1},{1,2},{2,3},{3,4},{4,5},{5,6},{6,7},{8,9},{9,10},{10,11},{11... | collective-permute-start | bytes 589832 | tf_op jit(solution)/shard_map/ppermute | solution.py:50
  18.0 8.0 %collective-permute-start.1 = (f32[4,24,512]{2,0,1:T(4,128)}, f32[4,24,512]{2,0,1:T(4,128)}, u32[]{:S(2)}, u32[]{:S(2)}) collective-permute-start(f32[4,24,512]{2,0,1:T(4,128)} %get-tuple-element.89), channel_id=1, source_target_pairs={{1,0},{2,1},{3,2},{4,3},{5,4},{6,5},{7,6},{9,8},{10,9},{11,10},{12... | collective-permute-start | bytes 589832 | tf_op jit(solution)/shard_map/ppermute | solution.py:51
  35.2 15.1 %collective-permute-start.6 = (f32[4,512]{1,0:T(4,128)}, f32[4,512]{1,0:T(4,128)S(1)}, u32[]{:S(2)}, u32[]{:S(2)}) collective-permute-start(f32[4,512]{1,0:T(4,128)} %get-tuple-element.113), channel_id=1, source_target_pairs={{0,1},{1,2},{2,3},{3,4},{4,5},{5,6},{6,7},{8,9},{9,10},{10,11},{11... | collective-permute-start | bytes 24584 | tf_op jit(solution)/shard_map/ppermute | solution.py:50
  37.1 13.2 %copy-start.9 = (f32[16,1,512]{2,0,1:T(8,128)S(1)}, f32[16,1,512]{2,0,1:T(8,128)}, u32[]{:S(2)}) copy-start(f32[16,1,512]{2,0,1:T(8,128)} %get-tuple-element.63) | copy-start | bytes 98308
  37.1 13.2 %copy-start.26 = (pred[14]{0:T(512)(128)(4,1)S(1)}, pred[14]{0:T(512)(128)(4,1)}, u32[]{:S(2)}) copy-start(pred[14]{0:T(512)(128)(4,1)} %copy-done.25) | copy-start | bytes 46
  37.1 13.2 %collective-permute-start.7 = (f32[4,512]{1,0:T(4,128)S(1)}, f32[4,512]{1,0:T(4,128)S(1)}, u32[]{:S(2)}, u32[]{:S(2)}) collective-permute-start(f32[4,512]{1,0:T(4,128)S(1)} %get-tuple-element.114), channel_id=1, source_target_pairs={{1,0},{2,1},{3,2},{4,3},{5,4},{6,5},{7,6},{9,8},{10,9},{11,10},{12... | collective-permute-start | bytes 24584 | tf_op jit(solution)/shard_map/ppermute | solution.py:51
  43.6 49.6 %collective-permute-start.2 = (f32[4,168,512]{2,0,1:T(4,128)}, f32[4,168,512]{2,0,1:T(4,128)}, u32[]{:S(2)}, u32[]{:S(2)}) collective-permute-start(f32[4,168,512]{2,0,1:T(4,128)} %get-tuple-element.67), channel_id=1, source_target_pairs={{0,1},{1,2},{2,3},{3,4},{4,5},{5,6},{6,7},{8,9},{9,10},{10,11},{11... | collective-permute-start | bytes 4128776 | tf_op jit(solution)/shard_map/ppermute | solution.py:50
  45.7 47.6 %collective-permute-start.3 = (f32[4,168,512]{2,0,1:T(4,128)}, f32[4,168,512]{2,0,1:T(4,128)}, u32[]{:S(2)}, u32[]{:S(2)}) collective-permute-start(f32[4,168,512]{2,0,1:T(4,128)} %get-tuple-element.68), channel_id=1, source_target_pairs={{1,0},{2,1},{3,2},{4,3},{5,4},{6,5},{7,6},{9,8},{10,9},{11,10},{12... | collective-permute-start | bytes 4128776 | tf_op jit(solution)/shard_map/ppermute | solution.py:51
  59.4 1.1 collective-permute-start.8
  61.9 12.9 %collective-permute-start.9 = (f32[2]{0:T(128)S(1)}, f32[2]{0:T(128)S(1)}, u32[]{:S(2)}, u32[]{:S(2)}) collective-permute-start(f32[2]{0:T(128)S(1)} %fusion.156), channel_id=1, source_target_pairs={{0,2},{1,3},{2,0},{3,1},{4,6},{5,7},{6,4},{7,5},{8,10},{9,11},{10,... | collective-permute-start | bytes 32 | tf_op jit(solution)/shard_map/ppermute | solution.py:77
  76.1 6.5 %collective-permute-start.10 = (f32[2]{0:T(128)S(1)}, f32[2]{0:T(128)S(1)}, u32[]{:S(2)}, u32[]{:S(2)}) collective-permute-start(f32[2]{0:T(128)S(1)} %fusion.157), channel_id=1, source_target_pairs={{0,4},{1,5},{2,6},{3,7},{4,0},{5,1},{6,2},{7,3},{8,12},{9,13},{10,... | collective-permute-start | bytes 32 | tf_op jit(solution)/shard_map/ppermute | solution.py:77
  82.7 3.5 %collective-permute-start.11 = (f32[2]{0:T(128)S(1)}, f32[2]{0:T(128)S(1)}, u32[]{:S(2)}, u32[]{:S(2)}) collective-permute-start(f32[2]{0:T(128)S(1)} %add.585), channel_id=1, source_target_pairs={{0,8},{8,0},{16,24},{24,16},{1,9},{9,1},{17,25},{25,17},{2,10},{10... | collective-permute-start | bytes 32 | tf_op jit(solution)/shard_map/ppermute | solution.py:77
  86.2 4.4 %collective-permute-start.12 = (f32[2]{0:T(128)S(1)}, f32[2]{0:T(128)S(1)}, u32[]{:S(2)}, u32[]{:S(2)}) collective-permute-start(f32[2]{0:T(128)S(1)} %add.586), channel_id=1, source_target_pairs={{0,16},{8,24},{16,0},{24,8},{1,17},{9,25},{17,1},{25,9},{2,18},{10... | collective-permute-start | bytes 32 | tf_op jit(solution)/shard_map/ppermute | solution.py:77
  109.8 12.3 %slice-start.2 = ((s8[8388608]{0:T(1024)(128)(4,1)}), s8[4194304]{0:T(1024)(128)(4,1)S(1)}, s32[]{:S(2)}) async-start(s8[8388608]{0:T(1024)(128)(4,1)} %bitcast.58), calls=%async_computation.2 | async-start | bytes 8388608
  110.4 11.6 %slice-start.3 = ((s8[8388608]{0:T(1024)(128)(4,1)}), s8[4194304]{0:T(1024)(128)(4,1)S(1)}, s32[]{:S(2)}) async-start(s8[8388608]{0:T(1024)(128)(4,1)} %bitcast.58), calls=%async_computation.3 | async-start | bytes 8388608
  112.1 6.9 %collective-permute-start.13 = (f32[4,512]{1,0:T(4,128)S(1)}, f32[4,512]{1,0:T(4,128)S(1)}, u32[]{:S(2)}, u32[]{:S(2)}) collective-permute-start(f32[4,512]{1,0:T(4,128)S(1)} %get-tuple-element.111), channel_id=1, source_target_pairs={{0,1},{1,2},{2,3},{3,4},{4,5},{5,6},{6,7},{8,9},{9,10},{10,11},{11... | collective-permute-start | bytes 24584 | tf_op jit(solution)/shard_map/ppermute | solution.py:50
  114.1 5.9 %collective-permute-start.14 = (f32[4,512]{1,0:T(4,128)S(1)}, f32[4,512]{1,0:T(4,128)S(1)}, u32[]{:S(2)}, u32[]{:S(2)}) collective-permute-start(f32[4,512]{1,0:T(4,128)S(1)} %get-tuple-element.112), channel_id=1, source_target_pairs={{1,0},{2,1},{3,2},{4,3},{5,4},{6,5},{7,6},{9,8},{10,9},{11,10},{12... | collective-permute-start | bytes 24584 | tf_op jit(solution)/shard_map/ppermute | solution.py:51
  126.0 7.2 %collective-permute-start.17 = (f32[33,512]{1,0:T(8,128)S(1)}, f32[33,512]{1,0:T(8,128)S(1)}, u32[]{:S(2)}, u32[]{:S(2)}) collective-permute-start(f32[33,512]{1,0:T(8,128)S(1)} %dynamic-update-slice.13), channel_id=1, source_target_pairs={{16,24},{17,25},{18,26},{19,27},{20,28},{21,29},{22,30},{23,31}} | collective-permute-start | bytes 202760 | tf_op jit(solution)/shard_map/ppermute | solution.py:171
  127.3 8.1 %collective-permute-start.16 = (f32[33,512]{1,0:T(8,128)S(1)}, f32[33,512]{1,0:T(8,128)S(1)}, u32[]{:S(2)}, u32[]{:S(2)}) collective-permute-start(f32[33,512]{1,0:T(8,128)S(1)} %dynamic-update-slice.13), channel_id=1, source_target_pairs={{8,24},{9,25},{10,26},{11,27},{12,28},{13,29},{14,30},{15,31}} | collective-permute-start | bytes 202760 | tf_op jit(solution)/shard_map/ppermute | solution.py:171
  128.6 8.1 %collective-permute-start.15 = (f32[33,512]{1,0:T(8,128)S(1)}, f32[33,512]{1,0:T(8,128)S(1)}, u32[]{:S(2)}, u32[]{:S(2)}) collective-permute-start(f32[33,512]{1,0:T(8,128)S(1)} %dynamic-update-slice.13), channel_id=1, source_target_pairs={{0,24},{1,25},{2,26},{3,27},{4,28},{5,29},{6,30},{7,31}} | collective-permute-start | bytes 202760 | tf_op jit(solution)/shard_map/ppermute | solution.py:171
  136.8 1.2 collective-permute-start.18
  138.0 3.5 %collective-permute-start.19 = (f32[4]{0:T(128)S(1)}, f32[4]{0:T(128)S(1)}, u32[]{:S(2)}, u32[]{:S(2)}) collective-permute-start(f32[4]{0:T(128)S(1)} %fusion.125), channel_id=1, source_target_pairs={{0,2},{1,3},{2,0},{3,1},{4,6},{5,7},{6,4},{7,5},{8,10},{9,11},{10,... | collective-permute-start | bytes 56 | tf_op jit(solution)/shard_map/ppermute | solution.py:77
  141.6 3.5 %collective-permute-start.20 = (f32[4]{0:T(128)S(1)}, f32[4]{0:T(128)S(1)}, u32[]{:S(2)}, u32[]{:S(2)}) collective-permute-start(f32[4]{0:T(128)S(1)} %add.650), channel_id=1, source_target_pairs={{0,4},{1,5},{2,6},{3,7},{4,0},{5,1},{6,2},{7,3},{8,12},{9,13},{10,... | collective-permute-start | bytes 56 | tf_op jit(solution)/shard_map/ppermute | solution.py:77
  (25 other events, 86.3 us)

commit v6 on v4

--- a/solution.py
+++ b/solution.py
@@ -50,6 +50,40 @@
     low = lax.ppermute(block[block.shape[0] - width :], "slab", forward)
     high = lax.ppermute(block[:width], "slab", backward)
     return jnp.concatenate([low, block, high], axis=0)
+
+
+def exchange(items):
+    count = lax.axis_size("slab")
+    forward, backward = ring_pairs(count)
+    cells = items[0][0].shape[-1]
+    sizes = [width * (a.size // a.shape[0]) // cells for a, width in items]
+    up = jnp.concatenate([a[a.shape[0] - w :].reshape(-1, cells) for a, w in items], axis=0)
+    down = jnp.concatenate([a[:w].reshape(-1, cells) for a, w in items], axis=0)
+    low = lax.ppermute(up, "slab", forward)
+    high = lax.ppermute(down, "slab", backward)
+    out, at = [], 0
+    for (a, w), n in zip(items, sizes):
+        shape = (w,) + a.shape[1:]
+        out.append(
+            jnp.concatenate([low[at : at + n].reshape(shape), a, high[at : at + n].reshape(shape)], axis=0)
+        )
+        at += n
+    return out
+
+
+def deep_step(q, rhs, coef, ok):
+    centre = q[1:-1]
+    zero = jnp.zeros_like(centre[:, :1])
+    new = stencil(
+        rhs,
+        coef,
+        q[2:],
+        q[:-2],
+        jnp.concatenate([centre[:, 1:], zero], axis=1),
+        jnp.concatenate([zero, centre[:, :-1]], axis=1),
+        centre,
+    )
+    return jnp.where(ok, new, 0.0)
 
 
 def deep_solve(q, rhs, coef, row_ok):
@@ -101,50 +135,62 @@
     onehot = (block_row[None, :] == jnp.arange(slab_rows)[:, None]).astype(jnp.float32) * own[:, 0][None, :]
     pick = (block_row[:, None] == jnp.arange(slab_rows)[None, :]).astype(jnp.float32)
 
-    packed = rims(
-        jnp.concatenate([start_here[:, :BAND], force_here[:, :BAND], coef_here[:, :BAND]], axis=1), HALO
+    deep_planes = planes - BAND
+    disp_zero = own_live * disp_init
+    plane_zero = jnp.sum(onehot[:, :, None] * (live * disp_zero)[None], axis=1)
+    packed, plane_zero_rims, init_deep, fc_deep = exchange(
+        [
+            (jnp.concatenate([start_here[:, :BAND], force_here[:, :BAND], coef_here[:, :BAND]], axis=1), HALO),
+            (plane_zero, HALO),
+            (start_here[:, BAND:], 2),
+            (jnp.concatenate([force_here[:, BAND:], coef_here[:, BAND:]], axis=1), 1),
+        ]
     )
     init_band, force_band, coef_band = (
         packed[:, :BAND],
         packed[:, BAND : 2 * BAND],
         packed[:, 2 * BAND :],
     )
+    init_deep = jnp.concatenate([init_band[HALO - 2 : HALO + slab_rows + 2], init_deep], axis=1)
+    force_deep = jnp.concatenate(
+        [force_band[HALO - 1 : HALO + slab_rows + 1], fc_deep[:, :deep_planes]], axis=1
+    )
+    coef_deep = jnp.concatenate([coef_band[HALO - 1 : HALO + slab_rows + 1], fc_deep[:, deep_planes:]], axis=1)
     global_row = slab_id * slab_rows + jnp.arange(slab_rows + 2 * HALO) - HALO
     total_rows = slab_rows * lax.axis_size("slab")
     row_ok = ((global_row >= 0) & (global_row < total_rows))[:, None, None]
 
-    def evaluate(disp):
-        plane = jnp.sum(onehot[:, :, None] * (live * disp)[None], axis=1)
-        rhs = force_band.at[:, 0, :].add(rims(plane, HALO))
+    ok_one = row_ok[HALO - 1 : HALO + slab_rows + 1]
+    ok_two = row_ok[HALO : HALO + slab_rows]
+
+    def evaluate(disp, plane_rims=None, extra=()):
+        if plane_rims is None:
+            plane = jnp.sum(onehot[:, :, None] * (live * disp)[None], axis=1)
+            got = exchange([(plane, HALO)] + list(extra))
+            plane_rims, extra = got[0], got[1:]
+        rhs = force_band.at[:, 0, :].add(plane_rims)
         band = band_solve(init_band, rhs, coef_band, row_ok)
         traction = PENALTY * jnp.sum(pick[:, :, None] * band[:, 0, :][None], axis=1)
         loaded = live * (shell_load - traction)
         tilde = own_live * jnp.sum(compliance * loaded[:, None, :], axis=-1)
-        return tilde, band
-
-    disp_zero = own_live * disp_init
-    tilde_zero, unused = evaluate(disp_zero)
+        return tilde, band, extra
+
+    tilde_zero, unused, unused_extra = evaluate(disp_zero, plane_zero_rims)
     resid_zero = tilde_zero - disp_zero
     disp_one = disp_zero + RELAX * resid_zero
-    tilde_one, unused = evaluate(disp_one)
+    tilde_one, unused, unused_extra = evaluate(disp_one)
+    init_deep, tilde_one = lax.optimization_barrier((init_deep, tilde_one))
+    deep = deep_step(init_deep, force_deep, coef_deep, ok_one)
+    deep = deep_step(deep, force_deep[1:-1], coef_deep[1:-1], ok_two)
     resid_one = tilde_one - disp_one
     diff_one = resid_one - resid_zero
     sums = allsum(jnp.stack([jnp.sum(diff_one * diff_one), jnp.sum(diff_one * resid_one)]))
     gram_aa, gram_ab = sums[0], sums[1]
     coeff = -gram_ab / (gram_aa + (0.001 * gram_aa + 1e-06))
-    deep_rims = rims(
-        jnp.concatenate([start_here[:, BAND:], force_here[:, BAND:], coef_here[:, BAND:]], axis=1), HALO
-    )
-    rest = planes - BAND
-    deep = deep_solve(
-        jnp.concatenate([init_band, deep_rims[:, :rest]], axis=1),
-        jnp.concatenate([force_band, deep_rims[:, rest : 2 * rest]], axis=1),
-        jnp.concatenate([coef_band, deep_rims[:, 2 * rest :]], axis=1),
-        row_ok,
-    )
-    coeff, deep = lax.optimization_barrier((coeff, deep))
     disp_two = tilde_one + coeff * (tilde_one - tilde_zero)
-    tilde_two, band_two = evaluate(disp_two)
+    tilde_two, band_two, (deep,) = evaluate(disp_two, extra=[(deep, 2)])
+    deep = deep_step(deep, force_deep, coef_deep, ok_one)
+    deep = deep_step(deep, force_deep[1:-1], coef_deep[1:-1], ok_two)
     resid_two = tilde_two - disp_two
     newer = resid_two - resid_one
     partial = jnp.stack(

time: 155 us -> 144 us (0.929)
  the two profiles are of different devices: /device:TPU:28 before, /device:TPU:0 now
where the time goes in v6:
time: 144 us; the launch traced here: 143 us
  starting transfers between devices  53 us (37%)
  other arithmetic  37.1 us (26%)
  local copies, waits for them, and re-layouts  29.4 us (20%)
  waiting for transfers between devices  12.4 us (9%)
  between operations  11.4 us (8%)
    ppermute x8, starting transfers between devices, allsum_axis(): v = v + lax.ppermute(v, axis, [(i, i ^ step) for i in range(count)])  22.9 us
    ppermute x3, starting transfers between devices, exchange(): low = lax.ppermute(up, 'slab', forward)  17.7 us
    ppermute x8, waiting for transfers between devices, allsum_axis(): v = v + lax.ppermute(v, axis, [(i, i ^ step) for i in range(count)])  11.6 us
    unnamed x62, local copies, waits for them, and re-layouts  10.1 us
    ppermute x3, starting transfers between devices, body(): lax.ppermute(outgoing, 'side', [(source, side_count - 1)])  8.31 us
    select_n x3, other arithmetic, deep_step(): return jnp.where(ok, new, 0.0)  6.97 us
    reduce_sum x3, other arithmetic, evaluate(): tilde = own_live * jnp.sum(compliance * loaded[:, None, :], axis=-1)  5.3 us
    slice x5, local copies, waits for them, and re-layouts, exchange(): high[at:at + n].reshape(shape)  4.62 us
  transfers between devices with their start and end apart: 17, of which 9 were waited for; matrix products, arithmetic and copies ran while one was open for 16% of the time, Pallas kernels for 0%

profile of v6, /device:TPU:0, one launch (start us, length us, event | category | flops | bytes accessed | tf_op | source)
XLA Modules:
  0.0 143.3 jit_solution(9718486983896867664)
XLA Ops:
  0.6 1.9 %copy.54 = f32[1,8,64,512]{3,1,2,0:T(8,128)S(1)} copy(f32[1,8,64,512]{3,2,1,0:T(8,128)} %param.15) | data formatting | bytes 2097152 | tf_op args[0]
  7.4 1.3 collective-permute-start.1
  9.8 3.1 %collective-permute-start = (f32[324,512]{1,0:T(8,128)}, f32[324,512]{1,0:T(8,128)S(1)}, u32[]{:S(2)}, u32[]{:S(2)}) collective-permute-start(f32[324,512]{1,0:T(8,128)} %pad_maximum_fusion.5), channel_id=1, source_target_pairs={{0,1},{1,2},{2,3},{3,4},{4,5},{5,6},{6,7},{8,9},{9,10},{10,11},{11... | collective-permute-start | bytes 1990664 | tf_op jit(solution)/shard_map/ppermute | solution.py:62
  23.1 10.9 %collective-permute-start.2 = (f32[4,512]{1,0:T(4,128)S(1)}, f32[4,512]{1,0:T(4,128)S(1)}, u32[]{:S(2)}, u32[]{:S(2)}) collective-permute-start(f32[4,512]{1,0:T(4,128)S(1)} %get-tuple-element.122), channel_id=1, source_target_pairs={{0,1},{1,2},{2,3},{3,4},{4,5},{5,6},{6,7},{8,9},{9,10},{10,11},{11... | collective-permute-start | bytes 24584 | tf_op jit(solution)/shard_map/ppermute | solution.py:62
  34.0 1.5 %collective-permute-start.3 = (f32[4,512]{1,0:T(4,128)S(1)}, f32[4,512]{1,0:T(4,128)S(1)}, u32[]{:S(2)}, u32[]{:S(2)}) collective-permute-start(f32[4,512]{1,0:T(4,128)S(1)} %get-tuple-element.123), channel_id=1, source_target_pairs={{1,0},{2,1},{3,2},{4,3},{5,4},{6,5},{7,6},{9,8},{10,9},{11,10},{12... | collective-permute-start | bytes 24584 | tf_op jit(solution)/shard_map/ppermute | solution.py:63
  41.2 2.2 %divide_select_fusion = f32[10,64,512]{2,0,1:T(8,128)S(1)} fusion(f32[10,64,511]{2,0,1:T(8,128)S(1)} %get-tuple-element.82, f32[10,64,511]{2,0,1:T(8,128)S(1)} %get-tuple-element.81, f32[10,63,512]{2,0,1:T(8,128)S(1)} %get-tuple-element.80, f32[10,63,512]{2,0,1:T(8,128)S(1)} %get-tuple-element.79, f32[12,64,512]{2,0,1:T(8,128)S(1)} %maximum_maximum_fusion, ...), kind=kLoop, calls=%fused_computation.20 | loop fusion | flops 3604480 | bytes 11750410 | tf_op jit(solution)/shard_map/jit(_where)/select_n | solution.py:86
  44.9 1.4 pad_maximum_fusion.13
  46.3 3.7 %collective-permute-start.4 = (f32[2]{0:T(128)S(1)}, f32[2]{0:T(128)S(1)}, u32[]{:S(2)}, u32[]{:S(2)}) collective-permute-start(f32[2]{0:T(128)S(1)} %pad_maximum_fusion.13), channel_id=1, source_target_pairs={{0,1},{1,0},{2,3},{3,2},{4,5},{5,4},{6,7},{7,6},{8,9},{9,8},{10,11... | collective-permute-start | bytes 32 | tf_op jit(solution)/shard_map/ppermute | solution.py:111
  50.0 2.7 %fusion.18 = (f32[8,64,512]{2,0,1:T(8,128)S(1)}, f32[8,64,512]{2,0,1:T(8,128)}, f32[8,64,512]{2,0,1:T(8,128)}) fusion(f32[8,64,511]{2,0,1:T(8,128)S(1)} %get-tuple-element.78, f32[8,64,511]{2,0,1:T(8,128)S(1)} %get-tuple-element.77, f32[8,63,512]{2,0,1:T(8,128)S(1)} %get-tuple-element.76, f32[8,63,512]{2,0,1:T(8,128)S(1)} %get-tuple-element.75, ...), kind=kLoop, calls=%fused_computation.38 | loop fusion | flops 2883584 | bytes 12021768 | tf_op jit(solution)/shard_map/jit(_where)/select_n | solution.py:86
  55.3 1.4 fusion.140
  56.7 5.3 %collective-permute-start.5 = (f32[2]{0:T(128)S(1)}, f32[2]{0:T(128)S(1)}, u32[]{:S(2)}, u32[]{:S(2)}) collective-permute-start(f32[2]{0:T(128)S(1)} %fusion.140), channel_id=1, source_target_pairs={{0,2},{1,3},{2,0},{3,1},{4,6},{5,7},{6,4},{7,5},{8,10},{9,11},{10,... | collective-permute-start | bytes 32 | tf_op jit(solution)/shard_map/ppermute | solution.py:111
  62.0 1.5 %collective-permute-done.5 = f32[2]{0:T(128)S(1)} collective-permute-done((f32[2]{0:T(128)S(1)}, f32[2]{0:T(128)S(1)}, u32[]{:S(2)}, u32[]{:S(2)}) %collective-permute-start.5) | collective-permute-done | bytes 40 | tf_op jit(solution)/shard_map/ppermute | solution.py:111
  63.5 1.4 fusion.141
  66.0 2.4 %collective-permute-done.6 = f32[2]{0:T(128)S(1)} collective-permute-done((f32[2]{0:T(128)S(1)}, f32[2]{0:T(128)S(1)}, u32[]{:S(2)}, u32[]{:S(2)}) %collective-permute-start.6) | collective-permute-done | bytes 40 | tf_op jit(solution)/shard_map/ppermute | solution.py:111
  68.4 1.6 %collective-permute-start.7 = (f32[2]{0:T(128)S(1)}, f32[2]{0:T(128)S(1)}, u32[]{:S(2)}, u32[]{:S(2)}) collective-permute-start(f32[2]{0:T(128)S(1)} %add.569), channel_id=1, source_target_pairs={{0,8},{8,0},{16,24},{24,16},{1,9},{9,1},{17,25},{25,17},{2,10},{10... | collective-permute-start | bytes 32 | tf_op jit(solution)/shard_map/ppermute | solution.py:111
  70.0 2.0 %collective-permute-done.7 = f32[2]{0:T(128)S(1)} collective-permute-done((f32[2]{0:T(128)S(1)}, f32[2]{0:T(128)S(1)}, u32[]{:S(2)}, u32[]{:S(2)}) %collective-permute-start.7) | collective-permute-done | bytes 40 | tf_op jit(solution)/shard_map/ppermute | solution.py:111
  72.0 2.6 %collective-permute-start.8 = (f32[2]{0:T(128)S(1)}, f32[2]{0:T(128)S(1)}, u32[]{:S(2)}, u32[]{:S(2)}) collective-permute-start(f32[2]{0:T(128)S(1)} %add.570), channel_id=1, source_target_pairs={{0,16},{8,24},{16,0},{24,8},{1,17},{9,25},{17,1},{25,9},{2,18},{10... | collective-permute-start | bytes 32 | tf_op jit(solution)/shard_map/ppermute | solution.py:111
  74.6 1.9 %collective-permute-done.8 = f32[2]{0:T(128)S(1)} collective-permute-done((f32[2]{0:T(128)S(1)}, f32[2]{0:T(128)S(1)}, u32[]{:S(2)}, u32[]{:S(2)}) %collective-permute-start.8) | collective-permute-done | bytes 40 | tf_op jit(solution)/shard_map/ppermute | solution.py:111
  79.2 1.7 %pad_maximum_fusion.9 = f32[132,512]{1,0:T(8,128)} fusion(f32[128,512]{1,0:T(8,128)} %bitcast.86, f32[4,512]{1,0:T(4,128)S(1)} %get-tuple-element.121), kind=kLoop, calls=%fused_computation.51 | loop fusion | flops 67584 | bytes 540672 | tf_op jit(solution)/shard_map/concatenate | solution.py:61
  82.2 1.7 %pad_maximum_fusion.8 = f32[132,512]{1,0:T(8,128)} fusion(f32[128,512]{1,0:T(8,128)} %bitcast.85, f32[4,512]{1,0:T(4,128)S(1)} %get-tuple-element.120), kind=kLoop, calls=%fused_computation.50 | loop fusion | flops 67584 | bytes 540672 | tf_op jit(solution)/shard_map/concatenate | solution.py:60
  83.9 3.7 %collective-permute-start.9 = (f32[132,512]{1,0:T(8,128)}, f32[132,512]{1,0:T(8,128)}, u32[]{:S(2)}, u32[]{:S(2)}) collective-permute-start(f32[132,512]{1,0:T(8,128)} %pad_maximum_fusion.8), channel_id=1, source_target_pairs={{0,1},{1,2},{2,3},{3,4},{4,5},{5,6},{6,7},{8,9},{9,10},{10,11},{11... | collective-permute-start | bytes 811016 | tf_op jit(solution)/shard_map/ppermute | solution.py:62
  92.7 4.0 %multiply_reduce_fusion = f32[8,512]{1,0:T(8,128)S(1)} fusion(f32[8,512,512]{2,1,0:T(8,128)} %param.18, f32[8,512]{1,0:T(8,128)S(1)} %subtract_select_fusion), kind=kLoop, calls=%fused_computation | loop fusion | flops 4190208 | bytes 8421376 | tf_op jit(solution)/shard_map/reduce_sum | solution.py:175
  97.6 2.6 %fusion.100 = f32[1,512]{1,0:T(1,128)S(1)} fusion(f32[]{:T(128)} %get-tuple-element.51, f32[]{:T(128)} %get-tuple-element.52, f32[]{:T(128)} %get-tuple-element.50, f32[]{:T(128)} %get-tuple-element.49), kind=kLoop, calls=%fused_computation.209 | loop fusion | flops 5632 | bytes 2064 | tf_op jit(solution)/shard_map/add | solution.py:208
  101.6 7.0 %collective-permute-start.11 = (f32[33,512]{1,0:T(8,128)S(1)}, f32[33,512]{1,0:T(8,128)S(1)}, u32[]{:S(2)}, u32[]{:S(2)}) collective-permute-start(f32[33,512]{1,0:T(8,128)S(1)} %dynamic-update-slice.13), channel_id=1, source_target_pairs={{0,24},{1,25},{2,26},{3,27},{4,28},{5,29},{6,30},{7,31}} | collective-permute-start | bytes 202760 | tf_op jit(solution)/shard_map/ppermute | solution.py:216
  111.0 1.6 %pad_maximum_fusion.3 = f32[12,64,512]{2,0,1:T(8,128)S(1)} fusion(f32[2,64,512]{2,0,1:T(2,128)S(1)} %copy.41, f32[8,64,512]{2,0,1:T(8,128)} %copy-done.2, f32[2,64,512]{2,0,1:T(2,128)S(1)} %copy.42), kind=kLoop, calls=%fused_computation.19 | loop fusion | flops 786432 | bytes 3145728 | tf_op jit(solution)/shard_map/concatenate | solution.py:68
  115.0 2.1 %fusion.7 = f32[10,64,512]{2,0,1:T(8,128)S(1)} fusion(f32[10,64,511]{2,0,1:T(8,128)S(1)} %get-tuple-element.74, f32[10,64,511]{2,0,1:T(8,128)S(1)} %get-tuple-element.73, f32[10,63,512]{2,0,1:T(8,128)S(1)} %get-tuple-element.72, f32[10,63,512]{2,0,1:T(8,128)S(1)} %get-tuple-element.71, f32[8,64,512]{2,0,1:T(8,128)S(1)} %copy-done.3, ...), kind=kLoop, calls=%fused_computation.21 | loop fusion | flops 4259840 | bytes 10701834 | tf_op jit(solution)/shard_map/jit(_where)/select_n | solution.py:86
  120.2 1.6 %copy.45 = f32[1,8,64,512]{3,2,1,0:T(8,128)} copy(f32[1,8,64,512]{3,1,2,0:T(8,128)S(1)} %maximum_select_fusion) | data formatting | bytes 2097152
  121.9 3.7 %collective-permute-start.14 = (f32[4]{0:T(128)S(1)}, f32[4]{0:T(128)S(1)}, u32[]{:S(2)}, u32[]{:S(2)}) collective-permute-start(f32[4]{0:T(128)S(1)} %slice_bitcast_fusion.1), channel_id=1, source_target_pairs={{0,1},{1,0},{2,3},{3,2},{4,5},{5,4},{6,7},{7,6},{8,9},{9,8},{10,11... | collective-permute-start | bytes 56 | tf_op jit(solution)/shard_map/ppermute | solution.py:111
  126.4 2.9 %collective-permute-start.15 = (f32[4]{0:T(128)S(1)}, f32[4]{0:T(128)S(1)}, u32[]{:S(2)}, u32[]{:S(2)}) collective-permute-start(f32[4]{0:T(128)S(1)} %fusion.102), channel_id=1, source_target_pairs={{0,2},{1,3},{2,0},{3,1},{4,6},{5,7},{6,4},{7,5},{8,10},{9,11},{10,... | collective-permute-start | bytes 56 | tf_op jit(solution)/shard_map/ppermute | solution.py:111
  129.3 1.5 %collective-permute-done.15 = f32[4]{0:T(128)S(1)} collective-permute-done((f32[4]{0:T(128)S(1)}, f32[4]{0:T(128)S(1)}, u32[]{:S(2)}, u32[]{:S(2)}) %collective-permute-start.15) | collective-permute-done | bytes 48 | tf_op jit(solution)/shard_map/ppermute | solution.py:111
  130.8 2.0 %collective-permute-start.16 = (f32[4]{0:T(128)S(1)}, f32[4]{0:T(128)S(1)}, u32[]{:S(2)}, u32[]{:S(2)}) collective-permute-start(f32[4]{0:T(128)S(1)} %add.616), channel_id=1, source_target_pairs={{0,4},{1,5},{2,6},{3,7},{4,0},{5,1},{6,2},{7,3},{8,12},{9,13},{10,... | collective-permute-start | bytes 56 | tf_op jit(solution)/shard_map/ppermute | solution.py:111
  132.9 1.5 %collective-permute-done.16 = f32[4]{0:T(128)S(1)} collective-permute-done((f32[4]{0:T(128)S(1)}, f32[4]{0:T(128)S(1)}, u32[]{:S(2)}, u32[]{:S(2)}) %collective-permute-start.16) | collective-permute-done | bytes 48 | tf_op jit(solution)/shard_map/ppermute | solution.py:111
  (213 shorter events, 45.6 us)
Async XLA Ops:
  0.6 2.0 %copy-start.9 = (f32[1,8,64,512]{3,2,1,0:T(8,128)S(1)}, f32[1,8,64,512]{3,2,1,0:T(8,128)}, u32[]{:S(2)}) copy-start(f32[1,8,64,512]{3,2,1,0:T(8,128)} %param.16) | copy-start | bytes 3145732
  3.9 1.8 %copy-start.22 = (s32[8]{0:T(128)S(1)}, s32[8]{0:T(128)}, u32[]{:S(2)}) copy-start(s32[8]{0:T(128)} %param.23) | copy-start | bytes 100
  3.9 1.8 %copy-start.14 = (f32[8,512]{1,0:T(8,128)S(1)}, f32[8,512]{1,0:T(8,128)}, u32[]{:S(2)}) copy-start(f32[8,512]{1,0:T(8,128)} %param.20) | copy-start | bytes 49156
  3.9 1.8 %copy-start.15 = (s32[8]{0:T(128)S(1)}, s32[8]{0:T(128)}, u32[]{:S(2)}) copy-start(s32[8]{0:T(128)} %param.21) | copy-start | bytes 100
  7.4 7.1 %collective-permute-start.1 = (f32[324,512]{1,0:T(8,128)}, f32[324,512]{1,0:T(8,128)}, u32[]{:S(2)}, u32[]{:S(2)}) collective-permute-start(f32[324,512]{1,0:T(8,128)} %pad_maximum_fusion.6), channel_id=1, source_target_pairs={{1,0},{2,1},{3,2},{4,3},{5,4},{6,5},{7,6},{9,8},{10,9},{11,10},{12... | collective-permute-start | bytes 1990664 | tf_op jit(solution)/shard_map/ppermute | solution.py:63
  9.8 5.8 %collective-permute-start = (f32[324,512]{1,0:T(8,128)}, f32[324,512]{1,0:T(8,128)S(1)}, u32[]{:S(2)}, u32[]{:S(2)}) collective-permute-start(f32[324,512]{1,0:T(8,128)} %pad_maximum_fusion.5), channel_id=1, source_target_pairs={{0,1},{1,2},{2,3},{3,4},{4,5},{5,6},{6,7},{8,9},{9,10},{10,11},{11... | collective-permute-start | bytes 1990664 | tf_op jit(solution)/shard_map/ppermute | solution.py:62
  12.9 28.3 %copy-start.16 = (pred[10]{0:T(512)(128)(4,1)}, pred[10]{0:T(512)(128)(4,1)S(1)}, u32[]{:S(2)}) copy-start(pred[10]{0:T(512)(128)(4,1)S(1)} %slice.677) | copy-start | bytes 34
  13.0 37.0 %copy-start.18 = (pred[8]{0:T(512)(128)(4,1)}, pred[8]{0:T(512)(128)(4,1)S(1)}, u32[]{:S(2)}) copy-start(pred[8]{0:T(512)(128)(4,1)S(1)} %slice.652) | copy-start | bytes 28
  13.1 24.7 %copy-start.21 = (pred[14]{0:T(512)(128)(4,1)}, pred[14]{0:T(512)(128)(4,1)S(1)}, u32[]{:S(2)}) copy-start(pred[14]{0:T(512)(128)(4,1)S(1)} %slice.681) | copy-start | bytes 46
  13.1 24.9 %copy-start.20 = (pred[12]{0:T(512)(128)(4,1)}, pred[12]{0:T(512)(128)(4,1)S(1)}, u32[]{:S(2)}) copy-start(pred[12]{0:T(512)(128)(4,1)S(1)} %slice.679) | copy-start | bytes 40
  16.9 5.3 %slice-start = ((s8[8388608]{0:T(1024)(128)(4,1)}), s8[4194304]{0:T(1024)(128)(4,1)S(1)}, s32[]{:S(2)}) async-start(s8[8388608]{0:T(1024)(128)(4,1)} %bitcast.74), calls=%async_computation | async-start | bytes 8388608
  18.1 19.6 %copy-start.8 = (f32[14,7,512]{2,0,1:T(8,128)}, f32[14,7,512]{2,0,1:T(8,128)S(1)}, u32[]{:S(2)}) copy-start(f32[14,7,512]{2,0,1:T(8,128)S(1)} %get-tuple-element.62) | copy-start | bytes 602116
  18.5 3.7 %slice-start.1 = ((s8[8388608]{0:T(1024)(128)(4,1)}), s8[4194304]{0:T(1024)(128)(4,1)S(1)}, s32[]{:S(2)}) async-start(s8[8388608]{0:T(1024)(128)(4,1)} %bitcast.74), calls=%async_computation.1 | async-start | bytes 8388608
  18.8 2.7 %copy-start.12 = (f32[324,512]{1,0:T(8,128)S(1)}, f32[324,512]{1,0:T(8,128)}, u32[]{:S(2)}) copy-start(f32[324,512]{1,0:T(8,128)} %copy-done.11) | copy-start | bytes 1990660
  20.0 2.1 %copy-start.13 = (f32[8,512]{1,0:T(8,128)S(1)}, f32[8,512]{1,0:T(8,128)}, u32[]{:S(2)}) copy-start(f32[8,512]{1,0:T(8,128)} %param.19) | copy-start | bytes 49156
  23.1 14.0 %collective-permute-start.2 = (f32[4,512]{1,0:T(4,128)S(1)}, f32[4,512]{1,0:T(4,128)S(1)}, u32[]{:S(2)}, u32[]{:S(2)}) collective-permute-start(f32[4,512]{1,0:T(4,128)S(1)} %get-tuple-element.122), channel_id=1, source_target_pairs={{0,1},{1,2},{2,3},{3,4},{4,5},{5,6},{6,7},{8,9},{9,10},{10,11},{11... | collective-permute-start | bytes 24584 | tf_op jit(solution)/shard_map/ppermute | solution.py:62
  34.0 3.7 %collective-permute-start.3 = (f32[4,512]{1,0:T(4,128)S(1)}, f32[4,512]{1,0:T(4,128)S(1)}, u32[]{:S(2)}, u32[]{:S(2)}) collective-permute-start(f32[4,512]{1,0:T(4,128)S(1)} %get-tuple-element.123), channel_id=1, source_target_pairs={{1,0},{2,1},{3,2},{4,3},{5,4},{6,5},{7,6},{9,8},{10,9},{11,10},{12... | collective-permute-start | bytes 24584 | tf_op jit(solution)/shard_map/ppermute | solution.py:63
  36.6 13.4 %copy-start = (f32[10,56,512]{2,0,1:T(8,128)}, f32[10,56,512]{2,0,1:T(8,128)S(1)}, u32[]{:S(2)}) copy-start(f32[10,56,512]{2,0,1:T(8,128)S(1)} %get-tuple-element.66) | copy-start | bytes 3440644
  46.3 9.1 %collective-permute-start.4 = (f32[2]{0:T(128)S(1)}, f32[2]{0:T(128)S(1)}, u32[]{:S(2)}, u32[]{:S(2)}) collective-permute-start(f32[2]{0:T(128)S(1)} %pad_maximum_fusion.13), channel_id=1, source_target_pairs={{0,1},{1,0},{2,3},{3,2},{4,5},{5,4},{6,7},{7,6},{8,9},{9,8},{10,11... | collective-permute-start | bytes 32 | tf_op jit(solution)/shard_map/ppermute | solution.py:111
  56.7 6.8 %collective-permute-start.5 = (f32[2]{0:T(128)S(1)}, f32[2]{0:T(128)S(1)}, u32[]{:S(2)}, u32[]{:S(2)}) collective-permute-start(f32[2]{0:T(128)S(1)} %fusion.140), channel_id=1, source_target_pairs={{0,2},{1,3},{2,0},{3,1},{4,6},{5,7},{6,4},{7,5},{8,10},{9,11},{10,... | collective-permute-start | bytes 32 | tf_op jit(solution)/shard_map/ppermute | solution.py:111
  64.9 3.5 %collective-permute-start.6 = (f32[2]{0:T(128)S(1)}, f32[2]{0:T(128)S(1)}, u32[]{:S(2)}, u32[]{:S(2)}) collective-permute-start(f32[2]{0:T(128)S(1)} %fusion.141), channel_id=1, source_target_pairs={{0,4},{1,5},{2,6},{3,7},{4,0},{5,1},{6,2},{7,3},{8,12},{9,13},{10,... | collective-permute-start | bytes 32 | tf_op jit(solution)/shard_map/ppermute | solution.py:111
  68.4 3.5 %collective-permute-start.7 = (f32[2]{0:T(128)S(1)}, f32[2]{0:T(128)S(1)}, u32[]{:S(2)}, u32[]{:S(2)}) collective-permute-start(f32[2]{0:T(128)S(1)} %add.569), channel_id=1, source_target_pairs={{0,8},{8,0},{16,24},{24,16},{1,9},{9,1},{17,25},{25,17},{2,10},{10... | collective-permute-start | bytes 32 | tf_op jit(solution)/shard_map/ppermute | solution.py:111
  72.0 4.4 %collective-permute-start.8 = (f32[2]{0:T(128)S(1)}, f32[2]{0:T(128)S(1)}, u32[]{:S(2)}, u32[]{:S(2)}) collective-permute-start(f32[2]{0:T(128)S(1)} %add.570), channel_id=1, source_target_pairs={{0,16},{8,24},{16,0},{24,8},{1,17},{9,25},{17,1},{25,9},{2,18},{10... | collective-permute-start | bytes 32 | tf_op jit(solution)/shard_map/ppermute | solution.py:111
  80.9 6.7 %collective-permute-start.10 = (f32[132,512]{1,0:T(8,128)}, f32[132,512]{1,0:T(8,128)}, u32[]{:S(2)}, u32[]{:S(2)}) collective-permute-start(f32[132,512]{1,0:T(8,128)} %pad_maximum_fusion.9), channel_id=1, source_target_pairs={{1,0},{2,1},{3,2},{4,3},{5,4},{6,5},{7,6},{9,8},{10,9},{11,10},{12... | collective-permute-start | bytes 811016 | tf_op jit(solution)/shard_map/ppermute | solution.py:63
  83.9 4.5 %collective-permute-start.9 = (f32[132,512]{1,0:T(8,128)}, f32[132,512]{1,0:T(8,128)}, u32[]{:S(2)}, u32[]{:S(2)}) collective-permute-start(f32[132,512]{1,0:T(8,128)} %pad_maximum_fusion.8), channel_id=1, source_target_pairs={{0,1},{1,2},{2,3},{3,4},{4,5},{5,6},{6,7},{8,9},{9,10},{10,11},{11... | collective-permute-start | bytes 811016 | tf_op jit(solution)/shard_map/ppermute | solution.py:62
  100.2 21.6 %collective-permute-start.13 = (f32[33,512]{1,0:T(8,128)S(1)}, f32[33,512]{1,0:T(8,128)S(1)}, u32[]{:S(2)}, u32[]{:S(2)}) collective-permute-start(f32[33,512]{1,0:T(8,128)S(1)} %dynamic-update-slice.13), channel_id=1, source_target_pairs={{16,24},{17,25},{18,26},{19,27},{20,28},{21,29},{22,30},{23,31}} | collective-permute-start | bytes 202760 | tf_op jit(solution)/shard_map/ppermute | solution.py:216
  100.9 20.9 %collective-permute-start.12 = (f32[33,512]{1,0:T(8,128)S(1)}, f32[33,512]{1,0:T(8,128)S(1)}, u32[]{:S(2)}, u32[]{:S(2)}) collective-permute-start(f32[33,512]{1,0:T(8,128)S(1)} %dynamic-update-slice.13), channel_id=1, source_target_pairs={{8,24},{9,25},{10,26},{11,27},{12,28},{13,29},{14,30},{15,31}} | collective-permute-start | bytes 202760 | tf_op jit(solution)/shard_map/ppermute | solution.py:216
  101.6 20.2 %collective-permute-start.11 = (f32[33,512]{1,0:T(8,128)S(1)}, f32[33,512]{1,0:T(8,128)S(1)}, u32[]{:S(2)}, u32[]{:S(2)}) collective-permute-start(f32[33,512]{1,0:T(8,128)S(1)} %dynamic-update-slice.13), channel_id=1, source_target_pairs={{0,24},{1,25},{2,26},{3,27},{4,28},{5,29},{6,30},{7,31}} | collective-permute-start | bytes 202760 | tf_op jit(solution)/shard_map/ppermute | solution.py:216
  113.2 1.8 %copy-start.3 = (f32[8,64,512]{2,0,1:T(8,128)S(1)}, f32[8,64,512]{2,0,1:T(8,128)}, u32[]{:S(2)}) copy-start(f32[8,64,512]{2,0,1:T(8,128)} %copy-done.2) | copy-start | bytes 3145732
  121.9 4.5 %collective-permute-start.14 = (f32[4]{0:T(128)S(1)}, f32[4]{0:T(128)S(1)}, u32[]{:S(2)}, u32[]{:S(2)}) collective-permute-start(f32[4]{0:T(128)S(1)} %slice_bitcast_fusion.1), channel_id=1, source_target_pairs={{0,1},{1,0},{2,3},{3,2},{4,5},{5,4},{6,7},{7,6},{8,9},{9,8},{10,11... | collective-permute-start | bytes 56 | tf_op jit(solution)/shard_map/ppermute | solution.py:111
  126.4 4.5 %collective-permute-start.15 = (f32[4]{0:T(128)S(1)}, f32[4]{0:T(128)S(1)}, u32[]{:S(2)}, u32[]{:S(2)}) collective-permute-start(f32[4]{0:T(128)S(1)} %fusion.102), channel_id=1, source_target_pairs={{0,2},{1,3},{2,0},{3,1},{4,6},{5,7},{6,4},{7,5},{8,10},{9,11},{10,... | collective-permute-start | bytes 56 | tf_op jit(solution)/shard_map/ppermute | solution.py:111
  130.8 3.5 %collective-permute-start.16 = (f32[4]{0:T(128)S(1)}, f32[4]{0:T(128)S(1)}, u32[]{:S(2)}, u32[]{:S(2)}) collective-permute-start(f32[4]{0:T(128)S(1)} %add.616), channel_id=1, source_target_pairs={{0,4},{1,5},{2,6},{3,7},{4,0},{5,1},{6,2},{7,3},{8,12},{9,13},{10,... | collective-permute-start | bytes 56 | tf_op jit(solution)/shard_map/ppermute | solution.py:111
  (12 other events, 14.9 us)

commit v7 on v6

--- a/solution.py
+++ b/solution.py
@@ -113,6 +113,17 @@
     return v
 
 
+def shell_sum(v, side_count):
+    count = lax.axis_size("slab")
+    base = (side_count - 1) * count
+    step = 1
+    while step < count:
+        pairs = [(base + i, base + (i ^ step)) for i in range(count)]
+        v = v + lax.ppermute(v, ("side", "slab"), pairs)
+        step *= 2
+    return v
+
+
 def allsum(v):
     return allsum_axis(allsum_axis(v, "slab"), "side")
 
@@ -138,10 +149,14 @@
     deep_planes = planes - BAND
     disp_zero = own_live * disp_init
     plane_zero = jnp.sum(onehot[:, :, None] * (live * disp_zero)[None], axis=1)
-    packed, plane_zero_rims, init_deep, fc_deep = exchange(
+    packed, plane_zero_rims = exchange(
         [
             (jnp.concatenate([start_here[:, :BAND], force_here[:, :BAND], coef_here[:, :BAND]], axis=1), HALO),
             (plane_zero, HALO),
+        ]
+    )
+    init_deep, fc_deep = exchange(
+        [
             (start_here[:, BAND:], 2),
             (jnp.concatenate([force_here[:, BAND:], coef_here[:, BAND:]], axis=1), 1),
         ]
@@ -180,8 +195,13 @@
     disp_one = disp_zero + RELAX * resid_zero
     tilde_one, unused, unused_extra = evaluate(disp_one)
     init_deep, tilde_one = lax.optimization_barrier((init_deep, tilde_one))
-    deep = deep_step(init_deep, force_deep, coef_deep, ok_one)
-    deep = deep_step(deep, force_deep[1:-1], coef_deep[1:-1], ok_two)
+    deep = lax.cond(
+        shell_flag,
+        lambda: jnp.zeros((slab_rows,) + init_deep.shape[1:], jnp.float32),
+        lambda: deep_step(
+            deep_step(init_deep, force_deep, coef_deep, ok_one), force_deep[1:-1], coef_deep[1:-1], ok_two
+        ),
+    )
     resid_one = tilde_one - disp_one
     diff_one = resid_one - resid_zero
     sums = allsum(jnp.stack([jnp.sum(diff_one * diff_one), jnp.sum(diff_one * resid_one)]))
@@ -189,8 +209,13 @@
     coeff = -gram_ab / (gram_aa + (0.001 * gram_aa + 1e-06))
     disp_two = tilde_one + coeff * (tilde_one - tilde_zero)
     tilde_two, band_two, (deep,) = evaluate(disp_two, extra=[(deep, 2)])
-    deep = deep_step(deep, force_deep, coef_deep, ok_one)
-    deep = deep_step(deep, force_deep[1:-1], coef_deep[1:-1], ok_two)
+    deep = lax.cond(
+        shell_flag,
+        lambda: jnp.zeros((slab_rows,) + deep.shape[1:], jnp.float32),
+        lambda: deep_step(
+            deep_step(deep, force_deep, coef_deep, ok_one), force_deep[1:-1], coef_deep[1:-1], ok_two
+        ),
+    )
     resid_two = tilde_two - disp_two
     newer = resid_two - resid_one
     partial = jnp.stack(
@@ -214,7 +239,7 @@
     gathered = outgoing
     for source in range(side_count - 1):
         gathered = gathered + lax.ppermute(outgoing, "side", [(source, side_count - 1)])
-    sums = allsum_axis(gathered[4 * patches_here, :4], "slab")
+    sums = shell_sum(gathered[4 * patches_here, :4], side_count)
     gram_nn, gram_no, proj_new, proj_old = sums[0], sums[1], sums[2], sums[3]
     tilde_two, tilde_one, tilde_zero, resid_two = (
         gathered[k * patches_here : (k + 1) * patches_here] for k in range(4)

time: 144 us -> 132 us (0.917)
  the two profiles are of different devices: /device:TPU:0 before, /device:TPU:28 now
where the time goes in v7:
time: 132 us; the launch traced here: 131 us
  starting transfers between devices  42.6 us (32%)
  waiting for transfers between devices  33.7 us (26%)
  other arithmetic  27.2 us (21%)
  local copies, waits for them, and re-layouts  16.1 us (12%)
  between operations  11.3 us (9%)
    ppermute x4, starting transfers between devices, exchange(): high = lax.ppermute(down, 'slab', backward)  13.8 us
    ppermute x5, waiting for transfers between devices, allsum_axis(): v = v + lax.ppermute(v, axis, [(i, i ^ step) for i in range(count)])  11.1 us
    ppermute x5, starting transfers between devices, allsum_axis(): v = v + lax.ppermute(v, axis, [(i, i ^ step) for i in range(count)])  10.4 us
    ppermute x4, starting transfers between devices, exchange(): low = lax.ppermute(up, 'slab', forward)  8.16 us
    ppermute x4, waiting for transfers between devices, exchange(): low = lax.ppermute(up, 'slab', forward)  7.44 us
    ppermute x3, waiting for transfers between devices, shell_sum(): v = v + lax.ppermute(v, ('side', 'slab'), pairs)  7.4 us
    unnamed x45, local copies, waits for them, and re-layouts  7.27 us
    ppermute x3, starting transfers between devices, shell_sum(): v = v + lax.ppermute(v, ('side', 'slab'), pairs)  6.44 us
  transfers between devices with their start and end apart: 19, of which 13 were waited for; matrix products, arithmetic and copies ran while one was open for 12% of the time, Pallas kernels for 0%

profile of v7, /device:TPU:28, one launch (start us, length us, event | category | flops | bytes accessed | tf_op | source)
XLA Modules:
  0.0 131.2 jit_solution(13170443259437963946)
XLA Ops:
  3.0 1.8 %copy.57 = f32[1,8,64,512]{3,1,2,0:T(8,128)S(1)} copy(f32[1,8,64,512]{3,2,1,0:T(8,128)} %param.20) | data formatting | bytes 2097152 | tf_op args[1]
  7.3 2.8 %collective-permute-start.1 = (f32[100,512]{1,0:T(8,128)S(1)}, f32[100,512]{1,0:T(8,128)S(1)}, u32[]{:S(2)}, u32[]{:S(2)}) collective-permute-start(f32[100,512]{1,0:T(8,128)S(1)} %pad_maximum_fusion.13), channel_id=1, source_target_pairs={{1,0},{2,1},{3,2},{4,3},{5,4},{6,5},{7,6},{9,8},{10,9},{11,10},{12... | collective-permute-start | bytes 614408 | tf_op jit(solution)/shard_map/ppermute | solution.py:63
  10.2 1.9 %collective-permute-start = (f32[100,512]{1,0:T(8,128)S(1)}, f32[100,512]{1,0:T(8,128)S(1)}, u32[]{:S(2)}, u32[]{:S(2)}) collective-permute-start(f32[100,512]{1,0:T(8,128)S(1)} %pad_maximum_fusion.12), channel_id=1, source_target_pairs={{0,1},{1,2},{2,3},{3,4},{4,5},{5,6},{6,7},{8,9},{9,10},{10,11},{11... | collective-permute-start | bytes 614408 | tf_op jit(solution)/shard_map/ppermute | solution.py:62
  14.3 4.5 %collective-permute-start.3 = (f32[224,512]{1,0:T(8,128)}, f32[224,512]{1,0:T(8,128)}, u32[]{:S(2)}, u32[]{:S(2)}) collective-permute-start(f32[224,512]{1,0:T(8,128)} %pad_maximum_fusion.6), channel_id=1, source_target_pairs={{1,0},{2,1},{3,2},{4,3},{5,4},{6,5},{7,6},{9,8},{10,9},{11,10},{12... | collective-permute-start | bytes 1376264 | tf_op jit(solution)/shard_map/ppermute | solution.py:63
  19.8 1.9 %collective-permute-start.2 = (f32[224,512]{1,0:T(8,128)}, f32[224,512]{1,0:T(8,128)}, u32[]{:S(2)}, u32[]{:S(2)}) collective-permute-start(f32[224,512]{1,0:T(8,128)} %pad_maximum_fusion.5), channel_id=1, source_target_pairs={{0,1},{1,2},{2,3},{3,4},{4,5},{5,6},{6,7},{8,9},{9,10},{10,11},{11... | collective-permute-start | bytes 1376264 | tf_op jit(solution)/shard_map/ppermute | solution.py:62
  27.7 4.5 %collective-permute-start.5 = (f32[4,512]{1,0:T(4,128)S(1)}, f32[4,512]{1,0:T(4,128)S(1)}, u32[]{:S(2)}, u32[]{:S(2)}) collective-permute-start(f32[4,512]{1,0:T(4,128)S(1)} %get-tuple-element.177), channel_id=1, source_target_pairs={{1,0},{2,1},{3,2},{4,3},{5,4},{6,5},{7,6},{9,8},{10,9},{11,10},{12... | collective-permute-start | bytes 24584 | tf_op jit(solution)/shard_map/ppermute | solution.py:63
  32.3 1.9 %collective-permute-start.4 = (f32[4,512]{1,0:T(4,128)S(1)}, f32[4,512]{1,0:T(4,128)S(1)}, u32[]{:S(2)}, u32[]{:S(2)}) collective-permute-start(f32[4,512]{1,0:T(4,128)S(1)} %get-tuple-element.176), channel_id=1, source_target_pairs={{0,1},{1,2},{2,3},{3,4},{4,5},{5,6},{6,7},{8,9},{9,10},{10,11},{11... | collective-permute-start | bytes 24584 | tf_op jit(solution)/shard_map/ppermute | solution.py:62
  34.3 3.8 %collective-permute-done.4 = f32[4,512]{1,0:T(4,128)S(1)} collective-permute-done((f32[4,512]{1,0:T(4,128)S(1)}, f32[4,512]{1,0:T(4,128)S(1)}, u32[]{:S(2)}, u32[]{:S(2)}) %collective-permute-start.4) | collective-permute-done | bytes 8224 | tf_op jit(solution)/shard_map/ppermute | solution.py:62
  43.8 1.4 %pad_maximum_fusion.15 = f32[2]{0:T(128)S(1)} fusion(f32[1]{0:T(128)} %bitcast.24, f32[1]{0:T(128)} %bitcast.23), kind=kLoop, calls=%fused_computation.210 | loop fusion | flops 2 | bytes 16 | tf_op jit(solution)/shard_map/stack | solution.py:207
  46.9 2.5 %pad_maximum_fusion.1 = (f32[10,64,512]{2,0,1:T(8,128)}, f32[10,64,512]{2,0,1:T(8,128)}) fusion(f32[10,56,512]{2,0,1:T(8,128)S(1)} %get-tuple-element.136, f32[10,8,512]{2,0,1:T(8,128)S(1)} %get-tuple-element.144, f32[10,56,512]{2,0,1:T(8,128)S(1)} %get-tuple-element.135, f32[10,8,512]{2,0,1:T(8,128)S(1)} %get-tuple-element.143), kind=kLoop, calls=%fused_computation.33 | loop fusion | flops 655360 | bytes 5242880 | tf_op jit(solution)/shard_map/concatenate | solution.py:170
  49.6 1.4 %fusion.137 = f32[2]{0:T(128)S(1)} fusion(f32[2]{0:T(128)S(1)} %collective-permute-done.6, f32[1]{0:T(128)} %bitcast.24, f32[1]{0:T(128)} %bitcast.23), kind=kLoop, calls=%fused_computation.247 | loop fusion | flops 4 | bytes 24 | tf_op jit(solution)/shard_map/add | solution.py:111
  51.0 3.5 %collective-permute-done.7 = f32[2]{0:T(128)S(1)} collective-permute-done((f32[2]{0:T(128)S(1)}, f32[2]{0:T(128)S(1)}, u32[]{:S(2)}, u32[]{:S(2)}) %collective-permute-start.7) | collective-permute-done | bytes 40 | tf_op jit(solution)/shard_map/ppermute | solution.py:111
  54.5 1.4 %fusion.138 = f32[2]{0:T(128)S(1)} fusion(f32[2]{0:T(128)S(1)} %collective-permute-done.7, f32[2]{0:T(128)S(1)} %collective-permute-done.6, f32[1]{0:T(128)} %bitcast.24, f32[1]{0:T(128)} %bitcast.23), kind=kLoop, calls=%fused_computation.248 | loop fusion | flops 6 | bytes 32 | tf_op jit(solution)/shard_map/add | solution.py:111
  55.9 3.5 %collective-permute-done.8 = f32[2]{0:T(128)S(1)} collective-permute-done((f32[2]{0:T(128)S(1)}, f32[2]{0:T(128)S(1)}, u32[]{:S(2)}, u32[]{:S(2)}) %collective-permute-start.8) | collective-permute-done | bytes 40 | tf_op jit(solution)/shard_map/ppermute | solution.py:111
  59.4 8.4 %collective-permute-start.9 = (f32[2]{0:T(128)S(1)}, f32[2]{0:T(128)S(1)}, u32[]{:S(2)}, u32[]{:S(2)}) collective-permute-start(f32[2]{0:T(128)S(1)} %add.573), channel_id=1, source_target_pairs={{0,8},{8,0},{16,24},{24,16},{1,9},{9,1},{17,25},{25,17},{2,10},{10... | collective-permute-start | bytes 32 | tf_op jit(solution)/shard_map/ppermute | solution.py:111
  67.9 1.5 %collective-permute-done.9 = f32[2]{0:T(128)S(1)} collective-permute-done((f32[2]{0:T(128)S(1)}, f32[2]{0:T(128)S(1)}, u32[]{:S(2)}, u32[]{:S(2)}) %collective-permute-start.9) | collective-permute-done | bytes 40 | tf_op jit(solution)/shard_map/ppermute | solution.py:111
  69.4 1.9 %collective-permute-start.10 = (f32[2]{0:T(128)S(1)}, f32[2]{0:T(128)S(1)}, u32[]{:S(2)}, u32[]{:S(2)}) collective-permute-start(f32[2]{0:T(128)S(1)} %add.574), channel_id=1, source_target_pairs={{0,16},{8,24},{16,0},{24,8},{1,17},{9,25},{17,1},{25,9},{2,18},{10... | collective-permute-start | bytes 32 | tf_op jit(solution)/shard_map/ppermute | solution.py:111
  71.3 2.5 %collective-permute-done.10 = f32[2]{0:T(128)S(1)} collective-permute-done((f32[2]{0:T(128)S(1)}, f32[2]{0:T(128)S(1)}, u32[]{:S(2)}, u32[]{:S(2)}) %collective-permute-start.10) | collective-permute-done | bytes 40 | tf_op jit(solution)/shard_map/ppermute | solution.py:111
  76.7 1.9 %collective-permute-start.12 = (f32[132,512]{1,0:T(8,128)S(1)}, f32[132,512]{1,0:T(8,128)S(1)}, u32[]{:S(2)}, u32[]{:S(2)}) collective-permute-start(f32[132,512]{1,0:T(8,128)S(1)} %pad_maximum_fusion.9), channel_id=1, source_target_pairs={{1,0},{2,1},{3,2},{4,3},{5,4},{6,5},{7,6},{9,8},{10,9},{11,10},{12... | collective-permute-start | bytes 811016 | tf_op jit(solution)/shard_map/ppermute | solution.py:63
  78.6 2.4 %collective-permute-start.11 = (f32[132,512]{1,0:T(8,128)S(1)}, f32[132,512]{1,0:T(8,128)S(1)}, u32[]{:S(2)}, u32[]{:S(2)}) collective-permute-start(f32[132,512]{1,0:T(8,128)S(1)} %pad_maximum_fusion.8), channel_id=1, source_target_pairs={{0,1},{1,2},{2,3},{3,4},{4,5},{5,6},{6,7},{8,9},{9,10},{10,11},{11... | collective-permute-start | bytes 811016 | tf_op jit(solution)/shard_map/ppermute | solution.py:62
  81.0 2.7 %collective-permute-done.12 = f32[132,512]{1,0:T(8,128)S(1)} collective-permute-done((f32[132,512]{1,0:T(8,128)S(1)}, f32[132,512]{1,0:T(8,128)S(1)}, u32[]{:S(2)}, u32[]{:S(2)}) %collective-permute-start.12) | collective-permute-done | bytes 270368 | tf_op jit(solution)/shard_map/ppermute | solution.py:63
  83.8 3.6 %collective-permute-done.11 = f32[132,512]{1,0:T(8,128)S(1)} collective-permute-done((f32[132,512]{1,0:T(8,128)S(1)}, f32[132,512]{1,0:T(8,128)S(1)}, u32[]{:S(2)}, u32[]{:S(2)}) %collective-permute-start.11) | collective-permute-done | bytes 270368 | tf_op jit(solution)/shard_map/ppermute | solution.py:62
  90.1 4.1 %multiply_reduce_fusion = f32[8,512]{1,0:T(8,128)S(1)} fusion(f32[8,512,512]{2,1,0:T(8,128)} %param.22, f32[8,512]{1,0:T(8,128)S(1)} %subtract_select_fusion), kind=kLoop, calls=%fused_computation.28 | loop fusion | flops 4190208 | bytes 8421376 | tf_op jit(solution)/shard_map/reduce_sum | solution.py:190
  95.0 2.6 %fusion.97 = f32[1,512]{1,0:T(1,128)S(1)} fusion(f32[]{:T(128)} %get-tuple-element.102, f32[]{:T(128)} %get-tuple-element.103, f32[]{:T(128)} %get-tuple-element.101, f32[]{:T(128)} %get-tuple-element.100), kind=kLoop, calls=%fused_computation.205 | loop fusion | flops 5632 | bytes 2064 | tf_op jit(solution)/shard_map/add | solution.py:233
  97.6 1.3 collective-permute-start.15
  104.4 2.2 %collective-permute-done.14 = f32[33,512]{1,0:T(8,128)S(1)} collective-permute-done((f32[33,512]{1,0:T(8,128)S(1)}, f32[33,512]{1,0:T(8,128)S(1)}, u32[]{:S(2)}, u32[]{:S(2)}) %collective-permute-start.14) | collective-permute-done | bytes 67616 | tf_op jit(solution)/shard_map/ppermute | solution.py:241
  106.6 1.7 %collective-permute-done.13 = f32[33,512]{1,0:T(8,128)S(1)} collective-permute-done((f32[33,512]{1,0:T(8,128)S(1)}, f32[33,512]{1,0:T(8,128)S(1)}, u32[]{:S(2)}, u32[]{:S(2)}) %collective-permute-start.13) | collective-permute-done | bytes 67616 | tf_op jit(solution)/shard_map/ppermute | solution.py:241
  108.4 1.9 %collective-permute-start.16 = (f32[4]{0:T(128)S(1)}, f32[4]{0:T(128)S(1)}, u32[]{:S(2)}, u32[]{:S(2)}) collective-permute-start(f32[4]{0:T(128)S(1)} %slice_bitcast_fusion.1), channel_id=1, source_target_pairs={{24,25},{25,24},{26,27},{27,26},{28,29},{29,28},{30,31},{31,30}} | collective-permute-start | bytes 56 | tf_op jit(solution)/shard_map/ppermute | solution.py:122
  111.4 2.6 %collective-permute-start.17 = (f32[4]{0:T(128)S(1)}, f32[4]{0:T(128)S(1)}, u32[]{:S(2)}, u32[]{:S(2)}) collective-permute-start(f32[4]{0:T(128)S(1)} %fusion.99), channel_id=1, source_target_pairs={{24,26},{25,27},{26,24},{27,25},{28,30},{29,31},{30,28},{31,29}} | collective-permute-start | bytes 56 | tf_op jit(solution)/shard_map/ppermute | solution.py:122
  114.0 2.8 %collective-permute-done.17 = f32[4]{0:T(128)S(1)} collective-permute-done((f32[4]{0:T(128)S(1)}, f32[4]{0:T(128)S(1)}, u32[]{:S(2)}, u32[]{:S(2)}) %collective-permute-start.17) | collective-permute-done | bytes 48 | tf_op jit(solution)/shard_map/ppermute | solution.py:122
  116.9 1.9 %collective-permute-start.18 = (f32[4]{0:T(128)S(1)}, f32[4]{0:T(128)S(1)}, u32[]{:S(2)}, u32[]{:S(2)}) collective-permute-start(f32[4]{0:T(128)S(1)} %add.606), channel_id=1, source_target_pairs={{24,28},{25,29},{26,30},{27,31},{28,24},{29,25},{30,26},{31,27}} | collective-permute-start | bytes 56 | tf_op jit(solution)/shard_map/ppermute | solution.py:122
  118.8 3.5 %collective-permute-done.18 = f32[4]{0:T(128)S(1)} collective-permute-done((f32[4]{0:T(128)S(1)}, f32[4]{0:T(128)S(1)}, u32[]{:S(2)}, u32[]{:S(2)}) %collective-permute-start.18) | collective-permute-done | bytes 48 | tf_op jit(solution)/shard_map/ppermute | solution.py:122
  (190 shorter events, 33.5 us)
Async XLA Ops:
  0.6 4.2 %copy-start.6 = (f32[1,8,64,512]{3,2,1,0:T(8,128)S(1)}, f32[1,8,64,512]{3,2,1,0:T(8,128)}, u32[]{:S(2)}) copy-start(f32[1,8,64,512]{3,2,1,0:T(8,128)} %param.19) | copy-start | bytes 3145732
  4.8 20.1 %copy-start.4 = (f32[1,8,64,512]{3,1,2,0:T(8,128)}, f32[1,8,64,512]{3,1,2,0:T(8,128)S(1)}, u32[]{:S(2)}) copy-start(f32[1,8,64,512]{3,1,2,0:T(8,128)S(1)} %copy.57) | copy-start | bytes 3145732
  4.8 1.6 %copy-start.7 = (f32[1,8,64,512]{3,2,1,0:T(8,128)S(1)}, f32[1,8,64,512]{3,2,1,0:T(8,128)}, u32[]{:S(2)}) copy-start(f32[1,8,64,512]{3,2,1,0:T(8,128)} %param.21) | copy-start | bytes 3145732
  7.3 15.8 %collective-permute-start.1 = (f32[100,512]{1,0:T(8,128)S(1)}, f32[100,512]{1,0:T(8,128)S(1)}, u32[]{:S(2)}, u32[]{:S(2)}) collective-permute-start(f32[100,512]{1,0:T(8,128)S(1)} %pad_maximum_fusion.13), channel_id=1, source_target_pairs={{1,0},{2,1},{3,2},{4,3},{5,4},{6,5},{7,6},{9,8},{10,9},{11,10},{12... | collective-permute-start | bytes 614408 | tf_op jit(solution)/shard_map/ppermute | solution.py:63
  10.2 13.1 %collective-permute-start = (f32[100,512]{1,0:T(8,128)S(1)}, f32[100,512]{1,0:T(8,128)S(1)}, u32[]{:S(2)}, u32[]{:S(2)}) collective-permute-start(f32[100,512]{1,0:T(8,128)S(1)} %pad_maximum_fusion.12), channel_id=1, source_target_pairs={{0,1},{1,2},{2,3},{3,4},{4,5},{5,6},{6,7},{8,9},{9,10},{10,11},{11... | collective-permute-start | bytes 614408 | tf_op jit(solution)/shard_map/ppermute | solution.py:62
  13.5 8.4 %copy-start.15 = (s32[8]{0:T(128)S(1)}, s32[8]{0:T(128)}, u32[]{:S(2)}) copy-start(s32[8]{0:T(128)} %param.27) | copy-start | bytes 100
  14.3 25.7 %collective-permute-start.3 = (f32[224,512]{1,0:T(8,128)}, f32[224,512]{1,0:T(8,128)}, u32[]{:S(2)}, u32[]{:S(2)}) collective-permute-start(f32[224,512]{1,0:T(8,128)} %pad_maximum_fusion.6), channel_id=1, source_target_pairs={{1,0},{2,1},{3,2},{4,3},{5,4},{6,5},{7,6},{9,8},{10,9},{11,10},{12... | collective-permute-start | bytes 1376264 | tf_op jit(solution)/shard_map/ppermute | solution.py:63
  19.8 21.6 %collective-permute-start.2 = (f32[224,512]{1,0:T(8,128)}, f32[224,512]{1,0:T(8,128)}, u32[]{:S(2)}, u32[]{:S(2)}) collective-permute-start(f32[224,512]{1,0:T(8,128)} %pad_maximum_fusion.5), channel_id=1, source_target_pairs={{0,1},{1,2},{2,3},{3,4},{4,5},{5,6},{6,7},{8,9},{9,10},{10,11},{11... | collective-permute-start | bytes 1376264 | tf_op jit(solution)/shard_map/ppermute | solution.py:62
  23.1 3.0 %slice-start = ((s8[8388608]{0:T(1024)(128)(4,1)}), s8[4194304]{0:T(1024)(128)(4,1)S(1)}, s32[]{:S(2)}) async-start(s8[8388608]{0:T(1024)(128)(4,1)} %bitcast.82), calls=%async_computation | async-start | bytes 8388608
  23.9 2.9 %slice-start.1 = ((s8[8388608]{0:T(1024)(128)(4,1)}), s8[4194304]{0:T(1024)(128)(4,1)S(1)}, s32[]{:S(2)}) async-start(s8[8388608]{0:T(1024)(128)(4,1)} %bitcast.82), calls=%async_computation.1 | async-start | bytes 8388608
  24.6 1.4 %copy-start.12 = (f32[8,512]{1,0:T(8,128)S(1)}, f32[8,512]{1,0:T(8,128)}, u32[]{:S(2)}) copy-start(f32[8,512]{1,0:T(8,128)} %param.23) | copy-start | bytes 49156
  27.7 6.6 %collective-permute-start.5 = (f32[4,512]{1,0:T(4,128)S(1)}, f32[4,512]{1,0:T(4,128)S(1)}, u32[]{:S(2)}, u32[]{:S(2)}) collective-permute-start(f32[4,512]{1,0:T(4,128)S(1)} %get-tuple-element.177), channel_id=1, source_target_pairs={{1,0},{2,1},{3,2},{4,3},{5,4},{6,5},{7,6},{9,8},{10,9},{11,10},{12... | collective-permute-start | bytes 24584 | tf_op jit(solution)/shard_map/ppermute | solution.py:63
  32.3 5.9 %collective-permute-start.4 = (f32[4,512]{1,0:T(4,128)S(1)}, f32[4,512]{1,0:T(4,128)S(1)}, u32[]{:S(2)}, u32[]{:S(2)}) collective-permute-start(f32[4,512]{1,0:T(4,128)S(1)} %get-tuple-element.176), channel_id=1, source_target_pairs={{0,1},{1,2},{2,3},{3,4},{4,5},{5,6},{6,7},{8,9},{9,10},{10,11},{11... | collective-permute-start | bytes 24584 | tf_op jit(solution)/shard_map/ppermute | solution.py:62
  40.0 2.6 %copy-start.5 = (f32[8,56,512]{2,0,1:T(8,128)S(1)}, f32[8,56,512]{2,0,1:T(8,128)}, u32[]{:S(2)}) copy-start(f32[8,56,512]{2,0,1:T(8,128)} %slice.839) | copy-start | bytes 2752516
  42.7 2.8 %copy-start.3 = (f32[8,56,512]{2,0,1:T(8,128)S(1)}, f32[8,56,512]{2,0,1:T(8,128)}, u32[]{:S(2)}) copy-start(f32[8,56,512]{2,0,1:T(8,128)} %copy-done.2) | copy-start | bytes 2752516
  43.1 2.4 %copy-start.1 = (f32[8,56,512]{2,0,1:T(8,128)S(1)}, f32[8,56,512]{2,0,1:T(8,128)}, u32[]{:S(2)}) copy-start(f32[8,56,512]{2,0,1:T(8,128)} %copy-done) | copy-start | bytes 2752516
  45.1 4.5 %collective-permute-start.6 = (f32[2]{0:T(128)S(1)}, f32[2]{0:T(128)S(1)}, u32[]{:S(2)}, u32[]{:S(2)}) collective-permute-start(f32[2]{0:T(128)S(1)} %pad_maximum_fusion.15), channel_id=1, source_target_pairs={{0,1},{1,0},{2,3},{3,2},{4,5},{5,4},{6,7},{7,6},{8,9},{9,8},{10,11... | collective-permute-start | bytes 32 | tf_op jit(solution)/shard_map/ppermute | solution.py:111
  51.0 3.5 %collective-permute-start.7 = (f32[2]{0:T(128)S(1)}, f32[2]{0:T(128)S(1)}, u32[]{:S(2)}, u32[]{:S(2)}) collective-permute-start(f32[2]{0:T(128)S(1)} %fusion.137), channel_id=1, source_target_pairs={{0,2},{1,3},{2,0},{3,1},{4,6},{5,7},{6,4},{7,5},{8,10},{9,11},{10,... | collective-permute-start | bytes 32 | tf_op jit(solution)/shard_map/ppermute | solution.py:111
  55.9 3.5 %collective-permute-start.8 = (f32[2]{0:T(128)S(1)}, f32[2]{0:T(128)S(1)}, u32[]{:S(2)}, u32[]{:S(2)}) collective-permute-start(f32[2]{0:T(128)S(1)} %fusion.138), channel_id=1, source_target_pairs={{0,4},{1,5},{2,6},{3,7},{4,0},{5,1},{6,2},{7,3},{8,12},{9,13},{10,... | collective-permute-start | bytes 32 | tf_op jit(solution)/shard_map/ppermute | solution.py:111
  59.4 10.0 %collective-permute-start.9 = (f32[2]{0:T(128)S(1)}, f32[2]{0:T(128)S(1)}, u32[]{:S(2)}, u32[]{:S(2)}) collective-permute-start(f32[2]{0:T(128)S(1)} %add.573), channel_id=1, source_target_pairs={{0,8},{8,0},{16,24},{24,16},{1,9},{9,1},{17,25},{25,17},{2,10},{10... | collective-permute-start | bytes 32 | tf_op jit(solution)/shard_map/ppermute | solution.py:111
  69.4 4.4 %collective-permute-start.10 = (f32[2]{0:T(128)S(1)}, f32[2]{0:T(128)S(1)}, u32[]{:S(2)}, u32[]{:S(2)}) collective-permute-start(f32[2]{0:T(128)S(1)} %add.574), channel_id=1, source_target_pairs={{0,16},{8,24},{16,0},{24,8},{1,17},{9,25},{17,1},{25,9},{2,18},{10... | collective-permute-start | bytes 32 | tf_op jit(solution)/shard_map/ppermute | solution.py:111
  76.7 7.1 %collective-permute-start.12 = (f32[132,512]{1,0:T(8,128)S(1)}, f32[132,512]{1,0:T(8,128)S(1)}, u32[]{:S(2)}, u32[]{:S(2)}) collective-permute-start(f32[132,512]{1,0:T(8,128)S(1)} %pad_maximum_fusion.9), channel_id=1, source_target_pairs={{1,0},{2,1},{3,2},{4,3},{5,4},{6,5},{7,6},{9,8},{10,9},{11,10},{12... | collective-permute-start | bytes 811016 | tf_op jit(solution)/shard_map/ppermute | solution.py:63
  78.6 8.8 %collective-permute-start.11 = (f32[132,512]{1,0:T(8,128)S(1)}, f32[132,512]{1,0:T(8,128)S(1)}, u32[]{:S(2)}, u32[]{:S(2)}) collective-permute-start(f32[132,512]{1,0:T(8,128)S(1)} %pad_maximum_fusion.8), channel_id=1, source_target_pairs={{0,1},{1,2},{2,3},{3,4},{4,5},{5,6},{6,7},{8,9},{9,10},{10,11},{11... | collective-permute-start | bytes 811016 | tf_op jit(solution)/shard_map/ppermute | solution.py:62
  83.8 3.6 %copy-start.8 = (f32[132,512]{1,0:T(8,128)}, f32[132,512]{1,0:T(8,128)S(1)}, u32[]{:S(2)}) copy-start(f32[132,512]{1,0:T(8,128)S(1)} %collective-permute-done.12) | copy-start | bytes 811012
  90.1 11.5 %copy-start.9 = (f32[132,512]{1,0:T(8,128)S(1)}, f32[132,512]{1,0:T(8,128)}, u32[]{:S(2)}) copy-start(f32[132,512]{1,0:T(8,128)} %copy-done.8) | copy-start | bytes 811012
  90.1 11.5 %copy-start.11 = (f32[132,512]{1,0:T(8,128)S(1)}, f32[132,512]{1,0:T(8,128)}, u32[]{:S(2)}) copy-start(f32[132,512]{1,0:T(8,128)} %copy-done.10) | copy-start | bytes 811012
  97.6 6.8 %collective-permute-start.15 = (f32[33,512]{1,0:T(8,128)S(1)}, f32[33,512]{1,0:T(8,128)S(1)}, u32[]{:S(2)}, u32[]{:S(2)}) collective-permute-start(f32[33,512]{1,0:T(8,128)S(1)} %dynamic-update-slice.13), channel_id=1, source_target_pairs={{16,24},{17,25},{18,26},{19,27},{20,28},{21,29},{22,30},{23,31}} | collective-permute-start | bytes 202760 | tf_op jit(solution)/shard_map/ppermute | solution.py:241
  98.9 7.7 %collective-permute-start.14 = (f32[33,512]{1,0:T(8,128)S(1)}, f32[33,512]{1,0:T(8,128)S(1)}, u32[]{:S(2)}, u32[]{:S(2)}) collective-permute-start(f32[33,512]{1,0:T(8,128)S(1)} %dynamic-update-slice.13), channel_id=1, source_target_pairs={{8,24},{9,25},{10,26},{11,27},{12,28},{13,29},{14,30},{15,31}} | collective-permute-start | bytes 202760 | tf_op jit(solution)/shard_map/ppermute | solution.py:241
  100.2 8.1 %collective-permute-start.13 = (f32[33,512]{1,0:T(8,128)S(1)}, f32[33,512]{1,0:T(8,128)S(1)}, u32[]{:S(2)}, u32[]{:S(2)}) collective-permute-start(f32[33,512]{1,0:T(8,128)S(1)} %dynamic-update-slice.13), channel_id=1, source_target_pairs={{0,24},{1,25},{2,26},{3,27},{4,28},{5,29},{6,30},{7,31}} | collective-permute-start | bytes 202760 | tf_op jit(solution)/shard_map/ppermute | solution.py:241
  108.4 3.0 %collective-permute-start.16 = (f32[4]{0:T(128)S(1)}, f32[4]{0:T(128)S(1)}, u32[]{:S(2)}, u32[]{:S(2)}) collective-permute-start(f32[4]{0:T(128)S(1)} %slice_bitcast_fusion.1), channel_id=1, source_target_pairs={{24,25},{25,24},{26,27},{27,26},{28,29},{29,28},{30,31},{31,30}} | collective-permute-start | bytes 56 | tf_op jit(solution)/shard_map/ppermute | solution.py:122
  111.4 5.4 %collective-permute-start.17 = (f32[4]{0:T(128)S(1)}, f32[4]{0:T(128)S(1)}, u32[]{:S(2)}, u32[]{:S(2)}) collective-permute-start(f32[4]{0:T(128)S(1)} %fusion.99), channel_id=1, source_target_pairs={{24,26},{25,27},{26,24},{27,25},{28,30},{29,31},{30,28},{31,29}} | collective-permute-start | bytes 56 | tf_op jit(solution)/shard_map/ppermute | solution.py:122
  116.9 5.4 %collective-permute-start.18 = (f32[4]{0:T(128)S(1)}, f32[4]{0:T(128)S(1)}, u32[]{:S(2)}, u32[]{:S(2)}) collective-permute-start(f32[4]{0:T(128)S(1)} %add.606), channel_id=1, source_target_pairs={{24,28},{25,29},{26,30},{27,31},{28,24},{29,25},{30,26},{31,27}} | collective-permute-start | bytes 56 | tf_op jit(solution)/shard_map/ppermute | solution.py:122
  (5 other events, 4.9 us)

commit v8 on v7

--- a/solution.py
+++ b/solution.py
@@ -4,6 +4,7 @@
 from jax.sharding import PartitionSpec as P
 
 SWEEPS = 4
+CAP = 4
 RELAX = 0.5
 PENALTY = 3.0
 HALO = SWEEPS
@@ -145,6 +146,11 @@
     own_live = own * live
     onehot = (block_row[None, :] == jnp.arange(slab_rows)[:, None]).astype(jnp.float32) * own[:, 0][None, :]
     pick = (block_row[:, None] == jnp.arange(slab_rows)[None, :]).astype(jnp.float32)
+    owned = (owner[:, 0] == side_id).astype(jnp.int32)
+    rank = jnp.cumsum(owned) - 1
+    slot_hit = (owned[None, :] == 1) & (rank[None, :] == jnp.arange(CAP)[:, None])
+    slot_of = slot_hit.astype(jnp.float32)
+    slot_patch = jnp.sum(slot_hit.astype(jnp.int32) * jnp.arange(owned.shape[0])[None, :], axis=1)
 
     deep_planes = planes - BAND
     disp_zero = own_live * disp_init
@@ -155,22 +161,11 @@
             (plane_zero, HALO),
         ]
     )
-    init_deep, fc_deep = exchange(
-        [
-            (start_here[:, BAND:], 2),
-            (jnp.concatenate([force_here[:, BAND:], coef_here[:, BAND:]], axis=1), 1),
-        ]
-    )
     init_band, force_band, coef_band = (
         packed[:, :BAND],
         packed[:, BAND : 2 * BAND],
         packed[:, 2 * BAND :],
     )
-    init_deep = jnp.concatenate([init_band[HALO - 2 : HALO + slab_rows + 2], init_deep], axis=1)
-    force_deep = jnp.concatenate(
-        [force_band[HALO - 1 : HALO + slab_rows + 1], fc_deep[:, :deep_planes]], axis=1
-    )
-    coef_deep = jnp.concatenate([coef_band[HALO - 1 : HALO + slab_rows + 1], fc_deep[:, deep_planes:]], axis=1)
     global_row = slab_id * slab_rows + jnp.arange(slab_rows + 2 * HALO) - HALO
     total_rows = slab_rows * lax.axis_size("slab")
     row_ok = ((global_row >= 0) & (global_row < total_rows))[:, None, None]
@@ -187,10 +182,26 @@
         band = band_solve(init_band, rhs, coef_band, row_ok)
         traction = PENALTY * jnp.sum(pick[:, :, None] * band[:, 0, :][None], axis=1)
         loaded = live * (shell_load - traction)
-        tilde = own_live * jnp.sum(compliance * loaded[:, None, :], axis=-1)
+        picked = jnp.sum(slot_of[:, :, None] * loaded[None], axis=1)
+        products = jnp.stack(
+            [
+                jnp.sum(lax.dynamic_index_in_dim(compliance, slot_patch[k], keepdims=False) * picked[k][None, :], axis=-1)
+                for k in range(CAP)
+            ]
+        )
+        tilde = own_live * jnp.sum(slot_of.T[:, :, None] * products[None], axis=1)
         return tilde, band, extra
 
     tilde_zero, unused, unused_extra = evaluate(disp_zero, plane_zero_rims)
+    deep_init_src, deep_fc_src, tilde_zero = lax.optimization_barrier(
+        (start_here[:, BAND:], jnp.concatenate([force_here[:, BAND:], coef_here[:, BAND:]], axis=1), tilde_zero)
+    )
+    init_deep, fc_deep = exchange([(deep_init_src, 2), (deep_fc_src, 1)])
+    init_deep = jnp.concatenate([init_band[HALO - 2 : HALO + slab_rows + 2], init_deep], axis=1)
+    force_deep = jnp.concatenate(
+        [force_band[HALO - 1 : HALO + slab_rows + 1], fc_deep[:, :deep_planes]], axis=1
+    )
+    coef_deep = jnp.concatenate([coef_band[HALO - 1 : HALO + slab_rows + 1], fc_deep[:, deep_planes:]], axis=1)
     resid_zero = tilde_zero - disp_zero
     disp_one = disp_zero + RELAX * resid_zero
     tilde_one, unused, unused_extra = evaluate(disp_one)

time: 132 us -> 149 us (1.13)
  between operations: 11.3 us -> 19.5 us
  local copies, waits for them, and re-layouts: 16.1 us -> 22.2 us
  other arithmetic: 27.2 us -> 30.3 us
  starting transfers between devices: 42.6 us -> 40.3 us
    concatenate x0 -> x2, other arithmetic: none -> 3.33 us  [the longest x1 1.73 us: body(): jnp.concatenate([coef_band[HALO - 1:HALO + slab_rows + 1], fc_deep[:, dee...]
    ppermute x4, waiting for transfers between devices: 7.44 us -> 10.1 us  [exchange(): low = lax.ppermute(up, 'slab', forward)]
    ppermute x4, starting transfers between devices: 13.8 us -> 11.2 us  [exchange(): high = lax.ppermute(down, 'slab', backward)]
    concatenate x1, other arithmetic: 2.51 us -> 0.22 us  [body(): jnp.concatenate([force_band[HALO - 1:HALO + slab_rows + 1], fc_deep[:, :d...]
    slice x4, local copies, waits for them, and re-layouts: 0.3 us -> 1.99 us  [band_solve(): q = jnp.where(row_ok[k:rows - k], new, 0.0)]
    reduce_sum x3 -> x10, other arithmetic: 5.36 us -> 4.34 us  [the longest x3 3.71 us: evaluate(): jnp.sum(lax.dynamic_index_in_dim(compliance, slot_patch[k], keepdims=Fals...]
    unnamed x45 -> x126, local copies, waits for them, and re-layouts: 7.27 us -> 7.79 us
where the time goes in v8:
time: 149 us; the launch traced here: 147 us
  starting transfers between devices  40.3 us (27%)
  waiting for transfers between devices  35 us (23%)
  other arithmetic  30.3 us (20%)
  local copies, waits for them, and re-layouts  22.2 us (15%)
  between operations  19.5 us (13%)
    ppermute x4, starting transfers between devices, exchange(): high = lax.ppermute(down, 'slab', backward)  11.2 us
    ppermute x5, waiting for transfers between devices, allsum_axis(): v = v + lax.ppermute(v, axis, [(i, i ^ step) for i in range(count)])  11.1 us
    ppermute x4, waiting for transfers between devices, exchange(): low = lax.ppermute(up, 'slab', forward)  10.1 us
    ppermute x5, starting transfers between devices, allsum_axis(): v = v + lax.ppermute(v, axis, [(i, i ^ step) for i in range(count)])  9.76 us
    ppermute x4, starting transfers between devices, exchange(): low = lax.ppermute(up, 'slab', forward)  9.04 us
    unnamed x126, local copies, waits for them, and re-layouts  7.79 us
    ppermute x3, waiting for transfers between devices, shell_sum(): v = v + lax.ppermute(v, ('side', 'slab'), pairs)  7.41 us
    ppermute x3, starting transfers between devices, shell_sum(): v = v + lax.ppermute(v, ('side', 'slab'), pairs)  6.43 us
  transfers between devices with their start and end apart: 19, of which 13 were waited for; matrix products, arithmetic and copies ran while one was open for 12% of the time, Pallas kernels for 0%

profile of v8, /device:TPU:28, one launch (start us, length us, event | category | flops | bytes accessed | tf_op | source)
XLA Modules:
  0.0 147.2 jit_solution(12605531054753210319)
XLA Ops:
  0.6 1.9 %copy.55 = f32[1,8,64,512]{3,1,2,0:T(8,128)S(1)} copy(f32[1,8,64,512]{3,2,1,0:T(8,128)} %param.21) | data formatting | bytes 2097152 | tf_op args[2]
  6.8 2.8 %collective-permute-start.1 = (f32[100,512]{1,0:T(8,128)}, f32[100,512]{1,0:T(8,128)}, u32[]{:S(2)}, u32[]{:S(2)}) collective-permute-start(f32[100,512]{1,0:T(8,128)} %pad_maximum_fusion.12), channel_id=1, source_target_pairs={{1,0},{2,1},{3,2},{4,3},{5,4},{6,5},{7,6},{9,8},{10,9},{11,10},{12... | collective-permute-start | bytes 614408 | tf_op jit(solution)/shard_map/ppermute | solution.py:64
  10.4 1.9 %collective-permute-start = (f32[100,512]{1,0:T(8,128)}, f32[100,512]{1,0:T(8,128)}, u32[]{:S(2)}, u32[]{:S(2)}) collective-permute-start(f32[100,512]{1,0:T(8,128)} %pad_maximum_fusion.11), channel_id=1, source_target_pairs={{0,1},{1,2},{2,3},{3,4},{4,5},{5,6},{6,7},{8,9},{9,10},{10,11},{11... | collective-permute-start | bytes 614408 | tf_op jit(solution)/shard_map/ppermute | solution.py:63
  24.4 1.6 %pad_maximum_fusion.3 = f32[8,112,512]{2,0,1:T(8,128)S(1)} fusion(f32[8,56,512]{2,0,1:T(8,128)} %slice.907, f32[8,56,512]{2,0,1:T(8,128)} %slice.906), kind=kLoop, calls=%fused_computation.32 | loop fusion | flops 458752 | bytes 3670016 | tf_op jit(solution)/shard_map/concatenate | solution.py:197
  40.0 4.5 %collective-permute-start.3 = (f32[224,512]{1,0:T(8,128)S(1)}, f32[224,512]{1,0:T(8,128)S(1)}, u32[]{:S(2)}, u32[]{:S(2)}) collective-permute-start(f32[224,512]{1,0:T(8,128)S(1)} %pad_maximum_fusion.7), channel_id=1, source_target_pairs={{1,0},{2,1},{3,2},{4,3},{5,4},{6,5},{7,6},{9,8},{10,9},{11,10},{12... | collective-permute-start | bytes 1376264 | tf_op jit(solution)/shard_map/ppermute | solution.py:64
  44.8 1.9 %collective-permute-start.5 = (f32[4,512]{1,0:T(4,128)S(1)}, f32[4,512]{1,0:T(4,128)S(1)}, u32[]{:S(2)}, u32[]{:S(2)}) collective-permute-start(f32[4,512]{1,0:T(4,128)S(1)} %get-tuple-element.197), channel_id=1, source_target_pairs={{1,0},{2,1},{3,2},{4,3},{5,4},{6,5},{7,6},{9,8},{10,9},{11,10},{12... | collective-permute-start | bytes 24584 | tf_op jit(solution)/shard_map/ppermute | solution.py:64
  46.7 2.4 %collective-permute-start.4 = (f32[4,512]{1,0:T(4,128)S(1)}, f32[4,512]{1,0:T(4,128)S(1)}, u32[]{:S(2)}, u32[]{:S(2)}) collective-permute-start(f32[4,512]{1,0:T(4,128)S(1)} %get-tuple-element.196), channel_id=1, source_target_pairs={{0,1},{1,2},{2,3},{3,4},{4,5},{5,6},{6,7},{8,9},{9,10},{10,11},{11... | collective-permute-start | bytes 24584 | tf_op jit(solution)/shard_map/ppermute | solution.py:63
  49.2 2.1 %collective-permute-start.2 = (f32[224,512]{1,0:T(8,128)S(1)}, f32[224,512]{1,0:T(8,128)S(1)}, u32[]{:S(2)}, u32[]{:S(2)}) collective-permute-start(f32[224,512]{1,0:T(8,128)S(1)} %pad_maximum_fusion.6), channel_id=1, source_target_pairs={{0,1},{1,2},{2,3},{3,4},{4,5},{5,6},{6,7},{8,9},{9,10},{10,11},{11... | collective-permute-start | bytes 1376264 | tf_op jit(solution)/shard_map/ppermute | solution.py:63
  54.7 5.2 %collective-permute-done.2 = f32[224,512]{1,0:T(8,128)S(1)} collective-permute-done((f32[224,512]{1,0:T(8,128)S(1)}, f32[224,512]{1,0:T(8,128)S(1)}, u32[]{:S(2)}, u32[]{:S(2)}) %collective-permute-start.2) | collective-permute-done | bytes 458784 | tf_op jit(solution)/shard_map/ppermute | solution.py:63
  64.7 1.7 %pad_maximum_fusion.2 = f32[10,64,512]{2,0,1:T(8,128)} fusion(f32[10,56,512]{2,0,1:T(8,128)S(1)} %get-tuple-element.155, f32[10,8,512]{2,0,1:T(8,128)S(1)} %get-tuple-element.163), kind=kLoop, calls=%fused_computation.31 | loop fusion | flops 327680 | bytes 2621440 | tf_op jit(solution)/shard_map/concatenate | solution.py:204
  66.9 1.4 fusion.156
  68.4 3.5 %collective-permute-done.7 = f32[2]{0:T(128)S(1)} collective-permute-done((f32[2]{0:T(128)S(1)}, f32[2]{0:T(128)S(1)}, u32[]{:S(2)}, u32[]{:S(2)}) %collective-permute-start.7) | collective-permute-done | bytes 40 | tf_op jit(solution)/shard_map/ppermute | solution.py:112
  71.9 1.4 fusion.157
  73.3 3.5 %collective-permute-done.8 = f32[2]{0:T(128)S(1)} collective-permute-done((f32[2]{0:T(128)S(1)}, f32[2]{0:T(128)S(1)}, u32[]{:S(2)}, u32[]{:S(2)}) %collective-permute-start.8) | collective-permute-done | bytes 40 | tf_op jit(solution)/shard_map/ppermute | solution.py:112
  76.9 7.8 %collective-permute-start.9 = (f32[2]{0:T(128)S(1)}, f32[2]{0:T(128)S(1)}, u32[]{:S(2)}, u32[]{:S(2)}) collective-permute-start(f32[2]{0:T(128)S(1)} %add.604), channel_id=1, source_target_pairs={{0,8},{8,0},{16,24},{24,16},{1,9},{9,1},{17,25},{25,17},{2,10},{10... | collective-permute-start | bytes 32 | tf_op jit(solution)/shard_map/ppermute | solution.py:112
  84.7 1.5 %collective-permute-done.9 = f32[2]{0:T(128)S(1)} collective-permute-done((f32[2]{0:T(128)S(1)}, f32[2]{0:T(128)S(1)}, u32[]{:S(2)}, u32[]{:S(2)}) %collective-permute-start.9) | collective-permute-done | bytes 40 | tf_op jit(solution)/shard_map/ppermute | solution.py:112
  86.2 1.9 %collective-permute-start.10 = (f32[2]{0:T(128)S(1)}, f32[2]{0:T(128)S(1)}, u32[]{:S(2)}, u32[]{:S(2)}) collective-permute-start(f32[2]{0:T(128)S(1)} %add.605), channel_id=1, source_target_pairs={{0,16},{8,24},{16,0},{24,8},{1,17},{9,25},{17,1},{25,9},{2,18},{10... | collective-permute-start | bytes 32 | tf_op jit(solution)/shard_map/ppermute | solution.py:112
  88.1 2.5 %collective-permute-done.10 = f32[2]{0:T(128)S(1)} collective-permute-done((f32[2]{0:T(128)S(1)}, f32[2]{0:T(128)S(1)}, u32[]{:S(2)}, u32[]{:S(2)}) %collective-permute-start.10) | collective-permute-done | bytes 40 | tf_op jit(solution)/shard_map/ppermute | solution.py:112
  93.4 1.9 %collective-permute-start.12 = (f32[132,512]{1,0:T(8,128)S(1)}, f32[132,512]{1,0:T(8,128)S(1)}, u32[]{:S(2)}, u32[]{:S(2)}) collective-permute-start(f32[132,512]{1,0:T(8,128)S(1)} %pad_maximum_fusion.10), channel_id=1, source_target_pairs={{1,0},{2,1},{3,2},{4,3},{5,4},{6,5},{7,6},{9,8},{10,9},{11,10},{12... | collective-permute-start | bytes 811016 | tf_op jit(solution)/shard_map/ppermute | solution.py:64
  95.3 2.6 %collective-permute-start.11 = (f32[132,512]{1,0:T(8,128)S(1)}, f32[132,512]{1,0:T(8,128)S(1)}, u32[]{:S(2)}, u32[]{:S(2)}) collective-permute-start(f32[132,512]{1,0:T(8,128)S(1)} %pad_maximum_fusion.9), channel_id=1, source_target_pairs={{0,1},{1,2},{2,3},{3,4},{4,5},{5,6},{6,7},{8,9},{9,10},{10,11},{11... | collective-permute-start | bytes 811016 | tf_op jit(solution)/shard_map/ppermute | solution.py:63
  98.0 2.5 %collective-permute-done.12 = f32[132,512]{1,0:T(8,128)S(1)} collective-permute-done((f32[132,512]{1,0:T(8,128)S(1)}, f32[132,512]{1,0:T(8,128)S(1)}, u32[]{:S(2)}, u32[]{:S(2)}) %collective-permute-start.12) | collective-permute-done | bytes 270368 | tf_op jit(solution)/shard_map/ppermute | solution.py:64
  100.5 3.6 %collective-permute-done.11 = f32[132,512]{1,0:T(8,128)S(1)} collective-permute-done((f32[132,512]{1,0:T(8,128)S(1)}, f32[132,512]{1,0:T(8,128)S(1)}, u32[]{:S(2)}, u32[]{:S(2)}) %collective-permute-start.11) | collective-permute-done | bytes 270368 | tf_op jit(solution)/shard_map/ppermute | solution.py:63
  107.2 3.0 %fusion.29 = (f32[512]{0:T(512)S(1)}, f32[512]{0:T(512)S(1)}, f32[512]{0:T(512)S(1)}, f32[512]{0:T(512)S(1)}) fusion(f32[8,512,512]{2,1,0:T(8,128)} %param.22, s32[]{:T(128)S(6)} %select_n.144, f32[512]{0:T(512)S(1)} %bitcast.178, f32[512]{0:T(512)S(1)} %bitcast.177, s32[]{:T(128)S(6)} %select_n.149, f32[512]{0:T(512)S(1)} %bitcast.176, s32[]{:T(128)S(6)} %select_n.150, ...), kind=kLoop, calls=%fused_computation.58 | loop fusion | flops 2095104 | bytes 4210704 | tf_op jit(solution)/shard_map/reduce_sum | solution.py:188
  111.0 2.6 %fusion.109 = f32[1,512]{1,0:T(1,128)S(1)} fusion(f32[]{:T(128)} %get-tuple-element.120, f32[]{:T(128)} %get-tuple-element.121, f32[]{:T(128)} %get-tuple-element.119, f32[]{:T(128)} %get-tuple-element.118), kind=kLoop, calls=%fused_computation.234 | loop fusion | flops 5632 | bytes 2064 | tf_op jit(solution)/shard_map/add | solution.py:244
  117.9 1.4 copy-done.1
  120.6 2.1 %collective-permute-done.14 = f32[33,512]{1,0:T(8,128)S(1)} collective-permute-done((f32[33,512]{1,0:T(8,128)S(1)}, f32[33,512]{1,0:T(8,128)S(1)}, u32[]{:S(2)}, u32[]{:S(2)}) %collective-permute-start.14) | collective-permute-done | bytes 67616 | tf_op jit(solution)/shard_map/ppermute | solution.py:252
  122.7 1.8 %collective-permute-done.13 = f32[33,512]{1,0:T(8,128)S(1)} collective-permute-done((f32[33,512]{1,0:T(8,128)S(1)}, f32[33,512]{1,0:T(8,128)S(1)}, u32[]{:S(2)}, u32[]{:S(2)}) %collective-permute-start.13) | collective-permute-done | bytes 67616 | tf_op jit(solution)/shard_map/ppermute | solution.py:252
  124.5 1.9 %collective-permute-start.16 = (f32[4]{0:T(128)S(1)}, f32[4]{0:T(128)S(1)}, u32[]{:S(2)}, u32[]{:S(2)}) collective-permute-start(f32[4]{0:T(128)S(1)} %slice_bitcast_fusion.3), channel_id=1, source_target_pairs={{24,25},{25,24},{26,27},{27,26},{28,29},{29,28},{30,31},{31,30}} | collective-permute-start | bytes 56 | tf_op jit(solution)/shard_map/ppermute | solution.py:123
  127.5 2.6 %collective-permute-start.17 = (f32[4]{0:T(128)S(1)}, f32[4]{0:T(128)S(1)}, u32[]{:S(2)}, u32[]{:S(2)}) collective-permute-start(f32[4]{0:T(128)S(1)} %fusion.115), channel_id=1, source_target_pairs={{24,26},{25,27},{26,24},{27,25},{28,30},{29,31},{30,28},{31,29}} | collective-permute-start | bytes 56 | tf_op jit(solution)/shard_map/ppermute | solution.py:123
  130.1 2.8 %collective-permute-done.17 = f32[4]{0:T(128)S(1)} collective-permute-done((f32[4]{0:T(128)S(1)}, f32[4]{0:T(128)S(1)}, u32[]{:S(2)}, u32[]{:S(2)}) %collective-permute-start.17) | collective-permute-done | bytes 48 | tf_op jit(solution)/shard_map/ppermute | solution.py:123
  133.0 1.9 %collective-permute-start.18 = (f32[4]{0:T(128)S(1)}, f32[4]{0:T(128)S(1)}, u32[]{:S(2)}, u32[]{:S(2)}) collective-permute-start(f32[4]{0:T(128)S(1)} %add.637), channel_id=1, source_target_pairs={{24,28},{25,29},{26,30},{27,31},{28,24},{29,25},{30,26},{31,27}} | collective-permute-start | bytes 56 | tf_op jit(solution)/shard_map/ppermute | solution.py:123
  134.9 3.5 %collective-permute-done.18 = f32[4]{0:T(128)S(1)} collective-permute-done((f32[4]{0:T(128)S(1)}, f32[4]{0:T(128)S(1)}, u32[]{:S(2)}, u32[]{:S(2)}) %collective-permute-start.18) | collective-permute-done | bytes 48 | tf_op jit(solution)/shard_map/ppermute | solution.py:123
  (292 shorter events, 44.0 us)
Async XLA Ops:
  4.2 8.2 %copy-start.2 = (f32[1,8,64,512]{3,1,2,0:T(8,128)}, f32[1,8,64,512]{3,1,2,0:T(8,128)S(1)}, u32[]{:S(2)}) copy-start(f32[1,8,64,512]{3,1,2,0:T(8,128)S(1)} %copy.53) | copy-start | bytes 3145732
  6.8 22.0 %collective-permute-start.1 = (f32[100,512]{1,0:T(8,128)}, f32[100,512]{1,0:T(8,128)}, u32[]{:S(2)}, u32[]{:S(2)}) collective-permute-start(f32[100,512]{1,0:T(8,128)} %pad_maximum_fusion.12), channel_id=1, source_target_pairs={{1,0},{2,1},{3,2},{4,3},{5,4},{6,5},{7,6},{9,8},{10,9},{11,10},{12... | collective-permute-start | bytes 614408 | tf_op jit(solution)/shard_map/ppermute | solution.py:64
  10.4 19.5 %collective-permute-start = (f32[100,512]{1,0:T(8,128)}, f32[100,512]{1,0:T(8,128)}, u32[]{:S(2)}, u32[]{:S(2)}) collective-permute-start(f32[100,512]{1,0:T(8,128)} %pad_maximum_fusion.11), channel_id=1, source_target_pairs={{0,1},{1,2},{2,3},{3,4},{4,5},{5,6},{6,7},{8,9},{9,10},{10,11},{11... | collective-permute-start | bytes 614408 | tf_op jit(solution)/shard_map/ppermute | solution.py:63
  28.8 24.7 %copy-start.47 = (pred[8]{0:T(512)(128)(4,1)}, pred[8]{0:T(512)(128)(4,1)S(1)}, u32[]{:S(2)}) copy-start(pred[8]{0:T(512)(128)(4,1)S(1)} %get-tuple-element.224) | copy-start | bytes 28
  28.8 37.6 %copy-start.53 = (pred[8,1,1]{0,2,1:T(4,128)(4,1)}, pred[8,1,1]{0,2,1:T(4,128)(4,1)S(1)}, u32[]{:S(2)}) copy-start(pred[8,1,1]{0,2,1:T(4,128)(4,1)S(1)} %get-tuple-element.225) | copy-start | bytes 28
  34.8 17.8 %copy-start.18 = (f32[16,1,512]{2,0,1:T(8,128)}, f32[16,1,512]{2,0,1:T(8,128)S(1)}, u32[]{:S(2)}) copy-start(f32[16,1,512]{2,0,1:T(8,128)S(1)} %get-tuple-element.136) | copy-start | bytes 98308
  35.0 17.6 %copy-start.12 = (f32[14,7,512]{2,0,1:T(8,128)}, f32[14,7,512]{2,0,1:T(8,128)S(1)}, u32[]{:S(2)}) copy-start(f32[14,7,512]{2,0,1:T(8,128)S(1)} %get-tuple-element.134) | copy-start | bytes 602116
  40.0 14.5 %collective-permute-start.3 = (f32[224,512]{1,0:T(8,128)S(1)}, f32[224,512]{1,0:T(8,128)S(1)}, u32[]{:S(2)}, u32[]{:S(2)}) collective-permute-start(f32[224,512]{1,0:T(8,128)S(1)} %pad_maximum_fusion.7), channel_id=1, source_target_pairs={{1,0},{2,1},{3,2},{4,3},{5,4},{6,5},{7,6},{9,8},{10,9},{11,10},{12... | collective-permute-start | bytes 1376264 | tf_op jit(solution)/shard_map/ppermute | solution.py:64
  44.8 6.5 %collective-permute-start.5 = (f32[4,512]{1,0:T(4,128)S(1)}, f32[4,512]{1,0:T(4,128)S(1)}, u32[]{:S(2)}, u32[]{:S(2)}) collective-permute-start(f32[4,512]{1,0:T(4,128)S(1)} %get-tuple-element.197), channel_id=1, source_target_pairs={{1,0},{2,1},{3,2},{4,3},{5,4},{6,5},{7,6},{9,8},{10,9},{11,10},{12... | collective-permute-start | bytes 24584 | tf_op jit(solution)/shard_map/ppermute | solution.py:64
  46.7 5.9 %collective-permute-start.4 = (f32[4,512]{1,0:T(4,128)S(1)}, f32[4,512]{1,0:T(4,128)S(1)}, u32[]{:S(2)}, u32[]{:S(2)}) collective-permute-start(f32[4,512]{1,0:T(4,128)S(1)} %get-tuple-element.196), channel_id=1, source_target_pairs={{0,1},{1,2},{2,3},{3,4},{4,5},{5,6},{6,7},{8,9},{9,10},{10,11},{11... | collective-permute-start | bytes 24584 | tf_op jit(solution)/shard_map/ppermute | solution.py:63
  49.2 10.7 %collective-permute-start.2 = (f32[224,512]{1,0:T(8,128)S(1)}, f32[224,512]{1,0:T(8,128)S(1)}, u32[]{:S(2)}, u32[]{:S(2)}) collective-permute-start(f32[224,512]{1,0:T(8,128)S(1)} %pad_maximum_fusion.6), channel_id=1, source_target_pairs={{0,1},{1,2},{2,3},{3,4},{4,5},{5,6},{6,7},{8,9},{9,10},{10,11},{11... | collective-permute-start | bytes 1376264 | tf_op jit(solution)/shard_map/ppermute | solution.py:63
  62.6 4.3 %collective-permute-start.6 = (f32[2]{0:T(128)S(1)}, f32[2]{0:T(128)S(1)}, u32[]{:S(2)}, u32[]{:S(2)}) collective-permute-start(f32[2]{0:T(128)S(1)} %pad_maximum_fusion.17), channel_id=1, source_target_pairs={{0,1},{1,0},{2,3},{3,2},{4,5},{5,4},{6,7},{7,6},{8,9},{9,8},{10,11... | collective-permute-start | bytes 32 | tf_op jit(solution)/shard_map/ppermute | solution.py:112
  66.7 26.4 %copy-start.17 = (f32[8,512]{1,0:T(8,128)S(1)}, f32[8,512]{1,0:T(8,128)}, u32[]{:S(2)}) copy-start(f32[8,512]{1,0:T(8,128)} %copy-done.16) | copy-start | bytes 49156
  66.7 26.4 %copy-start.33 = (s32[8]{0:T(128)S(1)}, s32[8]{0:T(128)}, u32[]{:S(2)}) copy-start(s32[8]{0:T(128)} %param.25) | copy-start | bytes 100
  66.7 26.5 %copy-start.28 = (f32[8,8]{1,0:T(8,128)S(1)}, f32[8,8]{1,0:T(8,128)}, u32[]{:S(2)}) copy-start(f32[8,8]{1,0:T(8,128)} %copy-done.26) | copy-start | bytes 772
  66.9 37.2 %copy-start.5 = (f32[16,8,512]{2,0,1:T(8,128)S(1)}, f32[16,8,512]{2,0,1:T(8,128)}, u32[]{:S(2)}) copy-start(f32[16,8,512]{2,0,1:T(8,128)} %copy.60) | copy-start | bytes 786436
  66.9 37.2 %copy-start.19 = (f32[16,1,512]{2,0,1:T(8,128)S(1)}, f32[16,1,512]{2,0,1:T(8,128)}, u32[]{:S(2)}) copy-start(f32[16,1,512]{2,0,1:T(8,128)} %copy-done.18) | copy-start | bytes 98308
  66.9 37.3 %copy-start.13 = (f32[14,7,512]{2,0,1:T(8,128)S(1)}, f32[14,7,512]{2,0,1:T(8,128)}, u32[]{:S(2)}) copy-start(f32[14,7,512]{2,0,1:T(8,128)} %copy-done.12) | copy-start | bytes 602116
  68.4 3.5 %collective-permute-start.7 = (f32[2]{0:T(128)S(1)}, f32[2]{0:T(128)S(1)}, u32[]{:S(2)}, u32[]{:S(2)}) collective-permute-start(f32[2]{0:T(128)S(1)} %fusion.156), channel_id=1, source_target_pairs={{0,2},{1,3},{2,0},{3,1},{4,6},{5,7},{6,4},{7,5},{8,10},{9,11},{10,... | collective-permute-start | bytes 32 | tf_op jit(solution)/shard_map/ppermute | solution.py:112
  73.3 3.5 %collective-permute-start.8 = (f32[2]{0:T(128)S(1)}, f32[2]{0:T(128)S(1)}, u32[]{:S(2)}, u32[]{:S(2)}) collective-permute-start(f32[2]{0:T(128)S(1)} %fusion.157), channel_id=1, source_target_pairs={{0,4},{1,5},{2,6},{3,7},{4,0},{5,1},{6,2},{7,3},{8,12},{9,13},{10,... | collective-permute-start | bytes 32 | tf_op jit(solution)/shard_map/ppermute | solution.py:112
  76.9 9.3 %collective-permute-start.9 = (f32[2]{0:T(128)S(1)}, f32[2]{0:T(128)S(1)}, u32[]{:S(2)}, u32[]{:S(2)}) collective-permute-start(f32[2]{0:T(128)S(1)} %add.604), channel_id=1, source_target_pairs={{0,8},{8,0},{16,24},{24,16},{1,9},{9,1},{17,25},{25,17},{2,10},{10... | collective-permute-start | bytes 32 | tf_op jit(solution)/shard_map/ppermute | solution.py:112
  86.2 4.4 %collective-permute-start.10 = (f32[2]{0:T(128)S(1)}, f32[2]{0:T(128)S(1)}, u32[]{:S(2)}, u32[]{:S(2)}) collective-permute-start(f32[2]{0:T(128)S(1)} %add.605), channel_id=1, source_target_pairs={{0,16},{8,24},{16,0},{24,8},{1,17},{9,25},{17,1},{25,9},{2,18},{10... | collective-permute-start | bytes 32 | tf_op jit(solution)/shard_map/ppermute | solution.py:112
  93.4 7.1 %collective-permute-start.12 = (f32[132,512]{1,0:T(8,128)S(1)}, f32[132,512]{1,0:T(8,128)S(1)}, u32[]{:S(2)}, u32[]{:S(2)}) collective-permute-start(f32[132,512]{1,0:T(8,128)S(1)} %pad_maximum_fusion.10), channel_id=1, source_target_pairs={{1,0},{2,1},{3,2},{4,3},{5,4},{6,5},{7,6},{9,8},{10,9},{11,10},{12... | collective-permute-start | bytes 811016 | tf_op jit(solution)/shard_map/ppermute | solution.py:64
  95.3 9.7 %copy-start.42 = (pred[12]{0:T(512)(128)(4,1)S(1)}, pred[12]{0:T(512)(128)(4,1)}, u32[]{:S(2)}) copy-start(pred[12]{0:T(512)(128)(4,1)} %slice.740) | copy-start | bytes 40
  95.3 8.8 %collective-permute-start.11 = (f32[132,512]{1,0:T(8,128)S(1)}, f32[132,512]{1,0:T(8,128)S(1)}, u32[]{:S(2)}, u32[]{:S(2)}) collective-permute-start(f32[132,512]{1,0:T(8,128)S(1)} %pad_maximum_fusion.9), channel_id=1, source_target_pairs={{0,1},{1,2},{2,3},{3,4},{4,5},{5,6},{6,7},{8,9},{9,10},{10,11},{11... | collective-permute-start | bytes 811016 | tf_op jit(solution)/shard_map/ppermute | solution.py:63
  107.2 10.5 %copy-start.21 = (f32[132,512]{1,0:T(8,128)S(1)}, f32[132,512]{1,0:T(8,128)}, u32[]{:S(2)}) copy-start(f32[132,512]{1,0:T(8,128)} %copy-done.20) | copy-start | bytes 811012
  113.7 6.9 %collective-permute-start.15 = (f32[33,512]{1,0:T(8,128)S(1)}, f32[33,512]{1,0:T(8,128)S(1)}, u32[]{:S(2)}, u32[]{:S(2)}) collective-permute-start(f32[33,512]{1,0:T(8,128)S(1)} %dynamic-update-slice.13), channel_id=1, source_target_pairs={{16,24},{17,25},{18,26},{19,27},{20,28},{21,29},{22,30},{23,31}} | collective-permute-start | bytes 202760 | tf_op jit(solution)/shard_map/ppermute | solution.py:252
  115.0 7.7 %collective-permute-start.14 = (f32[33,512]{1,0:T(8,128)S(1)}, f32[33,512]{1,0:T(8,128)S(1)}, u32[]{:S(2)}, u32[]{:S(2)}) collective-permute-start(f32[33,512]{1,0:T(8,128)S(1)} %dynamic-update-slice.13), channel_id=1, source_target_pairs={{8,24},{9,25},{10,26},{11,27},{12,28},{13,29},{14,30},{15,31}} | collective-permute-start | bytes 202760 | tf_op jit(solution)/shard_map/ppermute | solution.py:252
  116.3 8.1 %collective-permute-start.13 = (f32[33,512]{1,0:T(8,128)S(1)}, f32[33,512]{1,0:T(8,128)S(1)}, u32[]{:S(2)}, u32[]{:S(2)}) collective-permute-start(f32[33,512]{1,0:T(8,128)S(1)} %dynamic-update-slice.13), channel_id=1, source_target_pairs={{0,24},{1,25},{2,26},{3,27},{4,28},{5,29},{6,30},{7,31}} | collective-permute-start | bytes 202760 | tf_op jit(solution)/shard_map/ppermute | solution.py:252
  124.5 3.0 %collective-permute-start.16 = (f32[4]{0:T(128)S(1)}, f32[4]{0:T(128)S(1)}, u32[]{:S(2)}, u32[]{:S(2)}) collective-permute-start(f32[4]{0:T(128)S(1)} %slice_bitcast_fusion.3), channel_id=1, source_target_pairs={{24,25},{25,24},{26,27},{27,26},{28,29},{29,28},{30,31},{31,30}} | collective-permute-start | bytes 56 | tf_op jit(solution)/shard_map/ppermute | solution.py:123
  127.5 5.4 %collective-permute-start.17 = (f32[4]{0:T(128)S(1)}, f32[4]{0:T(128)S(1)}, u32[]{:S(2)}, u32[]{:S(2)}) collective-permute-start(f32[4]{0:T(128)S(1)} %fusion.115), channel_id=1, source_target_pairs={{24,26},{25,27},{26,24},{27,25},{28,30},{29,31},{30,28},{31,29}} | collective-permute-start | bytes 56 | tf_op jit(solution)/shard_map/ppermute | solution.py:123
  133.0 5.4 %collective-permute-start.18 = (f32[4]{0:T(128)S(1)}, f32[4]{0:T(128)S(1)}, u32[]{:S(2)}, u32[]{:S(2)}) collective-permute-start(f32[4]{0:T(128)S(1)} %add.637), channel_id=1, source_target_pairs={{24,28},{25,29},{26,30},{27,31},{28,24},{29,25},{30,26},{31,27}} | collective-permute-start | bytes 56 | tf_op jit(solution)/shard_map/ppermute | solution.py:123
  (46 other events, 105.1 us)

commit v9 on v7

--- a/solution.py
+++ b/solution.py
@@ -4,6 +4,7 @@
 from jax.sharding import PartitionSpec as P
 
 SWEEPS = 4
+CAP = 4
 RELAX = 0.5
 PENALTY = 3.0
 HALO = SWEEPS
@@ -145,6 +146,11 @@
     own_live = own * live
     onehot = (block_row[None, :] == jnp.arange(slab_rows)[:, None]).astype(jnp.float32) * own[:, 0][None, :]
     pick = (block_row[:, None] == jnp.arange(slab_rows)[None, :]).astype(jnp.float32)
+    owned = (owner[:, 0] == side_id).astype(jnp.int32)
+    rank = jnp.cumsum(owned) - 1
+    slot_hit = (owned[None, :] == 1) & (rank[None, :] == jnp.arange(CAP)[:, None])
+    slot_of = slot_hit.astype(jnp.float32)
+    slot_patch = jnp.sum(slot_hit.astype(jnp.int32) * jnp.arange(owned.shape[0])[None, :], axis=1)
 
     deep_planes = planes - BAND
     disp_zero = own_live * disp_init
@@ -187,7 +193,14 @@
         band = band_solve(init_band, rhs, coef_band, row_ok)
         traction = PENALTY * jnp.sum(pick[:, :, None] * band[:, 0, :][None], axis=1)
         loaded = live * (shell_load - traction)
-        tilde = own_live * jnp.sum(compliance * loaded[:, None, :], axis=-1)
+        picked = jnp.sum(slot_of[:, :, None] * loaded[None], axis=1)
+        products = jnp.stack(
+            [
+                jnp.sum(lax.dynamic_index_in_dim(compliance, slot_patch[k], keepdims=False) * picked[k][None, :], axis=-1)
+                for k in range(CAP)
+            ]
+        )
+        tilde = own_live * jnp.sum(slot_of.T[:, :, None] * products[None], axis=1)
         return tilde, band, extra
 
     tilde_zero, unused, unused_extra = evaluate(disp_zero, plane_zero_rims)

time: 132 us -> 140 us (1.061)
  between operations: 11.3 us -> 19.1 us
    reduce_sum x3 -> x10, other arithmetic: 5.36 us -> 4.34 us  [the longest x3 3.7 us: evaluate(): jnp.sum(lax.dynamic_index_in_dim(compliance, slot_patch[k], keepdims=Fals...]
where the time goes in v9:
time: 140 us; the launch traced here: 139 us
  starting transfers between devices  42.6 us (30%)
  waiting for transfers between devices  33.7 us (24%)
  other arithmetic  26.2 us (19%)
  between operations  19.1 us (14%)
  local copies, waits for them, and re-layouts  16.8 us (12%)
    ppermute x4, starting transfers between devices, exchange(): high = lax.ppermute(down, 'slab', backward)  13.8 us
    ppermute x5, waiting for transfers between devices, allsum_axis(): v = v + lax.ppermute(v, axis, [(i, i ^ step) for i in range(count)])  11.1 us
    ppermute x5, starting transfers between devices, allsum_axis(): v = v + lax.ppermute(v, axis, [(i, i ^ step) for i in range(count)])  10.4 us
    ppermute x4, starting transfers between devices, exchange(): low = lax.ppermute(up, 'slab', forward)  8.16 us
    ppermute x4, waiting for transfers between devices, exchange(): low = lax.ppermute(up, 'slab', forward)  7.44 us
    ppermute x3, waiting for transfers between devices, shell_sum(): v = v + lax.ppermute(v, ('side', 'slab'), pairs)  7.4 us
    unnamed x45, local copies, waits for them, and re-layouts  7.31 us
    ppermute x3, starting transfers between devices, shell_sum(): v = v + lax.ppermute(v, ('side', 'slab'), pairs)  6.44 us
  transfers between devices with their start and end apart: 19, of which 13 were waited for; matrix products, arithmetic and copies ran while one was open for 12% of the time, Pallas kernels for 0%

profile of v9, /device:TPU:28, one launch (start us, length us, event | category | flops | bytes accessed | tf_op | source)
XLA Modules:
  0.0 138.6 jit_solution(1616400127421305807)
XLA Ops:
  3.0 1.8 %copy.57 = f32[1,8,64,512]{3,1,2,0:T(8,128)S(1)} copy(f32[1,8,64,512]{3,2,1,0:T(8,128)} %param.20) | data formatting | bytes 2097152 | tf_op args[1]
  7.3 2.8 %collective-permute-start.1 = (f32[100,512]{1,0:T(8,128)S(1)}, f32[100,512]{1,0:T(8,128)S(1)}, u32[]{:S(2)}, u32[]{:S(2)}) collective-permute-start(f32[100,512]{1,0:T(8,128)S(1)} %pad_maximum_fusion.13), channel_id=1, source_target_pairs={{1,0},{2,1},{3,2},{4,3},{5,4},{6,5},{7,6},{9,8},{10,9},{11,10},{12... | collective-permute-start | bytes 614408 | tf_op jit(solution)/shard_map/ppermute | solution.py:64
  10.2 1.9 %collective-permute-start = (f32[100,512]{1,0:T(8,128)S(1)}, f32[100,512]{1,0:T(8,128)S(1)}, u32[]{:S(2)}, u32[]{:S(2)}) collective-permute-start(f32[100,512]{1,0:T(8,128)S(1)} %pad_maximum_fusion.12), channel_id=1, source_target_pairs={{0,1},{1,2},{2,3},{3,4},{4,5},{5,6},{6,7},{8,9},{9,10},{10,11},{11... | collective-permute-start | bytes 614408 | tf_op jit(solution)/shard_map/ppermute | solution.py:63
  14.3 4.5 %collective-permute-start.3 = (f32[224,512]{1,0:T(8,128)}, f32[224,512]{1,0:T(8,128)}, u32[]{:S(2)}, u32[]{:S(2)}) collective-permute-start(f32[224,512]{1,0:T(8,128)} %pad_maximum_fusion.6), channel_id=1, source_target_pairs={{1,0},{2,1},{3,2},{4,3},{5,4},{6,5},{7,6},{9,8},{10,9},{11,10},{12... | collective-permute-start | bytes 1376264 | tf_op jit(solution)/shard_map/ppermute | solution.py:64
  19.7 1.9 %collective-permute-start.2 = (f32[224,512]{1,0:T(8,128)}, f32[224,512]{1,0:T(8,128)}, u32[]{:S(2)}, u32[]{:S(2)}) collective-permute-start(f32[224,512]{1,0:T(8,128)} %pad_maximum_fusion.5), channel_id=1, source_target_pairs={{0,1},{1,2},{2,3},{3,4},{4,5},{5,6},{6,7},{8,9},{9,10},{10,11},{11... | collective-permute-start | bytes 1376264 | tf_op jit(solution)/shard_map/ppermute | solution.py:63
  36.2 4.5 %collective-permute-start.5 = (f32[4,512]{1,0:T(4,128)S(1)}, f32[4,512]{1,0:T(4,128)S(1)}, u32[]{:S(2)}, u32[]{:S(2)}) collective-permute-start(f32[4,512]{1,0:T(4,128)S(1)} %get-tuple-element.191), channel_id=1, source_target_pairs={{1,0},{2,1},{3,2},{4,3},{5,4},{6,5},{7,6},{9,8},{10,9},{11,10},{12... | collective-permute-start | bytes 24584 | tf_op jit(solution)/shard_map/ppermute | solution.py:64
  40.8 1.9 %collective-permute-start.4 = (f32[4,512]{1,0:T(4,128)S(1)}, f32[4,512]{1,0:T(4,128)S(1)}, u32[]{:S(2)}, u32[]{:S(2)}) collective-permute-start(f32[4,512]{1,0:T(4,128)S(1)} %get-tuple-element.190), channel_id=1, source_target_pairs={{0,1},{1,2},{2,3},{3,4},{4,5},{5,6},{6,7},{8,9},{9,10},{10,11},{11... | collective-permute-start | bytes 24584 | tf_op jit(solution)/shard_map/ppermute | solution.py:63
  42.8 3.8 %collective-permute-done.4 = f32[4,512]{1,0:T(4,128)S(1)} collective-permute-done((f32[4,512]{1,0:T(4,128)S(1)}, f32[4,512]{1,0:T(4,128)S(1)}, u32[]{:S(2)}, u32[]{:S(2)}) %collective-permute-start.4) | collective-permute-done | bytes 8224 | tf_op jit(solution)/shard_map/ppermute | solution.py:63
  52.2 1.4 pad_maximum_fusion.18
  55.3 2.4 %pad_maximum_fusion.1 = (f32[10,64,512]{2,0,1:T(8,128)}, f32[10,64,512]{2,0,1:T(8,128)}) fusion(f32[10,56,512]{2,0,1:T(8,128)S(1)} %get-tuple-element.150, f32[10,8,512]{2,0,1:T(8,128)S(1)} %get-tuple-element.158, f32[10,56,512]{2,0,1:T(8,128)S(1)} %get-tuple-element.149, f32[10,8,512]{2,0,1:T(8,128)S(1)} %get-tuple-element.157), kind=kLoop, calls=%fused_computation.30 | loop fusion | flops 655360 | bytes 5242880 | tf_op jit(solution)/shard_map/concatenate | solution.py:176
  57.9 1.4 fusion.157
  59.3 3.5 %collective-permute-done.7 = f32[2]{0:T(128)S(1)} collective-permute-done((f32[2]{0:T(128)S(1)}, f32[2]{0:T(128)S(1)}, u32[]{:S(2)}, u32[]{:S(2)}) %collective-permute-start.7) | collective-permute-done | bytes 40 | tf_op jit(solution)/shard_map/ppermute | solution.py:112
  62.8 1.4 fusion.158
  64.2 3.5 %collective-permute-done.8 = f32[2]{0:T(128)S(1)} collective-permute-done((f32[2]{0:T(128)S(1)}, f32[2]{0:T(128)S(1)}, u32[]{:S(2)}, u32[]{:S(2)}) %collective-permute-start.8) | collective-permute-done | bytes 40 | tf_op jit(solution)/shard_map/ppermute | solution.py:112
  67.7 8.5 %collective-permute-start.9 = (f32[2]{0:T(128)S(1)}, f32[2]{0:T(128)S(1)}, u32[]{:S(2)}, u32[]{:S(2)}) collective-permute-start(f32[2]{0:T(128)S(1)} %add.604), channel_id=1, source_target_pairs={{0,8},{8,0},{16,24},{24,16},{1,9},{9,1},{17,25},{25,17},{2,10},{10... | collective-permute-start | bytes 32 | tf_op jit(solution)/shard_map/ppermute | solution.py:112
  76.2 1.5 %collective-permute-done.9 = f32[2]{0:T(128)S(1)} collective-permute-done((f32[2]{0:T(128)S(1)}, f32[2]{0:T(128)S(1)}, u32[]{:S(2)}, u32[]{:S(2)}) %collective-permute-start.9) | collective-permute-done | bytes 40 | tf_op jit(solution)/shard_map/ppermute | solution.py:112
  77.7 1.9 %collective-permute-start.10 = (f32[2]{0:T(128)S(1)}, f32[2]{0:T(128)S(1)}, u32[]{:S(2)}, u32[]{:S(2)}) collective-permute-start(f32[2]{0:T(128)S(1)} %add.605), channel_id=1, source_target_pairs={{0,16},{8,24},{16,0},{24,8},{1,17},{9,25},{17,1},{25,9},{2,18},{10... | collective-permute-start | bytes 32 | tf_op jit(solution)/shard_map/ppermute | solution.py:112
  79.6 2.5 %collective-permute-done.10 = f32[2]{0:T(128)S(1)} collective-permute-done((f32[2]{0:T(128)S(1)}, f32[2]{0:T(128)S(1)}, u32[]{:S(2)}, u32[]{:S(2)}) %collective-permute-start.10) | collective-permute-done | bytes 40 | tf_op jit(solution)/shard_map/ppermute | solution.py:112
  85.0 1.9 %collective-permute-start.12 = (f32[132,512]{1,0:T(8,128)S(1)}, f32[132,512]{1,0:T(8,128)S(1)}, u32[]{:S(2)}, u32[]{:S(2)}) collective-permute-start(f32[132,512]{1,0:T(8,128)S(1)} %pad_maximum_fusion.9), channel_id=1, source_target_pairs={{1,0},{2,1},{3,2},{4,3},{5,4},{6,5},{7,6},{9,8},{10,9},{11,10},{12... | collective-permute-start | bytes 811016 | tf_op jit(solution)/shard_map/ppermute | solution.py:64
  86.9 2.4 %collective-permute-start.11 = (f32[132,512]{1,0:T(8,128)S(1)}, f32[132,512]{1,0:T(8,128)S(1)}, u32[]{:S(2)}, u32[]{:S(2)}) collective-permute-start(f32[132,512]{1,0:T(8,128)S(1)} %pad_maximum_fusion.8), channel_id=1, source_target_pairs={{0,1},{1,2},{2,3},{3,4},{4,5},{5,6},{6,7},{8,9},{9,10},{10,11},{11... | collective-permute-start | bytes 811016 | tf_op jit(solution)/shard_map/ppermute | solution.py:63
  89.4 2.7 %collective-permute-done.12 = f32[132,512]{1,0:T(8,128)S(1)} collective-permute-done((f32[132,512]{1,0:T(8,128)S(1)}, f32[132,512]{1,0:T(8,128)S(1)}, u32[]{:S(2)}, u32[]{:S(2)}) %collective-permute-start.12) | collective-permute-done | bytes 270368 | tf_op jit(solution)/shard_map/ppermute | solution.py:64
  92.1 3.6 %collective-permute-done.11 = f32[132,512]{1,0:T(8,128)S(1)} collective-permute-done((f32[132,512]{1,0:T(8,128)S(1)}, f32[132,512]{1,0:T(8,128)S(1)}, u32[]{:S(2)}, u32[]{:S(2)}) %collective-permute-start.11) | collective-permute-done | bytes 270368 | tf_op jit(solution)/shard_map/ppermute | solution.py:63
  98.5 3.0 %fusion.29 = (f32[512]{0:T(512)S(1)}, f32[512]{0:T(512)S(1)}, f32[512]{0:T(512)S(1)}, f32[512]{0:T(512)S(1)}) fusion(f32[8,512,512]{2,1,0:T(8,128)} %param.22, s32[]{:T(128)S(6)} %select_n.144, f32[512]{0:T(512)S(1)} %bitcast.183, f32[512]{0:T(512)S(1)} %bitcast.182, s32[]{:T(128)S(6)} %select_n.149, f32[512]{0:T(512)S(1)} %bitcast.181, s32[]{:T(128)S(6)} %select_n.150, ...), kind=kLoop, calls=%fused_computation.57 | loop fusion | flops 2095104 | bytes 4210704 | tf_op jit(solution)/shard_map/reduce_sum | solution.py:199
  102.4 2.5 %fusion.109 = f32[1,512]{1,0:T(1,128)S(1)} fusion(f32[]{:T(128)} %get-tuple-element.114, f32[]{:T(128)} %get-tuple-element.115, f32[]{:T(128)} %get-tuple-element.113, f32[]{:T(128)} %get-tuple-element.112), kind=kLoop, calls=%fused_computation.235 | loop fusion | flops 5632 | bytes 2064 | tf_op jit(solution)/shard_map/add | solution.py:246
  105.0 1.3 collective-permute-start.15
  111.8 2.2 %collective-permute-done.14 = f32[33,512]{1,0:T(8,128)S(1)} collective-permute-done((f32[33,512]{1,0:T(8,128)S(1)}, f32[33,512]{1,0:T(8,128)S(1)}, u32[]{:S(2)}, u32[]{:S(2)}) %collective-permute-start.14) | collective-permute-done | bytes 67616 | tf_op jit(solution)/shard_map/ppermute | solution.py:254
  114.0 1.7 %collective-permute-done.13 = f32[33,512]{1,0:T(8,128)S(1)} collective-permute-done((f32[33,512]{1,0:T(8,128)S(1)}, f32[33,512]{1,0:T(8,128)S(1)}, u32[]{:S(2)}, u32[]{:S(2)}) %collective-permute-start.13) | collective-permute-done | bytes 67616 | tf_op jit(solution)/shard_map/ppermute | solution.py:254
  115.7 1.9 %collective-permute-start.16 = (f32[4]{0:T(128)S(1)}, f32[4]{0:T(128)S(1)}, u32[]{:S(2)}, u32[]{:S(2)}) collective-permute-start(f32[4]{0:T(128)S(1)} %slice_bitcast_fusion.1), channel_id=1, source_target_pairs={{24,25},{25,24},{26,27},{27,26},{28,29},{29,28},{30,31},{31,30}} | collective-permute-start | bytes 56 | tf_op jit(solution)/shard_map/ppermute | solution.py:123
  118.8 2.6 %collective-permute-start.17 = (f32[4]{0:T(128)S(1)}, f32[4]{0:T(128)S(1)}, u32[]{:S(2)}, u32[]{:S(2)}) collective-permute-start(f32[4]{0:T(128)S(1)} %fusion.115), channel_id=1, source_target_pairs={{24,26},{25,27},{26,24},{27,25},{28,30},{29,31},{30,28},{31,29}} | collective-permute-start | bytes 56 | tf_op jit(solution)/shard_map/ppermute | solution.py:123
  121.4 2.8 %collective-permute-done.17 = f32[4]{0:T(128)S(1)} collective-permute-done((f32[4]{0:T(128)S(1)}, f32[4]{0:T(128)S(1)}, u32[]{:S(2)}, u32[]{:S(2)}) %collective-permute-start.17) | collective-permute-done | bytes 48 | tf_op jit(solution)/shard_map/ppermute | solution.py:123
  124.2 1.9 %collective-permute-start.18 = (f32[4]{0:T(128)S(1)}, f32[4]{0:T(128)S(1)}, u32[]{:S(2)}, u32[]{:S(2)}) collective-permute-start(f32[4]{0:T(128)S(1)} %add.637), channel_id=1, source_target_pairs={{24,28},{25,29},{26,30},{27,31},{28,24},{29,25},{30,26},{31,27}} | collective-permute-start | bytes 56 | tf_op jit(solution)/shard_map/ppermute | solution.py:123
  126.1 3.5 %collective-permute-done.18 = f32[4]{0:T(128)S(1)} collective-permute-done((f32[4]{0:T(128)S(1)}, f32[4]{0:T(128)S(1)}, u32[]{:S(2)}, u32[]{:S(2)}) %collective-permute-start.18) | collective-permute-done | bytes 48 | tf_op jit(solution)/shard_map/ppermute | solution.py:123
  (208 shorter events, 34.4 us)
Async XLA Ops:
  0.6 4.2 %copy-start.6 = (f32[1,8,64,512]{3,2,1,0:T(8,128)S(1)}, f32[1,8,64,512]{3,2,1,0:T(8,128)}, u32[]{:S(2)}) copy-start(f32[1,8,64,512]{3,2,1,0:T(8,128)} %param.19) | copy-start | bytes 3145732
  4.8 28.6 %copy-start.4 = (f32[1,8,64,512]{3,1,2,0:T(8,128)}, f32[1,8,64,512]{3,1,2,0:T(8,128)S(1)}, u32[]{:S(2)}) copy-start(f32[1,8,64,512]{3,1,2,0:T(8,128)S(1)} %copy.57) | copy-start | bytes 3145732
  4.8 1.6 %copy-start.7 = (f32[1,8,64,512]{3,2,1,0:T(8,128)S(1)}, f32[1,8,64,512]{3,2,1,0:T(8,128)}, u32[]{:S(2)}) copy-start(f32[1,8,64,512]{3,2,1,0:T(8,128)} %param.21) | copy-start | bytes 3145732
  7.3 24.3 %collective-permute-start.1 = (f32[100,512]{1,0:T(8,128)S(1)}, f32[100,512]{1,0:T(8,128)S(1)}, u32[]{:S(2)}, u32[]{:S(2)}) collective-permute-start(f32[100,512]{1,0:T(8,128)S(1)} %pad_maximum_fusion.13), channel_id=1, source_target_pairs={{1,0},{2,1},{3,2},{4,3},{5,4},{6,5},{7,6},{9,8},{10,9},{11,10},{12... | collective-permute-start | bytes 614408 | tf_op jit(solution)/shard_map/ppermute | solution.py:64
  10.2 21.6 %collective-permute-start = (f32[100,512]{1,0:T(8,128)S(1)}, f32[100,512]{1,0:T(8,128)S(1)}, u32[]{:S(2)}, u32[]{:S(2)}) collective-permute-start(f32[100,512]{1,0:T(8,128)S(1)} %pad_maximum_fusion.12), channel_id=1, source_target_pairs={{0,1},{1,2},{2,3},{3,4},{4,5},{5,6},{6,7},{8,9},{9,10},{10,11},{11... | collective-permute-start | bytes 614408 | tf_op jit(solution)/shard_map/ppermute | solution.py:63
  13.5 10.7 %copy-start.15 = (s32[8]{0:T(128)S(1)}, s32[8]{0:T(128)}, u32[]{:S(2)}) copy-start(s32[8]{0:T(128)} %param.27) | copy-start | bytes 100
  14.3 34.2 %collective-permute-start.3 = (f32[224,512]{1,0:T(8,128)}, f32[224,512]{1,0:T(8,128)}, u32[]{:S(2)}, u32[]{:S(2)}) collective-permute-start(f32[224,512]{1,0:T(8,128)} %pad_maximum_fusion.6), channel_id=1, source_target_pairs={{1,0},{2,1},{3,2},{4,3},{5,4},{6,5},{7,6},{9,8},{10,9},{11,10},{12... | collective-permute-start | bytes 1376264 | tf_op jit(solution)/shard_map/ppermute | solution.py:64
  19.7 30.1 %collective-permute-start.2 = (f32[224,512]{1,0:T(8,128)}, f32[224,512]{1,0:T(8,128)}, u32[]{:S(2)}, u32[]{:S(2)}) collective-permute-start(f32[224,512]{1,0:T(8,128)} %pad_maximum_fusion.5), channel_id=1, source_target_pairs={{0,1},{1,2},{2,3},{3,4},{4,5},{5,6},{6,7},{8,9},{9,10},{10,11},{11... | collective-permute-start | bytes 1376264 | tf_op jit(solution)/shard_map/ppermute | solution.py:63
  31.6 3.1 %slice-start = ((s8[8388608]{0:T(1024)(128)(4,1)}), s8[4194304]{0:T(1024)(128)(4,1)S(1)}, s32[]{:S(2)}) async-start(s8[8388608]{0:T(1024)(128)(4,1)} %bitcast.154), calls=%async_computation | async-start | bytes 8388608
  32.4 2.9 %slice-start.1 = ((s8[8388608]{0:T(1024)(128)(4,1)}), s8[4194304]{0:T(1024)(128)(4,1)S(1)}, s32[]{:S(2)}) async-start(s8[8388608]{0:T(1024)(128)(4,1)} %bitcast.154), calls=%async_computation.1 | async-start | bytes 8388608
  33.1 1.4 %copy-start.12 = (f32[8,512]{1,0:T(8,128)S(1)}, f32[8,512]{1,0:T(8,128)}, u32[]{:S(2)}) copy-start(f32[8,512]{1,0:T(8,128)} %param.23) | copy-start | bytes 49156
  36.2 6.6 %collective-permute-start.5 = (f32[4,512]{1,0:T(4,128)S(1)}, f32[4,512]{1,0:T(4,128)S(1)}, u32[]{:S(2)}, u32[]{:S(2)}) collective-permute-start(f32[4,512]{1,0:T(4,128)S(1)} %get-tuple-element.191), channel_id=1, source_target_pairs={{1,0},{2,1},{3,2},{4,3},{5,4},{6,5},{7,6},{9,8},{10,9},{11,10},{12... | collective-permute-start | bytes 24584 | tf_op jit(solution)/shard_map/ppermute | solution.py:64
  40.8 5.9 %collective-permute-start.4 = (f32[4,512]{1,0:T(4,128)S(1)}, f32[4,512]{1,0:T(4,128)S(1)}, u32[]{:S(2)}, u32[]{:S(2)}) collective-permute-start(f32[4,512]{1,0:T(4,128)S(1)} %get-tuple-element.190), channel_id=1, source_target_pairs={{0,1},{1,2},{2,3},{3,4},{4,5},{5,6},{6,7},{8,9},{9,10},{10,11},{11... | collective-permute-start | bytes 24584 | tf_op jit(solution)/shard_map/ppermute | solution.py:63
  48.5 2.6 %copy-start.5 = (f32[8,56,512]{2,0,1:T(8,128)S(1)}, f32[8,56,512]{2,0,1:T(8,128)}, u32[]{:S(2)}) copy-start(f32[8,56,512]{2,0,1:T(8,128)} %slice.911) | copy-start | bytes 2752516
  51.1 2.8 %copy-start.3 = (f32[8,56,512]{2,0,1:T(8,128)S(1)}, f32[8,56,512]{2,0,1:T(8,128)}, u32[]{:S(2)}) copy-start(f32[8,56,512]{2,0,1:T(8,128)} %copy-done.2) | copy-start | bytes 2752516
  51.5 2.4 %copy-start.1 = (f32[8,56,512]{2,0,1:T(8,128)S(1)}, f32[8,56,512]{2,0,1:T(8,128)}, u32[]{:S(2)}) copy-start(f32[8,56,512]{2,0,1:T(8,128)} %copy-done) | copy-start | bytes 2752516
  53.5 4.4 %collective-permute-start.6 = (f32[2]{0:T(128)S(1)}, f32[2]{0:T(128)S(1)}, u32[]{:S(2)}, u32[]{:S(2)}) collective-permute-start(f32[2]{0:T(128)S(1)} %pad_maximum_fusion.18), channel_id=1, source_target_pairs={{0,1},{1,0},{2,3},{3,2},{4,5},{5,4},{6,7},{7,6},{8,9},{9,8},{10,11... | collective-permute-start | bytes 32 | tf_op jit(solution)/shard_map/ppermute | solution.py:112
  59.3 3.5 %collective-permute-start.7 = (f32[2]{0:T(128)S(1)}, f32[2]{0:T(128)S(1)}, u32[]{:S(2)}, u32[]{:S(2)}) collective-permute-start(f32[2]{0:T(128)S(1)} %fusion.157), channel_id=1, source_target_pairs={{0,2},{1,3},{2,0},{3,1},{4,6},{5,7},{6,4},{7,5},{8,10},{9,11},{10,... | collective-permute-start | bytes 32 | tf_op jit(solution)/shard_map/ppermute | solution.py:112
  64.2 3.5 %collective-permute-start.8 = (f32[2]{0:T(128)S(1)}, f32[2]{0:T(128)S(1)}, u32[]{:S(2)}, u32[]{:S(2)}) collective-permute-start(f32[2]{0:T(128)S(1)} %fusion.158), channel_id=1, source_target_pairs={{0,4},{1,5},{2,6},{3,7},{4,0},{5,1},{6,2},{7,3},{8,12},{9,13},{10,... | collective-permute-start | bytes 32 | tf_op jit(solution)/shard_map/ppermute | solution.py:112
  67.7 10.0 %collective-permute-start.9 = (f32[2]{0:T(128)S(1)}, f32[2]{0:T(128)S(1)}, u32[]{:S(2)}, u32[]{:S(2)}) collective-permute-start(f32[2]{0:T(128)S(1)} %add.604), channel_id=1, source_target_pairs={{0,8},{8,0},{16,24},{24,16},{1,9},{9,1},{17,25},{25,17},{2,10},{10... | collective-permute-start | bytes 32 | tf_op jit(solution)/shard_map/ppermute | solution.py:112
  77.7 4.4 %collective-permute-start.10 = (f32[2]{0:T(128)S(1)}, f32[2]{0:T(128)S(1)}, u32[]{:S(2)}, u32[]{:S(2)}) collective-permute-start(f32[2]{0:T(128)S(1)} %add.605), channel_id=1, source_target_pairs={{0,16},{8,24},{16,0},{24,8},{1,17},{9,25},{17,1},{25,9},{2,18},{10... | collective-permute-start | bytes 32 | tf_op jit(solution)/shard_map/ppermute | solution.py:112
  85.0 7.1 %collective-permute-start.12 = (f32[132,512]{1,0:T(8,128)S(1)}, f32[132,512]{1,0:T(8,128)S(1)}, u32[]{:S(2)}, u32[]{:S(2)}) collective-permute-start(f32[132,512]{1,0:T(8,128)S(1)} %pad_maximum_fusion.9), channel_id=1, source_target_pairs={{1,0},{2,1},{3,2},{4,3},{5,4},{6,5},{7,6},{9,8},{10,9},{11,10},{12... | collective-permute-start | bytes 811016 | tf_op jit(solution)/shard_map/ppermute | solution.py:64
  86.9 8.8 %collective-permute-start.11 = (f32[132,512]{1,0:T(8,128)S(1)}, f32[132,512]{1,0:T(8,128)S(1)}, u32[]{:S(2)}, u32[]{:S(2)}) collective-permute-start(f32[132,512]{1,0:T(8,128)S(1)} %pad_maximum_fusion.8), channel_id=1, source_target_pairs={{0,1},{1,2},{2,3},{3,4},{4,5},{5,6},{6,7},{8,9},{9,10},{10,11},{11... | collective-permute-start | bytes 811016 | tf_op jit(solution)/shard_map/ppermute | solution.py:63
  92.1 3.6 %copy-start.8 = (f32[132,512]{1,0:T(8,128)}, f32[132,512]{1,0:T(8,128)S(1)}, u32[]{:S(2)}) copy-start(f32[132,512]{1,0:T(8,128)S(1)} %collective-permute-done.12) | copy-start | bytes 811012
  98.5 10.4 %copy-start.9 = (f32[132,512]{1,0:T(8,128)S(1)}, f32[132,512]{1,0:T(8,128)}, u32[]{:S(2)}) copy-start(f32[132,512]{1,0:T(8,128)} %copy-done.8) | copy-start | bytes 811012
  98.5 10.4 %copy-start.11 = (f32[132,512]{1,0:T(8,128)S(1)}, f32[132,512]{1,0:T(8,128)}, u32[]{:S(2)}) copy-start(f32[132,512]{1,0:T(8,128)} %copy-done.10) | copy-start | bytes 811012
  105.0 6.8 %collective-permute-start.15 = (f32[33,512]{1,0:T(8,128)S(1)}, f32[33,512]{1,0:T(8,128)S(1)}, u32[]{:S(2)}, u32[]{:S(2)}) collective-permute-start(f32[33,512]{1,0:T(8,128)S(1)} %dynamic-update-slice.13), channel_id=1, source_target_pairs={{16,24},{17,25},{18,26},{19,27},{20,28},{21,29},{22,30},{23,31}} | collective-permute-start | bytes 202760 | tf_op jit(solution)/shard_map/ppermute | solution.py:254
  106.3 7.7 %collective-permute-start.14 = (f32[33,512]{1,0:T(8,128)S(1)}, f32[33,512]{1,0:T(8,128)S(1)}, u32[]{:S(2)}, u32[]{:S(2)}) collective-permute-start(f32[33,512]{1,0:T(8,128)S(1)} %dynamic-update-slice.13), channel_id=1, source_target_pairs={{8,24},{9,25},{10,26},{11,27},{12,28},{13,29},{14,30},{15,31}} | collective-permute-start | bytes 202760 | tf_op jit(solution)/shard_map/ppermute | solution.py:254
  107.6 8.1 %collective-permute-start.13 = (f32[33,512]{1,0:T(8,128)S(1)}, f32[33,512]{1,0:T(8,128)S(1)}, u32[]{:S(2)}, u32[]{:S(2)}) collective-permute-start(f32[33,512]{1,0:T(8,128)S(1)} %dynamic-update-slice.13), channel_id=1, source_target_pairs={{0,24},{1,25},{2,26},{3,27},{4,28},{5,29},{6,30},{7,31}} | collective-permute-start | bytes 202760 | tf_op jit(solution)/shard_map/ppermute | solution.py:254
  115.7 3.0 %collective-permute-start.16 = (f32[4]{0:T(128)S(1)}, f32[4]{0:T(128)S(1)}, u32[]{:S(2)}, u32[]{:S(2)}) collective-permute-start(f32[4]{0:T(128)S(1)} %slice_bitcast_fusion.1), channel_id=1, source_target_pairs={{24,25},{25,24},{26,27},{27,26},{28,29},{29,28},{30,31},{31,30}} | collective-permute-start | bytes 56 | tf_op jit(solution)/shard_map/ppermute | solution.py:123
  118.8 5.4 %collective-permute-start.17 = (f32[4]{0:T(128)S(1)}, f32[4]{0:T(128)S(1)}, u32[]{:S(2)}, u32[]{:S(2)}) collective-permute-start(f32[4]{0:T(128)S(1)} %fusion.115), channel_id=1, source_target_pairs={{24,26},{25,27},{26,24},{27,25},{28,30},{29,31},{30,28},{31,29}} | collective-permute-start | bytes 56 | tf_op jit(solution)/shard_map/ppermute | solution.py:123
  124.2 5.4 %collective-permute-start.18 = (f32[4]{0:T(128)S(1)}, f32[4]{0:T(128)S(1)}, u32[]{:S(2)}, u32[]{:S(2)}) collective-permute-start(f32[4]{0:T(128)S(1)} %add.637), channel_id=1, source_target_pairs={{24,28},{25,29},{26,30},{27,31},{28,24},{29,25},{30,26},{31,27}} | collective-permute-start | bytes 56 | tf_op jit(solution)/shard_map/ppermute | solution.py:123
  (5 other events, 4.9 us)

commit v10 on v7

--- a/solution.py
+++ b/solution.py
@@ -178,10 +178,12 @@
     ok_one = row_ok[HALO - 1 : HALO + slab_rows + 1]
     ok_two = row_ok[HALO : HALO + slab_rows]
 
+    def plane_of(disp):
+        return jnp.sum(onehot[:, :, None] * (live * disp)[None], axis=1)
+
     def evaluate(disp, plane_rims=None, extra=()):
         if plane_rims is None:
-            plane = jnp.sum(onehot[:, :, None] * (live * disp)[None], axis=1)
-            got = exchange([(plane, HALO)] + list(extra))
+            got = exchange([(plane_of(disp), HALO)] + list(extra))
             plane_rims, extra = got[0], got[1:]
         rhs = force_band.at[:, 0, :].add(plane_rims)
         band = band_solve(init_band, rhs, coef_band, row_ok)
@@ -205,10 +207,24 @@
     resid_one = tilde_one - disp_one
     diff_one = resid_one - resid_zero
     sums = allsum(jnp.stack([jnp.sum(diff_one * diff_one), jnp.sum(diff_one * resid_one)]))
+    step_one = tilde_one - tilde_zero
+    rims_base, rims_step, deep = exchange(
+        [(plane_of(tilde_one), HALO), (plane_of(step_one), HALO), (deep, 2)]
+    )
+    band_base = band_solve(init_band, force_band.at[:, 0, :].add(rims_base), coef_band, row_ok)
+    band_step = band_solve(
+        jnp.zeros_like(init_band), jnp.zeros_like(force_band).at[:, 0, :].set(rims_step), coef_band, row_ok
+    )
+    both = jnp.stack([band_base[:, 0, :], band_step[:, 0, :]])
+    traction = PENALTY * jnp.sum(pick[None, :, :, None] * both[:, None], axis=2)
+    loaded = live[None] * (jnp.stack([shell_load, jnp.zeros_like(shell_load)]) - traction)
+    applied = own_live[None] * jnp.sum(compliance[None] * loaded[:, :, None, :], axis=-1)
+    tilde_base, tilde_step = applied[0], applied[1]
     gram_aa, gram_ab = sums[0], sums[1]
     coeff = -gram_ab / (gram_aa + (0.001 * gram_aa + 1e-06))
-    disp_two = tilde_one + coeff * (tilde_one - tilde_zero)
-    tilde_two, band_two, (deep,) = evaluate(disp_two, extra=[(deep, 2)])
+    disp_two = tilde_one + coeff * step_one
+    tilde_two = tilde_base + coeff * tilde_step
+    band_two = band_base + coeff * band_step
     deep = lax.cond(
         shell_flag,
         lambda: jnp.zeros((slab_rows,) + deep.shape[1:], jnp.float32),

time: 132 us -> 129 us (0.977)
  waiting for transfers between devices: 33.7 us -> 23.9 us
  starting transfers between devices: 42.6 us -> 45.2 us
  other arithmetic: 27.2 us -> 29.5 us
  local copies, waits for them, and re-layouts: 16.1 us -> 17.5 us
    reduce_sum x2 -> x4, other arithmetic: 0.21 us -> 5.03 us  [the longest x1 4.63 us: body(): jnp.sum(compliance[None] * loaded[:, :, None, :], axis=-1)]
    reduce_sum x3 -> x2, other arithmetic: 5.36 us -> 1.29 us  [evaluate(): tilde = own_live * jnp.sum(compliance * loaded[:, None, :], axis=-1)]
    ppermute x4, waiting for transfers between devices: 7.44 us -> 3.84 us  [exchange(): low = lax.ppermute(up, 'slab', forward)]
    ppermute x4, waiting for transfers between devices: 2.75 us -> 0.01 us  [exchange(): high = lax.ppermute(down, 'slab', backward)]
    slice x5, local copies, waits for them, and re-layouts: 1.12 us -> 2.89 us  [exchange(): low[at:at + n].reshape(shape)]
    ppermute x5, waiting for transfers between devices: 11.1 us -> 9.49 us  [allsum_axis(): v = v + lax.ppermute(v, axis, [(i, i ^ step) for i in range(count)])]
    ppermute x5, starting transfers between devices: 10.4 us -> 12 us  [allsum_axis(): v = v + lax.ppermute(v, axis, [(i, i ^ step) for i in range(count)])]
    unnamed x45 -> x41, local copies, waits for them, and re-layouts: 7.27 us -> 6.57 us
  transfers between devices with their start and end apart: 19 -> 19, of which waited for: 13 -> 10; matrix products, arithmetic and copies ran while one was open for 12% -> 17% of each run, Pallas kernels for 0% -> 0%
where the time goes in v10:
time: 129 us; the launch traced here: 128 us
  starting transfers between devices  45.2 us (35%)
  other arithmetic  29.5 us (23%)
  waiting for transfers between devices  23.9 us (19%)
  local copies, waits for them, and re-layouts  17.5 us (14%)
  between operations  11.2 us (9%)
    ppermute x4, starting transfers between devices, exchange(): high = lax.ppermute(down, 'slab', backward)  13.8 us
    ppermute x5, starting transfers between devices, allsum_axis(): v = v + lax.ppermute(v, axis, [(i, i ^ step) for i in range(count)])  12 us
    ppermute x5, waiting for transfers between devices, allsum_axis(): v = v + lax.ppermute(v, axis, [(i, i ^ step) for i in range(count)])  9.49 us
    ppermute x4, starting transfers between devices, exchange(): low = lax.ppermute(up, 'slab', forward)  8.15 us
    ppermute x3, starting transfers between devices, shell_sum(): v = v + lax.ppermute(v, ('side', 'slab'), pairs)  7.42 us
    unnamed x41, local copies, waits for them, and re-layouts  6.57 us
    ppermute x3, waiting for transfers between devices, shell_sum(): v = v + lax.ppermute(v, ('side', 'slab'), pairs)  6.42 us
    reduce_sum x1, other arithmetic, body(): jnp.sum(compliance[None] * loaded[:, :, None, :], axis=-1)  4.63 us
  transfers between devices with their start and end apart: 19, of which 10 were waited for; matrix products, arithmetic and copies ran while one was open for 17% of the time, Pallas kernels for 0%

profile of v10, /device:TPU:28, one launch (start us, length us, event | category | flops | bytes accessed | tf_op | source)
XLA Modules:
  0.0 127.5 jit_solution(1228737194163846012)
XLA Ops:
  3.0 1.8 %copy.89 = f32[1,8,64,512]{3,1,2,0:T(8,128)S(1)} copy(f32[1,8,64,512]{3,2,1,0:T(8,128)} %param.22) | data formatting | bytes 2097152 | tf_op args[1]
  7.3 2.8 %collective-permute-start.1 = (f32[100,512]{1,0:T(8,128)S(1)}, f32[100,512]{1,0:T(8,128)S(1)}, u32[]{:S(2)}, u32[]{:S(2)}) collective-permute-start(f32[100,512]{1,0:T(8,128)S(1)} %pad_maximum_fusion.13), channel_id=1, source_target_pairs={{1,0},{2,1},{3,2},{4,3},{5,4},{6,5},{7,6},{9,8},{10,9},{11,10},{12... | collective-permute-start | bytes 614408 | tf_op jit(solution)/shard_map/ppermute | solution.py:63
  10.2 1.9 %collective-permute-start = (f32[100,512]{1,0:T(8,128)S(1)}, f32[100,512]{1,0:T(8,128)S(1)}, u32[]{:S(2)}, u32[]{:S(2)}) collective-permute-start(f32[100,512]{1,0:T(8,128)S(1)} %pad_maximum_fusion.12), channel_id=1, source_target_pairs={{0,1},{1,2},{2,3},{3,4},{4,5},{5,6},{6,7},{8,9},{9,10},{10,11},{11... | collective-permute-start | bytes 614408 | tf_op jit(solution)/shard_map/ppermute | solution.py:62
  14.3 4.5 %collective-permute-start.3 = (f32[224,512]{1,0:T(8,128)}, f32[224,512]{1,0:T(8,128)}, u32[]{:S(2)}, u32[]{:S(2)}) collective-permute-start(f32[224,512]{1,0:T(8,128)} %pad_maximum_fusion.6), channel_id=1, source_target_pairs={{1,0},{2,1},{3,2},{4,3},{5,4},{6,5},{7,6},{9,8},{10,9},{11,10},{12... | collective-permute-start | bytes 1376264 | tf_op jit(solution)/shard_map/ppermute | solution.py:63
  19.8 1.9 %collective-permute-start.2 = (f32[224,512]{1,0:T(8,128)}, f32[224,512]{1,0:T(8,128)}, u32[]{:S(2)}, u32[]{:S(2)}) collective-permute-start(f32[224,512]{1,0:T(8,128)} %pad_maximum_fusion.5), channel_id=1, source_target_pairs={{0,1},{1,2},{2,3},{3,4},{4,5},{5,6},{6,7},{8,9},{9,10},{10,11},{11... | collective-permute-start | bytes 1376264 | tf_op jit(solution)/shard_map/ppermute | solution.py:62
  27.8 4.5 %collective-permute-start.5 = (f32[4,512]{1,0:T(4,128)S(1)}, f32[4,512]{1,0:T(4,128)S(1)}, u32[]{:S(2)}, u32[]{:S(2)}) collective-permute-start(f32[4,512]{1,0:T(4,128)S(1)} %get-tuple-element.243), channel_id=1, source_target_pairs={{1,0},{2,1},{3,2},{4,3},{5,4},{6,5},{7,6},{9,8},{10,9},{11,10},{12... | collective-permute-start | bytes 24584 | tf_op jit(solution)/shard_map/ppermute | solution.py:63
  32.3 1.9 %collective-permute-start.4 = (f32[4,512]{1,0:T(4,128)S(1)}, f32[4,512]{1,0:T(4,128)S(1)}, u32[]{:S(2)}, u32[]{:S(2)}) collective-permute-start(f32[4,512]{1,0:T(4,128)S(1)} %get-tuple-element.242), channel_id=1, source_target_pairs={{0,1},{1,2},{2,3},{3,4},{4,5},{5,6},{6,7},{8,9},{9,10},{10,11},{11... | collective-permute-start | bytes 24584 | tf_op jit(solution)/shard_map/ppermute | solution.py:62
  34.4 3.8 %collective-permute-done.4 = f32[4,512]{1,0:T(4,128)S(1)} collective-permute-done((f32[4,512]{1,0:T(4,128)S(1)}, f32[4,512]{1,0:T(4,128)S(1)}, u32[]{:S(2)}, u32[]{:S(2)}) %collective-permute-start.4) | collective-permute-done | bytes 8224 | tf_op jit(solution)/shard_map/ppermute | solution.py:62
  43.8 1.4 %pad_maximum_fusion.16 = f32[2]{0:T(128)S(1)} fusion(f32[1]{0:T(128)} %bitcast.33, f32[1]{0:T(128)} %bitcast.32), kind=kLoop, calls=%fused_computation.250 | loop fusion | flops 2 | bytes 16 | tf_op jit(solution)/shard_map/stack | solution.py:209
  47.2 2.5 %pad_maximum_fusion.1 = (f32[10,64,512]{2,0,1:T(8,128)}, f32[10,64,512]{2,0,1:T(8,128)}) fusion(f32[10,56,512]{2,0,1:T(8,128)S(1)} %get-tuple-element.184, f32[10,8,512]{2,0,1:T(8,128)S(1)} %get-tuple-element.196, f32[10,56,512]{2,0,1:T(8,128)S(1)} %get-tuple-element.183, f32[10,8,512]{2,0,1:T(8,128)S(1)} %get-tuple-element.195), kind=kLoop, calls=%fused_computation.33 | loop fusion | flops 655360 | bytes 5242880 | tf_op jit(solution)/shard_map/concatenate | solution.py:170
  50.6 1.9 %collective-permute-start.7 = (f32[136,512]{1,0:T(8,128)}, f32[136,512]{1,0:T(8,128)S(1)}, u32[]{:S(2)}, u32[]{:S(2)}) collective-permute-start(f32[136,512]{1,0:T(8,128)} %pad_maximum_fusion.9), channel_id=1, source_target_pairs={{1,0},{2,1},{3,2},{4,3},{5,4},{6,5},{7,6},{9,8},{10,9},{11,10},{12... | collective-permute-start | bytes 835592 | tf_op jit(solution)/shard_map/ppermute | solution.py:63
  53.3 2.4 %collective-permute-start.6 = (f32[136,512]{1,0:T(8,128)}, f32[136,512]{1,0:T(8,128)}, u32[]{:S(2)}, u32[]{:S(2)}) collective-permute-start(f32[136,512]{1,0:T(8,128)} %pad_maximum_fusion.8), channel_id=1, source_target_pairs={{0,1},{1,2},{2,3},{3,4},{4,5},{5,6},{6,7},{8,9},{9,10},{10,11},{11... | collective-permute-start | bytes 835592 | tf_op jit(solution)/shard_map/ppermute | solution.py:62
  55.7 1.4 %fusion.168 = f32[2]{0:T(128)S(1)} fusion(f32[2]{0:T(128)S(1)} %collective-permute-done.8, f32[1]{0:T(128)} %bitcast.33, f32[1]{0:T(128)} %bitcast.32), kind=kLoop, calls=%fused_computation.291 | loop fusion | flops 4 | bytes 24 | tf_op jit(solution)/shard_map/add | solution.py:111
  57.1 1.6 %collective-permute-start.9 = (f32[2]{0:T(128)S(1)}, f32[2]{0:T(128)S(1)}, u32[]{:S(2)}, u32[]{:S(2)}) collective-permute-start(f32[2]{0:T(128)S(1)} %fusion.168), channel_id=1, source_target_pairs={{0,2},{1,3},{2,0},{3,1},{4,6},{5,7},{6,4},{7,5},{8,10},{9,11},{10,... | collective-permute-start | bytes 32 | tf_op jit(solution)/shard_map/ppermute | solution.py:111
  58.7 1.9 %collective-permute-done.9 = f32[2]{0:T(128)S(1)} collective-permute-done((f32[2]{0:T(128)S(1)}, f32[2]{0:T(128)S(1)}, u32[]{:S(2)}, u32[]{:S(2)}) %collective-permute-start.9) | collective-permute-done | bytes 40 | tf_op jit(solution)/shard_map/ppermute | solution.py:111
  60.6 1.4 %fusion.169 = f32[2]{0:T(128)S(1)} fusion(f32[2]{0:T(128)S(1)} %collective-permute-done.9, f32[2]{0:T(128)S(1)} %collective-permute-done.8, f32[1]{0:T(128)} %bitcast.33, f32[1]{0:T(128)} %bitcast.32), kind=kLoop, calls=%fused_computation.292 | loop fusion | flops 6 | bytes 32 | tf_op jit(solution)/shard_map/add | solution.py:111
  62.0 3.5 %collective-permute-done.10 = f32[2]{0:T(128)S(1)} collective-permute-done((f32[2]{0:T(128)S(1)}, f32[2]{0:T(128)S(1)}, u32[]{:S(2)}, u32[]{:S(2)}) %collective-permute-start.10) | collective-permute-done | bytes 40 | tf_op jit(solution)/shard_map/ppermute | solution.py:111
  65.5 8.4 %collective-permute-start.11 = (f32[2]{0:T(128)S(1)}, f32[2]{0:T(128)S(1)}, u32[]{:S(2)}, u32[]{:S(2)}) collective-permute-start(f32[2]{0:T(128)S(1)} %add.716), channel_id=1, source_target_pairs={{0,8},{8,0},{16,24},{24,16},{1,9},{9,1},{17,25},{25,17},{2,10},{10... | collective-permute-start | bytes 32 | tf_op jit(solution)/shard_map/ppermute | solution.py:111
  73.9 1.5 %collective-permute-done.11 = f32[2]{0:T(128)S(1)} collective-permute-done((f32[2]{0:T(128)S(1)}, f32[2]{0:T(128)S(1)}, u32[]{:S(2)}, u32[]{:S(2)}) %collective-permute-start.11) | collective-permute-done | bytes 40 | tf_op jit(solution)/shard_map/ppermute | solution.py:111
  75.5 1.9 %collective-permute-start.12 = (f32[2]{0:T(128)S(1)}, f32[2]{0:T(128)S(1)}, u32[]{:S(2)}, u32[]{:S(2)}) collective-permute-start(f32[2]{0:T(128)S(1)} %add.717), channel_id=1, source_target_pairs={{0,16},{8,24},{16,0},{24,8},{1,17},{9,25},{17,1},{25,9},{2,18},{10... | collective-permute-start | bytes 32 | tf_op jit(solution)/shard_map/ppermute | solution.py:111
  77.4 2.5 %collective-permute-done.12 = f32[2]{0:T(128)S(1)} collective-permute-done((f32[2]{0:T(128)S(1)}, f32[2]{0:T(128)S(1)}, u32[]{:S(2)}, u32[]{:S(2)}) %collective-permute-start.12) | collective-permute-done | bytes 40 | tf_op jit(solution)/shard_map/ppermute | solution.py:111
  86.1 4.6 %multiply_reduce_fusion = f32[2,8,512]{2,1,0:T(8,128)S(1)} fusion(f32[2,8,512]{2,1,0:T(8,128)S(1)} %subtract_multiply_fusion, f32[8,512,512]{2,1,0:T(8,128)} %param.24), kind=kLoop, calls=%fused_computation.28 | loop fusion | flops 8380416 | bytes 8454144 | tf_op jit(solution)/shard_map/reduce_sum | solution.py:221
  91.5 2.6 %fusion.123 = f32[1,512]{1,0:T(1,128)S(1)} fusion(f32[]{:T(128)} %get-tuple-element.143, f32[]{:T(128)} %get-tuple-element.144, f32[]{:T(128)} %get-tuple-element.142, f32[]{:T(128)} %get-tuple-element.141), kind=kLoop, calls=%fused_computation.245 | loop fusion | flops 5632 | bytes 2064 | tf_op jit(solution)/shard_map/add | solution.py:249
  94.2 1.3 %collective-permute-start.15 = (f32[33,512]{1,0:T(8,128)S(1)}, f32[33,512]{1,0:T(8,128)S(1)}, u32[]{:S(2)}, u32[]{:S(2)}) collective-permute-start(f32[33,512]{1,0:T(8,128)S(1)} %dynamic-update-slice.16), channel_id=1, source_target_pairs={{16,24},{17,25},{18,26},{19,27},{20,28},{21,29},{22,30},{23,31}} | collective-permute-start | bytes 202760 | tf_op jit(solution)/shard_map/ppermute | solution.py:257
  95.5 1.3 %collective-permute-start.14 = (f32[33,512]{1,0:T(8,128)S(1)}, f32[33,512]{1,0:T(8,128)S(1)}, u32[]{:S(2)}, u32[]{:S(2)}) collective-permute-start(f32[33,512]{1,0:T(8,128)S(1)} %dynamic-update-slice.16), channel_id=1, source_target_pairs={{8,24},{9,25},{10,26},{11,27},{12,28},{13,29},{14,30},{15,31}} | collective-permute-start | bytes 202760 | tf_op jit(solution)/shard_map/ppermute | solution.py:257
  100.8 1.9 %collective-permute-done.14 = f32[33,512]{1,0:T(8,128)S(1)} collective-permute-done((f32[33,512]{1,0:T(8,128)S(1)}, f32[33,512]{1,0:T(8,128)S(1)}, u32[]{:S(2)}, u32[]{:S(2)}) %collective-permute-start.14) | collective-permute-done | bytes 67616 | tf_op jit(solution)/shard_map/ppermute | solution.py:257
  102.7 2.2 %collective-permute-done.13 = f32[33,512]{1,0:T(8,128)S(1)} collective-permute-done((f32[33,512]{1,0:T(8,128)S(1)}, f32[33,512]{1,0:T(8,128)S(1)}, u32[]{:S(2)}, u32[]{:S(2)}) %collective-permute-start.13) | collective-permute-done | bytes 67616 | tf_op jit(solution)/shard_map/ppermute | solution.py:257
  105.0 1.9 %collective-permute-start.16 = (f32[4]{0:T(128)S(1)}, f32[4]{0:T(128)S(1)}, u32[]{:S(2)}, u32[]{:S(2)}) collective-permute-start(f32[4]{0:T(128)S(1)} %slice_bitcast_fusion.2), channel_id=1, source_target_pairs={{24,25},{25,24},{26,27},{27,26},{28,29},{29,28},{30,31},{31,30}} | collective-permute-start | bytes 56 | tf_op jit(solution)/shard_map/ppermute | solution.py:122
  108.0 3.6 %collective-permute-start.17 = (f32[4]{0:T(128)S(1)}, f32[4]{0:T(128)S(1)}, u32[]{:S(2)}, u32[]{:S(2)}) collective-permute-start(f32[4]{0:T(128)S(1)} %fusion.125), channel_id=1, source_target_pairs={{24,26},{25,27},{26,24},{27,25},{28,30},{29,31},{30,28},{31,29}} | collective-permute-start | bytes 56 | tf_op jit(solution)/shard_map/ppermute | solution.py:122
  111.6 1.8 %collective-permute-done.17 = f32[4]{0:T(128)S(1)} collective-permute-done((f32[4]{0:T(128)S(1)}, f32[4]{0:T(128)S(1)}, u32[]{:S(2)}, u32[]{:S(2)}) %collective-permute-start.17) | collective-permute-done | bytes 48 | tf_op jit(solution)/shard_map/ppermute | solution.py:122
  113.4 1.9 %collective-permute-start.18 = (f32[4]{0:T(128)S(1)}, f32[4]{0:T(128)S(1)}, u32[]{:S(2)}, u32[]{:S(2)}) collective-permute-start(f32[4]{0:T(128)S(1)} %add.731), channel_id=1, source_target_pairs={{24,28},{25,29},{26,30},{27,31},{28,24},{29,25},{30,26},{31,27}} | collective-permute-start | bytes 56 | tf_op jit(solution)/shard_map/ppermute | solution.py:122
  115.3 3.5 %collective-permute-done.18 = f32[4]{0:T(128)S(1)} collective-permute-done((f32[4]{0:T(128)S(1)}, f32[4]{0:T(128)S(1)}, u32[]{:S(2)}, u32[]{:S(2)}) %collective-permute-start.18) | collective-permute-done | bytes 48 | tf_op jit(solution)/shard_map/ppermute | solution.py:122
  (198 shorter events, 34.3 us)
Async XLA Ops:
  0.6 4.2 %copy-start.6 = (f32[1,8,64,512]{3,2,1,0:T(8,128)S(1)}, f32[1,8,64,512]{3,2,1,0:T(8,128)}, u32[]{:S(2)}) copy-start(f32[1,8,64,512]{3,2,1,0:T(8,128)} %param.21) | copy-start | bytes 3145732
  4.8 20.1 %copy-start.4 = (f32[1,8,64,512]{3,1,2,0:T(8,128)}, f32[1,8,64,512]{3,1,2,0:T(8,128)S(1)}, u32[]{:S(2)}) copy-start(f32[1,8,64,512]{3,1,2,0:T(8,128)S(1)} %copy.89) | copy-start | bytes 3145732
  4.8 1.6 %copy-start.7 = (f32[1,8,64,512]{3,2,1,0:T(8,128)S(1)}, f32[1,8,64,512]{3,2,1,0:T(8,128)}, u32[]{:S(2)}) copy-start(f32[1,8,64,512]{3,2,1,0:T(8,128)} %param.23) | copy-start | bytes 3145732
  7.3 15.9 %collective-permute-start.1 = (f32[100,512]{1,0:T(8,128)S(1)}, f32[100,512]{1,0:T(8,128)S(1)}, u32[]{:S(2)}, u32[]{:S(2)}) collective-permute-start(f32[100,512]{1,0:T(8,128)S(1)} %pad_maximum_fusion.13), channel_id=1, source_target_pairs={{1,0},{2,1},{3,2},{4,3},{5,4},{6,5},{7,6},{9,8},{10,9},{11,10},{12... | collective-permute-start | bytes 614408 | tf_op jit(solution)/shard_map/ppermute | solution.py:63
  10.2 13.2 %collective-permute-start = (f32[100,512]{1,0:T(8,128)S(1)}, f32[100,512]{1,0:T(8,128)S(1)}, u32[]{:S(2)}, u32[]{:S(2)}) collective-permute-start(f32[100,512]{1,0:T(8,128)S(1)} %pad_maximum_fusion.12), channel_id=1, source_target_pairs={{0,1},{1,2},{2,3},{3,4},{4,5},{5,6},{6,7},{8,9},{9,10},{10,11},{11... | collective-permute-start | bytes 614408 | tf_op jit(solution)/shard_map/ppermute | solution.py:62
  12.2 1.2 copy-start.2
  13.5 8.4 %copy-start.13 = (s32[8]{0:T(128)S(1)}, s32[8]{0:T(128)}, u32[]{:S(2)}) copy-start(s32[8]{0:T(128)} %param.29) | copy-start | bytes 100
  14.3 25.8 %collective-permute-start.3 = (f32[224,512]{1,0:T(8,128)}, f32[224,512]{1,0:T(8,128)}, u32[]{:S(2)}, u32[]{:S(2)}) collective-permute-start(f32[224,512]{1,0:T(8,128)} %pad_maximum_fusion.6), channel_id=1, source_target_pairs={{1,0},{2,1},{3,2},{4,3},{5,4},{6,5},{7,6},{9,8},{10,9},{11,10},{12... | collective-permute-start | bytes 1376264 | tf_op jit(solution)/shard_map/ppermute | solution.py:63
  18.9 4.1 %copy-start.12 = (s32[8]{0:T(128)S(1)}, s32[8]{0:T(128)}, u32[]{:S(2)}) copy-start(s32[8]{0:T(128)} %param.27) | copy-start | bytes 100
  19.8 21.7 %collective-permute-start.2 = (f32[224,512]{1,0:T(8,128)}, f32[224,512]{1,0:T(8,128)}, u32[]{:S(2)}, u32[]{:S(2)}) collective-permute-start(f32[224,512]{1,0:T(8,128)} %pad_maximum_fusion.5), channel_id=1, source_target_pairs={{0,1},{1,2},{2,3},{3,4},{4,5},{5,6},{6,7},{8,9},{9,10},{10,11},{11... | collective-permute-start | bytes 1376264 | tf_op jit(solution)/shard_map/ppermute | solution.py:62
  23.2 3.0 %slice-start = ((s8[8388608]{0:T(1024)(128)(4,1)}), s8[4194304]{0:T(1024)(128)(4,1)S(1)}, s32[]{:S(2)}) async-start(s8[8388608]{0:T(1024)(128)(4,1)} %bitcast.95), calls=%async_computation | async-start | bytes 8388608
  24.0 2.9 %slice-start.1 = ((s8[8388608]{0:T(1024)(128)(4,1)}), s8[4194304]{0:T(1024)(128)(4,1)S(1)}, s32[]{:S(2)}) async-start(s8[8388608]{0:T(1024)(128)(4,1)} %bitcast.95), calls=%async_computation.1 | async-start | bytes 8388608
  24.7 1.4 %copy-start.10 = (f32[8,512]{1,0:T(8,128)S(1)}, f32[8,512]{1,0:T(8,128)}, u32[]{:S(2)}) copy-start(f32[8,512]{1,0:T(8,128)} %param.25) | copy-start | bytes 49156
  27.8 6.6 %collective-permute-start.5 = (f32[4,512]{1,0:T(4,128)S(1)}, f32[4,512]{1,0:T(4,128)S(1)}, u32[]{:S(2)}, u32[]{:S(2)}) collective-permute-start(f32[4,512]{1,0:T(4,128)S(1)} %get-tuple-element.243), channel_id=1, source_target_pairs={{1,0},{2,1},{3,2},{4,3},{5,4},{6,5},{7,6},{9,8},{10,9},{11,10},{12... | collective-permute-start | bytes 24584 | tf_op jit(solution)/shard_map/ppermute | solution.py:63
  32.3 5.9 %collective-permute-start.4 = (f32[4,512]{1,0:T(4,128)S(1)}, f32[4,512]{1,0:T(4,128)S(1)}, u32[]{:S(2)}, u32[]{:S(2)}) collective-permute-start(f32[4,512]{1,0:T(4,128)S(1)} %get-tuple-element.242), channel_id=1, source_target_pairs={{0,1},{1,2},{2,3},{3,4},{4,5},{5,6},{6,7},{8,9},{9,10},{10,11},{11... | collective-permute-start | bytes 24584 | tf_op jit(solution)/shard_map/ppermute | solution.py:62
  40.1 2.6 %copy-start.5 = (f32[8,56,512]{2,0,1:T(8,128)S(1)}, f32[8,56,512]{2,0,1:T(8,128)}, u32[]{:S(2)}) copy-start(f32[8,56,512]{2,0,1:T(8,128)} %slice.1016) | copy-start | bytes 2752516
  42.7 2.8 %copy-start.3 = (f32[8,56,512]{2,0,1:T(8,128)S(1)}, f32[8,56,512]{2,0,1:T(8,128)}, u32[]{:S(2)}) copy-start(f32[8,56,512]{2,0,1:T(8,128)} %copy-done.2) | copy-start | bytes 2752516
  43.1 2.4 %copy-start.1 = (f32[8,56,512]{2,0,1:T(8,128)S(1)}, f32[8,56,512]{2,0,1:T(8,128)}, u32[]{:S(2)}) copy-start(f32[8,56,512]{2,0,1:T(8,128)} %copy-done) | copy-start | bytes 2752516
  45.2 10.5 %collective-permute-start.8 = (f32[2]{0:T(128)S(1)}, f32[2]{0:T(128)S(1)}, u32[]{:S(2)}, u32[]{:S(2)}) collective-permute-start(f32[2]{0:T(128)S(1)} %pad_maximum_fusion.16), channel_id=1, source_target_pairs={{0,1},{1,0},{2,3},{3,2},{4,5},{5,4},{6,7},{7,6},{8,9},{9,8},{10,11... | collective-permute-start | bytes 32 | tf_op jit(solution)/shard_map/ppermute | solution.py:111
  50.6 31.9 %collective-permute-start.7 = (f32[136,512]{1,0:T(8,128)}, f32[136,512]{1,0:T(8,128)S(1)}, u32[]{:S(2)}, u32[]{:S(2)}) collective-permute-start(f32[136,512]{1,0:T(8,128)} %pad_maximum_fusion.9), channel_id=1, source_target_pairs={{1,0},{2,1},{3,2},{4,3},{5,4},{6,5},{7,6},{9,8},{10,9},{11,10},{12... | collective-permute-start | bytes 835592 | tf_op jit(solution)/shard_map/ppermute | solution.py:63
  53.3 29.3 %collective-permute-start.6 = (f32[136,512]{1,0:T(8,128)}, f32[136,512]{1,0:T(8,128)}, u32[]{:S(2)}, u32[]{:S(2)}) collective-permute-start(f32[136,512]{1,0:T(8,128)} %pad_maximum_fusion.8), channel_id=1, source_target_pairs={{0,1},{1,2},{2,3},{3,4},{4,5},{5,6},{6,7},{8,9},{9,10},{10,11},{11... | collective-permute-start | bytes 835592 | tf_op jit(solution)/shard_map/ppermute | solution.py:62
  57.1 3.5 %collective-permute-start.9 = (f32[2]{0:T(128)S(1)}, f32[2]{0:T(128)S(1)}, u32[]{:S(2)}, u32[]{:S(2)}) collective-permute-start(f32[2]{0:T(128)S(1)} %fusion.168), channel_id=1, source_target_pairs={{0,2},{1,3},{2,0},{3,1},{4,6},{5,7},{6,4},{7,5},{8,10},{9,11},{10,... | collective-permute-start | bytes 32 | tf_op jit(solution)/shard_map/ppermute | solution.py:111
  62.0 3.5 %collective-permute-start.10 = (f32[2]{0:T(128)S(1)}, f32[2]{0:T(128)S(1)}, u32[]{:S(2)}, u32[]{:S(2)}) collective-permute-start(f32[2]{0:T(128)S(1)} %fusion.169), channel_id=1, source_target_pairs={{0,4},{1,5},{2,6},{3,7},{4,0},{5,1},{6,2},{7,3},{8,12},{9,13},{10,... | collective-permute-start | bytes 32 | tf_op jit(solution)/shard_map/ppermute | solution.py:111
  65.5 9.9 %collective-permute-start.11 = (f32[2]{0:T(128)S(1)}, f32[2]{0:T(128)S(1)}, u32[]{:S(2)}, u32[]{:S(2)}) collective-permute-start(f32[2]{0:T(128)S(1)} %add.716), channel_id=1, source_target_pairs={{0,8},{8,0},{16,24},{24,16},{1,9},{9,1},{17,25},{25,17},{2,10},{10... | collective-permute-start | bytes 32 | tf_op jit(solution)/shard_map/ppermute | solution.py:111
  75.5 4.4 %collective-permute-start.12 = (f32[2]{0:T(128)S(1)}, f32[2]{0:T(128)S(1)}, u32[]{:S(2)}, u32[]{:S(2)}) collective-permute-start(f32[2]{0:T(128)S(1)} %add.717), channel_id=1, source_target_pairs={{0,16},{8,24},{16,0},{24,8},{1,17},{9,25},{17,1},{25,9},{2,18},{10... | collective-permute-start | bytes 32 | tf_op jit(solution)/shard_map/ppermute | solution.py:111
  86.0 12.1 %copy-start.9 = (f32[136,512]{1,0:T(8,128)S(1)}, f32[136,512]{1,0:T(8,128)}, u32[]{:S(2)}) copy-start(f32[136,512]{1,0:T(8,128)} %copy-done.8) | copy-start | bytes 835588
  94.2 6.6 %collective-permute-start.15 = (f32[33,512]{1,0:T(8,128)S(1)}, f32[33,512]{1,0:T(8,128)S(1)}, u32[]{:S(2)}, u32[]{:S(2)}) collective-permute-start(f32[33,512]{1,0:T(8,128)S(1)} %dynamic-update-slice.16), channel_id=1, source_target_pairs={{16,24},{17,25},{18,26},{19,27},{20,28},{21,29},{22,30},{23,31}} | collective-permute-start | bytes 202760 | tf_op jit(solution)/shard_map/ppermute | solution.py:257
  95.5 7.2 %collective-permute-start.14 = (f32[33,512]{1,0:T(8,128)S(1)}, f32[33,512]{1,0:T(8,128)S(1)}, u32[]{:S(2)}, u32[]{:S(2)}) collective-permute-start(f32[33,512]{1,0:T(8,128)S(1)} %dynamic-update-slice.16), channel_id=1, source_target_pairs={{8,24},{9,25},{10,26},{11,27},{12,28},{13,29},{14,30},{15,31}} | collective-permute-start | bytes 202760 | tf_op jit(solution)/shard_map/ppermute | solution.py:257
  96.8 8.1 %collective-permute-start.13 = (f32[33,512]{1,0:T(8,128)S(1)}, f32[33,512]{1,0:T(8,128)S(1)}, u32[]{:S(2)}, u32[]{:S(2)}) collective-permute-start(f32[33,512]{1,0:T(8,128)S(1)} %dynamic-update-slice.16), channel_id=1, source_target_pairs={{0,24},{1,25},{2,26},{3,27},{4,28},{5,29},{6,30},{7,31}} | collective-permute-start | bytes 202760 | tf_op jit(solution)/shard_map/ppermute | solution.py:257
  105.0 3.0 %collective-permute-start.16 = (f32[4]{0:T(128)S(1)}, f32[4]{0:T(128)S(1)}, u32[]{:S(2)}, u32[]{:S(2)}) collective-permute-start(f32[4]{0:T(128)S(1)} %slice_bitcast_fusion.2), channel_id=1, source_target_pairs={{24,25},{25,24},{26,27},{27,26},{28,29},{29,28},{30,31},{31,30}} | collective-permute-start | bytes 56 | tf_op jit(solution)/shard_map/ppermute | solution.py:122
  108.0 5.4 %collective-permute-start.17 = (f32[4]{0:T(128)S(1)}, f32[4]{0:T(128)S(1)}, u32[]{:S(2)}, u32[]{:S(2)}) collective-permute-start(f32[4]{0:T(128)S(1)} %fusion.125), channel_id=1, source_target_pairs={{24,26},{25,27},{26,24},{27,25},{28,30},{29,31},{30,28},{31,29}} | collective-permute-start | bytes 56 | tf_op jit(solution)/shard_map/ppermute | solution.py:122
  113.4 5.4 %collective-permute-start.18 = (f32[4]{0:T(128)S(1)}, f32[4]{0:T(128)S(1)}, u32[]{:S(2)}, u32[]{:S(2)}) collective-permute-start(f32[4]{0:T(128)S(1)} %add.731), channel_id=1, source_target_pairs={{24,28},{25,29},{26,30},{27,31},{28,24},{29,25},{30,26},{31,27}} | collective-permute-start | bytes 56 | tf_op jit(solution)/shard_map/ppermute | solution.py:122
  (3 other events, 2.7 us)

commit v11 on v10

--- a/solution.py
+++ b/solution.py
@@ -155,10 +155,11 @@
             (plane_zero, HALO),
         ]
     )
+    after_band = 0.0 * packed[0, 0, 0]
     init_deep, fc_deep = exchange(
         [
-            (start_here[:, BAND:], 2),
-            (jnp.concatenate([force_here[:, BAND:], coef_here[:, BAND:]], axis=1), 1),
+            (start_here[:, BAND:] + after_band, 2),
+            (jnp.concatenate([force_here[:, BAND:], coef_here[:, BAND:]], axis=1) + after_band, 1),
         ]
     )
     init_band, force_band, coef_band = (

time: 129 us -> 129 us (level)
  waiting for transfers between devices: 23.9 us -> 28.5 us
  starting transfers between devices: 45.2 us -> 42.3 us
  other arithmetic: 29.5 us -> 28 us
  local copies, waits for them, and re-layouts: 17.5 us -> 16 us
    ppermute x4, starting transfers between devices: 13.8 us -> 8.65 us  [exchange(): high = lax.ppermute(down, 'slab', backward)]
    ppermute x4, waiting for transfers between devices: 3.84 us -> 8.41 us  [exchange(): low = lax.ppermute(up, 'slab', forward)]
    ppermute x4, starting transfers between devices: 8.15 us -> 10.4 us  [exchange(): low = lax.ppermute(up, 'slab', forward)]
    unnamed x41 -> x43, local copies, waits for them, and re-layouts: 6.57 us -> 5.69 us
  transfers between devices with their start and end apart: 19 -> 19, of which waited for: 10 -> 11; matrix products, arithmetic and copies ran while one was open for 17% -> 14% of each run, Pallas kernels for 0% -> 0%
where the time goes in v11:
time: 129 us; the launch traced here: 127 us
  starting transfers between devices  42.3 us (33%)
  waiting for transfers between devices  28.5 us (22%)
  other arithmetic  28 us (22%)
  local copies, waits for them, and re-layouts  16 us (12%)
  between operations  12.3 us (10%)
    ppermute x5, starting transfers between devices, allsum_axis(): v = v + lax.ppermute(v, axis, [(i, i ^ step) for i in range(count)])  12 us
    ppermute x4, starting transfers between devices, exchange(): low = lax.ppermute(up, 'slab', forward)  10.4 us
    ppermute x5, waiting for transfers between devices, allsum_axis(): v = v + lax.ppermute(v, axis, [(i, i ^ step) for i in range(count)])  9.49 us
    ppermute x4, starting transfers between devices, exchange(): high = lax.ppermute(down, 'slab', backward)  8.65 us
    ppermute x4, waiting for transfers between devices, exchange(): low = lax.ppermute(up, 'slab', forward)  8.41 us
    ppermute x3, starting transfers between devices, shell_sum(): v = v + lax.ppermute(v, ('side', 'slab'), pairs)  7.42 us
    ppermute x3, waiting for transfers between devices, shell_sum(): v = v + lax.ppermute(v, ('side', 'slab'), pairs)  6.42 us
    unnamed x43, local copies, waits for them, and re-layouts  5.69 us
  transfers between devices with their start and end apart: 19, of which 11 were waited for; matrix products, arithmetic and copies ran while one was open for 14% of the time, Pallas kernels for 0%

profile of v11, /device:TPU:28, one launch (start us, length us, event | category | flops | bytes accessed | tf_op | source)
XLA Modules:
  0.0 127.4 jit_solution(14421539822677089624)
XLA Ops:
  3.0 1.8 %copy.89 = f32[1,8,64,512]{3,1,2,0:T(8,128)S(1)} copy(f32[1,8,64,512]{3,2,1,0:T(8,128)} %param.22) | data formatting | bytes 2097152 | tf_op args[1]
  8.1 2.8 %collective-permute-start.1 = (f32[100,512]{1,0:T(8,128)S(1)}, f32[100,512]{1,0:T(8,128)S(1)}, u32[]{:S(2)}, u32[]{:S(2)}) collective-permute-start(f32[100,512]{1,0:T(8,128)S(1)} %pad_maximum_fusion.11), channel_id=1, source_target_pairs={{1,0},{2,1},{3,2},{4,3},{5,4},{6,5},{7,6},{9,8},{10,9},{11,10},{12... | collective-permute-start | bytes 614408 | tf_op jit(solution)/shard_map/ppermute | solution.py:63
  10.9 1.9 %collective-permute-start = (f32[100,512]{1,0:T(8,128)S(1)}, f32[100,512]{1,0:T(8,128)S(1)}, u32[]{:S(2)}, u32[]{:S(2)}) collective-permute-start(f32[100,512]{1,0:T(8,128)S(1)} %pad_maximum_fusion.10), channel_id=1, source_target_pairs={{0,1},{1,2},{2,3},{3,4},{4,5},{5,6},{6,7},{8,9},{9,10},{10,11},{11... | collective-permute-start | bytes 614408 | tf_op jit(solution)/shard_map/ppermute | solution.py:62
  15.5 3.5 %collective-permute-done = f32[100,512]{1,0:T(8,128)S(1)} collective-permute-done((f32[100,512]{1,0:T(8,128)S(1)}, f32[100,512]{1,0:T(8,128)S(1)}, u32[]{:S(2)}, u32[]{:S(2)}) %collective-permute-start) | collective-permute-done | bytes 204832 | tf_op jit(solution)/shard_map/ppermute | solution.py:62
  23.8 2.1 %collective-permute-start.3 = (f32[224,512]{1,0:T(8,128)S(1)}, f32[224,512]{1,0:T(8,128)S(1)}, u32[]{:S(2)}, u32[]{:S(2)}) collective-permute-start(f32[224,512]{1,0:T(8,128)S(1)} %pad_maximum_fusion.6), channel_id=1, source_target_pairs={{1,0},{2,1},{3,2},{4,3},{5,4},{6,5},{7,6},{9,8},{10,9},{11,10},{12... | collective-permute-start | bytes 1376264 | tf_op jit(solution)/shard_map/ppermute | solution.py:63
  27.1 1.9 %collective-permute-start.5 = (f32[4,512]{1,0:T(4,128)S(1)}, f32[4,512]{1,0:T(4,128)S(1)}, u32[]{:S(2)}, u32[]{:S(2)}) collective-permute-start(f32[4,512]{1,0:T(4,128)S(1)} %get-tuple-element.243), channel_id=1, source_target_pairs={{1,0},{2,1},{3,2},{4,3},{5,4},{6,5},{7,6},{9,8},{10,9},{11,10},{12... | collective-permute-start | bytes 24584 | tf_op jit(solution)/shard_map/ppermute | solution.py:63
  29.1 2.4 %collective-permute-start.4 = (f32[4,512]{1,0:T(4,128)S(1)}, f32[4,512]{1,0:T(4,128)S(1)}, u32[]{:S(2)}, u32[]{:S(2)}) collective-permute-start(f32[4,512]{1,0:T(4,128)S(1)} %get-tuple-element.242), channel_id=1, source_target_pairs={{0,1},{1,2},{2,3},{3,4},{4,5},{5,6},{6,7},{8,9},{9,10},{10,11},{11... | collective-permute-start | bytes 24584 | tf_op jit(solution)/shard_map/ppermute | solution.py:62
  31.5 3.6 %collective-permute-start.2 = (f32[224,512]{1,0:T(8,128)S(1)}, f32[224,512]{1,0:T(8,128)S(1)}, u32[]{:S(2)}, u32[]{:S(2)}) collective-permute-start(f32[224,512]{1,0:T(8,128)S(1)} %pad_maximum_fusion.5), channel_id=1, source_target_pairs={{0,1},{1,2},{2,3},{3,4},{4,5},{5,6},{6,7},{8,9},{9,10},{10,11},{11... | collective-permute-start | bytes 1376264 | tf_op jit(solution)/shard_map/ppermute | solution.py:62
  37.3 4.9 %collective-permute-done.2 = f32[224,512]{1,0:T(8,128)S(1)} collective-permute-done((f32[224,512]{1,0:T(8,128)S(1)}, f32[224,512]{1,0:T(8,128)S(1)}, u32[]{:S(2)}, u32[]{:S(2)}) %collective-permute-start.2) | collective-permute-done | bytes 458784 | tf_op jit(solution)/shard_map/ppermute | solution.py:62
  43.5 1.4 %pad_maximum_fusion.14 = f32[2]{0:T(128)S(1)} fusion(f32[1]{0:T(128)} %bitcast.34, f32[1]{0:T(128)} %bitcast.33), kind=kLoop, calls=%fused_computation.250 | loop fusion | flops 2 | bytes 16 | tf_op jit(solution)/shard_map/stack | solution.py:210
  46.6 2.7 %pad_maximum_fusion.1 = (f32[10,64,512]{2,0,1:T(8,128)}, f32[10,64,512]{2,0,1:T(8,128)}) fusion(f32[10,56,512]{2,0,1:T(8,128)S(1)} %get-tuple-element.184, f32[10,8,512]{2,0,1:T(8,128)S(1)} %get-tuple-element.196, f32[10,56,512]{2,0,1:T(8,128)S(1)} %get-tuple-element.183, f32[10,8,512]{2,0,1:T(8,128)S(1)} %get-tuple-element.195), kind=kLoop, calls=%fused_computation.33 | loop fusion | flops 655360 | bytes 5242880 | tf_op jit(solution)/shard_map/concatenate | solution.py:171
  50.3 1.9 %collective-permute-start.7 = (f32[136,512]{1,0:T(8,128)}, f32[136,512]{1,0:T(8,128)S(1)}, u32[]{:S(2)}, u32[]{:S(2)}) collective-permute-start(f32[136,512]{1,0:T(8,128)} %pad_maximum_fusion.9), channel_id=1, source_target_pairs={{1,0},{2,1},{3,2},{4,3},{5,4},{6,5},{7,6},{9,8},{10,9},{11,10},{12... | collective-permute-start | bytes 835592 | tf_op jit(solution)/shard_map/ppermute | solution.py:63
  52.9 2.4 %collective-permute-start.6 = (f32[136,512]{1,0:T(8,128)}, f32[136,512]{1,0:T(8,128)}, u32[]{:S(2)}, u32[]{:S(2)}) collective-permute-start(f32[136,512]{1,0:T(8,128)} %pad_maximum_fusion.8), channel_id=1, source_target_pairs={{0,1},{1,2},{2,3},{3,4},{4,5},{5,6},{6,7},{8,9},{9,10},{10,11},{11... | collective-permute-start | bytes 835592 | tf_op jit(solution)/shard_map/ppermute | solution.py:62
  55.4 1.4 %fusion.169 = f32[2]{0:T(128)S(1)} fusion(f32[2]{0:T(128)S(1)} %collective-permute-done.8, f32[1]{0:T(128)} %bitcast.34, f32[1]{0:T(128)} %bitcast.33), kind=kLoop, calls=%fused_computation.292 | loop fusion | flops 4 | bytes 24 | tf_op jit(solution)/shard_map/add | solution.py:111
  56.7 1.6 %collective-permute-start.9 = (f32[2]{0:T(128)S(1)}, f32[2]{0:T(128)S(1)}, u32[]{:S(2)}, u32[]{:S(2)}) collective-permute-start(f32[2]{0:T(128)S(1)} %fusion.169), channel_id=1, source_target_pairs={{0,2},{1,3},{2,0},{3,1},{4,6},{5,7},{6,4},{7,5},{8,10},{9,11},{10,... | collective-permute-start | bytes 32 | tf_op jit(solution)/shard_map/ppermute | solution.py:111
  58.4 1.9 %collective-permute-done.9 = f32[2]{0:T(128)S(1)} collective-permute-done((f32[2]{0:T(128)S(1)}, f32[2]{0:T(128)S(1)}, u32[]{:S(2)}, u32[]{:S(2)}) %collective-permute-start.9) | collective-permute-done | bytes 40 | tf_op jit(solution)/shard_map/ppermute | solution.py:111
  60.3 1.4 %fusion.170 = f32[2]{0:T(128)S(1)} fusion(f32[2]{0:T(128)S(1)} %collective-permute-done.9, f32[2]{0:T(128)S(1)} %collective-permute-done.8, f32[1]{0:T(128)} %bitcast.34, f32[1]{0:T(128)} %bitcast.33), kind=kLoop, calls=%fused_computation.293 | loop fusion | flops 6 | bytes 32 | tf_op jit(solution)/shard_map/add | solution.py:111
  61.7 3.5 %collective-permute-done.10 = f32[2]{0:T(128)S(1)} collective-permute-done((f32[2]{0:T(128)S(1)}, f32[2]{0:T(128)S(1)}, u32[]{:S(2)}, u32[]{:S(2)}) %collective-permute-start.10) | collective-permute-done | bytes 40 | tf_op jit(solution)/shard_map/ppermute | solution.py:111
  65.2 8.5 %collective-permute-start.11 = (f32[2]{0:T(128)S(1)}, f32[2]{0:T(128)S(1)}, u32[]{:S(2)}, u32[]{:S(2)}) collective-permute-start(f32[2]{0:T(128)S(1)} %add.732), channel_id=1, source_target_pairs={{0,8},{8,0},{16,24},{24,16},{1,9},{9,1},{17,25},{25,17},{2,10},{10... | collective-permute-start | bytes 32 | tf_op jit(solution)/shard_map/ppermute | solution.py:111
  73.6 1.5 %collective-permute-done.11 = f32[2]{0:T(128)S(1)} collective-permute-done((f32[2]{0:T(128)S(1)}, f32[2]{0:T(128)S(1)}, u32[]{:S(2)}, u32[]{:S(2)}) %collective-permute-start.11) | collective-permute-done | bytes 40 | tf_op jit(solution)/shard_map/ppermute | solution.py:111
  75.2 1.9 %collective-permute-start.12 = (f32[2]{0:T(128)S(1)}, f32[2]{0:T(128)S(1)}, u32[]{:S(2)}, u32[]{:S(2)}) collective-permute-start(f32[2]{0:T(128)S(1)} %add.733), channel_id=1, source_target_pairs={{0,16},{8,24},{16,0},{24,8},{1,17},{9,25},{17,1},{25,9},{2,18},{10... | collective-permute-start | bytes 32 | tf_op jit(solution)/shard_map/ppermute | solution.py:111
  77.1 2.5 %collective-permute-done.12 = f32[2]{0:T(128)S(1)} collective-permute-done((f32[2]{0:T(128)S(1)}, f32[2]{0:T(128)S(1)}, u32[]{:S(2)}, u32[]{:S(2)}) %collective-permute-start.12) | collective-permute-done | bytes 40 | tf_op jit(solution)/shard_map/ppermute | solution.py:111
  85.8 4.6 %multiply_reduce_fusion = f32[2,8,512]{2,1,0:T(8,128)S(1)} fusion(f32[2,8,512]{2,1,0:T(8,128)S(1)} %subtract_multiply_fusion, f32[8,512,512]{2,1,0:T(8,128)} %param.24), kind=kLoop, calls=%fused_computation.28 | loop fusion | flops 8380416 | bytes 8454144 | tf_op jit(solution)/shard_map/reduce_sum | solution.py:222
  91.2 2.5 %fusion.123 = f32[1,512]{1,0:T(1,128)S(1)} fusion(f32[]{:T(128)} %get-tuple-element.143, f32[]{:T(128)} %get-tuple-element.144, f32[]{:T(128)} %get-tuple-element.142, f32[]{:T(128)} %get-tuple-element.141), kind=kLoop, calls=%fused_computation.245 | loop fusion | flops 5632 | bytes 2064 | tf_op jit(solution)/shard_map/add | solution.py:250
  93.9 1.3 %collective-permute-start.15 = (f32[33,512]{1,0:T(8,128)S(1)}, f32[33,512]{1,0:T(8,128)S(1)}, u32[]{:S(2)}, u32[]{:S(2)}) collective-permute-start(f32[33,512]{1,0:T(8,128)S(1)} %dynamic-update-slice.16), channel_id=1, source_target_pairs={{16,24},{17,25},{18,26},{19,27},{20,28},{21,29},{22,30},{23,31}} | collective-permute-start | bytes 202760 | tf_op jit(solution)/shard_map/ppermute | solution.py:258
  100.5 1.9 %collective-permute-done.14 = f32[33,512]{1,0:T(8,128)S(1)} collective-permute-done((f32[33,512]{1,0:T(8,128)S(1)}, f32[33,512]{1,0:T(8,128)S(1)}, u32[]{:S(2)}, u32[]{:S(2)}) %collective-permute-start.14) | collective-permute-done | bytes 67616 | tf_op jit(solution)/shard_map/ppermute | solution.py:258
  102.4 2.2 %collective-permute-done.13 = f32[33,512]{1,0:T(8,128)S(1)} collective-permute-done((f32[33,512]{1,0:T(8,128)S(1)}, f32[33,512]{1,0:T(8,128)S(1)}, u32[]{:S(2)}, u32[]{:S(2)}) %collective-permute-start.13) | collective-permute-done | bytes 67616 | tf_op jit(solution)/shard_map/ppermute | solution.py:258
  104.6 1.9 %collective-permute-start.16 = (f32[4]{0:T(128)S(1)}, f32[4]{0:T(128)S(1)}, u32[]{:S(2)}, u32[]{:S(2)}) collective-permute-start(f32[4]{0:T(128)S(1)} %slice_bitcast_fusion.2), channel_id=1, source_target_pairs={{24,25},{25,24},{26,27},{27,26},{28,29},{29,28},{30,31},{31,30}} | collective-permute-start | bytes 56 | tf_op jit(solution)/shard_map/ppermute | solution.py:122
  107.6 3.6 %collective-permute-start.17 = (f32[4]{0:T(128)S(1)}, f32[4]{0:T(128)S(1)}, u32[]{:S(2)}, u32[]{:S(2)}) collective-permute-start(f32[4]{0:T(128)S(1)} %fusion.125), channel_id=1, source_target_pairs={{24,26},{25,27},{26,24},{27,25},{28,30},{29,31},{30,28},{31,29}} | collective-permute-start | bytes 56 | tf_op jit(solution)/shard_map/ppermute | solution.py:122
  111.2 1.8 %collective-permute-done.17 = f32[4]{0:T(128)S(1)} collective-permute-done((f32[4]{0:T(128)S(1)}, f32[4]{0:T(128)S(1)}, u32[]{:S(2)}, u32[]{:S(2)}) %collective-permute-start.17) | collective-permute-done | bytes 48 | tf_op jit(solution)/shard_map/ppermute | solution.py:122
  113.1 1.9 %collective-permute-start.18 = (f32[4]{0:T(128)S(1)}, f32[4]{0:T(128)S(1)}, u32[]{:S(2)}, u32[]{:S(2)}) collective-permute-start(f32[4]{0:T(128)S(1)} %add.747), channel_id=1, source_target_pairs={{24,28},{25,29},{26,30},{27,31},{28,24},{29,25},{30,26},{31,27}} | collective-permute-start | bytes 56 | tf_op jit(solution)/shard_map/ppermute | solution.py:122
  115.0 3.5 %collective-permute-done.18 = f32[4]{0:T(128)S(1)} collective-permute-done((f32[4]{0:T(128)S(1)}, f32[4]{0:T(128)S(1)}, u32[]{:S(2)}, u32[]{:S(2)}) %collective-permute-start.18) | collective-permute-done | bytes 48 | tf_op jit(solution)/shard_map/ppermute | solution.py:122
  (202 shorter events, 32.5 us)
Async XLA Ops:
  0.6 4.2 %copy-start.5 = (f32[1,8,64,512]{3,2,1,0:T(8,128)S(1)}, f32[1,8,64,512]{3,2,1,0:T(8,128)}, u32[]{:S(2)}) copy-start(f32[1,8,64,512]{3,2,1,0:T(8,128)} %param.21) | copy-start | bytes 3145732
  4.8 15.8 %copy-start = (f32[1,8,64,512]{3,1,2,0:T(8,128)}, f32[1,8,64,512]{3,1,2,0:T(8,128)S(1)}, u32[]{:S(2)}) copy-start(f32[1,8,64,512]{3,1,2,0:T(8,128)S(1)} %copy.89) | copy-start | bytes 3145732
  4.8 1.6 %copy-start.6 = (f32[1,8,64,512]{3,2,1,0:T(8,128)S(1)}, f32[1,8,64,512]{3,2,1,0:T(8,128)}, u32[]{:S(2)}) copy-start(f32[1,8,64,512]{3,2,1,0:T(8,128)} %param.23) | copy-start | bytes 3145732
  7.1 6.0 %copy-start.14 = (s32[8]{0:T(128)S(1)}, s32[8]{0:T(128)}, u32[]{:S(2)}) copy-start(s32[8]{0:T(128)} %param.29) | copy-start | bytes 100
  8.1 7.3 %collective-permute-start.1 = (f32[100,512]{1,0:T(8,128)S(1)}, f32[100,512]{1,0:T(8,128)S(1)}, u32[]{:S(2)}, u32[]{:S(2)}) collective-permute-start(f32[100,512]{1,0:T(8,128)S(1)} %pad_maximum_fusion.11), channel_id=1, source_target_pairs={{1,0},{2,1},{3,2},{4,3},{5,4},{6,5},{7,6},{9,8},{10,9},{11,10},{12... | collective-permute-start | bytes 614408 | tf_op jit(solution)/shard_map/ppermute | solution.py:63
  10.9 8.1 %collective-permute-start = (f32[100,512]{1,0:T(8,128)S(1)}, f32[100,512]{1,0:T(8,128)S(1)}, u32[]{:S(2)}, u32[]{:S(2)}) collective-permute-start(f32[100,512]{1,0:T(8,128)S(1)} %pad_maximum_fusion.10), channel_id=1, source_target_pairs={{0,1},{1,2},{2,3},{3,4},{4,5},{5,6},{6,7},{8,9},{9,10},{10,11},{11... | collective-permute-start | bytes 614408 | tf_op jit(solution)/shard_map/ppermute | solution.py:62
  19.6 15.6 %copy-start.7 = (f32[16,1,512]{2,0,1:T(8,128)}, f32[16,1,512]{2,0,1:T(8,128)S(1)}, u32[]{:S(2)}) copy-start(f32[16,1,512]{2,0,1:T(8,128)S(1)} %get-tuple-element.164) | copy-start | bytes 98308
  20.0 2.2 %copy-start.2 = (f32[1,8,64,512]{3,1,2,0:T(8,128)S(1)}, f32[1,8,64,512]{3,1,2,0:T(8,128)}, u32[]{:S(2)}) copy-start(f32[1,8,64,512]{3,1,2,0:T(8,128)} %copy-done.1) | copy-start | bytes 3145732
  20.2 6.0 %slice-start = ((s8[8388608]{0:T(1024)(128)(4,1)}), s8[4194304]{0:T(1024)(128)(4,1)S(1)}, s32[]{:S(2)}) async-start(s8[8388608]{0:T(1024)(128)(4,1)} %bitcast.96), calls=%async_computation | async-start | bytes 8388608
  21.2 1.6 %copy-start.3 = (f32[8,56,512]{2,0,1:T(8,128)S(1)}, f32[8,56,512]{2,0,1:T(8,128)}, u32[]{:S(2)}) copy-start(f32[8,56,512]{2,0,1:T(8,128)} %slice.1018) | copy-start | bytes 2752516
  21.2 1.8 %copy-start.4 = (f32[8,56,512]{2,0,1:T(8,128)S(1)}, f32[8,56,512]{2,0,1:T(8,128)}, u32[]{:S(2)}) copy-start(f32[8,56,512]{2,0,1:T(8,128)} %slice.1017) | copy-start | bytes 2752516
  23.0 3.2 %slice-start.1 = ((s8[8388608]{0:T(1024)(128)(4,1)}), s8[4194304]{0:T(1024)(128)(4,1)S(1)}, s32[]{:S(2)}) async-start(s8[8388608]{0:T(1024)(128)(4,1)} %bitcast.96), calls=%async_computation.1 | async-start | bytes 8388608
  23.7 2.4 %copy-start.11 = (f32[8,512]{1,0:T(8,128)S(1)}, f32[8,512]{1,0:T(8,128)}, u32[]{:S(2)}) copy-start(f32[8,512]{1,0:T(8,128)} %param.25) | copy-start | bytes 49156
  23.8 13.3 %collective-permute-start.3 = (f32[224,512]{1,0:T(8,128)S(1)}, f32[224,512]{1,0:T(8,128)S(1)}, u32[]{:S(2)}, u32[]{:S(2)}) collective-permute-start(f32[224,512]{1,0:T(8,128)S(1)} %pad_maximum_fusion.6), channel_id=1, source_target_pairs={{1,0},{2,1},{3,2},{4,3},{5,4},{6,5},{7,6},{9,8},{10,9},{11,10},{12... | collective-permute-start | bytes 1376264 | tf_op jit(solution)/shard_map/ppermute | solution.py:63
  27.1 8.0 %collective-permute-start.5 = (f32[4,512]{1,0:T(4,128)S(1)}, f32[4,512]{1,0:T(4,128)S(1)}, u32[]{:S(2)}, u32[]{:S(2)}) collective-permute-start(f32[4,512]{1,0:T(4,128)S(1)} %get-tuple-element.243), channel_id=1, source_target_pairs={{1,0},{2,1},{3,2},{4,3},{5,4},{6,5},{7,6},{9,8},{10,9},{11,10},{12... | collective-permute-start | bytes 24584 | tf_op jit(solution)/shard_map/ppermute | solution.py:63
  29.1 6.1 %collective-permute-start.4 = (f32[4,512]{1,0:T(4,128)S(1)}, f32[4,512]{1,0:T(4,128)S(1)}, u32[]{:S(2)}, u32[]{:S(2)}) collective-permute-start(f32[4,512]{1,0:T(4,128)S(1)} %get-tuple-element.242), channel_id=1, source_target_pairs={{0,1},{1,2},{2,3},{3,4},{4,5},{5,6},{6,7},{8,9},{9,10},{10,11},{11... | collective-permute-start | bytes 24584 | tf_op jit(solution)/shard_map/ppermute | solution.py:62
  31.5 10.7 %collective-permute-start.2 = (f32[224,512]{1,0:T(8,128)S(1)}, f32[224,512]{1,0:T(8,128)S(1)}, u32[]{:S(2)}, u32[]{:S(2)}) collective-permute-start(f32[224,512]{1,0:T(8,128)S(1)} %pad_maximum_fusion.5), channel_id=1, source_target_pairs={{0,1},{1,2},{2,3},{3,4},{4,5},{5,6},{6,7},{8,9},{9,10},{10,11},{11... | collective-permute-start | bytes 1376264 | tf_op jit(solution)/shard_map/ppermute | solution.py:62
  44.9 10.5 %collective-permute-start.8 = (f32[2]{0:T(128)S(1)}, f32[2]{0:T(128)S(1)}, u32[]{:S(2)}, u32[]{:S(2)}) collective-permute-start(f32[2]{0:T(128)S(1)} %pad_maximum_fusion.14), channel_id=1, source_target_pairs={{0,1},{1,0},{2,3},{3,2},{4,5},{5,4},{6,7},{7,6},{8,9},{9,8},{10,11... | collective-permute-start | bytes 32 | tf_op jit(solution)/shard_map/ppermute | solution.py:111
  49.5 33.6 %copy-start.8 = (f32[16,1,512]{2,0,1:T(8,128)S(1)}, f32[16,1,512]{2,0,1:T(8,128)}, u32[]{:S(2)}) copy-start(f32[16,1,512]{2,0,1:T(8,128)} %copy-done.7) | copy-start | bytes 98308
  50.3 31.9 %collective-permute-start.7 = (f32[136,512]{1,0:T(8,128)}, f32[136,512]{1,0:T(8,128)S(1)}, u32[]{:S(2)}, u32[]{:S(2)}) collective-permute-start(f32[136,512]{1,0:T(8,128)} %pad_maximum_fusion.9), channel_id=1, source_target_pairs={{1,0},{2,1},{3,2},{4,3},{5,4},{6,5},{7,6},{9,8},{10,9},{11,10},{12... | collective-permute-start | bytes 835592 | tf_op jit(solution)/shard_map/ppermute | solution.py:63
  52.9 29.3 %collective-permute-start.6 = (f32[136,512]{1,0:T(8,128)}, f32[136,512]{1,0:T(8,128)}, u32[]{:S(2)}, u32[]{:S(2)}) collective-permute-start(f32[136,512]{1,0:T(8,128)} %pad_maximum_fusion.8), channel_id=1, source_target_pairs={{0,1},{1,2},{2,3},{3,4},{4,5},{5,6},{6,7},{8,9},{9,10},{10,11},{11... | collective-permute-start | bytes 835592 | tf_op jit(solution)/shard_map/ppermute | solution.py:62
  56.7 3.5 %collective-permute-start.9 = (f32[2]{0:T(128)S(1)}, f32[2]{0:T(128)S(1)}, u32[]{:S(2)}, u32[]{:S(2)}) collective-permute-start(f32[2]{0:T(128)S(1)} %fusion.169), channel_id=1, source_target_pairs={{0,2},{1,3},{2,0},{3,1},{4,6},{5,7},{6,4},{7,5},{8,10},{9,11},{10,... | collective-permute-start | bytes 32 | tf_op jit(solution)/shard_map/ppermute | solution.py:111
  61.6 3.5 %collective-permute-start.10 = (f32[2]{0:T(128)S(1)}, f32[2]{0:T(128)S(1)}, u32[]{:S(2)}, u32[]{:S(2)}) collective-permute-start(f32[2]{0:T(128)S(1)} %fusion.170), channel_id=1, source_target_pairs={{0,4},{1,5},{2,6},{3,7},{4,0},{5,1},{6,2},{7,3},{8,12},{9,13},{10,... | collective-permute-start | bytes 32 | tf_op jit(solution)/shard_map/ppermute | solution.py:111
  65.2 10.0 %collective-permute-start.11 = (f32[2]{0:T(128)S(1)}, f32[2]{0:T(128)S(1)}, u32[]{:S(2)}, u32[]{:S(2)}) collective-permute-start(f32[2]{0:T(128)S(1)} %add.732), channel_id=1, source_target_pairs={{0,8},{8,0},{16,24},{24,16},{1,9},{9,1},{17,25},{25,17},{2,10},{10... | collective-permute-start | bytes 32 | tf_op jit(solution)/shard_map/ppermute | solution.py:111
  75.2 4.4 %collective-permute-start.12 = (f32[2]{0:T(128)S(1)}, f32[2]{0:T(128)S(1)}, u32[]{:S(2)}, u32[]{:S(2)}) collective-permute-start(f32[2]{0:T(128)S(1)} %add.733), channel_id=1, source_target_pairs={{0,16},{8,24},{16,0},{24,8},{1,17},{9,25},{17,1},{25,9},{2,18},{10... | collective-permute-start | bytes 32 | tf_op jit(solution)/shard_map/ppermute | solution.py:111
  85.8 12.0 %copy-start.10 = (f32[136,512]{1,0:T(8,128)S(1)}, f32[136,512]{1,0:T(8,128)}, u32[]{:S(2)}) copy-start(f32[136,512]{1,0:T(8,128)} %copy-done.9) | copy-start | bytes 835588
  93.9 6.6 %collective-permute-start.15 = (f32[33,512]{1,0:T(8,128)S(1)}, f32[33,512]{1,0:T(8,128)S(1)}, u32[]{:S(2)}, u32[]{:S(2)}) collective-permute-start(f32[33,512]{1,0:T(8,128)S(1)} %dynamic-update-slice.16), channel_id=1, source_target_pairs={{16,24},{17,25},{18,26},{19,27},{20,28},{21,29},{22,30},{23,31}} | collective-permute-start | bytes 202760 | tf_op jit(solution)/shard_map/ppermute | solution.py:258
  95.2 7.2 %collective-permute-start.14 = (f32[33,512]{1,0:T(8,128)S(1)}, f32[33,512]{1,0:T(8,128)S(1)}, u32[]{:S(2)}, u32[]{:S(2)}) collective-permute-start(f32[33,512]{1,0:T(8,128)S(1)} %dynamic-update-slice.16), channel_id=1, source_target_pairs={{8,24},{9,25},{10,26},{11,27},{12,28},{13,29},{14,30},{15,31}} | collective-permute-start | bytes 202760 | tf_op jit(solution)/shard_map/ppermute | solution.py:258
  96.5 8.1 %collective-permute-start.13 = (f32[33,512]{1,0:T(8,128)S(1)}, f32[33,512]{1,0:T(8,128)S(1)}, u32[]{:S(2)}, u32[]{:S(2)}) collective-permute-start(f32[33,512]{1,0:T(8,128)S(1)} %dynamic-update-slice.16), channel_id=1, source_target_pairs={{0,24},{1,25},{2,26},{3,27},{4,28},{5,29},{6,30},{7,31}} | collective-permute-start | bytes 202760 | tf_op jit(solution)/shard_map/ppermute | solution.py:258
  104.6 3.0 %collective-permute-start.16 = (f32[4]{0:T(128)S(1)}, f32[4]{0:T(128)S(1)}, u32[]{:S(2)}, u32[]{:S(2)}) collective-permute-start(f32[4]{0:T(128)S(1)} %slice_bitcast_fusion.2), channel_id=1, source_target_pairs={{24,25},{25,24},{26,27},{27,26},{28,29},{29,28},{30,31},{31,30}} | collective-permute-start | bytes 56 | tf_op jit(solution)/shard_map/ppermute | solution.py:122
  107.6 5.4 %collective-permute-start.17 = (f32[4]{0:T(128)S(1)}, f32[4]{0:T(128)S(1)}, u32[]{:S(2)}, u32[]{:S(2)}) collective-permute-start(f32[4]{0:T(128)S(1)} %fusion.125), channel_id=1, source_target_pairs={{24,26},{25,27},{26,24},{27,25},{28,30},{29,31},{30,28},{31,29}} | collective-permute-start | bytes 56 | tf_op jit(solution)/shard_map/ppermute | solution.py:122
  113.1 5.4 %collective-permute-start.18 = (f32[4]{0:T(128)S(1)}, f32[4]{0:T(128)S(1)}, u32[]{:S(2)}, u32[]{:S(2)}) collective-permute-start(f32[4]{0:T(128)S(1)} %add.747), channel_id=1, source_target_pairs={{24,28},{25,29},{26,30},{27,31},{28,24},{29,25},{30,26},{31,27}} | collective-permute-start | bytes 56 | tf_op jit(solution)/shard_map/ppermute | solution.py:122
  (4 other events, 3.8 us)

commit v12 on v11

--- a/solution.py
+++ b/solution.py
@@ -124,6 +124,22 @@
     return v
 
 
+def fluid_sum(v, side_id, sectors):
+    count = lax.axis_size("slab")
+    got = [v]
+    for k in range(1, sectors):
+        pairs = [(s * count + j, ((s + k) % sectors) * count + j) for s in range(sectors) for j in range(count)]
+        got.append(lax.ppermute(v, ("side", "slab"), pairs))
+    total = None
+    for t in range(sectors):
+        term = got[0]
+        for k in range(1, sectors):
+            term = jnp.where(side_id == (t + k) % sectors, got[k], term)
+        term = jnp.where(side_id == t, got[0], term)
+        total = term if total is None else total + term
+    return total
+
+
 def allsum(v):
     return allsum_axis(allsum_axis(v, "slab"), "side")
 
@@ -207,7 +223,11 @@
     )
     resid_one = tilde_one - disp_one
     diff_one = resid_one - resid_zero
-    sums = allsum(jnp.stack([jnp.sum(diff_one * diff_one), jnp.sum(diff_one * resid_one)]))
+    sums = fluid_sum(
+        allsum_axis(jnp.stack([jnp.sum(diff_one * diff_one), jnp.sum(diff_one * resid_one)]), "slab"),
+        side_id,
+        side_count - 1,
+    )
     step_one = tilde_one - tilde_zero
     rims_base, rims_step, deep = exchange(
         [(plane_of(tilde_one), HALO), (plane_of(step_one), HALO), (deep, 2)]
@@ -249,7 +269,8 @@
             jnp.concatenate([tilde_two, tilde_one, tilde_zero, resid_two], axis=0),
             sum(
                 jnp.where(jnp.arange(line_cells) == k, partial[k], 0.0) for k in range(4)
-            )[None],
+            )[None]
+            + jnp.where((jnp.arange(line_cells) == 4) & (side_id == 0), gram_aa, 0.0)[None],
         ],
         axis=0,
     )
@@ -257,6 +278,7 @@
     for source in range(side_count - 1):
         gathered = gathered + lax.ppermute(outgoing, "side", [(source, side_count - 1)])
     sums = shell_sum(gathered[4 * patches_here, :4], side_count)
+    gram_aa = gathered[4 * patches_here, 4]
     gram_nn, gram_no, proj_new, proj_old = sums[0], sums[1], sums[2], sums[3]
     tilde_two, tilde_one, tilde_zero, resid_two = (
         gathered[k * patches_here : (k + 1) * patches_here] for k in range(4)

time: 129 us -> 129 us (level)
  starting transfers between devices: 42.3 us -> 33.3 us
  waiting for transfers between devices: 28.5 us -> 36.4 us
    ppermute x3, waiting for transfers between devices: 4.13 us -> 16.1 us  [body(): lax.ppermute(outgoing, 'side', [(source, side_count - 1)])]
    ppermute x5 -> x3, starting transfers between devices: 12 us -> 1.65 us  [allsum_axis(): v = v + lax.ppermute(v, axis, [(i, i ^ step) for i in range(count)])]
    ppermute x5 -> x3, waiting for transfers between devices: 9.49 us -> 5.45 us  [allsum_axis(): v = v + lax.ppermute(v, axis, [(i, i ^ step) for i in range(count)])]
    ppermute x0 -> x2, starting transfers between devices: none -> 1.31 us  [fluid_sum(): got.append(lax.ppermute(v, ('side', 'slab'), pairs))]
    add x5 -> x3, other arithmetic: 2.75 us -> 2.74 us  [allsum_axis(): v = v + lax.ppermute(v, axis, [(i, i ^ step) for i in range(count)])]
  transfers between devices with their start and end apart: 19 -> 19, of which waited for: 11 -> 10; matrix products, arithmetic and copies ran while one was open for 14% -> 14% of each run, Pallas kernels for 0% -> 0%
where the time goes in v12:
time: 129 us; the launch traced here: 128 us
  waiting for transfers between devices  36.4 us (28%)
  starting transfers between devices  33.3 us (26%)
  other arithmetic  28.7 us (22%)
  local copies, waits for them, and re-layouts  16.6 us (13%)
  between operations  12.4 us (10%)
    ppermute x3, waiting for transfers between devices, body(): lax.ppermute(outgoing, 'side', [(source, side_count - 1)])  16.1 us
    ppermute x4, starting transfers between devices, exchange(): low = lax.ppermute(up, 'slab', forward)  10.4 us
    ppermute x4, starting transfers between devices, exchange(): high = lax.ppermute(down, 'slab', backward)  8.65 us
    ppermute x4, waiting for transfers between devices, exchange(): low = lax.ppermute(up, 'slab', forward)  8.41 us
    ppermute x3, starting transfers between devices, shell_sum(): v = v + lax.ppermute(v, ('side', 'slab'), pairs)  7.41 us
    ppermute x3, waiting for transfers between devices, shell_sum(): v = v + lax.ppermute(v, ('side', 'slab'), pairs)  6.42 us
    unnamed x43, local copies, waits for them, and re-layouts  5.69 us
    ppermute x3, waiting for transfers between devices, allsum_axis(): v = v + lax.ppermute(v, axis, [(i, i ^ step) for i in range(count)])  5.45 us
  transfers between devices with their start and end apart: 19, of which 10 were waited for; matrix products, arithmetic and copies ran while one was open for 14% of the time, Pallas kernels for 0%

profile of v12, /device:TPU:28, one launch (start us, length us, event | category | flops | bytes accessed | tf_op | source)
XLA Modules:
  0.0 127.6 jit_solution(15278564747691546665)
XLA Ops:
  3.0 1.8 %copy.89 = f32[1,8,64,512]{3,1,2,0:T(8,128)S(1)} copy(f32[1,8,64,512]{3,2,1,0:T(8,128)} %param.22) | data formatting | bytes 2097152 | tf_op args[1]
  8.1 2.8 %collective-permute-start.1 = (f32[100,512]{1,0:T(8,128)S(1)}, f32[100,512]{1,0:T(8,128)S(1)}, u32[]{:S(2)}, u32[]{:S(2)}) collective-permute-start(f32[100,512]{1,0:T(8,128)S(1)} %pad_maximum_fusion.11), channel_id=1, source_target_pairs={{1,0},{2,1},{3,2},{4,3},{5,4},{6,5},{7,6},{9,8},{10,9},{11,10},{12... | collective-permute-start | bytes 614408 | tf_op jit(solution)/shard_map/ppermute | solution.py:63
  10.9 1.9 %collective-permute-start = (f32[100,512]{1,0:T(8,128)S(1)}, f32[100,512]{1,0:T(8,128)S(1)}, u32[]{:S(2)}, u32[]{:S(2)}) collective-permute-start(f32[100,512]{1,0:T(8,128)S(1)} %pad_maximum_fusion.10), channel_id=1, source_target_pairs={{0,1},{1,2},{2,3},{3,4},{4,5},{5,6},{6,7},{8,9},{9,10},{10,11},{11... | collective-permute-start | bytes 614408 | tf_op jit(solution)/shard_map/ppermute | solution.py:62
  15.5 3.5 %collective-permute-done = f32[100,512]{1,0:T(8,128)S(1)} collective-permute-done((f32[100,512]{1,0:T(8,128)S(1)}, f32[100,512]{1,0:T(8,128)S(1)}, u32[]{:S(2)}, u32[]{:S(2)}) %collective-permute-start) | collective-permute-done | bytes 204832 | tf_op jit(solution)/shard_map/ppermute | solution.py:62
  23.8 2.1 %collective-permute-start.3 = (f32[224,512]{1,0:T(8,128)S(1)}, f32[224,512]{1,0:T(8,128)S(1)}, u32[]{:S(2)}, u32[]{:S(2)}) collective-permute-start(f32[224,512]{1,0:T(8,128)S(1)} %pad_maximum_fusion.6), channel_id=1, source_target_pairs={{1,0},{2,1},{3,2},{4,3},{5,4},{6,5},{7,6},{9,8},{10,9},{11,10},{12... | collective-permute-start | bytes 1376264 | tf_op jit(solution)/shard_map/ppermute | solution.py:63
  27.1 1.9 %collective-permute-start.5 = (f32[4,512]{1,0:T(4,128)S(1)}, f32[4,512]{1,0:T(4,128)S(1)}, u32[]{:S(2)}, u32[]{:S(2)}) collective-permute-start(f32[4,512]{1,0:T(4,128)S(1)} %get-tuple-element.243), channel_id=1, source_target_pairs={{1,0},{2,1},{3,2},{4,3},{5,4},{6,5},{7,6},{9,8},{10,9},{11,10},{12... | collective-permute-start | bytes 24584 | tf_op jit(solution)/shard_map/ppermute | solution.py:63
  29.1 2.4 %collective-permute-start.4 = (f32[4,512]{1,0:T(4,128)S(1)}, f32[4,512]{1,0:T(4,128)S(1)}, u32[]{:S(2)}, u32[]{:S(2)}) collective-permute-start(f32[4,512]{1,0:T(4,128)S(1)} %get-tuple-element.242), channel_id=1, source_target_pairs={{0,1},{1,2},{2,3},{3,4},{4,5},{5,6},{6,7},{8,9},{9,10},{10,11},{11... | collective-permute-start | bytes 24584 | tf_op jit(solution)/shard_map/ppermute | solution.py:62
  31.5 3.6 %collective-permute-start.2 = (f32[224,512]{1,0:T(8,128)S(1)}, f32[224,512]{1,0:T(8,128)S(1)}, u32[]{:S(2)}, u32[]{:S(2)}) collective-permute-start(f32[224,512]{1,0:T(8,128)S(1)} %pad_maximum_fusion.5), channel_id=1, source_target_pairs={{0,1},{1,2},{2,3},{3,4},{4,5},{5,6},{6,7},{8,9},{9,10},{10,11},{11... | collective-permute-start | bytes 1376264 | tf_op jit(solution)/shard_map/ppermute | solution.py:62
  37.3 4.9 %collective-permute-done.2 = f32[224,512]{1,0:T(8,128)S(1)} collective-permute-done((f32[224,512]{1,0:T(8,128)S(1)}, f32[224,512]{1,0:T(8,128)S(1)}, u32[]{:S(2)}, u32[]{:S(2)}) %collective-permute-start.2) | collective-permute-done | bytes 458784 | tf_op jit(solution)/shard_map/ppermute | solution.py:62
  43.5 1.4 %pad_maximum_fusion.14 = f32[2]{0:T(128)S(1)} fusion(f32[1]{0:T(128)} %bitcast.34, f32[1]{0:T(128)} %bitcast.33), kind=kLoop, calls=%fused_computation.263 | loop fusion | flops 2 | bytes 16 | tf_op jit(solution)/shard_map/stack | solution.py:227
  46.6 2.7 %pad_maximum_fusion.1 = (f32[10,64,512]{2,0,1:T(8,128)}, f32[10,64,512]{2,0,1:T(8,128)}) fusion(f32[10,56,512]{2,0,1:T(8,128)S(1)} %get-tuple-element.184, f32[10,8,512]{2,0,1:T(8,128)S(1)} %get-tuple-element.196, f32[10,56,512]{2,0,1:T(8,128)S(1)} %get-tuple-element.183, f32[10,8,512]{2,0,1:T(8,128)S(1)} %get-tuple-element.195), kind=kLoop, calls=%fused_computation.33 | loop fusion | flops 655360 | bytes 5242880 | tf_op jit(solution)/shard_map/concatenate | solution.py:187
  50.3 1.9 %collective-permute-start.7 = (f32[136,512]{1,0:T(8,128)}, f32[136,512]{1,0:T(8,128)S(1)}, u32[]{:S(2)}, u32[]{:S(2)}) collective-permute-start(f32[136,512]{1,0:T(8,128)} %pad_maximum_fusion.9), channel_id=1, source_target_pairs={{1,0},{2,1},{3,2},{4,3},{5,4},{6,5},{7,6},{9,8},{10,9},{11,10},{12... | collective-permute-start | bytes 835592 | tf_op jit(solution)/shard_map/ppermute | solution.py:63
  52.9 2.4 %collective-permute-start.6 = (f32[136,512]{1,0:T(8,128)}, f32[136,512]{1,0:T(8,128)}, u32[]{:S(2)}, u32[]{:S(2)}) collective-permute-start(f32[136,512]{1,0:T(8,128)} %pad_maximum_fusion.8), channel_id=1, source_target_pairs={{0,1},{1,2},{2,3},{3,4},{4,5},{5,6},{6,7},{8,9},{9,10},{10,11},{11... | collective-permute-start | bytes 835592 | tf_op jit(solution)/shard_map/ppermute | solution.py:62
  55.4 1.4 %fusion.172 = f32[2]{0:T(128)S(1)} fusion(f32[2]{0:T(128)S(1)} %collective-permute-done.8, f32[1]{0:T(128)} %bitcast.34, f32[1]{0:T(128)} %bitcast.33), kind=kLoop, calls=%fused_computation.305 | loop fusion | flops 4 | bytes 24 | tf_op jit(solution)/shard_map/add | solution.py:111
  56.7 1.6 %collective-permute-start.9 = (f32[2]{0:T(128)S(1)}, f32[2]{0:T(128)S(1)}, u32[]{:S(2)}, u32[]{:S(2)}) collective-permute-start(f32[2]{0:T(128)S(1)} %fusion.172), channel_id=1, source_target_pairs={{0,2},{1,3},{2,0},{3,1},{4,6},{5,7},{6,4},{7,5},{8,10},{9,11},{10,... | collective-permute-start | bytes 32 | tf_op jit(solution)/shard_map/ppermute | solution.py:111
  58.4 1.9 %collective-permute-done.9 = f32[2]{0:T(128)S(1)} collective-permute-done((f32[2]{0:T(128)S(1)}, f32[2]{0:T(128)S(1)}, u32[]{:S(2)}, u32[]{:S(2)}) %collective-permute-start.9) | collective-permute-done | bytes 40 | tf_op jit(solution)/shard_map/ppermute | solution.py:111
  60.3 1.4 %fusion.173 = f32[2]{0:T(128)S(1)} fusion(f32[2]{0:T(128)S(1)} %collective-permute-done.9, f32[2]{0:T(128)S(1)} %collective-permute-done.8, f32[1]{0:T(128)} %bitcast.34, f32[1]{0:T(128)} %bitcast.33), kind=kLoop, calls=%fused_computation.306 | loop fusion | flops 6 | bytes 32 | tf_op jit(solution)/shard_map/add | solution.py:111
  61.7 3.5 %collective-permute-done.10 = f32[2]{0:T(128)S(1)} collective-permute-done((f32[2]{0:T(128)S(1)}, f32[2]{0:T(128)S(1)}, u32[]{:S(2)}, u32[]{:S(2)}) %collective-permute-start.10) | collective-permute-done | bytes 40 | tf_op jit(solution)/shard_map/ppermute | solution.py:111
  72.7 4.6 %multiply_reduce_fusion = f32[2,8,512]{2,1,0:T(8,128)S(1)} fusion(f32[2,8,512]{2,1,0:T(8,128)S(1)} %subtract_multiply_fusion, f32[8,512,512]{2,1,0:T(8,128)} %param.24), kind=kLoop, calls=%fused_computation.28 | loop fusion | flops 8380416 | bytes 8454144 | tf_op jit(solution)/shard_map/reduce_sum | solution.py:242
  78.2 3.2 %fusion.121 = f32[1,512]{1,0:T(1,128)S(1)} fusion(pred[]{:T(512)S(6)} %eq.143, f32[]{:T(128)} %bitcast.36, f32[]{:T(128)} %get-tuple-element.143, f32[]{:T(128)} %get-tuple-element.144, f32[]{:T(128)} %get-tuple-element.142, f32[]{:T(128)} %get-tuple-element.141), kind=kLoop, calls=%fused_computation.244 | loop fusion | flops 7680 | bytes 2069 | tf_op jit(solution)/shard_map/add | solution.py:270
  81.5 1.3 %collective-permute-start.15 = (f32[33,512]{1,0:T(8,128)S(1)}, f32[33,512]{1,0:T(8,128)S(1)}, u32[]{:S(2)}, u32[]{:S(2)}) collective-permute-start(f32[33,512]{1,0:T(8,128)S(1)} %dynamic-update-slice.16), channel_id=1, source_target_pairs={{16,24},{17,25},{18,26},{19,27},{20,28},{21,29},{22,30},{23,31}} | collective-permute-start | bytes 202760 | tf_op jit(solution)/shard_map/ppermute | solution.py:279
  82.8 1.3 %collective-permute-start.14 = (f32[33,512]{1,0:T(8,128)S(1)}, f32[33,512]{1,0:T(8,128)S(1)}, u32[]{:S(2)}, u32[]{:S(2)}) collective-permute-start(f32[33,512]{1,0:T(8,128)S(1)} %dynamic-update-slice.16), channel_id=1, source_target_pairs={{8,24},{9,25},{10,26},{11,27},{12,28},{13,29},{14,30},{15,31}} | collective-permute-start | bytes 202760 | tf_op jit(solution)/shard_map/ppermute | solution.py:279
  84.0 1.3 %collective-permute-start.13 = (f32[33,512]{1,0:T(8,128)S(1)}, f32[33,512]{1,0:T(8,128)S(1)}, u32[]{:S(2)}, u32[]{:S(2)}) collective-permute-start(f32[33,512]{1,0:T(8,128)S(1)} %dynamic-update-slice.16), channel_id=1, source_target_pairs={{0,24},{1,25},{2,26},{3,27},{4,28},{5,29},{6,30},{7,31}} | collective-permute-start | bytes 202760 | tf_op jit(solution)/shard_map/ppermute | solution.py:279
  86.9 1.1 maximum_select_fusion
  88.1 12.2 %collective-permute-done.15 = f32[33,512]{1,0:T(8,128)S(1)} collective-permute-done((f32[33,512]{1,0:T(8,128)S(1)}, f32[33,512]{1,0:T(8,128)S(1)}, u32[]{:S(2)}, u32[]{:S(2)}) %collective-permute-start.15) | collective-permute-done | bytes 67616 | tf_op jit(solution)/shard_map/ppermute | solution.py:279
  100.3 1.8 %collective-permute-done.14 = f32[33,512]{1,0:T(8,128)S(1)} collective-permute-done((f32[33,512]{1,0:T(8,128)S(1)}, f32[33,512]{1,0:T(8,128)S(1)}, u32[]{:S(2)}, u32[]{:S(2)}) %collective-permute-start.14) | collective-permute-done | bytes 67616 | tf_op jit(solution)/shard_map/ppermute | solution.py:279
  102.0 2.1 %collective-permute-done.13 = f32[33,512]{1,0:T(8,128)S(1)} collective-permute-done((f32[33,512]{1,0:T(8,128)S(1)}, f32[33,512]{1,0:T(8,128)S(1)}, u32[]{:S(2)}, u32[]{:S(2)}) %collective-permute-start.13) | collective-permute-done | bytes 67616 | tf_op jit(solution)/shard_map/ppermute | solution.py:279
  104.9 1.9 %collective-permute-start.16 = (f32[4]{0:T(128)S(1)}, f32[4]{0:T(128)S(1)}, u32[]{:S(2)}, u32[]{:S(2)}) collective-permute-start(f32[4]{0:T(128)S(1)} %slice_bitcast_fusion.2), channel_id=1, source_target_pairs={{24,25},{25,24},{26,27},{27,26},{28,29},{29,28},{30,31},{31,30}} | collective-permute-start | bytes 56 | tf_op jit(solution)/shard_map/ppermute | solution.py:122
  107.9 3.6 %collective-permute-start.17 = (f32[4]{0:T(128)S(1)}, f32[4]{0:T(128)S(1)}, u32[]{:S(2)}, u32[]{:S(2)}) collective-permute-start(f32[4]{0:T(128)S(1)} %fusion.128), channel_id=1, source_target_pairs={{24,26},{25,27},{26,24},{27,25},{28,30},{29,31},{30,28},{31,29}} | collective-permute-start | bytes 56 | tf_op jit(solution)/shard_map/ppermute | solution.py:122
  111.5 1.8 %collective-permute-done.17 = f32[4]{0:T(128)S(1)} collective-permute-done((f32[4]{0:T(128)S(1)}, f32[4]{0:T(128)S(1)}, u32[]{:S(2)}, u32[]{:S(2)}) %collective-permute-start.17) | collective-permute-done | bytes 48 | tf_op jit(solution)/shard_map/ppermute | solution.py:122
  113.3 1.9 %collective-permute-start.18 = (f32[4]{0:T(128)S(1)}, f32[4]{0:T(128)S(1)}, u32[]{:S(2)}, u32[]{:S(2)}) collective-permute-start(f32[4]{0:T(128)S(1)} %add.759), channel_id=1, source_target_pairs={{24,28},{25,29},{26,30},{27,31},{28,24},{29,25},{30,26},{31,27}} | collective-permute-start | bytes 56 | tf_op jit(solution)/shard_map/ppermute | solution.py:122
  115.2 3.5 %collective-permute-done.18 = f32[4]{0:T(128)S(1)} collective-permute-done((f32[4]{0:T(128)S(1)}, f32[4]{0:T(128)S(1)}, u32[]{:S(2)}, u32[]{:S(2)}) %collective-permute-start.18) | collective-permute-done | bytes 48 | tf_op jit(solution)/shard_map/ppermute | solution.py:122
  (202 shorter events, 30.7 us)
Async XLA Ops:
  0.6 4.2 %copy-start.5 = (f32[1,8,64,512]{3,2,1,0:T(8,128)S(1)}, f32[1,8,64,512]{3,2,1,0:T(8,128)}, u32[]{:S(2)}) copy-start(f32[1,8,64,512]{3,2,1,0:T(8,128)} %param.21) | copy-start | bytes 3145732
  4.8 15.8 %copy-start = (f32[1,8,64,512]{3,1,2,0:T(8,128)}, f32[1,8,64,512]{3,1,2,0:T(8,128)S(1)}, u32[]{:S(2)}) copy-start(f32[1,8,64,512]{3,1,2,0:T(8,128)S(1)} %copy.89) | copy-start | bytes 3145732
  4.8 1.6 %copy-start.6 = (f32[1,8,64,512]{3,2,1,0:T(8,128)S(1)}, f32[1,8,64,512]{3,2,1,0:T(8,128)}, u32[]{:S(2)}) copy-start(f32[1,8,64,512]{3,2,1,0:T(8,128)} %param.23) | copy-start | bytes 3145732
  7.1 6.0 %copy-start.14 = (s32[8]{0:T(128)S(1)}, s32[8]{0:T(128)}, u32[]{:S(2)}) copy-start(s32[8]{0:T(128)} %param.29) | copy-start | bytes 100
  8.1 7.3 %collective-permute-start.1 = (f32[100,512]{1,0:T(8,128)S(1)}, f32[100,512]{1,0:T(8,128)S(1)}, u32[]{:S(2)}, u32[]{:S(2)}) collective-permute-start(f32[100,512]{1,0:T(8,128)S(1)} %pad_maximum_fusion.11), channel_id=1, source_target_pairs={{1,0},{2,1},{3,2},{4,3},{5,4},{6,5},{7,6},{9,8},{10,9},{11,10},{12... | collective-permute-start | bytes 614408 | tf_op jit(solution)/shard_map/ppermute | solution.py:63
  10.9 8.1 %collective-permute-start = (f32[100,512]{1,0:T(8,128)S(1)}, f32[100,512]{1,0:T(8,128)S(1)}, u32[]{:S(2)}, u32[]{:S(2)}) collective-permute-start(f32[100,512]{1,0:T(8,128)S(1)} %pad_maximum_fusion.10), channel_id=1, source_target_pairs={{0,1},{1,2},{2,3},{3,4},{4,5},{5,6},{6,7},{8,9},{9,10},{10,11},{11... | collective-permute-start | bytes 614408 | tf_op jit(solution)/shard_map/ppermute | solution.py:62
  19.6 15.6 %copy-start.7 = (f32[16,1,512]{2,0,1:T(8,128)}, f32[16,1,512]{2,0,1:T(8,128)S(1)}, u32[]{:S(2)}) copy-start(f32[16,1,512]{2,0,1:T(8,128)S(1)} %get-tuple-element.164) | copy-start | bytes 98308
  20.0 2.2 %copy-start.2 = (f32[1,8,64,512]{3,1,2,0:T(8,128)S(1)}, f32[1,8,64,512]{3,1,2,0:T(8,128)}, u32[]{:S(2)}) copy-start(f32[1,8,64,512]{3,1,2,0:T(8,128)} %copy-done.1) | copy-start | bytes 3145732
  20.2 6.0 %slice-start = ((s8[8388608]{0:T(1024)(128)(4,1)}), s8[4194304]{0:T(1024)(128)(4,1)S(1)}, s32[]{:S(2)}) async-start(s8[8388608]{0:T(1024)(128)(4,1)} %bitcast.97), calls=%async_computation | async-start | bytes 8388608
  21.2 1.6 %copy-start.3 = (f32[8,56,512]{2,0,1:T(8,128)S(1)}, f32[8,56,512]{2,0,1:T(8,128)}, u32[]{:S(2)}) copy-start(f32[8,56,512]{2,0,1:T(8,128)} %slice.1022) | copy-start | bytes 2752516
  21.2 1.8 %copy-start.4 = (f32[8,56,512]{2,0,1:T(8,128)S(1)}, f32[8,56,512]{2,0,1:T(8,128)}, u32[]{:S(2)}) copy-start(f32[8,56,512]{2,0,1:T(8,128)} %slice.1021) | copy-start | bytes 2752516
  23.0 3.2 %slice-start.1 = ((s8[8388608]{0:T(1024)(128)(4,1)}), s8[4194304]{0:T(1024)(128)(4,1)S(1)}, s32[]{:S(2)}) async-start(s8[8388608]{0:T(1024)(128)(4,1)} %bitcast.97), calls=%async_computation.1 | async-start | bytes 8388608
  23.7 2.4 %copy-start.11 = (f32[8,512]{1,0:T(8,128)S(1)}, f32[8,512]{1,0:T(8,128)}, u32[]{:S(2)}) copy-start(f32[8,512]{1,0:T(8,128)} %param.25) | copy-start | bytes 49156
  23.8 13.3 %collective-permute-start.3 = (f32[224,512]{1,0:T(8,128)S(1)}, f32[224,512]{1,0:T(8,128)S(1)}, u32[]{:S(2)}, u32[]{:S(2)}) collective-permute-start(f32[224,512]{1,0:T(8,128)S(1)} %pad_maximum_fusion.6), channel_id=1, source_target_pairs={{1,0},{2,1},{3,2},{4,3},{5,4},{6,5},{7,6},{9,8},{10,9},{11,10},{12... | collective-permute-start | bytes 1376264 | tf_op jit(solution)/shard_map/ppermute | solution.py:63
  27.1 8.0 %collective-permute-start.5 = (f32[4,512]{1,0:T(4,128)S(1)}, f32[4,512]{1,0:T(4,128)S(1)}, u32[]{:S(2)}, u32[]{:S(2)}) collective-permute-start(f32[4,512]{1,0:T(4,128)S(1)} %get-tuple-element.243), channel_id=1, source_target_pairs={{1,0},{2,1},{3,2},{4,3},{5,4},{6,5},{7,6},{9,8},{10,9},{11,10},{12... | collective-permute-start | bytes 24584 | tf_op jit(solution)/shard_map/ppermute | solution.py:63
  29.1 6.1 %collective-permute-start.4 = (f32[4,512]{1,0:T(4,128)S(1)}, f32[4,512]{1,0:T(4,128)S(1)}, u32[]{:S(2)}, u32[]{:S(2)}) collective-permute-start(f32[4,512]{1,0:T(4,128)S(1)} %get-tuple-element.242), channel_id=1, source_target_pairs={{0,1},{1,2},{2,3},{3,4},{4,5},{5,6},{6,7},{8,9},{9,10},{10,11},{11... | collective-permute-start | bytes 24584 | tf_op jit(solution)/shard_map/ppermute | solution.py:62
  31.5 10.7 %collective-permute-start.2 = (f32[224,512]{1,0:T(8,128)S(1)}, f32[224,512]{1,0:T(8,128)S(1)}, u32[]{:S(2)}, u32[]{:S(2)}) collective-permute-start(f32[224,512]{1,0:T(8,128)S(1)} %pad_maximum_fusion.5), channel_id=1, source_target_pairs={{0,1},{1,2},{2,3},{3,4},{4,5},{5,6},{6,7},{8,9},{9,10},{10,11},{11... | collective-permute-start | bytes 1376264 | tf_op jit(solution)/shard_map/ppermute | solution.py:62
  44.9 10.5 %collective-permute-start.8 = (f32[2]{0:T(128)S(1)}, f32[2]{0:T(128)S(1)}, u32[]{:S(2)}, u32[]{:S(2)}) collective-permute-start(f32[2]{0:T(128)S(1)} %pad_maximum_fusion.14), channel_id=1, source_target_pairs={{0,1},{1,0},{2,3},{3,2},{4,5},{5,4},{6,7},{7,6},{8,9},{9,8},{10,11... | collective-permute-start | bytes 32 | tf_op jit(solution)/shard_map/ppermute | solution.py:111
  49.5 20.5 %copy-start.8 = (f32[16,1,512]{2,0,1:T(8,128)S(1)}, f32[16,1,512]{2,0,1:T(8,128)}, u32[]{:S(2)}) copy-start(f32[16,1,512]{2,0,1:T(8,128)} %copy-done.7) | copy-start | bytes 98308
  50.3 18.9 %collective-permute-start.7 = (f32[136,512]{1,0:T(8,128)}, f32[136,512]{1,0:T(8,128)S(1)}, u32[]{:S(2)}, u32[]{:S(2)}) collective-permute-start(f32[136,512]{1,0:T(8,128)} %pad_maximum_fusion.9), channel_id=1, source_target_pairs={{1,0},{2,1},{3,2},{4,3},{5,4},{6,5},{7,6},{9,8},{10,9},{11,10},{12... | collective-permute-start | bytes 835592 | tf_op jit(solution)/shard_map/ppermute | solution.py:63
  52.9 16.2 %collective-permute-start.6 = (f32[136,512]{1,0:T(8,128)}, f32[136,512]{1,0:T(8,128)}, u32[]{:S(2)}, u32[]{:S(2)}) collective-permute-start(f32[136,512]{1,0:T(8,128)} %pad_maximum_fusion.8), channel_id=1, source_target_pairs={{0,1},{1,2},{2,3},{3,4},{4,5},{5,6},{6,7},{8,9},{9,10},{10,11},{11... | collective-permute-start | bytes 835592 | tf_op jit(solution)/shard_map/ppermute | solution.py:62
  56.7 3.5 %collective-permute-start.9 = (f32[2]{0:T(128)S(1)}, f32[2]{0:T(128)S(1)}, u32[]{:S(2)}, u32[]{:S(2)}) collective-permute-start(f32[2]{0:T(128)S(1)} %fusion.172), channel_id=1, source_target_pairs={{0,2},{1,3},{2,0},{3,1},{4,6},{5,7},{6,4},{7,5},{8,10},{9,11},{10,... | collective-permute-start | bytes 32 | tf_op jit(solution)/shard_map/ppermute | solution.py:111
  61.6 3.5 %collective-permute-start.10 = (f32[2]{0:T(128)S(1)}, f32[2]{0:T(128)S(1)}, u32[]{:S(2)}, u32[]{:S(2)}) collective-permute-start(f32[2]{0:T(128)S(1)} %fusion.173), channel_id=1, source_target_pairs={{0,4},{1,5},{2,6},{3,7},{4,0},{5,1},{6,2},{7,3},{8,12},{9,13},{10,... | collective-permute-start | bytes 32 | tf_op jit(solution)/shard_map/ppermute | solution.py:111
  65.2 1.3 %collective-permute-start.11 = (f32[2]{0:T(128)S(1)}, f32[2]{0:T(128)S(1)}, u32[]{:S(2)}, u32[]{:S(2)}) collective-permute-start(f32[2]{0:T(128)S(1)} %add.743), channel_id=1, source_target_pairs={{0,16},{1,17},{2,18},{3,19},{4,20},{5,21},{6,22},{7,23},{8,0},{9,1... | collective-permute-start | bytes 32 | tf_op jit(solution)/shard_map/ppermute | solution.py:132
  65.9 0.7 collective-permute-start.12
  72.7 12.6 %copy-start.10 = (f32[136,512]{1,0:T(8,128)S(1)}, f32[136,512]{1,0:T(8,128)}, u32[]{:S(2)}) copy-start(f32[136,512]{1,0:T(8,128)} %copy-done.9) | copy-start | bytes 835588
  81.5 18.8 %collective-permute-start.15 = (f32[33,512]{1,0:T(8,128)S(1)}, f32[33,512]{1,0:T(8,128)S(1)}, u32[]{:S(2)}, u32[]{:S(2)}) collective-permute-start(f32[33,512]{1,0:T(8,128)S(1)} %dynamic-update-slice.16), channel_id=1, source_target_pairs={{16,24},{17,25},{18,26},{19,27},{20,28},{21,29},{22,30},{23,31}} | collective-permute-start | bytes 202760 | tf_op jit(solution)/shard_map/ppermute | solution.py:279
  82.8 19.3 %collective-permute-start.14 = (f32[33,512]{1,0:T(8,128)S(1)}, f32[33,512]{1,0:T(8,128)S(1)}, u32[]{:S(2)}, u32[]{:S(2)}) collective-permute-start(f32[33,512]{1,0:T(8,128)S(1)} %dynamic-update-slice.16), channel_id=1, source_target_pairs={{8,24},{9,25},{10,26},{11,27},{12,28},{13,29},{14,30},{15,31}} | collective-permute-start | bytes 202760 | tf_op jit(solution)/shard_map/ppermute | solution.py:279
  84.0 20.1 %collective-permute-start.13 = (f32[33,512]{1,0:T(8,128)S(1)}, f32[33,512]{1,0:T(8,128)S(1)}, u32[]{:S(2)}, u32[]{:S(2)}) collective-permute-start(f32[33,512]{1,0:T(8,128)S(1)} %dynamic-update-slice.16), channel_id=1, source_target_pairs={{0,24},{1,25},{2,26},{3,27},{4,28},{5,29},{6,30},{7,31}} | collective-permute-start | bytes 202760 | tf_op jit(solution)/shard_map/ppermute | solution.py:279
  104.9 3.0 %collective-permute-start.16 = (f32[4]{0:T(128)S(1)}, f32[4]{0:T(128)S(1)}, u32[]{:S(2)}, u32[]{:S(2)}) collective-permute-start(f32[4]{0:T(128)S(1)} %slice_bitcast_fusion.2), channel_id=1, source_target_pairs={{24,25},{25,24},{26,27},{27,26},{28,29},{29,28},{30,31},{31,30}} | collective-permute-start | bytes 56 | tf_op jit(solution)/shard_map/ppermute | solution.py:122
  107.9 5.4 %collective-permute-start.17 = (f32[4]{0:T(128)S(1)}, f32[4]{0:T(128)S(1)}, u32[]{:S(2)}, u32[]{:S(2)}) collective-permute-start(f32[4]{0:T(128)S(1)} %fusion.128), channel_id=1, source_target_pairs={{24,26},{25,27},{26,24},{27,25},{28,30},{29,31},{30,28},{31,29}} | collective-permute-start | bytes 56 | tf_op jit(solution)/shard_map/ppermute | solution.py:122
  113.3 5.4 %collective-permute-start.18 = (f32[4]{0:T(128)S(1)}, f32[4]{0:T(128)S(1)}, u32[]{:S(2)}, u32[]{:S(2)}) collective-permute-start(f32[4]{0:T(128)S(1)} %add.759), channel_id=1, source_target_pairs={{24,28},{25,29},{26,30},{27,31},{28,24},{29,25},{30,26},{31,27}} | collective-permute-start | bytes 56 | tf_op jit(solution)/shard_map/ppermute | solution.py:122
  (4 other events, 3.8 us)

commit v13 on v12

--- a/solution.py
+++ b/solution.py
@@ -257,28 +257,29 @@
     newer = resid_two - resid_one
     partial = jnp.stack(
         [
-            jnp.sum(newer * newer),
-            jnp.sum(newer * diff_one),
-            jnp.sum(newer * resid_two),
-            jnp.sum(diff_one * resid_two),
+            jnp.sum(newer * newer, axis=0),
+            jnp.sum(newer * diff_one, axis=0),
+            jnp.sum(newer * resid_two, axis=0),
+            jnp.sum(diff_one * resid_two, axis=0),
         ]
     )
     patches_here = tilde_two.shape[0]
     outgoing = jnp.concatenate(
         [
-            jnp.concatenate([tilde_two, tilde_one, tilde_zero, resid_two], axis=0),
-            sum(
-                jnp.where(jnp.arange(line_cells) == k, partial[k], 0.0) for k in range(4)
-            )[None]
-            + jnp.where((jnp.arange(line_cells) == 4) & (side_id == 0), gram_aa, 0.0)[None],
+            tilde_two,
+            tilde_one,
+            tilde_zero,
+            resid_two,
+            partial,
+            jnp.where((jnp.arange(line_cells) == 0) & (side_id == 0), gram_aa, 0.0)[None],
         ],
         axis=0,
     )
     gathered = outgoing
     for source in range(side_count - 1):
         gathered = gathered + lax.ppermute(outgoing, "side", [(source, side_count - 1)])
-    sums = shell_sum(gathered[4 * patches_here, :4], side_count)
-    gram_aa = gathered[4 * patches_here, 4]
+    sums = shell_sum(jnp.sum(gathered[4 * patches_here : 4 * patches_here + 4], axis=1), side_count)
+    gram_aa = gathered[4 * patches_here + 4, 0]
     gram_nn, gram_no, proj_new, proj_old = sums[0], sums[1], sums[2], sums[3]
     tilde_two, tilde_one, tilde_zero, resid_two = (
         gathered[k * patches_here : (k + 1) * patches_here] for k in range(4)

time: 129 us -> 129 us (level)
  other arithmetic: 28.7 us -> 25.8 us
  local copies, waits for them, and re-layouts: 16.6 us -> 19.5 us
    add x1 -> x0, other arithmetic: 3.18 us -> none  [body(): sum((jnp.where(jnp.arange(line_cells) == k, partial[k], 0.0) for k in ran...]
    slice x5, local copies, waits for them, and re-layouts: 1.84 us -> 3.69 us  [exchange(): low[at:at + n].reshape(shape)]
where the time goes in v13:
time: 129 us; the launch traced here: 127 us
  waiting for transfers between devices  36.5 us (28%)
  starting transfers between devices  33.1 us (26%)
  other arithmetic  25.8 us (20%)
  local copies, waits for them, and re-layouts  19.5 us (15%)
  between operations  12.1 us (9%)
    ppermute x3, waiting for transfers between devices, body(): lax.ppermute(outgoing, 'side', [(source, side_count - 1)])  16.1 us
    ppermute x4, starting transfers between devices, exchange(): low = lax.ppermute(up, 'slab', forward)  10.4 us
    ppermute x4, starting transfers between devices, exchange(): high = lax.ppermute(down, 'slab', backward)  8.52 us
    ppermute x4, waiting for transfers between devices, exchange(): low = lax.ppermute(up, 'slab', forward)  8.51 us
    ppermute x3, starting transfers between devices, shell_sum(): v = v + lax.ppermute(v, ('side', 'slab'), pairs)  7.41 us
    ppermute x3, waiting for transfers between devices, shell_sum(): v = v + lax.ppermute(v, ('side', 'slab'), pairs)  6.42 us
    unnamed x43, local copies, waits for them, and re-layouts  6.09 us
    ppermute x3, waiting for transfers between devices, allsum_axis(): v = v + lax.ppermute(v, axis, [(i, i ^ step) for i in range(count)])  5.45 us
  transfers between devices with their start and end apart: 19, of which 10 were waited for; matrix products, arithmetic and copies ran while one was open for 14% of the time, Pallas kernels for 0%

profile of v13, /device:TPU:28, one launch (start us, length us, event | category | flops | bytes accessed | tf_op | source)
XLA Modules:
  0.0 127.2 jit_solution(1823849422116524133)
XLA Ops:
  3.0 1.8 %copy.89 = f32[1,8,64,512]{3,1,2,0:T(8,128)S(1)} copy(f32[1,8,64,512]{3,2,1,0:T(8,128)} %param.22) | data formatting | bytes 2097152 | tf_op args[1]
  8.0 2.8 %collective-permute-start.1 = (f32[100,512]{1,0:T(8,128)S(1)}, f32[100,512]{1,0:T(8,128)S(1)}, u32[]{:S(2)}, u32[]{:S(2)}) collective-permute-start(f32[100,512]{1,0:T(8,128)S(1)} %pad_maximum_fusion.11), channel_id=1, source_target_pairs={{1,0},{2,1},{3,2},{4,3},{5,4},{6,5},{7,6},{9,8},{10,9},{11,10},{12... | collective-permute-start | bytes 614408 | tf_op jit(solution)/shard_map/ppermute | solution.py:63
  10.9 1.9 %collective-permute-start = (f32[100,512]{1,0:T(8,128)S(1)}, f32[100,512]{1,0:T(8,128)}, u32[]{:S(2)}, u32[]{:S(2)}) collective-permute-start(f32[100,512]{1,0:T(8,128)S(1)} %pad_maximum_fusion.10), channel_id=1, source_target_pairs={{0,1},{1,2},{2,3},{3,4},{4,5},{5,6},{6,7},{8,9},{9,10},{10,11},{11... | collective-permute-start | bytes 614408 | tf_op jit(solution)/shard_map/ppermute | solution.py:62
  15.5 3.6 %collective-permute-done = f32[100,512]{1,0:T(8,128)} collective-permute-done((f32[100,512]{1,0:T(8,128)S(1)}, f32[100,512]{1,0:T(8,128)}, u32[]{:S(2)}, u32[]{:S(2)}) %collective-permute-start) | collective-permute-done | bytes 204832 | tf_op jit(solution)/shard_map/ppermute | solution.py:62
  27.6 1.9 %collective-permute-start.3 = (f32[224,512]{1,0:T(8,128)S(1)}, f32[224,512]{1,0:T(8,128)S(1)}, u32[]{:S(2)}, u32[]{:S(2)}) collective-permute-start(f32[224,512]{1,0:T(8,128)S(1)} %pad_maximum_fusion.6), channel_id=1, source_target_pairs={{1,0},{2,1},{3,2},{4,3},{5,4},{6,5},{7,6},{9,8},{10,9},{11,10},{12... | collective-permute-start | bytes 1376264 | tf_op jit(solution)/shard_map/ppermute | solution.py:63
  29.8 1.9 %collective-permute-start.5 = (f32[4,512]{1,0:T(4,128)S(1)}, f32[4,512]{1,0:T(4,128)S(1)}, u32[]{:S(2)}, u32[]{:S(2)}) collective-permute-start(f32[4,512]{1,0:T(4,128)S(1)} %get-tuple-element.245), channel_id=1, source_target_pairs={{1,0},{2,1},{3,2},{4,3},{5,4},{6,5},{7,6},{9,8},{10,9},{11,10},{12... | collective-permute-start | bytes 24584 | tf_op jit(solution)/shard_map/ppermute | solution.py:63
  31.7 2.4 %collective-permute-start.4 = (f32[4,512]{1,0:T(4,128)S(1)}, f32[4,512]{1,0:T(4,128)S(1)}, u32[]{:S(2)}, u32[]{:S(2)}) collective-permute-start(f32[4,512]{1,0:T(4,128)S(1)} %get-tuple-element.244), channel_id=1, source_target_pairs={{0,1},{1,2},{2,3},{3,4},{4,5},{5,6},{6,7},{8,9},{9,10},{10,11},{11... | collective-permute-start | bytes 24584 | tf_op jit(solution)/shard_map/ppermute | solution.py:62
  34.2 3.6 %collective-permute-start.2 = (f32[224,512]{1,0:T(8,128)S(1)}, f32[224,512]{1,0:T(8,128)S(1)}, u32[]{:S(2)}, u32[]{:S(2)}) collective-permute-start(f32[224,512]{1,0:T(8,128)S(1)} %pad_maximum_fusion.5), channel_id=1, source_target_pairs={{0,1},{1,2},{2,3},{3,4},{4,5},{5,6},{6,7},{8,9},{9,10},{10,11},{11... | collective-permute-start | bytes 1376264 | tf_op jit(solution)/shard_map/ppermute | solution.py:62
  40.0 4.9 %collective-permute-done.2 = f32[224,512]{1,0:T(8,128)S(1)} collective-permute-done((f32[224,512]{1,0:T(8,128)S(1)}, f32[224,512]{1,0:T(8,128)S(1)}, u32[]{:S(2)}, u32[]{:S(2)}) %collective-permute-start.2) | collective-permute-done | bytes 458784 | tf_op jit(solution)/shard_map/ppermute | solution.py:62
  46.2 1.4 %pad_maximum_fusion.14 = f32[2]{0:T(128)S(1)} fusion(f32[1]{0:T(128)} %bitcast.34, f32[1]{0:T(128)} %bitcast.33), kind=kLoop, calls=%fused_computation.251 | loop fusion | flops 2 | bytes 16 | tf_op jit(solution)/shard_map/stack | solution.py:227
  49.5 2.9 %pad_maximum_fusion.1 = (f32[10,64,512]{2,0,1:T(8,128)}, f32[10,64,512]{2,0,1:T(8,128)}) fusion(f32[10,56,512]{2,0,1:T(8,128)S(1)} %get-tuple-element.187, f32[10,8,512]{2,0,1:T(8,128)S(1)} %get-tuple-element.199, f32[10,56,512]{2,0,1:T(8,128)S(1)} %get-tuple-element.186, f32[10,8,512]{2,0,1:T(8,128)S(1)} %get-tuple-element.198), kind=kLoop, calls=%fused_computation.33 | loop fusion | flops 655360 | bytes 5242880 | tf_op jit(solution)/shard_map/concatenate | solution.py:187
  53.4 1.9 %collective-permute-start.7 = (f32[136,512]{1,0:T(8,128)}, f32[136,512]{1,0:T(8,128)S(1)}, u32[]{:S(2)}, u32[]{:S(2)}) collective-permute-start(f32[136,512]{1,0:T(8,128)} %pad_maximum_fusion.9), channel_id=1, source_target_pairs={{1,0},{2,1},{3,2},{4,3},{5,4},{6,5},{7,6},{9,8},{10,9},{11,10},{12... | collective-permute-start | bytes 835592 | tf_op jit(solution)/shard_map/ppermute | solution.py:63
  56.0 2.4 %collective-permute-start.6 = (f32[136,512]{1,0:T(8,128)}, f32[136,512]{1,0:T(8,128)}, u32[]{:S(2)}, u32[]{:S(2)}) collective-permute-start(f32[136,512]{1,0:T(8,128)} %pad_maximum_fusion.8), channel_id=1, source_target_pairs={{0,1},{1,2},{2,3},{3,4},{4,5},{5,6},{6,7},{8,9},{9,10},{10,11},{11... | collective-permute-start | bytes 835592 | tf_op jit(solution)/shard_map/ppermute | solution.py:62
  58.4 1.4 %fusion.169 = f32[2]{0:T(128)S(1)} fusion(f32[2]{0:T(128)S(1)} %collective-permute-done.8, f32[1]{0:T(128)} %bitcast.34, f32[1]{0:T(128)} %bitcast.33), kind=kLoop, calls=%fused_computation.292 | loop fusion | flops 4 | bytes 24 | tf_op jit(solution)/shard_map/add | solution.py:111
  59.8 1.6 %collective-permute-start.9 = (f32[2]{0:T(128)S(1)}, f32[2]{0:T(128)S(1)}, u32[]{:S(2)}, u32[]{:S(2)}) collective-permute-start(f32[2]{0:T(128)S(1)} %fusion.169), channel_id=1, source_target_pairs={{0,2},{1,3},{2,0},{3,1},{4,6},{5,7},{6,4},{7,5},{8,10},{9,11},{10,... | collective-permute-start | bytes 32 | tf_op jit(solution)/shard_map/ppermute | solution.py:111
  61.4 1.9 %collective-permute-done.9 = f32[2]{0:T(128)S(1)} collective-permute-done((f32[2]{0:T(128)S(1)}, f32[2]{0:T(128)S(1)}, u32[]{:S(2)}, u32[]{:S(2)}) %collective-permute-start.9) | collective-permute-done | bytes 40 | tf_op jit(solution)/shard_map/ppermute | solution.py:111
  63.3 1.4 %fusion.170 = f32[2]{0:T(128)S(1)} fusion(f32[2]{0:T(128)S(1)} %collective-permute-done.9, f32[2]{0:T(128)S(1)} %collective-permute-done.8, f32[1]{0:T(128)} %bitcast.34, f32[1]{0:T(128)} %bitcast.33), kind=kLoop, calls=%fused_computation.293 | loop fusion | flops 6 | bytes 32 | tf_op jit(solution)/shard_map/add | solution.py:111
  64.7 3.5 %collective-permute-done.10 = f32[2]{0:T(128)S(1)} collective-permute-done((f32[2]{0:T(128)S(1)}, f32[2]{0:T(128)S(1)}, u32[]{:S(2)}, u32[]{:S(2)}) %collective-permute-start.10) | collective-permute-done | bytes 40 | tf_op jit(solution)/shard_map/ppermute | solution.py:111
  76.4 4.6 %multiply_reduce_fusion = f32[2,8,512]{2,1,0:T(8,128)S(1)} fusion(f32[2,8,512]{2,1,0:T(8,128)S(1)} %subtract_multiply_fusion, f32[8,512,512]{2,1,0:T(8,128)} %param.24), kind=kLoop, calls=%fused_computation.28 | loop fusion | flops 8380416 | bytes 8454144 | tf_op jit(solution)/shard_map/reduce_sum | solution.py:242
  81.2 1.3 %collective-permute-start.15 = (f32[37,512]{1,0:T(8,128)S(1)}, f32[37,512]{1,0:T(8,128)S(1)}, u32[]{:S(2)}, u32[]{:S(2)}) collective-permute-start(f32[37,512]{1,0:T(8,128)S(1)} %concatenate.312), channel_id=1, source_target_pairs={{16,24},{17,25},{18,26},{19,27},{20,28},{21,29},{22,30},{23,31}} | collective-permute-start | bytes 227336 | tf_op jit(solution)/shard_map/ppermute | solution.py:280
  82.5 1.3 %collective-permute-start.14 = (f32[37,512]{1,0:T(8,128)S(1)}, f32[37,512]{1,0:T(8,128)S(1)}, u32[]{:S(2)}, u32[]{:S(2)}) collective-permute-start(f32[37,512]{1,0:T(8,128)S(1)} %concatenate.312), channel_id=1, source_target_pairs={{8,24},{9,25},{10,26},{11,27},{12,28},{13,29},{14,30},{15,31}} | collective-permute-start | bytes 227336 | tf_op jit(solution)/shard_map/ppermute | solution.py:280
  83.8 1.3 %collective-permute-start.13 = (f32[37,512]{1,0:T(8,128)S(1)}, f32[37,512]{1,0:T(8,128)S(1)}, u32[]{:S(2)}, u32[]{:S(2)}) collective-permute-start(f32[37,512]{1,0:T(8,128)S(1)} %concatenate.312), channel_id=1, source_target_pairs={{0,24},{1,25},{2,26},{3,27},{4,28},{5,29},{6,30},{7,31}} | collective-permute-start | bytes 227336 | tf_op jit(solution)/shard_map/ppermute | solution.py:280
  86.7 1.1 maximum_select_fusion
  87.8 12.2 %collective-permute-done.15 = f32[37,512]{1,0:T(8,128)S(1)} collective-permute-done((f32[37,512]{1,0:T(8,128)S(1)}, f32[37,512]{1,0:T(8,128)S(1)}, u32[]{:S(2)}, u32[]{:S(2)}) %collective-permute-start.15) | collective-permute-done | bytes 75808 | tf_op jit(solution)/shard_map/ppermute | solution.py:280
  100.0 1.8 %collective-permute-done.14 = f32[37,512]{1,0:T(8,128)S(1)} collective-permute-done((f32[37,512]{1,0:T(8,128)S(1)}, f32[37,512]{1,0:T(8,128)S(1)}, u32[]{:S(2)}, u32[]{:S(2)}) %collective-permute-start.14) | collective-permute-done | bytes 75808 | tf_op jit(solution)/shard_map/ppermute | solution.py:280
  101.8 2.1 %collective-permute-done.13 = f32[37,512]{1,0:T(8,128)S(1)} collective-permute-done((f32[37,512]{1,0:T(8,128)S(1)}, f32[37,512]{1,0:T(8,128)S(1)}, u32[]{:S(2)}, u32[]{:S(2)}) %collective-permute-start.13) | collective-permute-done | bytes 75808 | tf_op jit(solution)/shard_map/ppermute | solution.py:280
  104.5 1.9 %collective-permute-start.16 = (f32[4]{0:T(128)S(1)}, f32[4]{0:T(128)S(1)}, u32[]{:S(2)}, u32[]{:S(2)}) collective-permute-start(f32[4]{0:T(128)S(1)} %slice_reduce_fusion), channel_id=1, source_target_pairs={{24,25},{25,24},{26,27},{27,26},{28,29},{29,28},{30,31},{31,30}} | collective-permute-start | bytes 56 | tf_op jit(solution)/shard_map/ppermute | solution.py:122
  106.4 1.1 collective-permute-done.16
  107.5 3.6 %collective-permute-start.17 = (f32[4]{0:T(128)S(1)}, f32[4]{0:T(128)S(1)}, u32[]{:S(2)}, u32[]{:S(2)}) collective-permute-start(f32[4]{0:T(128)S(1)} %add.713), channel_id=1, source_target_pairs={{24,26},{25,27},{26,24},{27,25},{28,30},{29,31},{30,28},{31,29}} | collective-permute-start | bytes 56 | tf_op jit(solution)/shard_map/ppermute | solution.py:122
  111.1 1.8 %collective-permute-done.17 = f32[4]{0:T(128)S(1)} collective-permute-done((f32[4]{0:T(128)S(1)}, f32[4]{0:T(128)S(1)}, u32[]{:S(2)}, u32[]{:S(2)}) %collective-permute-start.17) | collective-permute-done | bytes 48 | tf_op jit(solution)/shard_map/ppermute | solution.py:122
  113.0 1.9 %collective-permute-start.18 = (f32[4]{0:T(128)S(1)}, f32[4]{0:T(128)S(1)}, u32[]{:S(2)}, u32[]{:S(2)}) collective-permute-start(f32[4]{0:T(128)S(1)} %add.714), channel_id=1, source_target_pairs={{24,28},{25,29},{26,30},{27,31},{28,24},{29,25},{30,26},{31,27}} | collective-permute-start | bytes 56 | tf_op jit(solution)/shard_map/ppermute | solution.py:122
  114.9 3.5 %collective-permute-done.18 = f32[4]{0:T(128)S(1)} collective-permute-done((f32[4]{0:T(128)S(1)}, f32[4]{0:T(128)S(1)}, u32[]{:S(2)}, u32[]{:S(2)}) %collective-permute-start.18) | collective-permute-done | bytes 48 | tf_op jit(solution)/shard_map/ppermute | solution.py:122
  (202 shorter events, 32.5 us)
Async XLA Ops:
  0.6 4.2 %copy-start.5 = (f32[1,8,64,512]{3,2,1,0:T(8,128)S(1)}, f32[1,8,64,512]{3,2,1,0:T(8,128)}, u32[]{:S(2)}) copy-start(f32[1,8,64,512]{3,2,1,0:T(8,128)} %param.21) | copy-start | bytes 3145732
  4.8 18.4 %copy-start = (f32[1,8,64,512]{3,1,2,0:T(8,128)}, f32[1,8,64,512]{3,1,2,0:T(8,128)S(1)}, u32[]{:S(2)}) copy-start(f32[1,8,64,512]{3,1,2,0:T(8,128)S(1)} %copy.89) | copy-start | bytes 3145732
  4.8 1.6 %copy-start.6 = (f32[1,8,64,512]{3,2,1,0:T(8,128)S(1)}, f32[1,8,64,512]{3,2,1,0:T(8,128)}, u32[]{:S(2)}) copy-start(f32[1,8,64,512]{3,2,1,0:T(8,128)} %param.23) | copy-start | bytes 3145732
  7.1 6.0 %copy-start.15 = (s32[8]{0:T(128)S(1)}, s32[8]{0:T(128)}, u32[]{:S(2)}) copy-start(s32[8]{0:T(128)} %param.29) | copy-start | bytes 100
  8.0 7.3 %collective-permute-start.1 = (f32[100,512]{1,0:T(8,128)S(1)}, f32[100,512]{1,0:T(8,128)S(1)}, u32[]{:S(2)}, u32[]{:S(2)}) collective-permute-start(f32[100,512]{1,0:T(8,128)S(1)} %pad_maximum_fusion.11), channel_id=1, source_target_pairs={{1,0},{2,1},{3,2},{4,3},{5,4},{6,5},{7,6},{9,8},{10,9},{11,10},{12... | collective-permute-start | bytes 614408 | tf_op jit(solution)/shard_map/ppermute | solution.py:63
  10.9 8.2 %collective-permute-start = (f32[100,512]{1,0:T(8,128)S(1)}, f32[100,512]{1,0:T(8,128)}, u32[]{:S(2)}, u32[]{:S(2)}) collective-permute-start(f32[100,512]{1,0:T(8,128)S(1)} %pad_maximum_fusion.10), channel_id=1, source_target_pairs={{0,1},{1,2},{2,3},{3,4},{4,5},{5,6},{6,7},{8,9},{9,10},{10,11},{11... | collective-permute-start | bytes 614408 | tf_op jit(solution)/shard_map/ppermute | solution.py:62
  15.3 5.0 %copy-start.11 = (f32[100,512]{1,0:T(8,128)}, f32[100,512]{1,0:T(8,128)S(1)}, u32[]{:S(2)}) copy-start(f32[100,512]{1,0:T(8,128)S(1)} %collective-permute-done.1) | copy-start | bytes 614404
  20.2 4.0 %slice-start = ((s8[8388608]{0:T(1024)(128)(4,1)}), s8[4194304]{0:T(1024)(128)(4,1)S(1)}, s32[]{:S(2)}) async-start(s8[8388608]{0:T(1024)(128)(4,1)} %bitcast.93), calls=%async_computation | async-start | bytes 8388608
  20.4 1.8 %slice-start.2 = ((f32[100,512]{1,0:T(8,128)}), f32[4,512]{1,0:T(4,128)S(1)}, s32[]{:S(2)}) async-start(f32[100,512]{1,0:T(8,128)} %copy-done.11), calls=%async_computation.2 | async-start | bytes 16384 | tf_op jit(solution)/shard_map/slice | solution.py:68
  22.2 15.7 %copy-start.7 = (f32[16,1,512]{2,0,1:T(8,128)}, f32[16,1,512]{2,0,1:T(8,128)S(1)}, u32[]{:S(2)}) copy-start(f32[16,1,512]{2,0,1:T(8,128)S(1)} %get-tuple-element.167) | copy-start | bytes 98308
  22.4 2.2 %slice-start.1 = ((s8[8388608]{0:T(1024)(128)(4,1)}), s8[4194304]{0:T(1024)(128)(4,1)S(1)}, s32[]{:S(2)}) async-start(s8[8388608]{0:T(1024)(128)(4,1)} %bitcast.93), calls=%async_computation.1 | async-start | bytes 8388608
  24.6 1.6 %copy-start.2 = (f32[1,8,64,512]{3,1,2,0:T(8,128)S(1)}, f32[1,8,64,512]{3,1,2,0:T(8,128)}, u32[]{:S(2)}) copy-start(f32[1,8,64,512]{3,1,2,0:T(8,128)} %copy-done.1) | copy-start | bytes 3145732
  25.4 1.5 %copy-start.4 = (f32[8,56,512]{2,0,1:T(8,128)S(1)}, f32[8,56,512]{2,0,1:T(8,128)}, u32[]{:S(2)}) copy-start(f32[8,56,512]{2,0,1:T(8,128)} %slice.1021) | copy-start | bytes 2752516
  27.6 12.1 %collective-permute-start.3 = (f32[224,512]{1,0:T(8,128)S(1)}, f32[224,512]{1,0:T(8,128)S(1)}, u32[]{:S(2)}, u32[]{:S(2)}) collective-permute-start(f32[224,512]{1,0:T(8,128)S(1)} %pad_maximum_fusion.6), channel_id=1, source_target_pairs={{1,0},{2,1},{3,2},{4,3},{5,4},{6,5},{7,6},{9,8},{10,9},{11,10},{12... | collective-permute-start | bytes 1376264 | tf_op jit(solution)/shard_map/ppermute | solution.py:63
  29.8 8.0 %collective-permute-start.5 = (f32[4,512]{1,0:T(4,128)S(1)}, f32[4,512]{1,0:T(4,128)S(1)}, u32[]{:S(2)}, u32[]{:S(2)}) collective-permute-start(f32[4,512]{1,0:T(4,128)S(1)} %get-tuple-element.245), channel_id=1, source_target_pairs={{1,0},{2,1},{3,2},{4,3},{5,4},{6,5},{7,6},{9,8},{10,9},{11,10},{12... | collective-permute-start | bytes 24584 | tf_op jit(solution)/shard_map/ppermute | solution.py:63
  31.7 6.1 %collective-permute-start.4 = (f32[4,512]{1,0:T(4,128)S(1)}, f32[4,512]{1,0:T(4,128)S(1)}, u32[]{:S(2)}, u32[]{:S(2)}) collective-permute-start(f32[4,512]{1,0:T(4,128)S(1)} %get-tuple-element.244), channel_id=1, source_target_pairs={{0,1},{1,2},{2,3},{3,4},{4,5},{5,6},{6,7},{8,9},{9,10},{10,11},{11... | collective-permute-start | bytes 24584 | tf_op jit(solution)/shard_map/ppermute | solution.py:62
  34.2 10.7 %collective-permute-start.2 = (f32[224,512]{1,0:T(8,128)S(1)}, f32[224,512]{1,0:T(8,128)S(1)}, u32[]{:S(2)}, u32[]{:S(2)}) collective-permute-start(f32[224,512]{1,0:T(8,128)S(1)} %pad_maximum_fusion.5), channel_id=1, source_target_pairs={{0,1},{1,2},{2,3},{3,4},{4,5},{5,6},{6,7},{8,9},{9,10},{10,11},{11... | collective-permute-start | bytes 1376264 | tf_op jit(solution)/shard_map/ppermute | solution.py:62
  47.5 10.9 %collective-permute-start.8 = (f32[2]{0:T(128)S(1)}, f32[2]{0:T(128)S(1)}, u32[]{:S(2)}, u32[]{:S(2)}) collective-permute-start(f32[2]{0:T(128)S(1)} %pad_maximum_fusion.14), channel_id=1, source_target_pairs={{0,1},{1,0},{2,3},{3,2},{4,5},{5,4},{6,7},{7,6},{8,9},{9,8},{10,11... | collective-permute-start | bytes 32 | tf_op jit(solution)/shard_map/ppermute | solution.py:111
  52.6 21.1 %copy-start.8 = (f32[16,1,512]{2,0,1:T(8,128)S(1)}, f32[16,1,512]{2,0,1:T(8,128)}, u32[]{:S(2)}) copy-start(f32[16,1,512]{2,0,1:T(8,128)} %copy-done.7) | copy-start | bytes 98308
  53.4 19.5 %collective-permute-start.7 = (f32[136,512]{1,0:T(8,128)}, f32[136,512]{1,0:T(8,128)S(1)}, u32[]{:S(2)}, u32[]{:S(2)}) collective-permute-start(f32[136,512]{1,0:T(8,128)} %pad_maximum_fusion.9), channel_id=1, source_target_pairs={{1,0},{2,1},{3,2},{4,3},{5,4},{6,5},{7,6},{9,8},{10,9},{11,10},{12... | collective-permute-start | bytes 835592 | tf_op jit(solution)/shard_map/ppermute | solution.py:63
  56.0 16.9 %collective-permute-start.6 = (f32[136,512]{1,0:T(8,128)}, f32[136,512]{1,0:T(8,128)}, u32[]{:S(2)}, u32[]{:S(2)}) collective-permute-start(f32[136,512]{1,0:T(8,128)} %pad_maximum_fusion.8), channel_id=1, source_target_pairs={{0,1},{1,2},{2,3},{3,4},{4,5},{5,6},{6,7},{8,9},{9,10},{10,11},{11... | collective-permute-start | bytes 835592 | tf_op jit(solution)/shard_map/ppermute | solution.py:62
  59.8 3.5 %collective-permute-start.9 = (f32[2]{0:T(128)S(1)}, f32[2]{0:T(128)S(1)}, u32[]{:S(2)}, u32[]{:S(2)}) collective-permute-start(f32[2]{0:T(128)S(1)} %fusion.169), channel_id=1, source_target_pairs={{0,2},{1,3},{2,0},{3,1},{4,6},{5,7},{6,4},{7,5},{8,10},{9,11},{10,... | collective-permute-start | bytes 32 | tf_op jit(solution)/shard_map/ppermute | solution.py:111
  64.7 3.5 %collective-permute-start.10 = (f32[2]{0:T(128)S(1)}, f32[2]{0:T(128)S(1)}, u32[]{:S(2)}, u32[]{:S(2)}) collective-permute-start(f32[2]{0:T(128)S(1)} %fusion.170), channel_id=1, source_target_pairs={{0,4},{1,5},{2,6},{3,7},{4,0},{5,1},{6,2},{7,3},{8,12},{9,13},{10,... | collective-permute-start | bytes 32 | tf_op jit(solution)/shard_map/ppermute | solution.py:111
  68.3 1.3 %collective-permute-start.11 = (f32[2]{0:T(128)S(1)}, f32[2]{0:T(128)S(1)}, u32[]{:S(2)}, u32[]{:S(2)}) collective-permute-start(f32[2]{0:T(128)S(1)} %add.702), channel_id=1, source_target_pairs={{0,16},{1,17},{2,18},{3,19},{4,20},{5,21},{6,22},{7,23},{8,0},{9,1... | collective-permute-start | bytes 32 | tf_op jit(solution)/shard_map/ppermute | solution.py:132
  68.9 0.7 collective-permute-start.12
  76.4 8.6 %copy-start.10 = (f32[136,512]{1,0:T(8,128)S(1)}, f32[136,512]{1,0:T(8,128)}, u32[]{:S(2)}) copy-start(f32[136,512]{1,0:T(8,128)} %copy-done.9) | copy-start | bytes 835588
  81.2 18.8 %collective-permute-start.15 = (f32[37,512]{1,0:T(8,128)S(1)}, f32[37,512]{1,0:T(8,128)S(1)}, u32[]{:S(2)}, u32[]{:S(2)}) collective-permute-start(f32[37,512]{1,0:T(8,128)S(1)} %concatenate.312), channel_id=1, source_target_pairs={{16,24},{17,25},{18,26},{19,27},{20,28},{21,29},{22,30},{23,31}} | collective-permute-start | bytes 227336 | tf_op jit(solution)/shard_map/ppermute | solution.py:280
  82.5 19.3 %collective-permute-start.14 = (f32[37,512]{1,0:T(8,128)S(1)}, f32[37,512]{1,0:T(8,128)S(1)}, u32[]{:S(2)}, u32[]{:S(2)}) collective-permute-start(f32[37,512]{1,0:T(8,128)S(1)} %concatenate.312), channel_id=1, source_target_pairs={{8,24},{9,25},{10,26},{11,27},{12,28},{13,29},{14,30},{15,31}} | collective-permute-start | bytes 227336 | tf_op jit(solution)/shard_map/ppermute | solution.py:280
  83.8 20.1 %collective-permute-start.13 = (f32[37,512]{1,0:T(8,128)S(1)}, f32[37,512]{1,0:T(8,128)S(1)}, u32[]{:S(2)}, u32[]{:S(2)}) collective-permute-start(f32[37,512]{1,0:T(8,128)S(1)} %concatenate.312), channel_id=1, source_target_pairs={{0,24},{1,25},{2,26},{3,27},{4,28},{5,29},{6,30},{7,31}} | collective-permute-start | bytes 227336 | tf_op jit(solution)/shard_map/ppermute | solution.py:280
  104.5 3.0 %collective-permute-start.16 = (f32[4]{0:T(128)S(1)}, f32[4]{0:T(128)S(1)}, u32[]{:S(2)}, u32[]{:S(2)}) collective-permute-start(f32[4]{0:T(128)S(1)} %slice_reduce_fusion), channel_id=1, source_target_pairs={{24,25},{25,24},{26,27},{27,26},{28,29},{29,28},{30,31},{31,30}} | collective-permute-start | bytes 56 | tf_op jit(solution)/shard_map/ppermute | solution.py:122
  107.5 5.4 %collective-permute-start.17 = (f32[4]{0:T(128)S(1)}, f32[4]{0:T(128)S(1)}, u32[]{:S(2)}, u32[]{:S(2)}) collective-permute-start(f32[4]{0:T(128)S(1)} %add.713), channel_id=1, source_target_pairs={{24,26},{25,27},{26,24},{27,25},{28,30},{29,31},{30,28},{31,29}} | collective-permute-start | bytes 56 | tf_op jit(solution)/shard_map/ppermute | solution.py:122
  113.0 5.4 %collective-permute-start.18 = (f32[4]{0:T(128)S(1)}, f32[4]{0:T(128)S(1)}, u32[]{:S(2)}, u32[]{:S(2)}) collective-permute-start(f32[4]{0:T(128)S(1)} %add.714), channel_id=1, source_target_pairs={{24,28},{25,29},{26,30},{27,31},{28,24},{29,25},{30,26},{31,27}} | collective-permute-start | bytes 56 | tf_op jit(solution)/shard_map/ppermute | solution.py:122
  (6 other events, 6.1 us)

commit v14 on v13

--- a/solution.py
+++ b/solution.py
@@ -229,9 +229,7 @@
         side_count - 1,
     )
     step_one = tilde_one - tilde_zero
-    rims_base, rims_step, deep = exchange(
-        [(plane_of(tilde_one), HALO), (plane_of(step_one), HALO), (deep, 2)]
-    )
+    rims_base, rims_step = exchange([(plane_of(tilde_one), HALO), (plane_of(step_one), HALO)])
     band_base = band_solve(init_band, force_band.at[:, 0, :].add(rims_base), coef_band, row_ok)
     band_step = band_solve(
         jnp.zeros_like(init_band), jnp.zeros_like(force_band).at[:, 0, :].set(rims_step), coef_band, row_ok
@@ -246,13 +244,6 @@
     disp_two = tilde_one + coeff * step_one
     tilde_two = tilde_base + coeff * tilde_step
     band_two = band_base + coeff * band_step
-    deep = lax.cond(
-        shell_flag,
-        lambda: jnp.zeros((slab_rows,) + deep.shape[1:], jnp.float32),
-        lambda: deep_step(
-            deep_step(deep, force_deep, coef_deep, ok_one), force_deep[1:-1], coef_deep[1:-1], ok_two
-        ),
-    )
     resid_two = tilde_two - disp_two
     newer = resid_two - resid_one
     partial = jnp.stack(
@@ -274,6 +265,14 @@
             jnp.where((jnp.arange(line_cells) == 0) & (side_id == 0), gram_aa, 0.0)[None],
         ],
         axis=0,
+    )
+    (deep,) = exchange([(deep + 0.0 * outgoing[0, 0], 2)])
+    deep = lax.cond(
+        shell_flag,
+        lambda: jnp.zeros((slab_rows,) + deep.shape[1:], jnp.float32),
+        lambda: deep_step(
+            deep_step(deep, force_deep, coef_deep, ok_one), force_deep[1:-1], coef_deep[1:-1], ok_two
+        ),
     )
     gathered = outgoing
     for source in range(side_count - 1):

time: 129 us -> 134 us (1.039)
  starting transfers between devices: 33.1 us -> 38.9 us
  waiting for transfers between devices: 36.5 us -> 32.1 us
  other arithmetic: 25.8 us -> 27.5 us
    ppermute x4 -> x5, starting transfers between devices: 8.52 us -> 13.9 us  [exchange(): high = lax.ppermute(down, 'slab', backward)]
    ppermute x3, waiting for transfers between devices: 16.1 us -> 12 us  [body(): lax.ppermute(outgoing, 'side', [(source, side_count - 1)])]
    slice x4, local copies, waits for them, and re-layouts: 0.3 us -> 1.91 us  [band_solve(): q = jnp.where(row_ok[k:rows - k], new, 0.0)]
    slice x5 -> x4, local copies, waits for them, and re-layouts: 3.69 us -> 2.49 us  [exchange(): low[at:at + n].reshape(shape)]
    unnamed x43 -> x73, local copies, waits for them, and re-layouts: 6.09 us -> 6.6 us
    ppermute x4 -> x5, starting transfers between devices: 10.4 us -> 10.6 us  [exchange(): low = lax.ppermute(up, 'slab', forward)]
    ppermute x4 -> x5, waiting for transfers between devices: 8.51 us -> 8.35 us  [exchange(): low = lax.ppermute(up, 'slab', forward)]
  transfers between devices with their start and end apart: 19 -> 21, of which waited for: 10 -> 9; matrix products, arithmetic and copies ran while one was open for 14% -> 16% of each run, Pallas kernels for 0% -> 0%
where the time goes in v14:
time: 134 us; the launch traced here: 132 us
  starting transfers between devices  38.9 us (29%)
  waiting for transfers between devices  32.1 us (24%)
  other arithmetic  27.5 us (21%)
  local copies, waits for them, and re-layouts  20.3 us (15%)
  between operations  13.2 us (10%)
    ppermute x5, starting transfers between devices, exchange(): high = lax.ppermute(down, 'slab', backward)  13.9 us
    ppermute x3, waiting for transfers between devices, body(): lax.ppermute(outgoing, 'side', [(source, side_count - 1)])  12 us
    ppermute x5, starting transfers between devices, exchange(): low = lax.ppermute(up, 'slab', forward)  10.6 us
    ppermute x5, waiting for transfers between devices, exchange(): low = lax.ppermute(up, 'slab', forward)  8.35 us
    ppermute x3, starting transfers between devices, shell_sum(): v = v + lax.ppermute(v, ('side', 'slab'), pairs)  7.58 us
    unnamed x73, local copies, waits for them, and re-layouts  6.6 us
    ppermute x3, waiting for transfers between devices, shell_sum(): v = v + lax.ppermute(v, ('side', 'slab'), pairs)  6.25 us
    ppermute x3, waiting for transfers between devices, allsum_axis(): v = v + lax.ppermute(v, axis, [(i, i ^ step) for i in range(count)])  5.44 us
  transfers between devices with their start and end apart: 21, of which 9 were waited for; matrix products, arithmetic and copies ran while one was open for 16% of the time, Pallas kernels for 0%

profile of v14, /device:TPU:28, one launch (start us, length us, event | category | flops | bytes accessed | tf_op | source)
XLA Modules:
  0.0 132.2 jit_solution(8459405751519479859)
XLA Ops:
  3.0 1.8 %copy.90 = f32[1,8,64,512]{3,1,2,0:T(8,128)S(1)} copy(f32[1,8,64,512]{3,2,1,0:T(8,128)} %param.21) | data formatting | bytes 2097152 | tf_op args[0]
  7.7 2.8 %collective-permute-start.1 = (f32[100,512]{1,0:T(8,128)S(1)}, f32[100,512]{1,0:T(8,128)S(1)}, u32[]{:S(2)}, u32[]{:S(2)}) collective-permute-start(f32[100,512]{1,0:T(8,128)S(1)} %pad_maximum_fusion.9), channel_id=1, source_target_pairs={{1,0},{2,1},{3,2},{4,3},{5,4},{6,5},{7,6},{9,8},{10,9},{11,10},{12... | collective-permute-start | bytes 614408 | tf_op jit(solution)/shard_map/ppermute | solution.py:63
  10.6 1.9 %collective-permute-start = (f32[100,512]{1,0:T(8,128)S(1)}, f32[100,512]{1,0:T(8,128)}, u32[]{:S(2)}, u32[]{:S(2)}) collective-permute-start(f32[100,512]{1,0:T(8,128)S(1)} %pad_maximum_fusion.8), channel_id=1, source_target_pairs={{0,1},{1,2},{2,3},{3,4},{4,5},{5,6},{6,7},{8,9},{9,10},{10,11},{11... | collective-permute-start | bytes 614408 | tf_op jit(solution)/shard_map/ppermute | solution.py:62
  16.8 1.9 %collective-permute-done = f32[100,512]{1,0:T(8,128)} collective-permute-done((f32[100,512]{1,0:T(8,128)S(1)}, f32[100,512]{1,0:T(8,128)}, u32[]{:S(2)}, u32[]{:S(2)}) %collective-permute-start) | collective-permute-done | bytes 204832 | tf_op jit(solution)/shard_map/ppermute | solution.py:62
  26.0 2.8 %collective-permute-start.3 = (f32[224,512]{1,0:T(8,128)S(1)}, f32[224,512]{1,0:T(8,128)S(1)}, u32[]{:S(2)}, u32[]{:S(2)}) collective-permute-start(f32[224,512]{1,0:T(8,128)S(1)} %pad_maximum_fusion.6), channel_id=1, source_target_pairs={{1,0},{2,1},{3,2},{4,3},{5,4},{6,5},{7,6},{9,8},{10,9},{11,10},{12... | collective-permute-start | bytes 1376264 | tf_op jit(solution)/shard_map/ppermute | solution.py:63
  30.0 1.9 %collective-permute-start.4 = (f32[4,512]{1,0:T(4,128)S(1)}, f32[4,512]{1,0:T(4,128)S(1)}, u32[]{:S(2)}, u32[]{:S(2)}) collective-permute-start(f32[4,512]{1,0:T(4,128)S(1)} %get-tuple-element.225), channel_id=1, source_target_pairs={{0,1},{1,2},{2,3},{3,4},{4,5},{5,6},{6,7},{8,9},{9,10},{10,11},{11... | collective-permute-start | bytes 24584 | tf_op jit(solution)/shard_map/ppermute | solution.py:62
  31.9 4.5 %collective-permute-start.5 = (f32[4,512]{1,0:T(4,128)S(1)}, f32[4,512]{1,0:T(4,128)S(1)}, u32[]{:S(2)}, u32[]{:S(2)}) collective-permute-start(f32[4,512]{1,0:T(4,128)S(1)} %get-tuple-element.226), channel_id=1, source_target_pairs={{1,0},{2,1},{3,2},{4,3},{5,4},{6,5},{7,6},{9,8},{10,9},{11,10},{12... | collective-permute-start | bytes 24584 | tf_op jit(solution)/shard_map/ppermute | solution.py:63
  36.5 1.9 %collective-permute-start.2 = (f32[224,512]{1,0:T(8,128)S(1)}, f32[224,512]{1,0:T(8,128)S(1)}, u32[]{:S(2)}, u32[]{:S(2)}) collective-permute-start(f32[224,512]{1,0:T(8,128)S(1)} %pad_maximum_fusion.5), channel_id=1, source_target_pairs={{0,1},{1,2},{2,3},{3,4},{4,5},{5,6},{6,7},{8,9},{9,10},{10,11},{11... | collective-permute-start | bytes 1376264 | tf_op jit(solution)/shard_map/ppermute | solution.py:62
  40.7 6.4 %collective-permute-done.2 = f32[224,512]{1,0:T(8,128)S(1)} collective-permute-done((f32[224,512]{1,0:T(8,128)S(1)}, f32[224,512]{1,0:T(8,128)S(1)}, u32[]{:S(2)}, u32[]{:S(2)}) %collective-permute-start.2) | collective-permute-done | bytes 458784 | tf_op jit(solution)/shard_map/ppermute | solution.py:62
  48.7 1.9 %pad_maximum_fusion.14 = f32[2]{0:T(128)} fusion(f32[1]{0:T(128)} %bitcast.30, f32[1]{0:T(128)} %bitcast.29), kind=kLoop, calls=%fused_computation.252 | loop fusion | flops 2 | bytes 16 | tf_op jit(solution)/shard_map/stack | solution.py:227
  51.4 1.9 %collective-permute-start.7 = (f32[8,512]{1,0:T(8,128)}, f32[8,512]{1,0:T(8,128)}, u32[]{:S(2)}, u32[]{:S(2)}) collective-permute-start(f32[8,512]{1,0:T(8,128)} %pad_maximum_fusion.13), channel_id=1, source_target_pairs={{1,0},{2,1},{3,2},{4,3},{5,4},{6,5},{7,6},{9,8},{10,9},{11,10},{12... | collective-permute-start | bytes 49160 | tf_op jit(solution)/shard_map/ppermute | solution.py:63
  53.9 2.4 %collective-permute-start.6 = (f32[8,512]{1,0:T(8,128)}, f32[8,512]{1,0:T(8,128)}, u32[]{:S(2)}, u32[]{:S(2)}) collective-permute-start(f32[8,512]{1,0:T(8,128)} %pad_maximum_fusion.12), channel_id=1, source_target_pairs={{0,1},{1,2},{2,3},{3,4},{4,5},{5,6},{6,7},{8,9},{9,10},{10,11},{11... | collective-permute-start | bytes 49160 | tf_op jit(solution)/shard_map/ppermute | solution.py:62
  57.8 2.5 %pad_maximum_fusion.1 = (f32[10,64,512]{2,0,1:T(8,128)}, f32[10,64,512]{2,0,1:T(8,128)}) fusion(f32[10,56,512]{2,0,1:T(8,128)S(1)} %get-tuple-element.166, f32[10,8,512]{2,0,1:T(8,128)S(1)} %get-tuple-element.180, f32[10,56,512]{2,0,1:T(8,128)S(1)} %get-tuple-element.165, f32[10,8,512]{2,0,1:T(8,128)S(1)} %get-tuple-element.179), kind=kLoop, calls=%fused_computation.33 | loop fusion | flops 655360 | bytes 5242880 | tf_op jit(solution)/shard_map/concatenate | solution.py:187
  60.6 1.3 %fusion.169 = f32[2]{0:T(128)S(1)} fusion(f32[2]{0:T(128)S(1)} %collective-permute-done.8, f32[1]{0:T(128)} %bitcast.30, f32[1]{0:T(128)} %bitcast.29), kind=kLoop, calls=%fused_computation.293 | loop fusion | flops 4 | bytes 24 | tf_op jit(solution)/shard_map/add | solution.py:111
  62.0 1.6 %collective-permute-start.9 = (f32[2]{0:T(128)S(1)}, f32[2]{0:T(128)S(1)}, u32[]{:S(2)}, u32[]{:S(2)}) collective-permute-start(f32[2]{0:T(128)S(1)} %fusion.169), channel_id=1, source_target_pairs={{0,2},{1,3},{2,0},{3,1},{4,6},{5,7},{6,4},{7,5},{8,10},{9,11},{10,... | collective-permute-start | bytes 32 | tf_op jit(solution)/shard_map/ppermute | solution.py:111
  63.6 1.9 %collective-permute-done.9 = f32[2]{0:T(128)S(1)} collective-permute-done((f32[2]{0:T(128)S(1)}, f32[2]{0:T(128)S(1)}, u32[]{:S(2)}, u32[]{:S(2)}) %collective-permute-start.9) | collective-permute-done | bytes 40 | tf_op jit(solution)/shard_map/ppermute | solution.py:111
  65.5 1.3 %fusion.170 = f32[2]{0:T(128)S(1)} fusion(f32[2]{0:T(128)S(1)} %collective-permute-done.9, f32[2]{0:T(128)S(1)} %collective-permute-done.8, f32[1]{0:T(128)} %bitcast.30, f32[1]{0:T(128)} %bitcast.29), kind=kLoop, calls=%fused_computation.294 | loop fusion | flops 6 | bytes 32 | tf_op jit(solution)/shard_map/add | solution.py:111
  66.9 3.5 %collective-permute-done.10 = f32[2]{0:T(128)S(1)} collective-permute-done((f32[2]{0:T(128)S(1)}, f32[2]{0:T(128)S(1)}, u32[]{:S(2)}, u32[]{:S(2)}) %collective-permute-start.10) | collective-permute-done | bytes 40 | tf_op jit(solution)/shard_map/ppermute | solution.py:111
  80.3 4.7 %multiply_reduce_fusion = f32[2,8,512]{2,1,0:T(8,128)S(1)} fusion(f32[2,8,512]{2,1,0:T(8,128)S(1)} %subtract_multiply_fusion, f32[8,512,512]{2,1,0:T(8,128)} %param.24), kind=kLoop, calls=%fused_computation.28 | loop fusion | flops 8380416 | bytes 8454144 | tf_op jit(solution)/shard_map/reduce_sum | solution.py:240
  85.6 1.3 collective-permute-start.15
  86.9 1.3 collective-permute-start.14
  88.2 1.3 collective-permute-start.13
  90.4 1.9 %collective-permute-start.20 = (f32[128,512]{1,0:T(8,128)S(1)}, f32[128,512]{1,0:T(8,128)S(1)}, u32[]{:S(2)}, u32[]{:S(2)}) collective-permute-start(f32[128,512]{1,0:T(8,128)S(1)} %bitcast.118), channel_id=1, source_target_pairs={{1,0},{2,1},{3,2},{4,3},{5,4},{6,5},{7,6},{9,8},{10,9},{11,10},{12... | collective-permute-start | bytes 786440 | tf_op jit(solution)/shard_map/ppermute | solution.py:63
  92.3 2.4 %collective-permute-start.19 = (f32[128,512]{1,0:T(8,128)S(1)}, f32[128,512]{1,0:T(8,128)S(1)}, u32[]{:S(2)}, u32[]{:S(2)}) collective-permute-start(f32[128,512]{1,0:T(8,128)S(1)} %bitcast.117), channel_id=1, source_target_pairs={{0,1},{1,2},{2,3},{3,4},{4,5},{5,6},{6,7},{8,9},{9,10},{10,11},{11... | collective-permute-start | bytes 786440 | tf_op jit(solution)/shard_map/ppermute | solution.py:62
  94.7 10.3 %collective-permute-done.15 = f32[37,512]{1,0:T(8,128)S(1)} collective-permute-done((f32[37,512]{1,0:T(8,128)S(1)}, f32[37,512]{1,0:T(8,128)S(1)}, u32[]{:S(2)}, u32[]{:S(2)}) %collective-permute-start.15) | collective-permute-done | bytes 75808 | tf_op jit(solution)/shard_map/ppermute | solution.py:279
  105.0 1.8 %collective-permute-done.14 = f32[37,512]{1,0:T(8,128)S(1)} collective-permute-done((f32[37,512]{1,0:T(8,128)S(1)}, f32[37,512]{1,0:T(8,128)S(1)}, u32[]{:S(2)}, u32[]{:S(2)}) %collective-permute-start.14) | collective-permute-done | bytes 75808 | tf_op jit(solution)/shard_map/ppermute | solution.py:279
  107.4 1.9 %collective-permute-start.16 = (f32[4]{0:T(128)S(1)}, f32[4]{0:T(128)S(1)}, u32[]{:S(2)}, u32[]{:S(2)}) collective-permute-start(f32[4]{0:T(128)S(1)} %slice_reduce_fusion), channel_id=1, source_target_pairs={{24,25},{25,24},{26,27},{27,26},{28,29},{29,28},{30,31},{31,30}} | collective-permute-start | bytes 56 | tf_op jit(solution)/shard_map/ppermute | solution.py:122
  110.4 3.5 %collective-permute-start.17 = (f32[4]{0:T(128)S(1)}, f32[4]{0:T(128)S(1)}, u32[]{:S(2)}, u32[]{:S(2)}) collective-permute-start(f32[4]{0:T(128)S(1)} %add.705), channel_id=1, source_target_pairs={{24,26},{25,27},{26,24},{27,25},{28,30},{29,31},{30,28},{31,29}} | collective-permute-start | bytes 56 | tf_op jit(solution)/shard_map/ppermute | solution.py:122
  113.9 1.9 %collective-permute-done.17 = f32[4]{0:T(128)S(1)} collective-permute-done((f32[4]{0:T(128)S(1)}, f32[4]{0:T(128)S(1)}, u32[]{:S(2)}, u32[]{:S(2)}) %collective-permute-start.17) | collective-permute-done | bytes 48 | tf_op jit(solution)/shard_map/ppermute | solution.py:122
  115.8 2.1 %collective-permute-start.18 = (f32[4]{0:T(128)S(1)}, f32[4]{0:T(128)S(1)}, u32[]{:S(2)}, u32[]{:S(2)}) collective-permute-start(f32[4]{0:T(128)S(1)} %add.706), channel_id=1, source_target_pairs={{24,28},{25,29},{26,30},{27,31},{28,24},{29,25},{30,26},{31,27}} | collective-permute-start | bytes 56 | tf_op jit(solution)/shard_map/ppermute | solution.py:122
  118.0 3.3 %collective-permute-done.18 = f32[4]{0:T(128)S(1)} collective-permute-done((f32[4]{0:T(128)S(1)}, f32[4]{0:T(128)S(1)}, u32[]{:S(2)}, u32[]{:S(2)}) %collective-permute-start.18) | collective-permute-done | bytes 48 | tf_op jit(solution)/shard_map/ppermute | solution.py:122
  131.1 1.1 maximum_select_fusion
  (235 shorter events, 35.9 us)
Async XLA Ops:
  0.6 4.2 %copy-start.6 = (f32[1,8,64,512]{3,2,1,0:T(8,128)S(1)}, f32[1,8,64,512]{3,2,1,0:T(8,128)}, u32[]{:S(2)}) copy-start(f32[1,8,64,512]{3,2,1,0:T(8,128)} %param.22) | copy-start | bytes 3145732
  5.5 18.1 %copy-start = (f32[1,8,64,512]{3,1,2,0:T(8,128)}, f32[1,8,64,512]{3,1,2,0:T(8,128)S(1)}, u32[]{:S(2)}) copy-start(f32[1,8,64,512]{3,1,2,0:T(8,128)S(1)} %copy.89) | copy-start | bytes 3145732
  6.7 7.6 %copy-start.28 = (s32[8]{0:T(128)S(1)}, s32[8]{0:T(128)}, u32[]{:S(2)}) copy-start(s32[8]{0:T(128)} %param.29) | copy-start | bytes 100
  6.8 8.3 %copy-start.17 = (s32[8]{0:T(128)S(1)}, s32[8]{0:T(128)}, u32[]{:S(2)}) copy-start(s32[8]{0:T(128)} %param.27) | copy-start | bytes 100
  7.7 12.7 %collective-permute-start.1 = (f32[100,512]{1,0:T(8,128)S(1)}, f32[100,512]{1,0:T(8,128)S(1)}, u32[]{:S(2)}, u32[]{:S(2)}) collective-permute-start(f32[100,512]{1,0:T(8,128)S(1)} %pad_maximum_fusion.9), channel_id=1, source_target_pairs={{1,0},{2,1},{3,2},{4,3},{5,4},{6,5},{7,6},{9,8},{10,9},{11,10},{12... | collective-permute-start | bytes 614408 | tf_op jit(solution)/shard_map/ppermute | solution.py:63
  10.6 8.2 %collective-permute-start = (f32[100,512]{1,0:T(8,128)S(1)}, f32[100,512]{1,0:T(8,128)}, u32[]{:S(2)}, u32[]{:S(2)}) collective-permute-start(f32[100,512]{1,0:T(8,128)S(1)} %pad_maximum_fusion.8), channel_id=1, source_target_pairs={{0,1},{1,2},{2,3},{3,4},{4,5},{5,6},{6,7},{8,9},{9,10},{10,11},{11... | collective-permute-start | bytes 614408 | tf_op jit(solution)/shard_map/ppermute | solution.py:62
  16.8 22.2 %copy-start.24 = (pred[10]{0:T(512)(128)(4,1)}, pred[10]{0:T(512)(128)(4,1)S(1)}, u32[]{:S(2)}) copy-start(pred[10]{0:T(512)(128)(4,1)S(1)} %get-tuple-element.231) | copy-start | bytes 34
  16.8 43.4 %copy-start.26 = (pred[10,1,1]{0,2,1:T(4,128)(4,1)}, pred[10,1,1]{0,2,1:T(4,128)(4,1)S(1)}, u32[]{:S(2)}) copy-start(pred[10,1,1]{0,2,1:T(4,128)(4,1)S(1)} %get-tuple-element.230) | copy-start | bytes 34
  22.4 16.0 %copy-start.8 = (f32[16,1,512]{2,0,1:T(8,128)}, f32[16,1,512]{2,0,1:T(8,128)S(1)}, u32[]{:S(2)}) copy-start(f32[16,1,512]{2,0,1:T(8,128)S(1)} %get-tuple-element.148) | copy-start | bytes 98308
  23.1 6.0 %slice-start = ((s8[8388608]{0:T(1024)(128)(4,1)}), s8[4194304]{0:T(1024)(128)(4,1)S(1)}, s32[]{:S(2)}) async-start(s8[8388608]{0:T(1024)(128)(4,1)} %bitcast.94), calls=%async_computation | async-start | bytes 8388608
  26.0 14.4 %collective-permute-start.3 = (f32[224,512]{1,0:T(8,128)S(1)}, f32[224,512]{1,0:T(8,128)S(1)}, u32[]{:S(2)}, u32[]{:S(2)}) collective-permute-start(f32[224,512]{1,0:T(8,128)S(1)} %pad_maximum_fusion.6), channel_id=1, source_target_pairs={{1,0},{2,1},{3,2},{4,3},{5,4},{6,5},{7,6},{9,8},{10,9},{11,10},{12... | collective-permute-start | bytes 1376264 | tf_op jit(solution)/shard_map/ppermute | solution.py:63
  30.0 8.4 %collective-permute-start.4 = (f32[4,512]{1,0:T(4,128)S(1)}, f32[4,512]{1,0:T(4,128)S(1)}, u32[]{:S(2)}, u32[]{:S(2)}) collective-permute-start(f32[4,512]{1,0:T(4,128)S(1)} %get-tuple-element.225), channel_id=1, source_target_pairs={{0,1},{1,2},{2,3},{3,4},{4,5},{5,6},{6,7},{8,9},{9,10},{10,11},{11... | collective-permute-start | bytes 24584 | tf_op jit(solution)/shard_map/ppermute | solution.py:62
  31.9 6.5 %collective-permute-start.5 = (f32[4,512]{1,0:T(4,128)S(1)}, f32[4,512]{1,0:T(4,128)S(1)}, u32[]{:S(2)}, u32[]{:S(2)}) collective-permute-start(f32[4,512]{1,0:T(4,128)S(1)} %get-tuple-element.226), channel_id=1, source_target_pairs={{1,0},{2,1},{3,2},{4,3},{5,4},{6,5},{7,6},{9,8},{10,9},{11,10},{12... | collective-permute-start | bytes 24584 | tf_op jit(solution)/shard_map/ppermute | solution.py:63
  36.5 10.7 %collective-permute-start.2 = (f32[224,512]{1,0:T(8,128)S(1)}, f32[224,512]{1,0:T(8,128)S(1)}, u32[]{:S(2)}, u32[]{:S(2)}) collective-permute-start(f32[224,512]{1,0:T(8,128)S(1)} %pad_maximum_fusion.5), channel_id=1, source_target_pairs={{0,1},{1,2},{2,3},{3,4},{4,5},{5,6},{6,7},{8,9},{9,10},{10,11},{11... | collective-permute-start | bytes 1376264 | tf_op jit(solution)/shard_map/ppermute | solution.py:62
  50.6 10.0 %collective-permute-start.8 = (f32[2]{0:T(128)}, f32[2]{0:T(128)S(1)}, u32[]{:S(2)}, u32[]{:S(2)}) collective-permute-start(f32[2]{0:T(128)} %pad_maximum_fusion.14), channel_id=1, source_target_pairs={{0,1},{1,0},{2,3},{3,2},{4,5},{5,4},{6,7},{7,6},{8,9},{9,8},{10,11... | collective-permute-start | bytes 32 | tf_op jit(solution)/shard_map/ppermute | solution.py:111
  51.4 23.6 %collective-permute-start.7 = (f32[8,512]{1,0:T(8,128)}, f32[8,512]{1,0:T(8,128)}, u32[]{:S(2)}, u32[]{:S(2)}) collective-permute-start(f32[8,512]{1,0:T(8,128)} %pad_maximum_fusion.13), channel_id=1, source_target_pairs={{1,0},{2,1},{3,2},{4,3},{5,4},{6,5},{7,6},{9,8},{10,9},{11,10},{12... | collective-permute-start | bytes 49160 | tf_op jit(solution)/shard_map/ppermute | solution.py:63
  53.9 21.9 %collective-permute-start.6 = (f32[8,512]{1,0:T(8,128)}, f32[8,512]{1,0:T(8,128)}, u32[]{:S(2)}, u32[]{:S(2)}) collective-permute-start(f32[8,512]{1,0:T(8,128)} %pad_maximum_fusion.12), channel_id=1, source_target_pairs={{0,1},{1,2},{2,3},{3,4},{4,5},{5,6},{6,7},{8,9},{9,10},{10,11},{11... | collective-permute-start | bytes 49160 | tf_op jit(solution)/shard_map/ppermute | solution.py:62
  60.3 16.4 %copy-start.9 = (f32[16,1,512]{2,0,1:T(8,128)S(1)}, f32[16,1,512]{2,0,1:T(8,128)}, u32[]{:S(2)}) copy-start(f32[16,1,512]{2,0,1:T(8,128)} %copy-done.8) | copy-start | bytes 98308
  60.6 17.0 %copy-start.1 = (f32[8,64,512]{2,1,0:T(8,128)}, f32[8,64,512]{2,1,0:T(8,128)S(1)}, u32[]{:S(2)}) copy-start(f32[8,64,512]{2,1,0:T(8,128)S(1)} %get-tuple-element.244) | copy-start | bytes 3145732
  62.0 3.5 %collective-permute-start.9 = (f32[2]{0:T(128)S(1)}, f32[2]{0:T(128)S(1)}, u32[]{:S(2)}, u32[]{:S(2)}) collective-permute-start(f32[2]{0:T(128)S(1)} %fusion.169), channel_id=1, source_target_pairs={{0,2},{1,3},{2,0},{3,1},{4,6},{5,7},{6,4},{7,5},{8,10},{9,11},{10,... | collective-permute-start | bytes 32 | tf_op jit(solution)/shard_map/ppermute | solution.py:111
  66.9 3.5 %collective-permute-start.10 = (f32[2]{0:T(128)S(1)}, f32[2]{0:T(128)S(1)}, u32[]{:S(2)}, u32[]{:S(2)}) collective-permute-start(f32[2]{0:T(128)S(1)} %fusion.170), channel_id=1, source_target_pairs={{0,4},{1,5},{2,6},{3,7},{4,0},{5,1},{6,2},{7,3},{8,12},{9,13},{10,... | collective-permute-start | bytes 32 | tf_op jit(solution)/shard_map/ppermute | solution.py:111
  70.4 1.3 %collective-permute-start.12 = (f32[2]{0:T(128)S(1)}, f32[2]{0:T(128)S(1)}, u32[]{:S(2)}, u32[]{:S(2)}) collective-permute-start(f32[2]{0:T(128)S(1)} %add.694), channel_id=1, source_target_pairs={{0,8},{1,9},{2,10},{3,11},{4,12},{5,13},{6,14},{7,15},{8,16},{9,17... | collective-permute-start | bytes 32 | tf_op jit(solution)/shard_map/ppermute | solution.py:132
  71.1 0.7 collective-permute-start.11
  80.3 9.8 %copy-start.2 = (f32[8,64,512]{2,1,0:T(8,128)S(1)}, f32[8,64,512]{2,1,0:T(8,128)}, u32[]{:S(2)}) copy-start(f32[8,64,512]{2,1,0:T(8,128)} %copy-done.1) | copy-start | bytes 3145732
  85.6 19.4 %collective-permute-start.15 = (f32[37,512]{1,0:T(8,128)S(1)}, f32[37,512]{1,0:T(8,128)S(1)}, u32[]{:S(2)}, u32[]{:S(2)}) collective-permute-start(f32[37,512]{1,0:T(8,128)S(1)} %concatenate.309), channel_id=1, source_target_pairs={{16,24},{17,25},{18,26},{19,27},{20,28},{21,29},{22,30},{23,31}} | collective-permute-start | bytes 227336 | tf_op jit(solution)/shard_map/ppermute | solution.py:279
  86.9 19.9 %collective-permute-start.14 = (f32[37,512]{1,0:T(8,128)S(1)}, f32[37,512]{1,0:T(8,128)S(1)}, u32[]{:S(2)}, u32[]{:S(2)}) collective-permute-start(f32[37,512]{1,0:T(8,128)S(1)} %concatenate.309), channel_id=1, source_target_pairs={{8,24},{9,25},{10,26},{11,27},{12,28},{13,29},{14,30},{15,31}} | collective-permute-start | bytes 227336 | tf_op jit(solution)/shard_map/ppermute | solution.py:279
  88.2 18.6 %collective-permute-start.13 = (f32[37,512]{1,0:T(8,128)S(1)}, f32[37,512]{1,0:T(8,128)S(1)}, u32[]{:S(2)}, u32[]{:S(2)}) collective-permute-start(f32[37,512]{1,0:T(8,128)S(1)} %concatenate.309), channel_id=1, source_target_pairs={{0,24},{1,25},{2,26},{3,27},{4,28},{5,29},{6,30},{7,31}} | collective-permute-start | bytes 227336 | tf_op jit(solution)/shard_map/ppermute | solution.py:279
  90.4 40.0 %collective-permute-start.20 = (f32[128,512]{1,0:T(8,128)S(1)}, f32[128,512]{1,0:T(8,128)S(1)}, u32[]{:S(2)}, u32[]{:S(2)}) collective-permute-start(f32[128,512]{1,0:T(8,128)S(1)} %bitcast.118), channel_id=1, source_target_pairs={{1,0},{2,1},{3,2},{4,3},{5,4},{6,5},{7,6},{9,8},{10,9},{11,10},{12... | collective-permute-start | bytes 786440 | tf_op jit(solution)/shard_map/ppermute | solution.py:63
  92.3 38.0 %collective-permute-start.19 = (f32[128,512]{1,0:T(8,128)S(1)}, f32[128,512]{1,0:T(8,128)S(1)}, u32[]{:S(2)}, u32[]{:S(2)}) collective-permute-start(f32[128,512]{1,0:T(8,128)S(1)} %bitcast.117), channel_id=1, source_target_pairs={{0,1},{1,2},{2,3},{3,4},{4,5},{5,6},{6,7},{8,9},{9,10},{10,11},{11... | collective-permute-start | bytes 786440 | tf_op jit(solution)/shard_map/ppermute | solution.py:62
  107.4 3.0 %collective-permute-start.16 = (f32[4]{0:T(128)S(1)}, f32[4]{0:T(128)S(1)}, u32[]{:S(2)}, u32[]{:S(2)}) collective-permute-start(f32[4]{0:T(128)S(1)} %slice_reduce_fusion), channel_id=1, source_target_pairs={{24,25},{25,24},{26,27},{27,26},{28,29},{29,28},{30,31},{31,30}} | collective-permute-start | bytes 56 | tf_op jit(solution)/shard_map/ppermute | solution.py:122
  110.4 5.4 %collective-permute-start.17 = (f32[4]{0:T(128)S(1)}, f32[4]{0:T(128)S(1)}, u32[]{:S(2)}, u32[]{:S(2)}) collective-permute-start(f32[4]{0:T(128)S(1)} %add.705), channel_id=1, source_target_pairs={{24,26},{25,27},{26,24},{27,25},{28,30},{29,31},{30,28},{31,29}} | collective-permute-start | bytes 56 | tf_op jit(solution)/shard_map/ppermute | solution.py:122
  115.8 5.4 %collective-permute-start.18 = (f32[4]{0:T(128)S(1)}, f32[4]{0:T(128)S(1)}, u32[]{:S(2)}, u32[]{:S(2)}) collective-permute-start(f32[4]{0:T(128)S(1)} %add.706), channel_id=1, source_target_pairs={{24,28},{25,29},{26,30},{27,31},{28,24},{29,25},{30,26},{31,27}} | collective-permute-start | bytes 56 | tf_op jit(solution)/shard_map/ppermute | solution.py:122
  (23 other events, 35.6 us)

commit v15 on v14

--- a/solution.py
+++ b/solution.py
@@ -214,12 +214,17 @@
     disp_one = disp_zero + RELAX * resid_zero
     tilde_one, unused, unused_extra = evaluate(disp_one)
     init_deep, tilde_one = lax.optimization_barrier((init_deep, tilde_one))
-    deep = lax.cond(
-        shell_flag,
-        lambda: jnp.zeros((slab_rows,) + init_deep.shape[1:], jnp.float32),
-        lambda: deep_step(
-            deep_step(init_deep, force_deep, coef_deep, ok_one), force_deep[1:-1], coef_deep[1:-1], ok_two
-        ),
+
+    def face_rows():
+        r = slab_rows
+        low = deep_step(init_deep[0:6], force_deep[0:4], coef_deep[0:4], ok_one[0:4])
+        low = deep_step(low, force_deep[1:3], coef_deep[1:3], ok_two[0:2])
+        high = deep_step(init_deep[r - 2 : r + 4], force_deep[r - 2 : r + 2], coef_deep[r - 2 : r + 2], ok_one[r - 2 : r + 2])
+        high = deep_step(high, force_deep[r - 1 : r + 1], coef_deep[r - 1 : r + 1], ok_two[r - 2 : r])
+        return jnp.concatenate([low, high], axis=0)
+
+    faces = lax.cond(
+        shell_flag, lambda: jnp.zeros((4,) + init_deep.shape[1:], jnp.float32), face_rows
     )
     resid_one = tilde_one - disp_one
     diff_one = resid_one - resid_zero
@@ -229,7 +234,9 @@
         side_count - 1,
     )
     step_one = tilde_one - tilde_zero
-    rims_base, rims_step = exchange([(plane_of(tilde_one), HALO), (plane_of(step_one), HALO)])
+    rims_base, rims_step, faces = exchange(
+        [(plane_of(tilde_one), HALO), (plane_of(step_one), HALO), (faces, 2)]
+    )
     band_base = band_solve(init_band, force_band.at[:, 0, :].add(rims_base), coef_band, row_ok)
     band_step = band_solve(
         jnp.zeros_like(init_band), jnp.zeros_like(force_band).at[:, 0, :].set(rims_step), coef_band, row_ok
@@ -266,13 +273,19 @@
         ],
         axis=0,
     )
-    (deep,) = exchange([(deep + 0.0 * outgoing[0, 0], 2)])
+    late_init = init_deep + 0.0 * outgoing[0, 0]
+
+    def deep_rest():
+        q = deep_step(
+            deep_step(late_init, force_deep, coef_deep, ok_one), force_deep[1:-1], coef_deep[1:-1], ok_two
+        )
+        q = jnp.concatenate([faces[:2], q, faces[-2:]], axis=0)
+        return deep_step(
+            deep_step(q, force_deep, coef_deep, ok_one), force_deep[1:-1], coef_deep[1:-1], ok_two
+        )
+
     deep = lax.cond(
-        shell_flag,
-        lambda: jnp.zeros((slab_rows,) + deep.shape[1:], jnp.float32),
-        lambda: deep_step(
-            deep_step(deep, force_deep, coef_deep, ok_one), force_deep[1:-1], coef_deep[1:-1], ok_two
-        ),
+        shell_flag, lambda: jnp.zeros((slab_rows,) + init_deep.shape[1:], jnp.float32), deep_rest
     )
     gathered = outgoing
     for source in range(side_count - 1):

time: 134 us -> 140 us (1.045)
  the two profiles are of different devices: /device:TPU:28 before, /device:TPU:0 now
where the time goes in v15:
time: 140 us; the launch traced here: 138 us
  starting transfers between devices  42.4 us (30%)
  other arithmetic  41 us (29%)
  local copies, waits for them, and re-layouts  34.1 us (24%)
  between operations  12.1 us (9%)
  waiting for transfers between devices  7.47 us (5%)
    ppermute x4, starting transfers between devices, exchange(): low = lax.ppermute(up, 'slab', forward)  16.2 us
    ppermute x3, starting transfers between devices, allsum_axis(): v = v + lax.ppermute(v, axis, [(i, i ^ step) for i in range(count)])  10.1 us
    select_n x5, other arithmetic, deep_step(): return jnp.where(ok, new, 0.0)  8.65 us
    unnamed x75, local copies, waits for them, and re-layouts  7.5 us
    ppermute x2, starting transfers between devices, fluid_sum(): got.append(lax.ppermute(v, ('side', 'slab'), pairs))  6.41 us
    another operation x3, local copies, waits for them, and re-layouts  5.62 us
    ppermute x4, starting transfers between devices, exchange(): high = lax.ppermute(down, 'slab', backward)  5.14 us
    reduce_sum x1, other arithmetic, body(): jnp.sum(compliance[None] * loaded[:, :, None, :], axis=-1)  4.59 us
  transfers between devices with their start and end apart: 19, of which 3 were waited for; matrix products, arithmetic and copies ran while one was open for 33% of the time, Pallas kernels for 0%

profile of v15, /device:TPU:0, one launch (start us, length us, event | category | flops | bytes accessed | tf_op | source)
XLA Modules:
  0.0 138.1 jit_solution(11077227683895352146)
XLA Ops:
  3.0 1.8 %copy.91 = f32[1,8,64,512]{3,1,2,0:T(8,128)S(1)} copy(f32[1,8,64,512]{3,2,1,0:T(8,128)} %param.22) | data formatting | bytes 2097152 | tf_op args[1]
  8.1 1.3 collective-permute-start.1
  9.5 3.0 %collective-permute-start = (f32[100,512]{1,0:T(8,128)S(1)}, f32[100,512]{1,0:T(8,128)S(1)}, u32[]{:S(2)}, u32[]{:S(2)}) collective-permute-start(f32[100,512]{1,0:T(8,128)S(1)} %pad_maximum_fusion.10), channel_id=1, source_target_pairs={{0,1},{1,2},{2,3},{3,4},{4,5},{5,6},{6,7},{8,9},{9,10},{10,11},{11... | collective-permute-start | bytes 614408 | tf_op jit(solution)/shard_map/ppermute | solution.py:62
  19.1 1.5 %slice-done.2 = f32[4,512]{1,0:T(4,128)S(1)} async-done(((f32[100,512]{1,0:T(8,128)}), f32[4,512]{1,0:T(4,128)S(1)}, s32[]{:S(2)}) %slice-start.2) | async-done | bytes 8216 | tf_op jit(solution)/shard_map/slice | solution.py:68
  26.2 1.3 collective-permute-start.3
  27.7 1.3 collective-permute-start.5
  29.0 5.7 %collective-permute-start.4 = (f32[4,512]{1,0:T(4,128)S(1)}, f32[4,512]{1,0:T(4,128)S(1)}, u32[]{:S(2)}, u32[]{:S(2)}) collective-permute-start(f32[4,512]{1,0:T(4,128)S(1)} %get-tuple-element.294), channel_id=1, source_target_pairs={{0,1},{1,2},{2,3},{3,4},{4,5},{5,6},{6,7},{8,9},{9,10},{10,11},{11... | collective-permute-start | bytes 24584 | tf_op jit(solution)/shard_map/ppermute | solution.py:62
  34.7 3.7 %collective-permute-start.2 = (f32[224,512]{1,0:T(8,128)S(1)}, f32[224,512]{1,0:T(8,128)S(1)}, u32[]{:S(2)}, u32[]{:S(2)}) collective-permute-start(f32[224,512]{1,0:T(8,128)S(1)} %pad_maximum_fusion.5), channel_id=1, source_target_pairs={{0,1},{1,2},{2,3},{3,4},{4,5},{5,6},{6,7},{8,9},{9,10},{10,11},{11... | collective-permute-start | bytes 1376264 | tf_op jit(solution)/shard_map/ppermute | solution.py:62
  41.9 1.8 %pad_maximum_fusion.14 = f32[2]{0:T(128)} fusion(f32[1]{0:T(128)} %bitcast.39, f32[1]{0:T(128)} %bitcast.38), kind=kLoop, calls=%fused_computation.298 | loop fusion | flops 2 | bytes 16 | tf_op jit(solution)/shard_map/stack | solution.py:232
  43.8 3.9 %collective-permute-start.8 = (f32[2]{0:T(128)}, f32[2]{0:T(128)}, u32[]{:S(2)}, u32[]{:S(2)}) collective-permute-start(f32[2]{0:T(128)} %pad_maximum_fusion.14), channel_id=1, source_target_pairs={{0,1},{1,0},{2,3},{3,2},{4,5},{5,4},{6,7},{7,6},{8,9},{9,8},{10,11... | collective-permute-start | bytes 32 | tf_op jit(solution)/shard_map/ppermute | solution.py:111
  50.8 2.5 %pad_maximum_fusion.2 = (f32[10,64,512]{2,0,1:T(8,128)}, f32[10,64,512]{2,0,1:T(8,128)}) fusion(f32[10,56,512]{2,0,1:T(8,128)S(1)} %get-tuple-element.237, f32[10,8,512]{2,0,1:T(8,128)S(1)} %get-tuple-element.249, f32[10,56,512]{2,0,1:T(8,128)S(1)} %get-tuple-element.236, f32[10,8,512]{2,0,1:T(8,128)S(1)} %get-tuple-element.248), kind=kLoop, calls=%fused_computation.81 | loop fusion | flops 655360 | bytes 5242880 | tf_op jit(solution)/shard_map/concatenate | solution.py:187
  53.3 8.3 %conditional.2 = (f32[128,512]{1,0:T(8,128)S(1)}, f32[128,512]{1,0:T(8,128)S(1)}) conditional(s32[]{:T(128)} %convert_element_type.32, (pred[8,1,1]{0,2,1:T(4,128)(4,1)S(1)}, f32[10,64,512]{2,0,1:T(8,128)}, pred[10,1,1]{0,2,1:T(4,128)(4,1)S(1)}, f32[12,64,512]{2,0,1:T(8,128)S(1)}, f32[10,64,512]{2,0,1:T(8,128)}) %tuple.148, () %tuple.49), branch_computations={%region_8.9_spmd, %region_9.10_spmd} | conditional | flops 3538944 | bytes 34961460 | solution.py:226
  53.3 2.4 %copy.76 = f32[10,64,512]{2,1,0:T(8,128)S(1)} copy(f32[10,64,512]{2,0,1:T(8,128)} %get-tuple-element.156) | data formatting | bytes 2621440 | tf_op jit(solution)/shard_map
  56.6 2.4 %copy.74 = f32[10,64,512]{2,1,0:T(8,128)S(1)} copy(f32[10,64,512]{2,0,1:T(8,128)} %get-tuple-element.153) | data formatting | bytes 2621440 | tf_op jit(solution)/shard_map
  61.6 1.5 %pad_maximum_fusion.9 = f32[136,512]{1,0:T(8,128)} fusion(f32[128,512]{1,0:T(8,128)S(1)} %get-tuple-element.125, f32[4,512]{1,0:T(4,128)} %get-tuple-element.293, f32[4,512]{1,0:T(4,128)} %get-tuple-element.291), kind=kLoop, calls=%fused_computation.98 | loop fusion | flops 139264 | bytes 557056 | tf_op jit(solution)/shard_map/concatenate | solution.py:61
  63.1 1.3 collective-permute-start.7
  64.4 1.4 %pad_maximum_fusion.8 = f32[136,512]{1,0:T(8,128)} fusion(f32[128,512]{1,0:T(8,128)S(1)} %get-tuple-element.124, f32[4,512]{1,0:T(4,128)S(1)} %get-tuple-element.292, f32[4,512]{1,0:T(4,128)} %get-tuple-element.290), kind=kLoop, calls=%fused_computation.97 | loop fusion | flops 139264 | bytes 557056 | tf_op jit(solution)/shard_map/concatenate | solution.py:60
  65.8 3.7 %collective-permute-start.6 = (f32[136,512]{1,0:T(8,128)}, f32[136,512]{1,0:T(8,128)}, u32[]{:S(2)}, u32[]{:S(2)}) collective-permute-start(f32[136,512]{1,0:T(8,128)} %pad_maximum_fusion.8), channel_id=1, source_target_pairs={{0,1},{1,2},{2,3},{3,4},{4,5},{5,6},{6,7},{8,9},{9,10},{10,11},{11... | collective-permute-start | bytes 835592 | tf_op jit(solution)/shard_map/ppermute | solution.py:62
  69.5 2.0 %fusion.208 = f32[2]{0:T(128)S(1)} fusion(f32[2]{0:T(128)} %collective-permute-done.8, f32[1]{0:T(128)} %bitcast.39, f32[1]{0:T(128)} %bitcast.38), kind=kLoop, calls=%fused_computation.344 | loop fusion | flops 4 | bytes 24 | tf_op jit(solution)/shard_map/add | solution.py:111
  71.5 2.3 %collective-permute-start.9 = (f32[2]{0:T(128)S(1)}, f32[2]{0:T(128)S(1)}, u32[]{:S(2)}, u32[]{:S(2)}) collective-permute-start(f32[2]{0:T(128)S(1)} %fusion.208), channel_id=1, source_target_pairs={{0,2},{1,3},{2,0},{3,1},{4,6},{5,7},{6,4},{7,5},{8,10},{9,11},{10,... | collective-permute-start | bytes 32 | tf_op jit(solution)/shard_map/ppermute | solution.py:111
  73.8 1.5 %collective-permute-done.9 = f32[2]{0:T(128)S(1)} collective-permute-done((f32[2]{0:T(128)S(1)}, f32[2]{0:T(128)S(1)}, u32[]{:S(2)}, u32[]{:S(2)}) %collective-permute-start.9) | collective-permute-done | bytes 40 | tf_op jit(solution)/shard_map/ppermute | solution.py:111
  75.4 2.0 %fusion.209 = f32[2]{0:T(128)S(1)} fusion(f32[2]{0:T(128)S(1)} %collective-permute-done.9, f32[2]{0:T(128)} %collective-permute-done.8, f32[1]{0:T(128)} %bitcast.39, f32[1]{0:T(128)} %bitcast.38), kind=kLoop, calls=%fused_computation.345 | loop fusion | flops 6 | bytes 32 | tf_op jit(solution)/shard_map/add | solution.py:111
  77.3 3.8 %collective-permute-start.10 = (f32[2]{0:T(128)S(1)}, f32[2]{0:T(128)S(1)}, u32[]{:S(2)}, u32[]{:S(2)}) collective-permute-start(f32[2]{0:T(128)S(1)} %fusion.209), channel_id=1, source_target_pairs={{0,4},{1,5},{2,6},{3,7},{4,0},{5,1},{6,2},{7,3},{8,12},{9,13},{10,... | collective-permute-start | bytes 32 | tf_op jit(solution)/shard_map/ppermute | solution.py:111
  81.2 1.5 %collective-permute-done.10 = f32[2]{0:T(128)S(1)} collective-permute-done((f32[2]{0:T(128)S(1)}, f32[2]{0:T(128)S(1)}, u32[]{:S(2)}, u32[]{:S(2)}) %collective-permute-start.10) | collective-permute-done | bytes 40 | tf_op jit(solution)/shard_map/ppermute | solution.py:111
  82.7 4.5 %collective-permute-start.11 = (f32[2]{0:T(128)S(1)}, f32[2]{0:T(128)S(1)}, u32[]{:S(2)}, u32[]{:S(2)}) collective-permute-start(f32[2]{0:T(128)S(1)} %add.836), channel_id=1, source_target_pairs={{0,16},{1,17},{2,18},{3,19},{4,20},{5,21},{6,22},{7,23},{8,0},{9,1... | collective-permute-start | bytes 32 | tf_op jit(solution)/shard_map/ppermute | solution.py:132
  87.2 1.9 %collective-permute-start.12 = (f32[2]{0:T(128)S(1)}, f32[2]{0:T(128)S(1)}, u32[]{:S(2)}, u32[]{:S(2)}) collective-permute-start(f32[2]{0:T(128)S(1)} %add.836), channel_id=1, source_target_pairs={{0,8},{1,9},{2,10},{3,11},{4,12},{5,13},{6,14},{7,15},{8,16},{9,17... | collective-permute-start | bytes 32 | tf_op jit(solution)/shard_map/ppermute | solution.py:132
  89.1 4.4 %collective-permute-done.12 = f32[2]{0:T(128)S(1)} collective-permute-done((f32[2]{0:T(128)S(1)}, f32[2]{0:T(128)S(1)}, u32[]{:S(2)}, u32[]{:S(2)}) %collective-permute-start.12) | collective-permute-done | bytes 40 | tf_op jit(solution)/shard_map/ppermute | solution.py:132
  102.4 4.6 %multiply_reduce_fusion = f32[2,8,512]{2,1,0:T(8,128)S(1)} fusion(f32[2,8,512]{2,1,0:T(8,128)S(1)} %subtract_multiply_fusion, f32[8,512,512]{2,1,0:T(8,128)} %param.24), kind=kLoop, calls=%fused_computation.76 | loop fusion | flops 8380416 | bytes 8454144 | tf_op jit(solution)/shard_map/reduce_sum | solution.py:247
  108.5 1.3 collective-permute-start.13
  109.8 15.6 %conditional.3 = (f32[1,8,60,512]{3,2,1,0:T(8,128)S(1)}) conditional(s32[]{:T(128)} %convert_element_type.32, (pred[8,1,1]{0,2,1:T(4,128)(4,1)S(1)}, f32[10,64,512]{2,0,1:T(8,128)}, pred[10,1,1]{0,2,1:T(4,128)(4,1)S(1)}, f32[8,512]{1,0:T(8,128)S(1)}, f32[12,64,512]{2,0,1:T(8,128)S(1)}, /*index=5*/f32[10,64,512]{2,0,1:T(8,128)}, ...), branch_computations={%region_19.20_spmd, %region_20.21_spmd} | conditional | flops 12091393 | bytes 92563520 | solution.py:287
  113.0 4.8 %fusion.40 = (f32[10,64,512]{2,1,0:T(8,128)S(1)}, f32[10,64,512]{2,1,0:T(8,128)S(1)}, f32[10,64,512]{2,1,0:T(8,128)S(1)}) fusion(f32[10,64,511]{2,1,0:T(8,128)S(1)} %get-tuple-element.224, f32[10,64,511]{2,1,0:T(8,128)S(1)} %get-tuple-element.223, f32[10,63,512]{2,1,0:T(8,128)S(1)} %get-tuple-element.222, f32[10,63,512]{2,1,0:T(8,128)S(1)} %get-tuple-element.221, ...), kind=kLoop, calls=%fused_computation.56 | loop fusion | flops 2949120 | bytes 14371850 | tf_op jit(solution)/shard_map/cond/branch_0_fun/jit(_where)/select_n | solution.py:86
  122.2 1.3 fusion.41
  (257 shorter events, 48.6 us)
Async XLA Ops:
  0.6 4.2 %copy-start.5 = (f32[1,8,64,512]{3,2,1,0:T(8,128)S(1)}, f32[1,8,64,512]{3,2,1,0:T(8,128)}, u32[]{:S(2)}) copy-start(f32[1,8,64,512]{3,2,1,0:T(8,128)} %param.21) | copy-start | bytes 3145732
  4.8 17.2 %copy-start = (f32[1,8,64,512]{3,1,2,0:T(8,128)}, f32[1,8,64,512]{3,1,2,0:T(8,128)S(1)}, u32[]{:S(2)}) copy-start(f32[1,8,64,512]{3,1,2,0:T(8,128)S(1)} %copy.91) | copy-start | bytes 3145732
  7.1 7.3 %copy-start.31 = (s32[8]{0:T(128)S(1)}, s32[8]{0:T(128)}, u32[]{:S(2)}) copy-start(s32[8]{0:T(128)} %param.29) | copy-start | bytes 100
  8.1 9.7 %collective-permute-start.1 = (f32[100,512]{1,0:T(8,128)S(1)}, f32[100,512]{1,0:T(8,128)S(1)}, u32[]{:S(2)}, u32[]{:S(2)}) collective-permute-start(f32[100,512]{1,0:T(8,128)S(1)} %pad_maximum_fusion.11), channel_id=1, source_target_pairs={{1,0},{2,1},{3,2},{4,3},{5,4},{6,5},{7,6},{9,8},{10,9},{11,10},{12... | collective-permute-start | bytes 614408 | tf_op jit(solution)/shard_map/ppermute | solution.py:63
  9.5 8.5 %collective-permute-start = (f32[100,512]{1,0:T(8,128)S(1)}, f32[100,512]{1,0:T(8,128)S(1)}, u32[]{:S(2)}, u32[]{:S(2)}) collective-permute-start(f32[100,512]{1,0:T(8,128)S(1)} %pad_maximum_fusion.10), channel_id=1, source_target_pairs={{0,1},{1,2},{2,3},{3,4},{4,5},{5,6},{6,7},{8,9},{9,10},{10,11},{11... | collective-permute-start | bytes 614408 | tf_op jit(solution)/shard_map/ppermute | solution.py:62
  17.8 21.5 %copy-start.26 = (pred[8]{0:T(512)(128)(4,1)}, pred[8]{0:T(512)(128)(4,1)S(1)}, u32[]{:S(2)}) copy-start(pred[8]{0:T(512)(128)(4,1)S(1)} %get-tuple-element.306) | copy-start | bytes 28
  17.8 35.5 %copy-start.22 = (pred[8,1,1]{0,2,1:T(4,128)(4,1)}, pred[8,1,1]{0,2,1:T(4,128)(4,1)S(1)}, u32[]{:S(2)}) copy-start(pred[8,1,1]{0,2,1:T(4,128)(4,1)S(1)} %get-tuple-element.305) | copy-start | bytes 28
  18.6 4.5 %slice-start = ((s8[8388608]{0:T(1024)(128)(4,1)}), s8[4194304]{0:T(1024)(128)(4,1)S(1)}, s32[]{:S(2)}) async-start(s8[8388608]{0:T(1024)(128)(4,1)} %bitcast.100), calls=%async_computation | async-start | bytes 8388608
  18.8 1.8 %slice-start.3 = ((f32[100,512]{1,0:T(8,128)}), f32[4,512]{1,0:T(4,128)S(1)}, s32[]{:S(2)}) async-start(f32[100,512]{1,0:T(8,128)} %copy-done.10), calls=%async_computation.3 | async-start | bytes 16384 | tf_op jit(solution)/shard_map/slice | solution.py:68
  18.9 1.8 %copy-start.28 = (pred[14]{0:T(512)(128)(4,1)S(1)}, pred[14]{0:T(512)(128)(4,1)}, u32[]{:S(2)}) copy-start(pred[14]{0:T(512)(128)(4,1)} %slice.1000) | copy-start | bytes 46
  20.7 17.8 %copy-start.7 = (f32[16,1,512]{2,0,1:T(8,128)}, f32[16,1,512]{2,0,1:T(8,128)S(1)}, u32[]{:S(2)}) copy-start(f32[16,1,512]{2,0,1:T(8,128)S(1)} %get-tuple-element.188) | copy-start | bytes 98308
  20.9 2.2 %slice-start.1 = ((s8[8388608]{0:T(1024)(128)(4,1)}), s8[4194304]{0:T(1024)(128)(4,1)S(1)}, s32[]{:S(2)}) async-start(s8[8388608]{0:T(1024)(128)(4,1)} %bitcast.100), calls=%async_computation.1 | async-start | bytes 8388608
  26.2 14.2 %collective-permute-start.3 = (f32[224,512]{1,0:T(8,128)S(1)}, f32[224,512]{1,0:T(8,128)S(1)}, u32[]{:S(2)}, u32[]{:S(2)}) collective-permute-start(f32[224,512]{1,0:T(8,128)S(1)} %pad_maximum_fusion.6), channel_id=1, source_target_pairs={{1,0},{2,1},{3,2},{4,3},{5,4},{6,5},{7,6},{9,8},{10,9},{11,10},{12... | collective-permute-start | bytes 1376264 | tf_op jit(solution)/shard_map/ppermute | solution.py:63
  27.7 10.7 %collective-permute-start.5 = (f32[4,512]{1,0:T(4,128)S(1)}, f32[4,512]{1,0:T(4,128)S(1)}, u32[]{:S(2)}, u32[]{:S(2)}) collective-permute-start(f32[4,512]{1,0:T(4,128)S(1)} %get-tuple-element.295), channel_id=1, source_target_pairs={{1,0},{2,1},{3,2},{4,3},{5,4},{6,5},{7,6},{9,8},{10,9},{11,10},{12... | collective-permute-start | bytes 24584 | tf_op jit(solution)/shard_map/ppermute | solution.py:63
  29.0 9.4 %collective-permute-start.4 = (f32[4,512]{1,0:T(4,128)S(1)}, f32[4,512]{1,0:T(4,128)S(1)}, u32[]{:S(2)}, u32[]{:S(2)}) collective-permute-start(f32[4,512]{1,0:T(4,128)S(1)} %get-tuple-element.294), channel_id=1, source_target_pairs={{0,1},{1,2},{2,3},{3,4},{4,5},{5,6},{6,7},{8,9},{9,10},{10,11},{11... | collective-permute-start | bytes 24584 | tf_op jit(solution)/shard_map/ppermute | solution.py:62
  34.7 5.8 %collective-permute-start.2 = (f32[224,512]{1,0:T(8,128)S(1)}, f32[224,512]{1,0:T(8,128)S(1)}, u32[]{:S(2)}, u32[]{:S(2)}) collective-permute-start(f32[224,512]{1,0:T(8,128)S(1)} %pad_maximum_fusion.5), channel_id=1, source_target_pairs={{0,1},{1,2},{2,3},{3,4},{4,5},{5,6},{6,7},{8,9},{9,10},{10,11},{11... | collective-permute-start | bytes 1376264 | tf_op jit(solution)/shard_map/ppermute | solution.py:62
  43.8 25.8 %collective-permute-start.8 = (f32[2]{0:T(128)}, f32[2]{0:T(128)}, u32[]{:S(2)}, u32[]{:S(2)}) collective-permute-start(f32[2]{0:T(128)} %pad_maximum_fusion.14), channel_id=1, source_target_pairs={{0,1},{1,0},{2,3},{3,2},{4,5},{5,4},{6,7},{7,6},{8,9},{9,8},{10,11... | collective-permute-start | bytes 32 | tf_op jit(solution)/shard_map/ppermute | solution.py:111
  50.8 2.5 %copy-start.21 = (pred[10,1,1]{0,2,1:T(4,128)(4,1)S(1)}, pred[10,1,1]{0,2,1:T(4,128)(4,1)}, u32[]{:S(2)}) copy-start(pred[10,1,1]{0,2,1:T(4,128)(4,1)} %get-tuple-element.303) | copy-start | bytes 34
  61.6 36.7 %copy-start.8 = (f32[16,1,512]{2,0,1:T(8,128)S(1)}, f32[16,1,512]{2,0,1:T(8,128)}, u32[]{:S(2)}) copy-start(f32[16,1,512]{2,0,1:T(8,128)} %copy-done.7) | copy-start | bytes 98308
  63.1 33.6 %collective-permute-start.7 = (f32[136,512]{1,0:T(8,128)}, f32[136,512]{1,0:T(8,128)}, u32[]{:S(2)}, u32[]{:S(2)}) collective-permute-start(f32[136,512]{1,0:T(8,128)} %pad_maximum_fusion.9), channel_id=1, source_target_pairs={{1,0},{2,1},{3,2},{4,3},{5,4},{6,5},{7,6},{9,8},{10,9},{11,10},{12... | collective-permute-start | bytes 835592 | tf_op jit(solution)/shard_map/ppermute | solution.py:63
  65.8 31.7 %collective-permute-start.6 = (f32[136,512]{1,0:T(8,128)}, f32[136,512]{1,0:T(8,128)}, u32[]{:S(2)}, u32[]{:S(2)}) collective-permute-start(f32[136,512]{1,0:T(8,128)} %pad_maximum_fusion.8), channel_id=1, source_target_pairs={{0,1},{1,2},{2,3},{3,4},{4,5},{5,6},{6,7},{8,9},{9,10},{10,11},{11... | collective-permute-start | bytes 835592 | tf_op jit(solution)/shard_map/ppermute | solution.py:62
  71.5 3.8 %collective-permute-start.9 = (f32[2]{0:T(128)S(1)}, f32[2]{0:T(128)S(1)}, u32[]{:S(2)}, u32[]{:S(2)}) collective-permute-start(f32[2]{0:T(128)S(1)} %fusion.208), channel_id=1, source_target_pairs={{0,2},{1,3},{2,0},{3,1},{4,6},{5,7},{6,4},{7,5},{8,10},{9,11},{10,... | collective-permute-start | bytes 32 | tf_op jit(solution)/shard_map/ppermute | solution.py:111
  77.3 5.4 %collective-permute-start.10 = (f32[2]{0:T(128)S(1)}, f32[2]{0:T(128)S(1)}, u32[]{:S(2)}, u32[]{:S(2)}) collective-permute-start(f32[2]{0:T(128)S(1)} %fusion.209), channel_id=1, source_target_pairs={{0,4},{1,5},{2,6},{3,7},{4,0},{5,1},{6,2},{7,3},{8,12},{9,13},{10,... | collective-permute-start | bytes 32 | tf_op jit(solution)/shard_map/ppermute | solution.py:111
  82.7 6.4 %collective-permute-start.11 = (f32[2]{0:T(128)S(1)}, f32[2]{0:T(128)S(1)}, u32[]{:S(2)}, u32[]{:S(2)}) collective-permute-start(f32[2]{0:T(128)S(1)} %add.836), channel_id=1, source_target_pairs={{0,16},{1,17},{2,18},{3,19},{4,20},{5,21},{6,22},{7,23},{8,0},{9,1... | collective-permute-start | bytes 32 | tf_op jit(solution)/shard_map/ppermute | solution.py:132
  87.2 6.3 %collective-permute-start.12 = (f32[2]{0:T(128)S(1)}, f32[2]{0:T(128)S(1)}, u32[]{:S(2)}, u32[]{:S(2)}) collective-permute-start(f32[2]{0:T(128)S(1)} %add.836), channel_id=1, source_target_pairs={{0,8},{1,9},{2,10},{3,11},{4,12},{5,13},{6,14},{7,15},{8,16},{9,17... | collective-permute-start | bytes 32 | tf_op jit(solution)/shard_map/ppermute | solution.py:132
  102.4 7.4 %copy-start.23 = (pred[8,1,1]{0,2,1:T(4,128)(4,1)S(1)}, pred[8,1,1]{0,2,1:T(4,128)(4,1)}, u32[]{:S(2)}) copy-start(pred[8,1,1]{0,2,1:T(4,128)(4,1)} %copy-done.22) | copy-start | bytes 28
  107.1 19.4 %collective-permute-start.15 = (f32[37,512]{1,0:T(8,128)S(1)}, f32[37,512]{1,0:T(8,128)S(1)}, u32[]{:S(2)}, u32[]{:S(2)}) collective-permute-start(f32[37,512]{1,0:T(8,128)S(1)} %concatenate.368), channel_id=1, source_target_pairs={{16,24},{17,25},{18,26},{19,27},{20,28},{21,29},{22,30},{23,31}} | collective-permute-start | bytes 227336 | tf_op jit(solution)/shard_map/ppermute | solution.py:292
  107.8 18.8 %collective-permute-start.14 = (f32[37,512]{1,0:T(8,128)S(1)}, f32[37,512]{1,0:T(8,128)S(1)}, u32[]{:S(2)}, u32[]{:S(2)}) collective-permute-start(f32[37,512]{1,0:T(8,128)S(1)} %concatenate.368), channel_id=1, source_target_pairs={{8,24},{9,25},{10,26},{11,27},{12,28},{13,29},{14,30},{15,31}} | collective-permute-start | bytes 227336 | tf_op jit(solution)/shard_map/ppermute | solution.py:292
  108.5 18.1 %collective-permute-start.13 = (f32[37,512]{1,0:T(8,128)S(1)}, f32[37,512]{1,0:T(8,128)S(1)}, u32[]{:S(2)}, u32[]{:S(2)}) collective-permute-start(f32[37,512]{1,0:T(8,128)S(1)} %concatenate.368), channel_id=1, source_target_pairs={{0,24},{1,25},{2,26},{3,27},{4,28},{5,29},{6,30},{7,31}} | collective-permute-start | bytes 227336 | tf_op jit(solution)/shard_map/ppermute | solution.py:292
  127.3 0.7 collective-permute-start.16
  127.9 0.7 collective-permute-start.17
  128.6 0.7 collective-permute-start.18
  (23 other events, 24.9 us)

commit v16 on v13

--- a/solution.py
+++ b/solution.py
@@ -229,9 +229,7 @@
         side_count - 1,
     )
     step_one = tilde_one - tilde_zero
-    rims_base, rims_step, deep = exchange(
-        [(plane_of(tilde_one), HALO), (plane_of(step_one), HALO), (deep, 2)]
-    )
+    rims_base, rims_step = exchange([(plane_of(tilde_one), HALO), (plane_of(step_one), HALO)])
     band_base = band_solve(init_band, force_band.at[:, 0, :].add(rims_base), coef_band, row_ok)
     band_step = band_solve(
         jnp.zeros_like(init_band), jnp.zeros_like(force_band).at[:, 0, :].set(rims_step), coef_band, row_ok
@@ -244,6 +242,7 @@
     gram_aa, gram_ab = sums[0], sums[1]
     coeff = -gram_ab / (gram_aa + (0.001 * gram_aa + 1e-06))
     disp_two = tilde_one + coeff * step_one
+    (deep,) = exchange([(deep + 0.0 * coeff, 2)])
     tilde_two = tilde_base + coeff * tilde_step
     band_two = band_base + coeff * band_step
     deep = lax.cond(

time: 129 us -> 128 us (level)
  starting transfers between devices: 33.1 us -> 38.2 us
  other arithmetic: 25.8 us -> 22.5 us
  waiting for transfers between devices: 36.5 us -> 34.9 us
    ppermute x4 -> x5, starting transfers between devices: 8.52 us -> 12.7 us  [exchange(): high = lax.ppermute(down, 'slab', backward)]
    reduce_sum x1, other arithmetic: 4.63 us -> 1.22 us  [body(): jnp.sum(compliance[None] * loaded[:, :, None, :], axis=-1)]
    ppermute x3, waiting for transfers between devices: 16.1 us -> 12.8 us  [body(): lax.ppermute(outgoing, 'side', [(source, side_count - 1)])]
    slice x5 -> x4, local copies, waits for them, and re-layouts: 3.69 us -> 1.69 us  [exchange(): low[at:at + n].reshape(shape)]
    ppermute x4 -> x5, waiting for transfers between devices: 8.51 us -> 10.4 us  [exchange(): low = lax.ppermute(up, 'slab', forward)]
    ppermute x4 -> x5, starting transfers between devices: 10.4 us -> 11.1 us  [exchange(): low = lax.ppermute(up, 'slab', forward)]
    unnamed x43 -> x61, local copies, waits for them, and re-layouts: 6.09 us -> 6.53 us
  transfers between devices with their start and end apart: 19 -> 21, of which waited for: 10 -> 9; matrix products, arithmetic and copies ran while one was open for 14% -> 15% of each run, Pallas kernels for 0% -> 0%
where the time goes in v16:
time: 128 us; the launch traced here: 127 us
  starting transfers between devices  38.2 us (30%)
  waiting for transfers between devices  34.9 us (27%)
  other arithmetic  22.5 us (18%)
  local copies, waits for them, and re-layouts  18.6 us (15%)
  between operations  12.4 us (10%)
    ppermute x3, waiting for transfers between devices, body(): lax.ppermute(outgoing, 'side', [(source, side_count - 1)])  12.8 us
    ppermute x5, starting transfers between devices, exchange(): high = lax.ppermute(down, 'slab', backward)  12.7 us
    ppermute x5, starting transfers between devices, exchange(): low = lax.ppermute(up, 'slab', forward)  11.1 us
    ppermute x5, waiting for transfers between devices, exchange(): low = lax.ppermute(up, 'slab', forward)  10.4 us
    ppermute x3, starting transfers between devices, shell_sum(): v = v + lax.ppermute(v, ('side', 'slab'), pairs)  7.57 us
    unnamed x61, local copies, waits for them, and re-layouts  6.53 us
    ppermute x3, waiting for transfers between devices, shell_sum(): v = v + lax.ppermute(v, ('side', 'slab'), pairs)  6.26 us
    ppermute x3, waiting for transfers between devices, allsum_axis(): v = v + lax.ppermute(v, axis, [(i, i ^ step) for i in range(count)])  5.44 us
  transfers between devices with their start and end apart: 21, of which 9 were waited for; matrix products, arithmetic and copies ran while one was open for 15% of the time, Pallas kernels for 0%

profile of v16, /device:TPU:28, one launch (start us, length us, event | category | flops | bytes accessed | tf_op | source)
XLA Modules:
  0.0 126.7 jit_solution(2517054578074512931)
XLA Ops:
  3.0 1.8 %copy.90 = f32[1,8,64,512]{3,1,2,0:T(8,128)S(1)} copy(f32[1,8,64,512]{3,2,1,0:T(8,128)} %param.21) | data formatting | bytes 2097152 | tf_op args[0]
  7.7 2.8 %collective-permute-start.1 = (f32[100,512]{1,0:T(8,128)S(1)}, f32[100,512]{1,0:T(8,128)}, u32[]{:S(2)}, u32[]{:S(2)}) collective-permute-start(f32[100,512]{1,0:T(8,128)S(1)} %pad_maximum_fusion.9), channel_id=1, source_target_pairs={{1,0},{2,1},{3,2},{4,3},{5,4},{6,5},{7,6},{9,8},{10,9},{11,10},{12... | collective-permute-start | bytes 614408 | tf_op jit(solution)/shard_map/ppermute | solution.py:63
  10.6 1.9 %collective-permute-start = (f32[100,512]{1,0:T(8,128)S(1)}, f32[100,512]{1,0:T(8,128)}, u32[]{:S(2)}, u32[]{:S(2)}) collective-permute-start(f32[100,512]{1,0:T(8,128)S(1)} %pad_maximum_fusion.8), channel_id=1, source_target_pairs={{0,1},{1,2},{2,3},{3,4},{4,5},{5,6},{6,7},{8,9},{9,10},{10,11},{11... | collective-permute-start | bytes 614408 | tf_op jit(solution)/shard_map/ppermute | solution.py:62
  14.6 4.1 %collective-permute-done = f32[100,512]{1,0:T(8,128)} collective-permute-done((f32[100,512]{1,0:T(8,128)S(1)}, f32[100,512]{1,0:T(8,128)}, u32[]{:S(2)}, u32[]{:S(2)}) %collective-permute-start) | collective-permute-done | bytes 204832 | tf_op jit(solution)/shard_map/ppermute | solution.py:62
  26.6 2.1 %collective-permute-start.3 = (f32[224,512]{1,0:T(8,128)S(1)}, f32[224,512]{1,0:T(8,128)S(1)}, u32[]{:S(2)}, u32[]{:S(2)}) collective-permute-start(f32[224,512]{1,0:T(8,128)S(1)} %pad_maximum_fusion.6), channel_id=1, source_target_pairs={{1,0},{2,1},{3,2},{4,3},{5,4},{6,5},{7,6},{9,8},{10,9},{11,10},{12... | collective-permute-start | bytes 1376264 | tf_op jit(solution)/shard_map/ppermute | solution.py:63
  29.8 2.4 %collective-permute-start.4 = (f32[4,512]{1,0:T(4,128)S(1)}, f32[4,512]{1,0:T(4,128)S(1)}, u32[]{:S(2)}, u32[]{:S(2)}) collective-permute-start(f32[4,512]{1,0:T(4,128)S(1)} %get-tuple-element.225), channel_id=1, source_target_pairs={{0,1},{1,2},{2,3},{3,4},{4,5},{5,6},{6,7},{8,9},{9,10},{10,11},{11... | collective-permute-start | bytes 24584 | tf_op jit(solution)/shard_map/ppermute | solution.py:62
  32.3 4.1 %collective-permute-start.5 = (f32[4,512]{1,0:T(4,128)S(1)}, f32[4,512]{1,0:T(4,128)S(1)}, u32[]{:S(2)}, u32[]{:S(2)}) collective-permute-start(f32[4,512]{1,0:T(4,128)S(1)} %get-tuple-element.226), channel_id=1, source_target_pairs={{1,0},{2,1},{3,2},{4,3},{5,4},{6,5},{7,6},{9,8},{10,9},{11,10},{12... | collective-permute-start | bytes 24584 | tf_op jit(solution)/shard_map/ppermute | solution.py:63
  36.4 1.9 %collective-permute-start.2 = (f32[224,512]{1,0:T(8,128)S(1)}, f32[224,512]{1,0:T(8,128)S(1)}, u32[]{:S(2)}, u32[]{:S(2)}) collective-permute-start(f32[224,512]{1,0:T(8,128)S(1)} %pad_maximum_fusion.5), channel_id=1, source_target_pairs={{0,1},{1,2},{2,3},{3,4},{4,5},{5,6},{6,7},{8,9},{9,10},{10,11},{11... | collective-permute-start | bytes 1376264 | tf_op jit(solution)/shard_map/ppermute | solution.py:62
  40.8 6.2 %collective-permute-done.2 = f32[224,512]{1,0:T(8,128)S(1)} collective-permute-done((f32[224,512]{1,0:T(8,128)S(1)}, f32[224,512]{1,0:T(8,128)S(1)}, u32[]{:S(2)}, u32[]{:S(2)}) %collective-permute-start.2) | collective-permute-done | bytes 458784 | tf_op jit(solution)/shard_map/ppermute | solution.py:62
  47.8 1.4 %multiply_reduce_fusion.15 = (f32[]{:T(128)}, f32[]{:T(128)}, f32[8,512]{1,0:T(8,128)S(1)}, f32[8,512]{1,0:T(8,128)}, f32[8,512]{1,0:T(8,128)S(1)}, /*index=5*/f32[8,512]{1,0:T(8,128)S(1)}, f32[8,512]{1,0:T(8,128)}) fusion(f32[8,512]{1,0:T(8,128)S(1)} %get-tuple-element.144, f32[8,512]{1,0:T(8,128)S(1)} %copy-done.8, f32[8]{0:T(128)S(1)} %fusion.123, ...), kind=kLoop, calls=%fused_computation.215 | loop fusion | flops 61438 | bytes 131144 | tf_op jit(solution)/shard_map/reduce_sum | solution.py:227
  49.2 1.3 %pad_maximum_fusion.14 = f32[2]{0:T(128)S(1)} fusion(f32[1]{0:T(128)} %bitcast.30, f32[1]{0:T(128)} %bitcast.29), kind=kLoop, calls=%fused_computation.252 | loop fusion | flops 2 | bytes 16 | tf_op jit(solution)/shard_map/stack | solution.py:227
  50.7 1.9 %collective-permute-start.7 = (f32[8,512]{1,0:T(8,128)S(1)}, f32[8,512]{1,0:T(8,128)S(1)}, u32[]{:S(2)}, u32[]{:S(2)}) collective-permute-start(f32[8,512]{1,0:T(8,128)S(1)} %pad_maximum_fusion.13), channel_id=1, source_target_pairs={{1,0},{2,1},{3,2},{4,3},{5,4},{6,5},{7,6},{9,8},{10,9},{11,10},{12... | collective-permute-start | bytes 49160 | tf_op jit(solution)/shard_map/ppermute | solution.py:63
  52.7 2.4 %collective-permute-start.6 = (f32[8,512]{1,0:T(8,128)S(1)}, f32[8,512]{1,0:T(8,128)S(1)}, u32[]{:S(2)}, u32[]{:S(2)}) collective-permute-start(f32[8,512]{1,0:T(8,128)S(1)} %pad_maximum_fusion.12), channel_id=1, source_target_pairs={{0,1},{1,2},{2,3},{3,4},{4,5},{5,6},{6,7},{8,9},{9,10},{10,11},{11... | collective-permute-start | bytes 49160 | tf_op jit(solution)/shard_map/ppermute | solution.py:62
  56.6 2.5 %pad_maximum_fusion.1 = (f32[10,64,512]{2,0,1:T(8,128)}, f32[10,64,512]{2,0,1:T(8,128)}) fusion(f32[10,56,512]{2,0,1:T(8,128)S(1)} %get-tuple-element.166, f32[10,8,512]{2,0,1:T(8,128)S(1)} %get-tuple-element.180, f32[10,56,512]{2,0,1:T(8,128)S(1)} %get-tuple-element.165, f32[10,8,512]{2,0,1:T(8,128)S(1)} %get-tuple-element.179), kind=kLoop, calls=%fused_computation.33 | loop fusion | flops 655360 | bytes 5242880 | tf_op jit(solution)/shard_map/concatenate | solution.py:187
  59.2 1.3 %fusion.169 = f32[2]{0:T(128)S(1)} fusion(f32[2]{0:T(128)S(1)} %collective-permute-done.8, f32[1]{0:T(128)} %bitcast.30, f32[1]{0:T(128)} %bitcast.29), kind=kLoop, calls=%fused_computation.293 | loop fusion | flops 4 | bytes 24 | tf_op jit(solution)/shard_map/add | solution.py:111
  60.5 1.6 %collective-permute-start.9 = (f32[2]{0:T(128)S(1)}, f32[2]{0:T(128)S(1)}, u32[]{:S(2)}, u32[]{:S(2)}) collective-permute-start(f32[2]{0:T(128)S(1)} %fusion.169), channel_id=1, source_target_pairs={{0,2},{1,3},{2,0},{3,1},{4,6},{5,7},{6,4},{7,5},{8,10},{9,11},{10,... | collective-permute-start | bytes 32 | tf_op jit(solution)/shard_map/ppermute | solution.py:111
  62.1 1.9 %collective-permute-done.9 = f32[2]{0:T(128)S(1)} collective-permute-done((f32[2]{0:T(128)S(1)}, f32[2]{0:T(128)S(1)}, u32[]{:S(2)}, u32[]{:S(2)}) %collective-permute-start.9) | collective-permute-done | bytes 40 | tf_op jit(solution)/shard_map/ppermute | solution.py:111
  64.1 1.3 %fusion.170 = f32[2]{0:T(128)S(1)} fusion(f32[2]{0:T(128)S(1)} %collective-permute-done.9, f32[2]{0:T(128)S(1)} %collective-permute-done.8, f32[1]{0:T(128)} %bitcast.30, f32[1]{0:T(128)} %bitcast.29), kind=kLoop, calls=%fused_computation.294 | loop fusion | flops 6 | bytes 32 | tf_op jit(solution)/shard_map/add | solution.py:111
  65.4 3.5 %collective-permute-done.10 = f32[2]{0:T(128)S(1)} collective-permute-done((f32[2]{0:T(128)S(1)}, f32[2]{0:T(128)S(1)}, u32[]{:S(2)}, u32[]{:S(2)}) %collective-permute-start.10) | collective-permute-done | bytes 40 | tf_op jit(solution)/shard_map/ppermute | solution.py:111
  78.6 1.2 multiply_reduce_fusion
  80.0 1.3 %collective-permute-start.15 = (f32[37,512]{1,0:T(8,128)S(1)}, f32[37,512]{1,0:T(8,128)S(1)}, u32[]{:S(2)}, u32[]{:S(2)}) collective-permute-start(f32[37,512]{1,0:T(8,128)S(1)} %concatenate.309), channel_id=1, source_target_pairs={{16,24},{17,25},{18,26},{19,27},{20,28},{21,29},{22,30},{23,31}} | collective-permute-start | bytes 227336 | tf_op jit(solution)/shard_map/ppermute | solution.py:279
  81.3 1.3 %collective-permute-start.14 = (f32[37,512]{1,0:T(8,128)S(1)}, f32[37,512]{1,0:T(8,128)S(1)}, u32[]{:S(2)}, u32[]{:S(2)}) collective-permute-start(f32[37,512]{1,0:T(8,128)S(1)} %concatenate.309), channel_id=1, source_target_pairs={{8,24},{9,25},{10,26},{11,27},{12,28},{13,29},{14,30},{15,31}} | collective-permute-start | bytes 227336 | tf_op jit(solution)/shard_map/ppermute | solution.py:279
  82.6 1.3 %collective-permute-start.13 = (f32[37,512]{1,0:T(8,128)S(1)}, f32[37,512]{1,0:T(8,128)S(1)}, u32[]{:S(2)}, u32[]{:S(2)}) collective-permute-start(f32[37,512]{1,0:T(8,128)S(1)} %concatenate.309), channel_id=1, source_target_pairs={{0,24},{1,25},{2,26},{3,27},{4,28},{5,29},{6,30},{7,31}} | collective-permute-start | bytes 227336 | tf_op jit(solution)/shard_map/ppermute | solution.py:279
  83.9 1.9 %collective-permute-start.20 = (f32[128,512]{1,0:T(8,128)S(1)}, f32[128,512]{1,0:T(8,128)S(1)}, u32[]{:S(2)}, u32[]{:S(2)}) collective-permute-start(f32[128,512]{1,0:T(8,128)S(1)} %bitcast.119), channel_id=1, source_target_pairs={{1,0},{2,1},{3,2},{4,3},{5,4},{6,5},{7,6},{9,8},{10,9},{11,10},{12... | collective-permute-start | bytes 786440 | tf_op jit(solution)/shard_map/ppermute | solution.py:63
  85.8 2.4 %collective-permute-start.19 = (f32[128,512]{1,0:T(8,128)S(1)}, f32[128,512]{1,0:T(8,128)S(1)}, u32[]{:S(2)}, u32[]{:S(2)}) collective-permute-start(f32[128,512]{1,0:T(8,128)S(1)} %bitcast.118), channel_id=1, source_target_pairs={{0,1},{1,2},{2,3},{3,4},{4,5},{5,6},{6,7},{8,9},{9,10},{10,11},{11... | collective-permute-start | bytes 786440 | tf_op jit(solution)/shard_map/ppermute | solution.py:62
  88.3 11.0 %collective-permute-done.15 = f32[37,512]{1,0:T(8,128)S(1)} collective-permute-done((f32[37,512]{1,0:T(8,128)S(1)}, f32[37,512]{1,0:T(8,128)S(1)}, u32[]{:S(2)}, u32[]{:S(2)}) %collective-permute-start.15) | collective-permute-done | bytes 75808 | tf_op jit(solution)/shard_map/ppermute | solution.py:279
  99.3 1.8 %collective-permute-done.14 = f32[37,512]{1,0:T(8,128)S(1)} collective-permute-done((f32[37,512]{1,0:T(8,128)S(1)}, f32[37,512]{1,0:T(8,128)S(1)}, u32[]{:S(2)}, u32[]{:S(2)}) %collective-permute-start.14) | collective-permute-done | bytes 75808 | tf_op jit(solution)/shard_map/ppermute | solution.py:279
  101.8 1.9 %collective-permute-start.16 = (f32[4]{0:T(128)S(1)}, f32[4]{0:T(128)S(1)}, u32[]{:S(2)}, u32[]{:S(2)}) collective-permute-start(f32[4]{0:T(128)S(1)} %slice_reduce_fusion), channel_id=1, source_target_pairs={{24,25},{25,24},{26,27},{27,26},{28,29},{29,28},{30,31},{31,30}} | collective-permute-start | bytes 56 | tf_op jit(solution)/shard_map/ppermute | solution.py:122
  104.8 3.5 %collective-permute-start.17 = (f32[4]{0:T(128)S(1)}, f32[4]{0:T(128)S(1)}, u32[]{:S(2)}, u32[]{:S(2)}) collective-permute-start(f32[4]{0:T(128)S(1)} %add.705), channel_id=1, source_target_pairs={{24,26},{25,27},{26,24},{27,25},{28,30},{29,31},{30,28},{31,29}} | collective-permute-start | bytes 56 | tf_op jit(solution)/shard_map/ppermute | solution.py:122
  108.4 1.9 %collective-permute-done.17 = f32[4]{0:T(128)S(1)} collective-permute-done((f32[4]{0:T(128)S(1)}, f32[4]{0:T(128)S(1)}, u32[]{:S(2)}, u32[]{:S(2)}) %collective-permute-start.17) | collective-permute-done | bytes 48 | tf_op jit(solution)/shard_map/ppermute | solution.py:122
  110.3 2.1 %collective-permute-start.18 = (f32[4]{0:T(128)S(1)}, f32[4]{0:T(128)S(1)}, u32[]{:S(2)}, u32[]{:S(2)}) collective-permute-start(f32[4]{0:T(128)S(1)} %add.706), channel_id=1, source_target_pairs={{24,28},{25,29},{26,30},{27,31},{28,24},{29,25},{30,26},{31,27}} | collective-permute-start | bytes 56 | tf_op jit(solution)/shard_map/ppermute | solution.py:122
  112.4 3.3 %collective-permute-done.18 = f32[4]{0:T(128)S(1)} collective-permute-done((f32[4]{0:T(128)S(1)}, f32[4]{0:T(128)S(1)}, u32[]{:S(2)}, u32[]{:S(2)}) %collective-permute-start.18) | collective-permute-done | bytes 48 | tf_op jit(solution)/shard_map/ppermute | solution.py:122
  (222 shorter events, 32.9 us)
Async XLA Ops:
  5.5 18.7 %copy-start.1 = (f32[1,8,64,512]{3,1,2,0:T(8,128)}, f32[1,8,64,512]{3,1,2,0:T(8,128)S(1)}, u32[]{:S(2)}) copy-start(f32[1,8,64,512]{3,1,2,0:T(8,128)S(1)} %copy.89) | copy-start | bytes 3145732
  6.7 6.5 %copy-start.21 = (s32[8]{0:T(128)S(1)}, s32[8]{0:T(128)}, u32[]{:S(2)}) copy-start(s32[8]{0:T(128)} %param.29) | copy-start | bytes 100
  6.7 6.6 %copy-start.11 = (s32[8]{0:T(128)S(1)}, s32[8]{0:T(128)}, u32[]{:S(2)}) copy-start(s32[8]{0:T(128)} %param.27) | copy-start | bytes 100
  7.7 12.6 %collective-permute-start.1 = (f32[100,512]{1,0:T(8,128)S(1)}, f32[100,512]{1,0:T(8,128)}, u32[]{:S(2)}, u32[]{:S(2)}) collective-permute-start(f32[100,512]{1,0:T(8,128)S(1)} %pad_maximum_fusion.9), channel_id=1, source_target_pairs={{1,0},{2,1},{3,2},{4,3},{5,4},{6,5},{7,6},{9,8},{10,9},{11,10},{12... | collective-permute-start | bytes 614408 | tf_op jit(solution)/shard_map/ppermute | solution.py:63
  10.6 8.2 %collective-permute-start = (f32[100,512]{1,0:T(8,128)S(1)}, f32[100,512]{1,0:T(8,128)}, u32[]{:S(2)}, u32[]{:S(2)}) collective-permute-start(f32[100,512]{1,0:T(8,128)S(1)} %pad_maximum_fusion.8), channel_id=1, source_target_pairs={{0,1},{1,2},{2,3},{3,4},{4,5},{5,6},{6,7},{8,9},{9,10},{10,11},{11... | collective-permute-start | bytes 614408 | tf_op jit(solution)/shard_map/ppermute | solution.py:62
  12.6 10.7 %copy-start.15 = (pred[14]{0:T(512)(128)(4,1)}, pred[14]{0:T(512)(128)(4,1)S(1)}, u32[]{:S(2)}) copy-start(pred[14]{0:T(512)(128)(4,1)S(1)} %slice.818) | copy-start | bytes 46
  13.3 15.4 %copy-start.12 = (pred[8]{0:T(512)(128)(4,1)}, pred[8]{0:T(512)(128)(4,1)S(1)}, u32[]{:S(2)}) copy-start(pred[8]{0:T(512)(128)(4,1)S(1)} %get-tuple-element.233) | copy-start | bytes 28
  14.6 24.4 %copy-start.17 = (pred[10]{0:T(512)(128)(4,1)}, pred[10]{0:T(512)(128)(4,1)S(1)}, u32[]{:S(2)}) copy-start(pred[10]{0:T(512)(128)(4,1)S(1)} %get-tuple-element.231) | copy-start | bytes 34
  14.6 44.5 %copy-start.19 = (pred[10,1,1]{0,2,1:T(4,128)(4,1)}, pred[10,1,1]{0,2,1:T(4,128)(4,1)S(1)}, u32[]{:S(2)}) copy-start(pred[10,1,1]{0,2,1:T(4,128)(4,1)S(1)} %get-tuple-element.230) | copy-start | bytes 34
  23.7 5.2 %slice-start = ((s8[8388608]{0:T(1024)(128)(4,1)}), s8[4194304]{0:T(1024)(128)(4,1)S(1)}, s32[]{:S(2)}) async-start(s8[8388608]{0:T(1024)(128)(4,1)} %bitcast.93), calls=%async_computation | async-start | bytes 8388608
  26.6 13.9 %collective-permute-start.3 = (f32[224,512]{1,0:T(8,128)S(1)}, f32[224,512]{1,0:T(8,128)S(1)}, u32[]{:S(2)}, u32[]{:S(2)}) collective-permute-start(f32[224,512]{1,0:T(8,128)S(1)} %pad_maximum_fusion.6), channel_id=1, source_target_pairs={{1,0},{2,1},{3,2},{4,3},{5,4},{6,5},{7,6},{9,8},{10,9},{11,10},{12... | collective-permute-start | bytes 1376264 | tf_op jit(solution)/shard_map/ppermute | solution.py:63
  28.9 9.4 %copy-start.16 = (pred[14]{0:T(512)(128)(4,1)S(1)}, pred[14]{0:T(512)(128)(4,1)}, u32[]{:S(2)}) copy-start(pred[14]{0:T(512)(128)(4,1)} %copy-done.15) | copy-start | bytes 46
  29.8 8.4 %collective-permute-start.4 = (f32[4,512]{1,0:T(4,128)S(1)}, f32[4,512]{1,0:T(4,128)S(1)}, u32[]{:S(2)}, u32[]{:S(2)}) collective-permute-start(f32[4,512]{1,0:T(4,128)S(1)} %get-tuple-element.225), channel_id=1, source_target_pairs={{0,1},{1,2},{2,3},{3,4},{4,5},{5,6},{6,7},{8,9},{9,10},{10,11},{11... | collective-permute-start | bytes 24584 | tf_op jit(solution)/shard_map/ppermute | solution.py:62
  32.3 6.0 %collective-permute-start.5 = (f32[4,512]{1,0:T(4,128)S(1)}, f32[4,512]{1,0:T(4,128)S(1)}, u32[]{:S(2)}, u32[]{:S(2)}) collective-permute-start(f32[4,512]{1,0:T(4,128)S(1)} %get-tuple-element.226), channel_id=1, source_target_pairs={{1,0},{2,1},{3,2},{4,3},{5,4},{6,5},{7,6},{9,8},{10,9},{11,10},{12... | collective-permute-start | bytes 24584 | tf_op jit(solution)/shard_map/ppermute | solution.py:63
  36.4 10.7 %collective-permute-start.2 = (f32[224,512]{1,0:T(8,128)S(1)}, f32[224,512]{1,0:T(8,128)S(1)}, u32[]{:S(2)}, u32[]{:S(2)}) collective-permute-start(f32[224,512]{1,0:T(8,128)S(1)} %pad_maximum_fusion.5), channel_id=1, source_target_pairs={{0,1},{1,2},{2,3},{3,4},{4,5},{5,6},{6,7},{8,9},{9,10},{10,11},{11... | collective-permute-start | bytes 1376264 | tf_op jit(solution)/shard_map/ppermute | solution.py:62
  50.5 8.6 %collective-permute-start.8 = (f32[2]{0:T(128)S(1)}, f32[2]{0:T(128)S(1)}, u32[]{:S(2)}, u32[]{:S(2)}) collective-permute-start(f32[2]{0:T(128)S(1)} %pad_maximum_fusion.14), channel_id=1, source_target_pairs={{0,1},{1,0},{2,3},{3,2},{4,5},{5,4},{6,7},{7,6},{8,9},{9,8},{10,11... | collective-permute-start | bytes 32 | tf_op jit(solution)/shard_map/ppermute | solution.py:111
  50.7 24.2 %collective-permute-start.7 = (f32[8,512]{1,0:T(8,128)S(1)}, f32[8,512]{1,0:T(8,128)S(1)}, u32[]{:S(2)}, u32[]{:S(2)}) collective-permute-start(f32[8,512]{1,0:T(8,128)S(1)} %pad_maximum_fusion.13), channel_id=1, source_target_pairs={{1,0},{2,1},{3,2},{4,3},{5,4},{6,5},{7,6},{9,8},{10,9},{11,10},{12... | collective-permute-start | bytes 49160 | tf_op jit(solution)/shard_map/ppermute | solution.py:63
  52.7 22.3 %collective-permute-start.6 = (f32[8,512]{1,0:T(8,128)S(1)}, f32[8,512]{1,0:T(8,128)S(1)}, u32[]{:S(2)}, u32[]{:S(2)}) collective-permute-start(f32[8,512]{1,0:T(8,128)S(1)} %pad_maximum_fusion.12), channel_id=1, source_target_pairs={{0,1},{1,2},{2,3},{3,4},{4,5},{5,6},{6,7},{8,9},{9,10},{10,11},{11... | collective-permute-start | bytes 49160 | tf_op jit(solution)/shard_map/ppermute | solution.py:62
  60.5 3.5 %collective-permute-start.9 = (f32[2]{0:T(128)S(1)}, f32[2]{0:T(128)S(1)}, u32[]{:S(2)}, u32[]{:S(2)}) collective-permute-start(f32[2]{0:T(128)S(1)} %fusion.169), channel_id=1, source_target_pairs={{0,2},{1,3},{2,0},{3,1},{4,6},{5,7},{6,4},{7,5},{8,10},{9,11},{10,... | collective-permute-start | bytes 32 | tf_op jit(solution)/shard_map/ppermute | solution.py:111
  65.4 3.5 %collective-permute-start.10 = (f32[2]{0:T(128)S(1)}, f32[2]{0:T(128)S(1)}, u32[]{:S(2)}, u32[]{:S(2)}) collective-permute-start(f32[2]{0:T(128)S(1)} %fusion.170), channel_id=1, source_target_pairs={{0,4},{1,5},{2,6},{3,7},{4,0},{5,1},{6,2},{7,3},{8,12},{9,13},{10,... | collective-permute-start | bytes 32 | tf_op jit(solution)/shard_map/ppermute | solution.py:111
  68.9 1.3 %collective-permute-start.12 = (f32[2]{0:T(128)S(1)}, f32[2]{0:T(128)S(1)}, u32[]{:S(2)}, u32[]{:S(2)}) collective-permute-start(f32[2]{0:T(128)S(1)} %add.694), channel_id=1, source_target_pairs={{0,8},{1,9},{2,10},{3,11},{4,12},{5,13},{6,14},{7,15},{8,16},{9,17... | collective-permute-start | bytes 32 | tf_op jit(solution)/shard_map/ppermute | solution.py:132
  69.6 0.7 collective-permute-start.11
  72.7 5.8 %slice-start.2 = ((s8[8388608]{0:T(1024)(128)(4,1)}), s8[4194304]{0:T(1024)(128)(4,1)S(1)}, s32[]{:S(2)}) async-start(s8[8388608]{0:T(1024)(128)(4,1)} %bitcast.95), calls=%async_computation.2 | async-start | bytes 8388608
  78.6 5.2 %copy-start = (f32[8,64,512]{2,1,0:T(8,128)S(1)}, f32[8,64,512]{2,1,0:T(8,128)}, u32[]{:S(2)}) copy-start(f32[8,64,512]{2,1,0:T(8,128)} %broadcast_add_fusion) | copy-start | bytes 3145732
  80.0 19.4 %collective-permute-start.15 = (f32[37,512]{1,0:T(8,128)S(1)}, f32[37,512]{1,0:T(8,128)S(1)}, u32[]{:S(2)}, u32[]{:S(2)}) collective-permute-start(f32[37,512]{1,0:T(8,128)S(1)} %concatenate.309), channel_id=1, source_target_pairs={{16,24},{17,25},{18,26},{19,27},{20,28},{21,29},{22,30},{23,31}} | collective-permute-start | bytes 227336 | tf_op jit(solution)/shard_map/ppermute | solution.py:279
  81.3 19.8 %collective-permute-start.14 = (f32[37,512]{1,0:T(8,128)S(1)}, f32[37,512]{1,0:T(8,128)S(1)}, u32[]{:S(2)}, u32[]{:S(2)}) collective-permute-start(f32[37,512]{1,0:T(8,128)S(1)} %concatenate.309), channel_id=1, source_target_pairs={{8,24},{9,25},{10,26},{11,27},{12,28},{13,29},{14,30},{15,31}} | collective-permute-start | bytes 227336 | tf_op jit(solution)/shard_map/ppermute | solution.py:279
  82.6 18.5 %collective-permute-start.13 = (f32[37,512]{1,0:T(8,128)S(1)}, f32[37,512]{1,0:T(8,128)S(1)}, u32[]{:S(2)}, u32[]{:S(2)}) collective-permute-start(f32[37,512]{1,0:T(8,128)S(1)} %concatenate.309), channel_id=1, source_target_pairs={{0,24},{1,25},{2,26},{3,27},{4,28},{5,29},{6,30},{7,31}} | collective-permute-start | bytes 227336 | tf_op jit(solution)/shard_map/ppermute | solution.py:279
  83.9 40.8 %collective-permute-start.20 = (f32[128,512]{1,0:T(8,128)S(1)}, f32[128,512]{1,0:T(8,128)S(1)}, u32[]{:S(2)}, u32[]{:S(2)}) collective-permute-start(f32[128,512]{1,0:T(8,128)S(1)} %bitcast.119), channel_id=1, source_target_pairs={{1,0},{2,1},{3,2},{4,3},{5,4},{6,5},{7,6},{9,8},{10,9},{11,10},{12... | collective-permute-start | bytes 786440 | tf_op jit(solution)/shard_map/ppermute | solution.py:63
  85.8 38.9 %collective-permute-start.19 = (f32[128,512]{1,0:T(8,128)S(1)}, f32[128,512]{1,0:T(8,128)S(1)}, u32[]{:S(2)}, u32[]{:S(2)}) collective-permute-start(f32[128,512]{1,0:T(8,128)S(1)} %bitcast.118), channel_id=1, source_target_pairs={{0,1},{1,2},{2,3},{3,4},{4,5},{5,6},{6,7},{8,9},{9,10},{10,11},{11... | collective-permute-start | bytes 786440 | tf_op jit(solution)/shard_map/ppermute | solution.py:62
  101.8 3.0 %collective-permute-start.16 = (f32[4]{0:T(128)S(1)}, f32[4]{0:T(128)S(1)}, u32[]{:S(2)}, u32[]{:S(2)}) collective-permute-start(f32[4]{0:T(128)S(1)} %slice_reduce_fusion), channel_id=1, source_target_pairs={{24,25},{25,24},{26,27},{27,26},{28,29},{29,28},{30,31},{31,30}} | collective-permute-start | bytes 56 | tf_op jit(solution)/shard_map/ppermute | solution.py:122
  104.8 5.4 %collective-permute-start.17 = (f32[4]{0:T(128)S(1)}, f32[4]{0:T(128)S(1)}, u32[]{:S(2)}, u32[]{:S(2)}) collective-permute-start(f32[4]{0:T(128)S(1)} %add.705), channel_id=1, source_target_pairs={{24,26},{25,27},{26,24},{27,25},{28,30},{29,31},{30,28},{31,29}} | collective-permute-start | bytes 56 | tf_op jit(solution)/shard_map/ppermute | solution.py:122
  110.3 5.4 %collective-permute-start.18 = (f32[4]{0:T(128)S(1)}, f32[4]{0:T(128)S(1)}, u32[]{:S(2)}, u32[]{:S(2)}) collective-permute-start(f32[4]{0:T(128)S(1)} %add.706), channel_id=1, source_target_pairs={{24,28},{25,29},{26,30},{27,31},{28,24},{29,25},{30,26},{31,27}} | collective-permute-start | bytes 56 | tf_op jit(solution)/shard_map/ppermute | solution.py:122
  (16 other events, 26.7 us)

commit v17 on v16

--- a/solution.py
+++ b/solution.py
@@ -243,6 +243,7 @@
     coeff = -gram_ab / (gram_aa + (0.001 * gram_aa + 1e-06))
     disp_two = tilde_one + coeff * step_one
     (deep,) = exchange([(deep + 0.0 * coeff, 2)])
+    faces_in = deep[0, 0, 0]
     tilde_two = tilde_base + coeff * tilde_step
     band_two = band_base + coeff * band_step
     deep = lax.cond(
@@ -274,6 +275,7 @@
         ],
         axis=0,
     )
+    outgoing = outgoing + 0.0 * faces_in
     gathered = outgoing
     for source in range(side_count - 1):
         gathered = gathered + lax.ppermute(outgoing, "side", [(source, side_count - 1)])

time: 128 us -> 134 us (1.047)
  waiting for transfers between devices: 34.9 us -> 39 us
  starting transfers between devices: 38.2 us -> 39.6 us
    ppermute x3, waiting for transfers between devices: 12.8 us -> 15.8 us  [body(): lax.ppermute(outgoing, 'side', [(source, side_count - 1)])]
    ppermute x5, starting transfers between devices: 12.7 us -> 15.3 us  [exchange(): high = lax.ppermute(down, 'slab', backward)]
    unnamed x61 -> x41, local copies, waits for them, and re-layouts: 6.53 us -> 4.95 us
  transfers between devices with their start and end apart: 21 -> 21, of which waited for: 9 -> 9; matrix products, arithmetic and copies ran while one was open for 15% -> 18% of each run, Pallas kernels for 0% -> 0%
where the time goes in v17:
time: 134 us; the launch traced here: 133 us
  starting transfers between devices  39.6 us (30%)
  waiting for transfers between devices  39 us (29%)
  other arithmetic  22.2 us (17%)
  local copies, waits for them, and re-layouts  18.9 us (14%)
  between operations  13.1 us (10%)
    ppermute x3, waiting for transfers between devices, body(): lax.ppermute(outgoing, 'side', [(source, side_count - 1)])  15.8 us
    ppermute x5, starting transfers between devices, exchange(): high = lax.ppermute(down, 'slab', backward)  15.3 us
    ppermute x5, waiting for transfers between devices, exchange(): low = lax.ppermute(up, 'slab', forward)  10.7 us
    ppermute x5, starting transfers between devices, exchange(): low = lax.ppermute(up, 'slab', forward)  10.6 us
    ppermute x3, waiting for transfers between devices, shell_sum(): v = v + lax.ppermute(v, ('side', 'slab'), pairs)  7.02 us
    ppermute x3, starting transfers between devices, shell_sum(): v = v + lax.ppermute(v, ('side', 'slab'), pairs)  6.81 us
    ppermute x3, waiting for transfers between devices, allsum_axis(): v = v + lax.ppermute(v, axis, [(i, i ^ step) for i in range(count)])  5.44 us
    unnamed x41, local copies, waits for them, and re-layouts  4.95 us
  transfers between devices with their start and end apart: 21, of which 9 were waited for; matrix products, arithmetic and copies ran while one was open for 18% of the time, Pallas kernels for 0%

profile of v17, /device:TPU:28, one launch (start us, length us, event | category | flops | bytes accessed | tf_op | source)
XLA Modules:
  0.0 133.1 jit_solution(6691115417523704976)
XLA Ops:
  3.0 1.8 %copy.91 = f32[1,8,64,512]{3,1,2,0:T(8,128)S(1)} copy(f32[1,8,64,512]{3,2,1,0:T(8,128)} %param.21) | data formatting | bytes 2097152 | tf_op args[0]
  7.7 2.8 %collective-permute-start.1 = (f32[100,512]{1,0:T(8,128)S(1)}, f32[100,512]{1,0:T(8,128)}, u32[]{:S(2)}, u32[]{:S(2)}) collective-permute-start(f32[100,512]{1,0:T(8,128)S(1)} %pad_maximum_fusion.9), channel_id=1, source_target_pairs={{1,0},{2,1},{3,2},{4,3},{5,4},{6,5},{7,6},{9,8},{10,9},{11,10},{12... | collective-permute-start | bytes 614408 | tf_op jit(solution)/shard_map/ppermute | solution.py:63
  10.5 1.9 %collective-permute-start = (f32[100,512]{1,0:T(8,128)S(1)}, f32[100,512]{1,0:T(8,128)}, u32[]{:S(2)}, u32[]{:S(2)}) collective-permute-start(f32[100,512]{1,0:T(8,128)S(1)} %pad_maximum_fusion.8), channel_id=1, source_target_pairs={{0,1},{1,2},{2,3},{3,4},{4,5},{5,6},{6,7},{8,9},{9,10},{10,11},{11... | collective-permute-start | bytes 614408 | tf_op jit(solution)/shard_map/ppermute | solution.py:62
  14.5 4.2 %collective-permute-done = f32[100,512]{1,0:T(8,128)} collective-permute-done((f32[100,512]{1,0:T(8,128)S(1)}, f32[100,512]{1,0:T(8,128)}, u32[]{:S(2)}, u32[]{:S(2)}) %collective-permute-start) | collective-permute-done | bytes 204832 | tf_op jit(solution)/shard_map/ppermute | solution.py:62
  26.5 2.1 %collective-permute-start.3 = (f32[224,512]{1,0:T(8,128)S(1)}, f32[224,512]{1,0:T(8,128)S(1)}, u32[]{:S(2)}, u32[]{:S(2)}) collective-permute-start(f32[224,512]{1,0:T(8,128)S(1)} %pad_maximum_fusion.6), channel_id=1, source_target_pairs={{1,0},{2,1},{3,2},{4,3},{5,4},{6,5},{7,6},{9,8},{10,9},{11,10},{12... | collective-permute-start | bytes 1376264 | tf_op jit(solution)/shard_map/ppermute | solution.py:63
  29.8 2.4 %collective-permute-start.4 = (f32[4,512]{1,0:T(4,128)S(1)}, f32[4,512]{1,0:T(4,128)S(1)}, u32[]{:S(2)}, u32[]{:S(2)}) collective-permute-start(f32[4,512]{1,0:T(4,128)S(1)} %get-tuple-element.225), channel_id=1, source_target_pairs={{0,1},{1,2},{2,3},{3,4},{4,5},{5,6},{6,7},{8,9},{9,10},{10,11},{11... | collective-permute-start | bytes 24584 | tf_op jit(solution)/shard_map/ppermute | solution.py:62
  32.2 4.1 %collective-permute-start.5 = (f32[4,512]{1,0:T(4,128)S(1)}, f32[4,512]{1,0:T(4,128)S(1)}, u32[]{:S(2)}, u32[]{:S(2)}) collective-permute-start(f32[4,512]{1,0:T(4,128)S(1)} %get-tuple-element.226), channel_id=1, source_target_pairs={{1,0},{2,1},{3,2},{4,3},{5,4},{6,5},{7,6},{9,8},{10,9},{11,10},{12... | collective-permute-start | bytes 24584 | tf_op jit(solution)/shard_map/ppermute | solution.py:63
  36.3 1.9 %collective-permute-start.2 = (f32[224,512]{1,0:T(8,128)S(1)}, f32[224,512]{1,0:T(8,128)S(1)}, u32[]{:S(2)}, u32[]{:S(2)}) collective-permute-start(f32[224,512]{1,0:T(8,128)S(1)} %pad_maximum_fusion.5), channel_id=1, source_target_pairs={{0,1},{1,2},{2,3},{3,4},{4,5},{5,6},{6,7},{8,9},{9,10},{10,11},{11... | collective-permute-start | bytes 1376264 | tf_op jit(solution)/shard_map/ppermute | solution.py:62
  40.6 6.5 %collective-permute-done.2 = f32[224,512]{1,0:T(8,128)S(1)} collective-permute-done((f32[224,512]{1,0:T(8,128)S(1)}, f32[224,512]{1,0:T(8,128)S(1)}, u32[]{:S(2)}, u32[]{:S(2)}) %collective-permute-start.2) | collective-permute-done | bytes 458784 | tf_op jit(solution)/shard_map/ppermute | solution.py:62
  48.5 1.3 pad_maximum_fusion.14
  50.0 1.9 %collective-permute-start.7 = (f32[8,512]{1,0:T(8,128)S(1)}, f32[8,512]{1,0:T(8,128)S(1)}, u32[]{:S(2)}, u32[]{:S(2)}) collective-permute-start(f32[8,512]{1,0:T(8,128)S(1)} %pad_maximum_fusion.13), channel_id=1, source_target_pairs={{1,0},{2,1},{3,2},{4,3},{5,4},{6,5},{7,6},{9,8},{10,9},{11,10},{12... | collective-permute-start | bytes 49160 | tf_op jit(solution)/shard_map/ppermute | solution.py:63
  51.9 2.4 %collective-permute-start.6 = (f32[8,512]{1,0:T(8,128)S(1)}, f32[8,512]{1,0:T(8,128)S(1)}, u32[]{:S(2)}, u32[]{:S(2)}) collective-permute-start(f32[8,512]{1,0:T(8,128)S(1)} %pad_maximum_fusion.12), channel_id=1, source_target_pairs={{0,1},{1,2},{2,3},{3,4},{4,5},{5,6},{6,7},{8,9},{9,10},{10,11},{11... | collective-permute-start | bytes 49160 | tf_op jit(solution)/shard_map/ppermute | solution.py:62
  55.8 2.5 %pad_maximum_fusion.1 = (f32[10,64,512]{2,0,1:T(8,128)}, f32[10,64,512]{2,0,1:T(8,128)}) fusion(f32[10,56,512]{2,0,1:T(8,128)S(1)} %get-tuple-element.166, f32[10,8,512]{2,0,1:T(8,128)S(1)} %get-tuple-element.180, f32[10,56,512]{2,0,1:T(8,128)S(1)} %get-tuple-element.165, f32[10,8,512]{2,0,1:T(8,128)S(1)} %get-tuple-element.179), kind=kLoop, calls=%fused_computation.33 | loop fusion | flops 655360 | bytes 5242880 | tf_op jit(solution)/shard_map/concatenate | solution.py:187
  58.4 1.3 fusion.169
  59.7 1.6 %collective-permute-start.9 = (f32[2]{0:T(128)S(1)}, f32[2]{0:T(128)S(1)}, u32[]{:S(2)}, u32[]{:S(2)}) collective-permute-start(f32[2]{0:T(128)S(1)} %fusion.169), channel_id=1, source_target_pairs={{0,2},{1,3},{2,0},{3,1},{4,6},{5,7},{6,4},{7,5},{8,10},{9,11},{10,... | collective-permute-start | bytes 32 | tf_op jit(solution)/shard_map/ppermute | solution.py:111
  61.3 1.9 %collective-permute-done.9 = f32[2]{0:T(128)S(1)} collective-permute-done((f32[2]{0:T(128)S(1)}, f32[2]{0:T(128)S(1)}, u32[]{:S(2)}, u32[]{:S(2)}) %collective-permute-start.9) | collective-permute-done | bytes 40 | tf_op jit(solution)/shard_map/ppermute | solution.py:111
  63.2 1.3 fusion.170
  64.5 3.5 %collective-permute-done.10 = f32[2]{0:T(128)S(1)} collective-permute-done((f32[2]{0:T(128)S(1)}, f32[2]{0:T(128)S(1)}, u32[]{:S(2)}, u32[]{:S(2)}) %collective-permute-start.10) | collective-permute-done | bytes 40 | tf_op jit(solution)/shard_map/ppermute | solution.py:111
  72.9 1.4 %and_select_fusion = f32[1,512]{1,0:T(1,128)S(1)} fusion(pred[]{:T(512)S(6)} %eq.91, f32[]{:T(128)} %bitcast.32), kind=kLoop, calls=%fused_computation.234 | loop fusion | flops 1536 | bytes 2053 | tf_op jit(solution)/shard_map/jit(_where)/select_n | solution.py:274
  74.4 1.9 %collective-permute-start.13 = (f32[128,512]{1,0:T(8,128)}, f32[128,512]{1,0:T(8,128)}, u32[]{:S(2)}, u32[]{:S(2)}) collective-permute-start(f32[128,512]{1,0:T(8,128)} %bitcast.40), channel_id=1, source_target_pairs={{0,1},{1,2},{2,3},{3,4},{4,5},{5,6},{6,7},{8,9},{9,10},{10,11},{11... | collective-permute-start | bytes 786440 | tf_op jit(solution)/shard_map/ppermute | solution.py:62
  76.3 4.5 %collective-permute-start.20 = (f32[128,512]{1,0:T(8,128)}, f32[128,512]{1,0:T(8,128)}, u32[]{:S(2)}, u32[]{:S(2)}) collective-permute-start(f32[128,512]{1,0:T(8,128)} %bitcast.53), channel_id=1, source_target_pairs={{1,0},{2,1},{3,2},{4,3},{5,4},{6,5},{7,6},{9,8},{10,9},{11,10},{12... | collective-permute-start | bytes 786440 | tf_op jit(solution)/shard_map/ppermute | solution.py:63
  83.9 1.2 multiply_reduce_fusion
  87.1 1.3 collective-permute-start.15
  88.4 1.3 collective-permute-start.16
  89.7 1.3 collective-permute-start.14
  93.7 14.5 %collective-permute-done.15 = f32[37,512]{1,0:T(8,128)S(1)} collective-permute-done((f32[37,512]{1,0:T(8,128)S(1)}, f32[37,512]{1,0:T(8,128)S(1)}, u32[]{:S(2)}, u32[]{:S(2)}) %collective-permute-start.15) | collective-permute-done | bytes 75808 | tf_op jit(solution)/shard_map/ppermute | solution.py:281
  108.2 1.3 %collective-permute-done.16 = f32[37,512]{1,0:T(8,128)S(1)} collective-permute-done((f32[37,512]{1,0:T(8,128)S(1)}, f32[37,512]{1,0:T(8,128)S(1)}, u32[]{:S(2)}, u32[]{:S(2)}) %collective-permute-start.16) | collective-permute-done | bytes 75808 | tf_op jit(solution)/shard_map/ppermute | solution.py:281
  110.2 1.9 %collective-permute-start.17 = (f32[4]{0:T(128)S(1)}, f32[4]{0:T(128)S(1)}, u32[]{:S(2)}, u32[]{:S(2)}) collective-permute-start(f32[4]{0:T(128)S(1)} %slice_reduce_fusion), channel_id=1, source_target_pairs={{24,25},{25,24},{26,27},{27,26},{28,29},{29,28},{30,31},{31,30}} | collective-permute-start | bytes 56 | tf_op jit(solution)/shard_map/ppermute | solution.py:122
  113.2 3.0 %collective-permute-start.18 = (f32[4]{0:T(128)S(1)}, f32[4]{0:T(128)S(1)}, u32[]{:S(2)}, u32[]{:S(2)}) collective-permute-start(f32[4]{0:T(128)S(1)} %add.715), channel_id=1, source_target_pairs={{24,26},{25,27},{26,24},{27,25},{28,30},{29,31},{30,28},{31,29}} | collective-permute-start | bytes 56 | tf_op jit(solution)/shard_map/ppermute | solution.py:122
  116.2 2.4 %collective-permute-done.18 = f32[4]{0:T(128)S(1)} collective-permute-done((f32[4]{0:T(128)S(1)}, f32[4]{0:T(128)S(1)}, u32[]{:S(2)}, u32[]{:S(2)}) %collective-permute-start.18) | collective-permute-done | bytes 48 | tf_op jit(solution)/shard_map/ppermute | solution.py:122
  118.6 1.9 %collective-permute-start.19 = (f32[4]{0:T(128)S(1)}, f32[4]{0:T(128)S(1)}, u32[]{:S(2)}, u32[]{:S(2)}) collective-permute-start(f32[4]{0:T(128)S(1)} %add.716), channel_id=1, source_target_pairs={{24,28},{25,29},{26,30},{27,31},{28,24},{29,25},{30,26},{31,27}} | collective-permute-start | bytes 56 | tf_op jit(solution)/shard_map/ppermute | solution.py:122
  120.5 3.5 %collective-permute-done.19 = f32[4]{0:T(128)S(1)} collective-permute-done((f32[4]{0:T(128)S(1)}, f32[4]{0:T(128)S(1)}, u32[]{:S(2)}, u32[]{:S(2)}) %collective-permute-start.19) | collective-permute-done | bytes 48 | tf_op jit(solution)/shard_map/ppermute | solution.py:122
  (204 shorter events, 33.3 us)
Async XLA Ops:
  0.6 4.2 %copy-start.6 = (f32[1,8,64,512]{3,2,1,0:T(8,128)S(1)}, f32[1,8,64,512]{3,2,1,0:T(8,128)}, u32[]{:S(2)}) copy-start(f32[1,8,64,512]{3,2,1,0:T(8,128)} %param.22) | copy-start | bytes 3145732
  5.5 18.7 %copy-start.2 = (f32[1,8,64,512]{3,1,2,0:T(8,128)}, f32[1,8,64,512]{3,1,2,0:T(8,128)S(1)}, u32[]{:S(2)}) copy-start(f32[1,8,64,512]{3,1,2,0:T(8,128)S(1)} %copy.90) | copy-start | bytes 3145732
  6.7 6.5 %copy-start.11 = (s32[8]{0:T(128)S(1)}, s32[8]{0:T(128)}, u32[]{:S(2)}) copy-start(s32[8]{0:T(128)} %param.29) | copy-start | bytes 100
  6.7 6.6 %copy-start.10 = (s32[8]{0:T(128)S(1)}, s32[8]{0:T(128)}, u32[]{:S(2)}) copy-start(s32[8]{0:T(128)} %param.27) | copy-start | bytes 100
  7.7 12.6 %collective-permute-start.1 = (f32[100,512]{1,0:T(8,128)S(1)}, f32[100,512]{1,0:T(8,128)}, u32[]{:S(2)}, u32[]{:S(2)}) collective-permute-start(f32[100,512]{1,0:T(8,128)S(1)} %pad_maximum_fusion.9), channel_id=1, source_target_pairs={{1,0},{2,1},{3,2},{4,3},{5,4},{6,5},{7,6},{9,8},{10,9},{11,10},{12... | collective-permute-start | bytes 614408 | tf_op jit(solution)/shard_map/ppermute | solution.py:63
  10.5 8.2 %collective-permute-start = (f32[100,512]{1,0:T(8,128)S(1)}, f32[100,512]{1,0:T(8,128)}, u32[]{:S(2)}, u32[]{:S(2)}) collective-permute-start(f32[100,512]{1,0:T(8,128)S(1)} %pad_maximum_fusion.8), channel_id=1, source_target_pairs={{0,1},{1,2},{2,3},{3,4},{4,5},{5,6},{6,7},{8,9},{9,10},{10,11},{11... | collective-permute-start | bytes 614408 | tf_op jit(solution)/shard_map/ppermute | solution.py:62
  23.7 5.2 %slice-start = ((s8[8388608]{0:T(1024)(128)(4,1)}), s8[4194304]{0:T(1024)(128)(4,1)S(1)}, s32[]{:S(2)}) async-start(s8[8388608]{0:T(1024)(128)(4,1)} %bitcast.94), calls=%async_computation | async-start | bytes 8388608
  25.7 3.2 %slice-start.1 = ((s8[8388608]{0:T(1024)(128)(4,1)}), s8[4194304]{0:T(1024)(128)(4,1)S(1)}, s32[]{:S(2)}) async-start(s8[8388608]{0:T(1024)(128)(4,1)} %bitcast.94), calls=%async_computation.1 | async-start | bytes 8388608
  26.2 2.6 %copy-start.8 = (f32[8,512]{1,0:T(8,128)S(1)}, f32[8,512]{1,0:T(8,128)}, u32[]{:S(2)}) copy-start(f32[8,512]{1,0:T(8,128)} %param.25) | copy-start | bytes 49156
  26.5 13.6 %collective-permute-start.3 = (f32[224,512]{1,0:T(8,128)S(1)}, f32[224,512]{1,0:T(8,128)S(1)}, u32[]{:S(2)}, u32[]{:S(2)}) collective-permute-start(f32[224,512]{1,0:T(8,128)S(1)} %pad_maximum_fusion.6), channel_id=1, source_target_pairs={{1,0},{2,1},{3,2},{4,3},{5,4},{6,5},{7,6},{9,8},{10,9},{11,10},{12... | collective-permute-start | bytes 1376264 | tf_op jit(solution)/shard_map/ppermute | solution.py:63
  29.8 8.4 %collective-permute-start.4 = (f32[4,512]{1,0:T(4,128)S(1)}, f32[4,512]{1,0:T(4,128)S(1)}, u32[]{:S(2)}, u32[]{:S(2)}) collective-permute-start(f32[4,512]{1,0:T(4,128)S(1)} %get-tuple-element.225), channel_id=1, source_target_pairs={{0,1},{1,2},{2,3},{3,4},{4,5},{5,6},{6,7},{8,9},{9,10},{10,11},{11... | collective-permute-start | bytes 24584 | tf_op jit(solution)/shard_map/ppermute | solution.py:62
  32.2 6.0 %collective-permute-start.5 = (f32[4,512]{1,0:T(4,128)S(1)}, f32[4,512]{1,0:T(4,128)S(1)}, u32[]{:S(2)}, u32[]{:S(2)}) collective-permute-start(f32[4,512]{1,0:T(4,128)S(1)} %get-tuple-element.226), channel_id=1, source_target_pairs={{1,0},{2,1},{3,2},{4,3},{5,4},{6,5},{7,6},{9,8},{10,9},{11,10},{12... | collective-permute-start | bytes 24584 | tf_op jit(solution)/shard_map/ppermute | solution.py:63
  36.3 10.7 %collective-permute-start.2 = (f32[224,512]{1,0:T(8,128)S(1)}, f32[224,512]{1,0:T(8,128)S(1)}, u32[]{:S(2)}, u32[]{:S(2)}) collective-permute-start(f32[224,512]{1,0:T(8,128)S(1)} %pad_maximum_fusion.5), channel_id=1, source_target_pairs={{0,1},{1,2},{2,3},{3,4},{4,5},{5,6},{6,7},{8,9},{9,10},{10,11},{11... | collective-permute-start | bytes 1376264 | tf_op jit(solution)/shard_map/ppermute | solution.py:62
  49.8 8.6 %collective-permute-start.8 = (f32[2]{0:T(128)S(1)}, f32[2]{0:T(128)S(1)}, u32[]{:S(2)}, u32[]{:S(2)}) collective-permute-start(f32[2]{0:T(128)S(1)} %pad_maximum_fusion.14), channel_id=1, source_target_pairs={{0,1},{1,0},{2,3},{3,2},{4,5},{5,4},{6,7},{7,6},{8,9},{9,8},{10,11... | collective-permute-start | bytes 32 | tf_op jit(solution)/shard_map/ppermute | solution.py:111
  50.0 30.9 %collective-permute-start.7 = (f32[8,512]{1,0:T(8,128)S(1)}, f32[8,512]{1,0:T(8,128)S(1)}, u32[]{:S(2)}, u32[]{:S(2)}) collective-permute-start(f32[8,512]{1,0:T(8,128)S(1)} %pad_maximum_fusion.13), channel_id=1, source_target_pairs={{1,0},{2,1},{3,2},{4,3},{5,4},{6,5},{7,6},{9,8},{10,9},{11,10},{12... | collective-permute-start | bytes 49160 | tf_op jit(solution)/shard_map/ppermute | solution.py:63
  51.9 29.0 %collective-permute-start.6 = (f32[8,512]{1,0:T(8,128)S(1)}, f32[8,512]{1,0:T(8,128)S(1)}, u32[]{:S(2)}, u32[]{:S(2)}) collective-permute-start(f32[8,512]{1,0:T(8,128)S(1)} %pad_maximum_fusion.12), channel_id=1, source_target_pairs={{0,1},{1,2},{2,3},{3,4},{4,5},{5,6},{6,7},{8,9},{9,10},{10,11},{11... | collective-permute-start | bytes 49160 | tf_op jit(solution)/shard_map/ppermute | solution.py:62
  55.8 2.5 %copy-start.12 = (pred[8,1,1]{0,2,1:T(4,128)(4,1)S(1)}, pred[8,1,1]{0,2,1:T(4,128)(4,1)}, u32[]{:S(2)}) copy-start(pred[8,1,1]{0,2,1:T(4,128)(4,1)} %get-tuple-element.236) | copy-start | bytes 28
  59.7 3.5 %collective-permute-start.9 = (f32[2]{0:T(128)S(1)}, f32[2]{0:T(128)S(1)}, u32[]{:S(2)}, u32[]{:S(2)}) collective-permute-start(f32[2]{0:T(128)S(1)} %fusion.169), channel_id=1, source_target_pairs={{0,2},{1,3},{2,0},{3,1},{4,6},{5,7},{6,4},{7,5},{8,10},{9,11},{10,... | collective-permute-start | bytes 32 | tf_op jit(solution)/shard_map/ppermute | solution.py:111
  64.5 3.5 %collective-permute-start.10 = (f32[2]{0:T(128)S(1)}, f32[2]{0:T(128)S(1)}, u32[]{:S(2)}, u32[]{:S(2)}) collective-permute-start(f32[2]{0:T(128)S(1)} %fusion.170), channel_id=1, source_target_pairs={{0,4},{1,5},{2,6},{3,7},{4,0},{5,1},{6,2},{7,3},{8,12},{9,13},{10,... | collective-permute-start | bytes 32 | tf_op jit(solution)/shard_map/ppermute | solution.py:111
  68.0 1.3 collective-permute-start.12
  68.7 0.7 collective-permute-start.11
  72.0 11.9 %slice-start.2 = ((s8[8388608]{0:T(1024)(128)(4,1)}), s8[4194304]{0:T(1024)(128)(4,1)S(1)}, s32[]{:S(2)}) async-start(s8[8388608]{0:T(1024)(128)(4,1)} %bitcast.96), calls=%async_computation.2 | async-start | bytes 8388608
  72.1 9.0 %copy-start = (f32[8,64,512]{2,1,0:T(8,128)}, f32[8,64,512]{2,1,0:T(8,128)S(1)}, u32[]{:S(2)}) copy-start(f32[8,64,512]{2,1,0:T(8,128)S(1)} %broadcast_add_fusion) | copy-start | bytes 3145732
  74.4 10.9 %collective-permute-start.13 = (f32[128,512]{1,0:T(8,128)}, f32[128,512]{1,0:T(8,128)}, u32[]{:S(2)}, u32[]{:S(2)}) collective-permute-start(f32[128,512]{1,0:T(8,128)} %bitcast.40), channel_id=1, source_target_pairs={{0,1},{1,2},{2,3},{3,4},{4,5},{5,6},{6,7},{8,9},{9,10},{10,11},{11... | collective-permute-start | bytes 786440 | tf_op jit(solution)/shard_map/ppermute | solution.py:62
  76.3 14.7 %collective-permute-start.20 = (f32[128,512]{1,0:T(8,128)}, f32[128,512]{1,0:T(8,128)}, u32[]{:S(2)}, u32[]{:S(2)}) collective-permute-start(f32[128,512]{1,0:T(8,128)} %bitcast.53), channel_id=1, source_target_pairs={{1,0},{2,1},{3,2},{4,3},{5,4},{6,5},{7,6},{9,8},{10,9},{11,10},{12... | collective-permute-start | bytes 786440 | tf_op jit(solution)/shard_map/ppermute | solution.py:63
  83.9 7.2 %copy-start.1 = (f32[8,64,512]{2,1,0:T(8,128)S(1)}, f32[8,64,512]{2,1,0:T(8,128)}, u32[]{:S(2)}) copy-start(f32[8,64,512]{2,1,0:T(8,128)} %copy-done) | copy-start | bytes 3145732
  87.1 21.1 %collective-permute-start.15 = (f32[37,512]{1,0:T(8,128)S(1)}, f32[37,512]{1,0:T(8,128)S(1)}, u32[]{:S(2)}, u32[]{:S(2)}) collective-permute-start(f32[37,512]{1,0:T(8,128)S(1)} %broadcast_add_fusion.1), channel_id=1, source_target_pairs={{8,24},{9,25},{10,26},{11,27},{12,28},{13,29},{14,30},{15,31}} | collective-permute-start | bytes 227336 | tf_op jit(solution)/shard_map/ppermute | solution.py:281
  88.4 21.1 %collective-permute-start.16 = (f32[37,512]{1,0:T(8,128)S(1)}, f32[37,512]{1,0:T(8,128)S(1)}, u32[]{:S(2)}, u32[]{:S(2)}) collective-permute-start(f32[37,512]{1,0:T(8,128)S(1)} %broadcast_add_fusion.1), channel_id=1, source_target_pairs={{16,24},{17,25},{18,26},{19,27},{20,28},{21,29},{22,30},{23,31}} | collective-permute-start | bytes 227336 | tf_op jit(solution)/shard_map/ppermute | solution.py:281
  89.7 19.8 %collective-permute-start.14 = (f32[37,512]{1,0:T(8,128)S(1)}, f32[37,512]{1,0:T(8,128)S(1)}, u32[]{:S(2)}, u32[]{:S(2)}) collective-permute-start(f32[37,512]{1,0:T(8,128)S(1)} %broadcast_add_fusion.1), channel_id=1, source_target_pairs={{0,24},{1,25},{2,26},{3,27},{4,28},{5,29},{6,30},{7,31}} | collective-permute-start | bytes 227336 | tf_op jit(solution)/shard_map/ppermute | solution.py:281
  110.2 3.0 %collective-permute-start.17 = (f32[4]{0:T(128)S(1)}, f32[4]{0:T(128)S(1)}, u32[]{:S(2)}, u32[]{:S(2)}) collective-permute-start(f32[4]{0:T(128)S(1)} %slice_reduce_fusion), channel_id=1, source_target_pairs={{24,25},{25,24},{26,27},{27,26},{28,29},{29,28},{30,31},{31,30}} | collective-permute-start | bytes 56 | tf_op jit(solution)/shard_map/ppermute | solution.py:122
  113.2 5.4 %collective-permute-start.18 = (f32[4]{0:T(128)S(1)}, f32[4]{0:T(128)S(1)}, u32[]{:S(2)}, u32[]{:S(2)}) collective-permute-start(f32[4]{0:T(128)S(1)} %add.715), channel_id=1, source_target_pairs={{24,26},{25,27},{26,24},{27,25},{28,30},{29,31},{30,28},{31,29}} | collective-permute-start | bytes 56 | tf_op jit(solution)/shard_map/ppermute | solution.py:122
  118.6 5.4 %collective-permute-start.19 = (f32[4]{0:T(128)S(1)}, f32[4]{0:T(128)S(1)}, u32[]{:S(2)}, u32[]{:S(2)}) collective-permute-start(f32[4]{0:T(128)S(1)} %add.716), channel_id=1, source_target_pairs={{24,28},{25,29},{26,30},{27,31},{28,24},{29,25},{30,26},{31,27}} | collective-permute-start | bytes 56 | tf_op jit(solution)/shard_map/ppermute | solution.py:122
  (6 other events, 8.2 us)

commit v18 on v16

--- a/solution.py
+++ b/solution.py
@@ -248,8 +248,14 @@
     deep = lax.cond(
         shell_flag,
         lambda: jnp.zeros((slab_rows,) + deep.shape[1:], jnp.float32),
-        lambda: deep_step(
-            deep_step(deep, force_deep, coef_deep, ok_one), force_deep[1:-1], coef_deep[1:-1], ok_two
+        lambda: jnp.concatenate(
+            [
+                band_two,
+                deep_step(
+                    deep_step(deep, force_deep, coef_deep, ok_one), force_deep[1:-1], coef_deep[1:-1], ok_two
+                )[:, band_two.shape[1] :],
+            ],
+            axis=1,
         ),
     )
     resid_two = tilde_two - disp_two
@@ -294,10 +300,9 @@
         tilde_two + coeff_new * (tilde_two - tilde_one) + coeff_old * (tilde_one - tilde_zero)
     )
 
-    flow_state = jnp.concatenate([band_two, deep[:, band_two.shape[1] :]], axis=1)
     disp_next = jnp.where(shell_flag, disp_three, 0.0)[None]
     residual = jnp.where(shell_flag, resid_two, 0.0)[None]
-    flow_final = jnp.where(shell_flag, 0.0, flow_state)[None]
+    flow_final = deep[None]
     return (disp_next, residual, flow_final)
 
 

time: 128 us -> 128 us (level)
  local copies, waits for them, and re-layouts: 18.6 us -> 22.1 us
    ppermute x5, waiting for transfers between devices: 10.4 us -> 7.54 us  [exchange(): low = lax.ppermute(up, 'slab', forward)]
    unnamed x61, local copies, waits for them, and re-layouts: 6.53 us -> 8.4 us
    ppermute x3, waiting for transfers between devices: 12.8 us -> 14.4 us  [body(): lax.ppermute(outgoing, 'side', [(source, side_count - 1)])]
    select_n x9 -> x10, other arithmetic: 1.6 us -> 2.59 us  [band_solve(): q = jnp.where(row_ok[k:rows - k], new, 0.0)]
  transfers between devices with their start and end apart: 21 -> 21, of which waited for: 9 -> 11; matrix products, arithmetic and copies ran while one was open for 15% -> 15% of each run, Pallas kernels for 0% -> 0%
where the time goes in v18:
time: 128 us; the launch traced here: 127 us
  starting transfers between devices  37.4 us (29%)
  waiting for transfers between devices  33.9 us (26%)
  local copies, waits for them, and re-layouts  22.1 us (17%)
  other arithmetic  21.5 us (17%)
  between operations  12.3 us (10%)
    ppermute x3, waiting for transfers between devices, body(): lax.ppermute(outgoing, 'side', [(source, side_count - 1)])  14.4 us
    ppermute x5, starting transfers between devices, exchange(): high = lax.ppermute(down, 'slab', backward)  12.1 us
    ppermute x5, starting transfers between devices, exchange(): low = lax.ppermute(up, 'slab', forward)  11.2 us
    unnamed x61, local copies, waits for them, and re-layouts  8.4 us
    ppermute x5, waiting for transfers between devices, exchange(): low = lax.ppermute(up, 'slab', forward)  7.54 us
    ppermute x3, starting transfers between devices, shell_sum(): v = v + lax.ppermute(v, ('side', 'slab'), pairs)  7.34 us
    ppermute x3, waiting for transfers between devices, shell_sum(): v = v + lax.ppermute(v, ('side', 'slab'), pairs)  6.48 us
    ppermute x3, waiting for transfers between devices, allsum_axis(): v = v + lax.ppermute(v, axis, [(i, i ^ step) for i in range(count)])  5.44 us
  transfers between devices with their start and end apart: 21, of which 11 were waited for; matrix products, arithmetic and copies ran while one was open for 15% of the time, Pallas kernels for 0%

profile of v18, /device:TPU:28, one launch (start us, length us, event | category | flops | bytes accessed | tf_op | source)
XLA Modules:
  0.0 127.2 jit_solution(16793349889026655801)
XLA Ops:
  3.0 1.8 %copy.65 = f32[1,8,64,512]{3,1,2,0:T(8,128)S(1)} copy(f32[1,8,64,512]{3,2,1,0:T(8,128)} %param.22) | data formatting | bytes 2097152 | tf_op args[1]
  8.1 2.8 %collective-permute-start.1 = (f32[100,512]{1,0:T(8,128)S(1)}, f32[100,512]{1,0:T(8,128)}, u32[]{:S(2)}, u32[]{:S(2)}) collective-permute-start(f32[100,512]{1,0:T(8,128)S(1)} %pad_maximum_fusion.9), channel_id=1, source_target_pairs={{1,0},{2,1},{3,2},{4,3},{5,4},{6,5},{7,6},{9,8},{10,9},{11,10},{12... | collective-permute-start | bytes 614408 | tf_op jit(solution)/shard_map/ppermute | solution.py:63
  10.9 1.9 %collective-permute-start = (f32[100,512]{1,0:T(8,128)S(1)}, f32[100,512]{1,0:T(8,128)}, u32[]{:S(2)}, u32[]{:S(2)}) collective-permute-start(f32[100,512]{1,0:T(8,128)S(1)} %pad_maximum_fusion.8), channel_id=1, source_target_pairs={{0,1},{1,2},{2,3},{3,4},{4,5},{5,6},{6,7},{8,9},{9,10},{10,11},{11... | collective-permute-start | bytes 614408 | tf_op jit(solution)/shard_map/ppermute | solution.py:62
  27.7 3.5 %collective-permute-start.3 = (f32[224,512]{1,0:T(8,128)S(1)}, f32[224,512]{1,0:T(8,128)S(1)}, u32[]{:S(2)}, u32[]{:S(2)}) collective-permute-start(f32[224,512]{1,0:T(8,128)S(1)} %pad_maximum_fusion.6), channel_id=1, source_target_pairs={{1,0},{2,1},{3,2},{4,3},{5,4},{6,5},{7,6},{9,8},{10,9},{11,10},{12... | collective-permute-start | bytes 1376264 | tf_op jit(solution)/shard_map/ppermute | solution.py:63
  31.4 1.9 %collective-permute-start.5 = (f32[4,512]{1,0:T(4,128)S(1)}, f32[4,512]{1,0:T(4,128)S(1)}, u32[]{:S(2)}, u32[]{:S(2)}) collective-permute-start(f32[4,512]{1,0:T(4,128)S(1)} %get-tuple-element.233), channel_id=1, source_target_pairs={{1,0},{2,1},{3,2},{4,3},{5,4},{6,5},{7,6},{9,8},{10,9},{11,10},{12... | collective-permute-start | bytes 24584 | tf_op jit(solution)/shard_map/ppermute | solution.py:63
  33.4 2.4 %collective-permute-start.4 = (f32[4,512]{1,0:T(4,128)S(1)}, f32[4,512]{1,0:T(4,128)S(1)}, u32[]{:S(2)}, u32[]{:S(2)}) collective-permute-start(f32[4,512]{1,0:T(4,128)S(1)} %get-tuple-element.232), channel_id=1, source_target_pairs={{0,1},{1,2},{2,3},{3,4},{4,5},{5,6},{6,7},{8,9},{9,10},{10,11},{11... | collective-permute-start | bytes 24584 | tf_op jit(solution)/shard_map/ppermute | solution.py:62
  35.8 2.0 %collective-permute-start.2 = (f32[224,512]{1,0:T(8,128)S(1)}, f32[224,512]{1,0:T(8,128)S(1)}, u32[]{:S(2)}, u32[]{:S(2)}) collective-permute-start(f32[224,512]{1,0:T(8,128)S(1)} %pad_maximum_fusion.5), channel_id=1, source_target_pairs={{0,1},{1,2},{2,3},{3,4},{4,5},{5,6},{6,7},{8,9},{9,10},{10,11},{11... | collective-permute-start | bytes 1376264 | tf_op jit(solution)/shard_map/ppermute | solution.py:62
  37.9 1.4 %collective-permute-done.4 = f32[4,512]{1,0:T(4,128)S(1)} collective-permute-done((f32[4,512]{1,0:T(4,128)S(1)}, f32[4,512]{1,0:T(4,128)S(1)}, u32[]{:S(2)}, u32[]{:S(2)}) %collective-permute-start.4) | collective-permute-done | bytes 8224 | tf_op jit(solution)/shard_map/ppermute | solution.py:62
  41.4 5.2 %collective-permute-done.2 = f32[224,512]{1,0:T(8,128)S(1)} collective-permute-done((f32[224,512]{1,0:T(8,128)S(1)}, f32[224,512]{1,0:T(8,128)S(1)}, u32[]{:S(2)}, u32[]{:S(2)}) %collective-permute-start.2) | collective-permute-done | bytes 458784 | tf_op jit(solution)/shard_map/ppermute | solution.py:62
  47.9 1.3 %pad_maximum_fusion.14 = f32[2]{0:T(128)S(1)} fusion(f32[1]{0:T(128)} %bitcast.30, f32[1]{0:T(128)} %bitcast.29), kind=kLoop, calls=%fused_computation.252 | loop fusion | flops 2 | bytes 16 | tf_op jit(solution)/shard_map/stack | solution.py:227
  49.4 1.9 %collective-permute-start.7 = (f32[8,512]{1,0:T(8,128)S(1)}, f32[8,512]{1,0:T(8,128)S(1)}, u32[]{:S(2)}, u32[]{:S(2)}) collective-permute-start(f32[8,512]{1,0:T(8,128)S(1)} %pad_maximum_fusion.13), channel_id=1, source_target_pairs={{1,0},{2,1},{3,2},{4,3},{5,4},{6,5},{7,6},{9,8},{10,9},{11,10},{12... | collective-permute-start | bytes 49160 | tf_op jit(solution)/shard_map/ppermute | solution.py:63
  51.4 2.4 %collective-permute-start.6 = (f32[8,512]{1,0:T(8,128)S(1)}, f32[8,512]{1,0:T(8,128)S(1)}, u32[]{:S(2)}, u32[]{:S(2)}) collective-permute-start(f32[8,512]{1,0:T(8,128)S(1)} %pad_maximum_fusion.12), channel_id=1, source_target_pairs={{0,1},{1,2},{2,3},{3,4},{4,5},{5,6},{6,7},{8,9},{9,10},{10,11},{11... | collective-permute-start | bytes 49160 | tf_op jit(solution)/shard_map/ppermute | solution.py:62
  55.6 2.5 %pad_maximum_fusion.1 = (f32[10,64,512]{2,0,1:T(8,128)}, f32[10,64,512]{2,0,1:T(8,128)}) fusion(f32[10,56,512]{2,0,1:T(8,128)S(1)} %get-tuple-element.171, f32[10,8,512]{2,0,1:T(8,128)S(1)} %get-tuple-element.187, f32[10,56,512]{2,0,1:T(8,128)S(1)} %get-tuple-element.170, f32[10,8,512]{2,0,1:T(8,128)S(1)} %get-tuple-element.186), kind=kLoop, calls=%fused_computation.35 | loop fusion | flops 655360 | bytes 5242880 | tf_op jit(solution)/shard_map/concatenate | solution.py:187
  58.2 1.3 %fusion.166 = f32[2]{0:T(128)S(1)} fusion(f32[2]{0:T(128)S(1)} %collective-permute-done.8, f32[1]{0:T(128)} %bitcast.30, f32[1]{0:T(128)} %bitcast.29), kind=kLoop, calls=%fused_computation.293 | loop fusion | flops 4 | bytes 24 | tf_op jit(solution)/shard_map/add | solution.py:111
  59.6 1.6 %collective-permute-start.9 = (f32[2]{0:T(128)S(1)}, f32[2]{0:T(128)S(1)}, u32[]{:S(2)}, u32[]{:S(2)}) collective-permute-start(f32[2]{0:T(128)S(1)} %fusion.166), channel_id=1, source_target_pairs={{0,2},{1,3},{2,0},{3,1},{4,6},{5,7},{6,4},{7,5},{8,10},{9,11},{10,... | collective-permute-start | bytes 32 | tf_op jit(solution)/shard_map/ppermute | solution.py:111
  61.2 1.9 %collective-permute-done.9 = f32[2]{0:T(128)S(1)} collective-permute-done((f32[2]{0:T(128)S(1)}, f32[2]{0:T(128)S(1)}, u32[]{:S(2)}, u32[]{:S(2)}) %collective-permute-start.9) | collective-permute-done | bytes 40 | tf_op jit(solution)/shard_map/ppermute | solution.py:111
  63.1 1.3 %fusion.167 = f32[2]{0:T(128)S(1)} fusion(f32[2]{0:T(128)S(1)} %collective-permute-done.9, f32[2]{0:T(128)S(1)} %collective-permute-done.8, f32[1]{0:T(128)} %bitcast.30, f32[1]{0:T(128)} %bitcast.29), kind=kLoop, calls=%fused_computation.294 | loop fusion | flops 6 | bytes 32 | tf_op jit(solution)/shard_map/add | solution.py:111
  64.5 3.5 %collective-permute-done.10 = f32[2]{0:T(128)S(1)} collective-permute-done((f32[2]{0:T(128)S(1)}, f32[2]{0:T(128)S(1)}, u32[]{:S(2)}, u32[]{:S(2)}) %collective-permute-start.10) | collective-permute-done | bytes 40 | tf_op jit(solution)/shard_map/ppermute | solution.py:111
  77.8 1.2 multiply_reduce_fusion
  79.1 1.3 %collective-permute-start.15 = (f32[37,512]{1,0:T(8,128)S(1)}, f32[37,512]{1,0:T(8,128)S(1)}, u32[]{:S(2)}, u32[]{:S(2)}) collective-permute-start(f32[37,512]{1,0:T(8,128)S(1)} %concatenate.296), channel_id=1, source_target_pairs={{16,24},{17,25},{18,26},{19,27},{20,28},{21,29},{22,30},{23,31}} | collective-permute-start | bytes 227336 | tf_op jit(solution)/shard_map/ppermute | solution.py:285
  80.4 1.3 %collective-permute-start.14 = (f32[37,512]{1,0:T(8,128)S(1)}, f32[37,512]{1,0:T(8,128)S(1)}, u32[]{:S(2)}, u32[]{:S(2)}) collective-permute-start(f32[37,512]{1,0:T(8,128)S(1)} %concatenate.296), channel_id=1, source_target_pairs={{8,24},{9,25},{10,26},{11,27},{12,28},{13,29},{14,30},{15,31}} | collective-permute-start | bytes 227336 | tf_op jit(solution)/shard_map/ppermute | solution.py:285
  81.7 1.3 %collective-permute-start.13 = (f32[37,512]{1,0:T(8,128)S(1)}, f32[37,512]{1,0:T(8,128)S(1)}, u32[]{:S(2)}, u32[]{:S(2)}) collective-permute-start(f32[37,512]{1,0:T(8,128)S(1)} %concatenate.296), channel_id=1, source_target_pairs={{0,24},{1,25},{2,26},{3,27},{4,28},{5,29},{6,30},{7,31}} | collective-permute-start | bytes 227336 | tf_op jit(solution)/shard_map/ppermute | solution.py:285
  83.1 1.9 %collective-permute-start.20 = (f32[128,512]{1,0:T(8,128)S(1)}, f32[128,512]{1,0:T(8,128)S(1)}, u32[]{:S(2)}, u32[]{:S(2)}) collective-permute-start(f32[128,512]{1,0:T(8,128)S(1)} %bitcast.117), channel_id=1, source_target_pairs={{1,0},{2,1},{3,2},{4,3},{5,4},{6,5},{7,6},{9,8},{10,9},{11,10},{12... | collective-permute-start | bytes 786440 | tf_op jit(solution)/shard_map/ppermute | solution.py:63
  85.0 2.4 %collective-permute-start.19 = (f32[128,512]{1,0:T(8,128)S(1)}, f32[128,512]{1,0:T(8,128)S(1)}, u32[]{:S(2)}, u32[]{:S(2)}) collective-permute-start(f32[128,512]{1,0:T(8,128)S(1)} %bitcast.116), channel_id=1, source_target_pairs={{0,1},{1,2},{2,3},{3,4},{4,5},{5,6},{6,7},{8,9},{9,10},{10,11},{11... | collective-permute-start | bytes 786440 | tf_op jit(solution)/shard_map/ppermute | solution.py:62
  87.4 10.5 %collective-permute-done.15 = f32[37,512]{1,0:T(8,128)S(1)} collective-permute-done((f32[37,512]{1,0:T(8,128)S(1)}, f32[37,512]{1,0:T(8,128)S(1)}, u32[]{:S(2)}, u32[]{:S(2)}) %collective-permute-start.15) | collective-permute-done | bytes 75808 | tf_op jit(solution)/shard_map/ppermute | solution.py:285
  98.0 1.8 %collective-permute-done.14 = f32[37,512]{1,0:T(8,128)S(1)} collective-permute-done((f32[37,512]{1,0:T(8,128)S(1)}, f32[37,512]{1,0:T(8,128)S(1)}, u32[]{:S(2)}, u32[]{:S(2)}) %collective-permute-start.14) | collective-permute-done | bytes 75808 | tf_op jit(solution)/shard_map/ppermute | solution.py:285
  99.7 2.1 %collective-permute-done.13 = f32[37,512]{1,0:T(8,128)S(1)} collective-permute-done((f32[37,512]{1,0:T(8,128)S(1)}, f32[37,512]{1,0:T(8,128)S(1)}, u32[]{:S(2)}, u32[]{:S(2)}) %collective-permute-start.13) | collective-permute-done | bytes 75808 | tf_op jit(solution)/shard_map/ppermute | solution.py:285
  102.6 1.9 %collective-permute-start.16 = (f32[4]{0:T(128)S(1)}, f32[4]{0:T(128)S(1)}, u32[]{:S(2)}, u32[]{:S(2)}) collective-permute-start(f32[4]{0:T(128)S(1)} %slice_reduce_fusion), channel_id=1, source_target_pairs={{24,25},{25,24},{26,27},{27,26},{28,29},{29,28},{30,31},{31,30}} | collective-permute-start | bytes 56 | tf_op jit(solution)/shard_map/ppermute | solution.py:122
  105.6 3.5 %collective-permute-start.17 = (f32[4]{0:T(128)S(1)}, f32[4]{0:T(128)S(1)}, u32[]{:S(2)}, u32[]{:S(2)}) collective-permute-start(f32[4]{0:T(128)S(1)} %add.706), channel_id=1, source_target_pairs={{24,26},{25,27},{26,24},{27,25},{28,30},{29,31},{30,28},{31,29}} | collective-permute-start | bytes 56 | tf_op jit(solution)/shard_map/ppermute | solution.py:122
  109.1 1.9 %collective-permute-done.17 = f32[4]{0:T(128)S(1)} collective-permute-done((f32[4]{0:T(128)S(1)}, f32[4]{0:T(128)S(1)}, u32[]{:S(2)}, u32[]{:S(2)}) %collective-permute-start.17) | collective-permute-done | bytes 48 | tf_op jit(solution)/shard_map/ppermute | solution.py:122
  111.0 1.9 %collective-permute-start.18 = (f32[4]{0:T(128)S(1)}, f32[4]{0:T(128)S(1)}, u32[]{:S(2)}, u32[]{:S(2)}) collective-permute-start(f32[4]{0:T(128)S(1)} %add.707), channel_id=1, source_target_pairs={{24,28},{25,29},{26,30},{27,31},{28,24},{29,25},{30,26},{31,27}} | collective-permute-start | bytes 56 | tf_op jit(solution)/shard_map/ppermute | solution.py:122
  112.9 3.5 %collective-permute-done.18 = f32[4]{0:T(128)S(1)} collective-permute-done((f32[4]{0:T(128)S(1)}, f32[4]{0:T(128)S(1)}, u32[]{:S(2)}, u32[]{:S(2)}) %collective-permute-start.18) | collective-permute-done | bytes 48 | tf_op jit(solution)/shard_map/ppermute | solution.py:122
  (220 shorter events, 37.7 us)
Async XLA Ops:
  0.6 4.2 %copy-start.6 = (f32[1,8,64,512]{3,2,1,0:T(8,128)S(1)}, f32[1,8,64,512]{3,2,1,0:T(8,128)}, u32[]{:S(2)}) copy-start(f32[1,8,64,512]{3,2,1,0:T(8,128)} %param.21) | copy-start | bytes 3145732
  4.8 18.4 %copy-start.1 = (f32[1,8,64,512]{3,1,2,0:T(8,128)}, f32[1,8,64,512]{3,1,2,0:T(8,128)S(1)}, u32[]{:S(2)}) copy-start(f32[1,8,64,512]{3,1,2,0:T(8,128)S(1)} %copy.65) | copy-start | bytes 3145732
  7.1 7.1 %copy-start.20 = (s32[8]{0:T(128)S(1)}, s32[8]{0:T(128)}, u32[]{:S(2)}) copy-start(s32[8]{0:T(128)} %param.29) | copy-start | bytes 100
  8.1 8.9 %collective-permute-start.1 = (f32[100,512]{1,0:T(8,128)S(1)}, f32[100,512]{1,0:T(8,128)}, u32[]{:S(2)}, u32[]{:S(2)}) collective-permute-start(f32[100,512]{1,0:T(8,128)S(1)} %pad_maximum_fusion.9), channel_id=1, source_target_pairs={{1,0},{2,1},{3,2},{4,3},{5,4},{6,5},{7,6},{9,8},{10,9},{11,10},{12... | collective-permute-start | bytes 614408 | tf_op jit(solution)/shard_map/ppermute | solution.py:63
  10.9 8.2 %collective-permute-start = (f32[100,512]{1,0:T(8,128)S(1)}, f32[100,512]{1,0:T(8,128)}, u32[]{:S(2)}, u32[]{:S(2)}) collective-permute-start(f32[100,512]{1,0:T(8,128)S(1)} %pad_maximum_fusion.8), channel_id=1, source_target_pairs={{0,1},{1,2},{2,3},{3,4},{4,5},{5,6},{6,7},{8,9},{9,10},{10,11},{11... | collective-permute-start | bytes 614408 | tf_op jit(solution)/shard_map/ppermute | solution.py:62
  17.0 23.1 %copy-start.13 = (pred[8]{0:T(512)(128)(4,1)}, pred[8]{0:T(512)(128)(4,1)S(1)}, u32[]{:S(2)}) copy-start(pred[8]{0:T(512)(128)(4,1)S(1)} %get-tuple-element.240) | copy-start | bytes 28
  17.0 41.1 %copy-start.21 = (pred[8,1,1]{0,2,1:T(4,128)(4,1)}, pred[8,1,1]{0,2,1:T(4,128)(4,1)S(1)}, u32[]{:S(2)}) copy-start(pred[8,1,1]{0,2,1:T(4,128)(4,1)S(1)} %get-tuple-element.239) | copy-start | bytes 28
  20.2 4.1 %slice-start = ((s8[8388608]{0:T(1024)(128)(4,1)}), s8[4194304]{0:T(1024)(128)(4,1)S(1)}, s32[]{:S(2)}) async-start(s8[8388608]{0:T(1024)(128)(4,1)} %bitcast.91), calls=%async_computation | async-start | bytes 8388608
  27.7 13.5 %collective-permute-start.3 = (f32[224,512]{1,0:T(8,128)S(1)}, f32[224,512]{1,0:T(8,128)S(1)}, u32[]{:S(2)}, u32[]{:S(2)}) collective-permute-start(f32[224,512]{1,0:T(8,128)S(1)} %pad_maximum_fusion.6), channel_id=1, source_target_pairs={{1,0},{2,1},{3,2},{4,3},{5,4},{6,5},{7,6},{9,8},{10,9},{11,10},{12... | collective-permute-start | bytes 1376264 | tf_op jit(solution)/shard_map/ppermute | solution.py:63
  31.4 6.4 %collective-permute-start.5 = (f32[4,512]{1,0:T(4,128)S(1)}, f32[4,512]{1,0:T(4,128)S(1)}, u32[]{:S(2)}, u32[]{:S(2)}) collective-permute-start(f32[4,512]{1,0:T(4,128)S(1)} %get-tuple-element.233), channel_id=1, source_target_pairs={{1,0},{2,1},{3,2},{4,3},{5,4},{6,5},{7,6},{9,8},{10,9},{11,10},{12... | collective-permute-start | bytes 24584 | tf_op jit(solution)/shard_map/ppermute | solution.py:63
  33.4 5.9 %collective-permute-start.4 = (f32[4,512]{1,0:T(4,128)S(1)}, f32[4,512]{1,0:T(4,128)S(1)}, u32[]{:S(2)}, u32[]{:S(2)}) collective-permute-start(f32[4,512]{1,0:T(4,128)S(1)} %get-tuple-element.232), channel_id=1, source_target_pairs={{0,1},{1,2},{2,3},{3,4},{4,5},{5,6},{6,7},{8,9},{9,10},{10,11},{11... | collective-permute-start | bytes 24584 | tf_op jit(solution)/shard_map/ppermute | solution.py:62
  35.8 10.7 %collective-permute-start.2 = (f32[224,512]{1,0:T(8,128)S(1)}, f32[224,512]{1,0:T(8,128)S(1)}, u32[]{:S(2)}, u32[]{:S(2)}) collective-permute-start(f32[224,512]{1,0:T(8,128)S(1)} %pad_maximum_fusion.5), channel_id=1, source_target_pairs={{0,1},{1,2},{2,3},{3,4},{4,5},{5,6},{6,7},{8,9},{9,10},{10,11},{11... | collective-permute-start | bytes 1376264 | tf_op jit(solution)/shard_map/ppermute | solution.py:62
  49.2 9.0 %collective-permute-start.8 = (f32[2]{0:T(128)S(1)}, f32[2]{0:T(128)S(1)}, u32[]{:S(2)}, u32[]{:S(2)}) collective-permute-start(f32[2]{0:T(128)S(1)} %pad_maximum_fusion.14), channel_id=1, source_target_pairs={{0,1},{1,0},{2,3},{3,2},{4,5},{5,4},{6,7},{7,6},{8,9},{9,8},{10,11... | collective-permute-start | bytes 32 | tf_op jit(solution)/shard_map/ppermute | solution.py:111
  49.4 24.7 %collective-permute-start.7 = (f32[8,512]{1,0:T(8,128)S(1)}, f32[8,512]{1,0:T(8,128)S(1)}, u32[]{:S(2)}, u32[]{:S(2)}) collective-permute-start(f32[8,512]{1,0:T(8,128)S(1)} %pad_maximum_fusion.13), channel_id=1, source_target_pairs={{1,0},{2,1},{3,2},{4,3},{5,4},{6,5},{7,6},{9,8},{10,9},{11,10},{12... | collective-permute-start | bytes 49160 | tf_op jit(solution)/shard_map/ppermute | solution.py:63
  51.4 22.8 %collective-permute-start.6 = (f32[8,512]{1,0:T(8,128)S(1)}, f32[8,512]{1,0:T(8,128)S(1)}, u32[]{:S(2)}, u32[]{:S(2)}) collective-permute-start(f32[8,512]{1,0:T(8,128)S(1)} %pad_maximum_fusion.12), channel_id=1, source_target_pairs={{0,1},{1,2},{2,3},{3,4},{4,5},{5,6},{6,7},{8,9},{9,10},{10,11},{11... | collective-permute-start | bytes 49160 | tf_op jit(solution)/shard_map/ppermute | solution.py:62
  55.6 2.5 %copy-start.19 = (pred[10,1,1]{0,2,1:T(4,128)(4,1)S(1)}, pred[10,1,1]{0,2,1:T(4,128)(4,1)}, u32[]{:S(2)}) copy-start(pred[10,1,1]{0,2,1:T(4,128)(4,1)} %get-tuple-element.237) | copy-start | bytes 34
  58.2 16.0 %copy-start.16 = (pred[14]{0:T(512)(128)(4,1)S(1)}, pred[14]{0:T(512)(128)(4,1)}, u32[]{:S(2)}) copy-start(pred[14]{0:T(512)(128)(4,1)} %slice.816) | copy-start | bytes 46
  59.6 3.5 %collective-permute-start.9 = (f32[2]{0:T(128)S(1)}, f32[2]{0:T(128)S(1)}, u32[]{:S(2)}, u32[]{:S(2)}) collective-permute-start(f32[2]{0:T(128)S(1)} %fusion.166), channel_id=1, source_target_pairs={{0,2},{1,3},{2,0},{3,1},{4,6},{5,7},{6,4},{7,5},{8,10},{9,11},{10,... | collective-permute-start | bytes 32 | tf_op jit(solution)/shard_map/ppermute | solution.py:111
  64.5 3.5 %collective-permute-start.10 = (f32[2]{0:T(128)S(1)}, f32[2]{0:T(128)S(1)}, u32[]{:S(2)}, u32[]{:S(2)}) collective-permute-start(f32[2]{0:T(128)S(1)} %fusion.167), channel_id=1, source_target_pairs={{0,4},{1,5},{2,6},{3,7},{4,0},{5,1},{6,2},{7,3},{8,12},{9,13},{10,... | collective-permute-start | bytes 32 | tf_op jit(solution)/shard_map/ppermute | solution.py:111
  68.0 1.3 %collective-permute-start.11 = (f32[2]{0:T(128)S(1)}, f32[2]{0:T(128)S(1)}, u32[]{:S(2)}, u32[]{:S(2)}) collective-permute-start(f32[2]{0:T(128)S(1)} %add.695), channel_id=1, source_target_pairs={{0,16},{1,17},{2,18},{3,19},{4,20},{5,21},{6,22},{7,23},{8,0},{9,1... | collective-permute-start | bytes 32 | tf_op jit(solution)/shard_map/ppermute | solution.py:132
  68.7 0.7 collective-permute-start.12
  71.9 5.9 %slice-start.2 = ((s8[8388608]{0:T(1024)(128)(4,1)}), s8[4194304]{0:T(1024)(128)(4,1)S(1)}, s32[]{:S(2)}) async-start(s8[8388608]{0:T(1024)(128)(4,1)} %bitcast.93), calls=%async_computation.2 | async-start | bytes 8388608
  74.7 3.1 %slice-start.3 = ((s8[8388608]{0:T(1024)(128)(4,1)}), s8[4194304]{0:T(1024)(128)(4,1)S(1)}, s32[]{:S(2)}) async-start(s8[8388608]{0:T(1024)(128)(4,1)} %bitcast.93), calls=%async_computation.3 | async-start | bytes 8388608
  77.8 5.2 %copy-start = (f32[8,64,512]{2,1,0:T(8,128)S(1)}, f32[8,64,512]{2,1,0:T(8,128)}, u32[]{:S(2)}) copy-start(f32[8,64,512]{2,1,0:T(8,128)} %broadcast_add_fusion) | copy-start | bytes 3145732
  79.1 18.8 %collective-permute-start.15 = (f32[37,512]{1,0:T(8,128)S(1)}, f32[37,512]{1,0:T(8,128)S(1)}, u32[]{:S(2)}, u32[]{:S(2)}) collective-permute-start(f32[37,512]{1,0:T(8,128)S(1)} %concatenate.296), channel_id=1, source_target_pairs={{16,24},{17,25},{18,26},{19,27},{20,28},{21,29},{22,30},{23,31}} | collective-permute-start | bytes 227336 | tf_op jit(solution)/shard_map/ppermute | solution.py:285
  80.4 19.3 %collective-permute-start.14 = (f32[37,512]{1,0:T(8,128)S(1)}, f32[37,512]{1,0:T(8,128)S(1)}, u32[]{:S(2)}, u32[]{:S(2)}) collective-permute-start(f32[37,512]{1,0:T(8,128)S(1)} %concatenate.296), channel_id=1, source_target_pairs={{8,24},{9,25},{10,26},{11,27},{12,28},{13,29},{14,30},{15,31}} | collective-permute-start | bytes 227336 | tf_op jit(solution)/shard_map/ppermute | solution.py:285
  81.7 20.1 %collective-permute-start.13 = (f32[37,512]{1,0:T(8,128)S(1)}, f32[37,512]{1,0:T(8,128)S(1)}, u32[]{:S(2)}, u32[]{:S(2)}) collective-permute-start(f32[37,512]{1,0:T(8,128)S(1)} %concatenate.296), channel_id=1, source_target_pairs={{0,24},{1,25},{2,26},{3,27},{4,28},{5,29},{6,30},{7,31}} | collective-permute-start | bytes 227336 | tf_op jit(solution)/shard_map/ppermute | solution.py:285
  83.1 42.4 %collective-permute-start.20 = (f32[128,512]{1,0:T(8,128)S(1)}, f32[128,512]{1,0:T(8,128)S(1)}, u32[]{:S(2)}, u32[]{:S(2)}) collective-permute-start(f32[128,512]{1,0:T(8,128)S(1)} %bitcast.117), channel_id=1, source_target_pairs={{1,0},{2,1},{3,2},{4,3},{5,4},{6,5},{7,6},{9,8},{10,9},{11,10},{12... | collective-permute-start | bytes 786440 | tf_op jit(solution)/shard_map/ppermute | solution.py:63
  85.0 40.4 %collective-permute-start.19 = (f32[128,512]{1,0:T(8,128)S(1)}, f32[128,512]{1,0:T(8,128)S(1)}, u32[]{:S(2)}, u32[]{:S(2)}) collective-permute-start(f32[128,512]{1,0:T(8,128)S(1)} %bitcast.116), channel_id=1, source_target_pairs={{0,1},{1,2},{2,3},{3,4},{4,5},{5,6},{6,7},{8,9},{9,10},{10,11},{11... | collective-permute-start | bytes 786440 | tf_op jit(solution)/shard_map/ppermute | solution.py:62
  102.6 3.0 %collective-permute-start.16 = (f32[4]{0:T(128)S(1)}, f32[4]{0:T(128)S(1)}, u32[]{:S(2)}, u32[]{:S(2)}) collective-permute-start(f32[4]{0:T(128)S(1)} %slice_reduce_fusion), channel_id=1, source_target_pairs={{24,25},{25,24},{26,27},{27,26},{28,29},{29,28},{30,31},{31,30}} | collective-permute-start | bytes 56 | tf_op jit(solution)/shard_map/ppermute | solution.py:122
  105.6 5.4 %collective-permute-start.17 = (f32[4]{0:T(128)S(1)}, f32[4]{0:T(128)S(1)}, u32[]{:S(2)}, u32[]{:S(2)}) collective-permute-start(f32[4]{0:T(128)S(1)} %add.706), channel_id=1, source_target_pairs={{24,26},{25,27},{26,24},{27,25},{28,30},{29,31},{30,28},{31,29}} | collective-permute-start | bytes 56 | tf_op jit(solution)/shard_map/ppermute | solution.py:122
  111.0 5.4 %collective-permute-start.18 = (f32[4]{0:T(128)S(1)}, f32[4]{0:T(128)S(1)}, u32[]{:S(2)}, u32[]{:S(2)}) collective-permute-start(f32[4]{0:T(128)S(1)} %add.707), channel_id=1, source_target_pairs={{24,28},{25,29},{26,30},{27,31},{28,24},{29,25},{30,26},{31,27}} | collective-permute-start | bytes 56 | tf_op jit(solution)/shard_map/ppermute | solution.py:122
  (16 other events, 19.5 us)

commit v19 on v16

--- a/solution.py
+++ b/solution.py
@@ -263,25 +263,20 @@
         ]
     )
     patches_here = tilde_two.shape[0]
-    outgoing = jnp.concatenate(
-        [
-            tilde_two,
-            tilde_one,
-            tilde_zero,
-            resid_two,
-            partial,
-            jnp.where((jnp.arange(line_cells) == 0) & (side_id == 0), gram_aa, 0.0)[None],
-        ],
-        axis=0,
-    )
-    gathered = outgoing
+    sums_out = jnp.concatenate(
+        [partial, jnp.where((jnp.arange(line_cells) == 0) & (side_id == 0), gram_aa, 0.0)[None]], axis=0
+    )
+    data_out = jnp.concatenate([tilde_two, tilde_one, tilde_zero, resid_two], axis=0)
+    sums_in, data_in = sums_out, data_out
     for source in range(side_count - 1):
-        gathered = gathered + lax.ppermute(outgoing, "side", [(source, side_count - 1)])
-    sums = shell_sum(jnp.sum(gathered[4 * patches_here : 4 * patches_here + 4], axis=1), side_count)
-    gram_aa = gathered[4 * patches_here + 4, 0]
+        sums_in = sums_in + lax.ppermute(sums_out, "side", [(source, side_count - 1)])
+    for source in range(side_count - 1):
+        data_in = data_in + lax.ppermute(data_out, "side", [(source, side_count - 1)])
+    sums = shell_sum(jnp.sum(sums_in[:4], axis=1), side_count)
+    gram_aa = sums_in[4, 0]
     gram_nn, gram_no, proj_new, proj_old = sums[0], sums[1], sums[2], sums[3]
     tilde_two, tilde_one, tilde_zero, resid_two = (
-        gathered[k * patches_here : (k + 1) * patches_here] for k in range(4)
+        data_in[k * patches_here : (k + 1) * patches_here] for k in range(4)
     )
 
     shift_two = 0.001 * (gram_nn + gram_aa) + 1e-06

time: 128 us -> 147 us (1.15)
  the two profiles are of different devices: /device:TPU:28 before, /device:TPU:0 now
where the time goes in v19:
time: 147 us; the launch traced here: 145 us
  starting transfers between devices  71.9 us (49%)
  other arithmetic  34.1 us (23%)
  local copies, waits for them, and re-layouts  21.3 us (14%)
  between operations  12.6 us (9%)
  waiting for transfers between devices  5.25 us (4%)
    ppermute x5, starting transfers between devices, exchange(): low = lax.ppermute(up, 'slab', forward)  20.8 us
    ppermute x3, starting transfers between devices, body(): lax.ppermute(data_out, 'side', [(source, side_count - 1)])  20.3 us
    ppermute x3, starting transfers between devices, allsum_axis(): v = v + lax.ppermute(v, axis, [(i, i ^ step) for i in range(count)])  12.8 us
    select_n x3, other arithmetic, deep_step(): return jnp.where(ok, new, 0.0)  10.5 us
    ppermute x2, starting transfers between devices, fluid_sum(): got.append(lax.ppermute(v, ('side', 'slab'), pairs))  6.73 us
    ppermute x5, starting transfers between devices, exchange(): high = lax.ppermute(down, 'slab', backward)  6.58 us
    unnamed x41, local copies, waits for them, and re-layouts  4.95 us
    slice x17, local copies, waits for them, and re-layouts, shift_y(): a[..., 1:]  3.07 us
  transfers between devices with their start and end apart: 24, of which 3 were waited for; matrix products, arithmetic and copies ran while one was open for 21% of the time, Pallas kernels for 0%

profile of v19, /device:TPU:0, one launch (start us, length us, event | category | flops | bytes accessed | tf_op | source)
XLA Modules:
  0.0 145.5 jit_solution(1203716158895987561)
XLA Ops:
  3.0 1.8 %copy.90 = f32[1,8,64,512]{3,1,2,0:T(8,128)S(1)} copy(f32[1,8,64,512]{3,2,1,0:T(8,128)} %param.21) | data formatting | bytes 2097152 | tf_op args[0]
  7.7 1.3 collective-permute-start.1
  9.0 3.7 %collective-permute-start = (f32[100,512]{1,0:T(8,128)S(1)}, f32[100,512]{1,0:T(8,128)}, u32[]{:S(2)}, u32[]{:S(2)}) collective-permute-start(f32[100,512]{1,0:T(8,128)S(1)} %pad_maximum_fusion.8), channel_id=1, source_target_pairs={{0,1},{1,2},{2,3},{3,4},{4,5},{5,6},{6,7},{8,9},{9,10},{10,11},{11... | collective-permute-start | bytes 614408 | tf_op jit(solution)/shard_map/ppermute | solution.py:62
  22.7 1.4 collective-permute-start.3
  25.3 5.1 %collective-permute-start.4 = (f32[4,512]{1,0:T(4,128)S(1)}, f32[4,512]{1,0:T(4,128)S(1)}, u32[]{:S(2)}, u32[]{:S(2)}) collective-permute-start(f32[4,512]{1,0:T(4,128)S(1)} %get-tuple-element.225), channel_id=1, source_target_pairs={{0,1},{1,2},{2,3},{3,4},{4,5},{5,6},{6,7},{8,9},{9,10},{10,11},{11... | collective-permute-start | bytes 24584 | tf_op jit(solution)/shard_map/ppermute | solution.py:62
  30.4 1.3 collective-permute-start.5
  31.8 5.2 %collective-permute-start.2 = (f32[224,512]{1,0:T(8,128)S(1)}, f32[224,512]{1,0:T(8,128)S(1)}, u32[]{:S(2)}, u32[]{:S(2)}) collective-permute-start(f32[224,512]{1,0:T(8,128)S(1)} %pad_maximum_fusion.5), channel_id=1, source_target_pairs={{0,1},{1,2},{2,3},{3,4},{4,5},{5,6},{6,7},{8,9},{9,10},{10,11},{11... | collective-permute-start | bytes 1376264 | tf_op jit(solution)/shard_map/ppermute | solution.py:62
  40.7 1.3 pad_maximum_fusion.15
  42.0 4.8 %collective-permute-start.8 = (f32[2]{0:T(128)S(1)}, f32[2]{0:T(128)S(1)}, u32[]{:S(2)}, u32[]{:S(2)}) collective-permute-start(f32[2]{0:T(128)S(1)} %pad_maximum_fusion.15), channel_id=1, source_target_pairs={{0,1},{1,0},{2,3},{3,2},{4,5},{5,4},{6,7},{7,6},{8,9},{9,8},{10,11... | collective-permute-start | bytes 32 | tf_op jit(solution)/shard_map/ppermute | solution.py:111
  47.0 1.3 collective-permute-start.7
  48.3 3.0 %collective-permute-start.6 = (f32[8,512]{1,0:T(8,128)S(1)}, f32[8,512]{1,0:T(8,128)S(1)}, u32[]{:S(2)}, u32[]{:S(2)}) collective-permute-start(f32[8,512]{1,0:T(8,128)S(1)} %pad_maximum_fusion.13), channel_id=1, source_target_pairs={{0,1},{1,2},{2,3},{3,4},{4,5},{5,6},{6,7},{8,9},{9,10},{10,11},{11... | collective-permute-start | bytes 49160 | tf_op jit(solution)/shard_map/ppermute | solution.py:62
  52.8 2.5 %pad_maximum_fusion.1 = (f32[10,64,512]{2,0,1:T(8,128)}, f32[10,64,512]{2,0,1:T(8,128)}) fusion(f32[10,56,512]{2,0,1:T(8,128)S(1)} %get-tuple-element.166, f32[10,8,512]{2,0,1:T(8,128)S(1)} %get-tuple-element.180, f32[10,56,512]{2,0,1:T(8,128)S(1)} %get-tuple-element.165, f32[10,8,512]{2,0,1:T(8,128)S(1)} %get-tuple-element.179), kind=kLoop, calls=%fused_computation.33 | loop fusion | flops 655360 | bytes 5242880 | tf_op jit(solution)/shard_map/concatenate | solution.py:187
  55.2 8.1 %conditional.2 = (f32[8,64,512]{2,1,0:T(8,128)S(1)}) conditional(s32[]{:T(128)} %convert_element_type.32, (pred[8,1,1]{0,2,1:T(4,128)(4,1)S(1)}, f32[10,64,512]{2,0,1:T(8,128)}, pred[10,1,1]{0,2,1:T(4,128)(4,1)S(1)}, f32[12,64,512]{2,0,1:T(8,128)S(1)}, f32[10,64,512]{2,0,1:T(8,128)}) %tuple.123, () %tuple.41), branch_computations={%region_17.18_spmd, %region_18.19_spmd} | conditional | flops 5308416 | bytes 45626392 | solution.py:217
  56.9 4.8 %fusion.6 = (f32[10,64,512]{2,1,0:T(8,128)S(1)}, f32[10,64,512]{2,1,0:T(8,128)S(1)}, f32[10,64,512]{2,1,0:T(8,128)S(1)}) fusion(f32[10,64,511]{2,1,0:T(8,128)S(1)} %get-tuple-element.152, f32[10,64,511]{2,1,0:T(8,128)S(1)} %get-tuple-element.151, f32[10,63,512]{2,1,0:T(8,128)S(1)} %get-tuple-element.150, f32[10,63,512]{2,1,0:T(8,128)S(1)} %get-tuple-element.149, ...), kind=kLoop, calls=%fused_computation.7 | loop fusion | flops 2949120 | bytes 14371850 | tf_op jit(solution)/shard_map/cond/branch_0_fun/jit(_where)/select_n | solution.py:86
  63.4 1.3 fusion.169
  64.6 4.2 %collective-permute-start.9 = (f32[2]{0:T(128)S(1)}, f32[2]{0:T(128)S(1)}, u32[]{:S(2)}, u32[]{:S(2)}) collective-permute-start(f32[2]{0:T(128)S(1)} %fusion.169), channel_id=1, source_target_pairs={{0,2},{1,3},{2,0},{3,1},{4,6},{5,7},{6,4},{7,5},{8,10},{9,11},{10,... | collective-permute-start | bytes 32 | tf_op jit(solution)/shard_map/ppermute | solution.py:111
  68.8 1.5 %collective-permute-done.9 = f32[2]{0:T(128)S(1)} collective-permute-done((f32[2]{0:T(128)S(1)}, f32[2]{0:T(128)S(1)}, u32[]{:S(2)}, u32[]{:S(2)}) %collective-permute-start.9) | collective-permute-done | bytes 40 | tf_op jit(solution)/shard_map/ppermute | solution.py:111
  70.3 1.3 fusion.170
  71.6 3.8 %collective-permute-start.10 = (f32[2]{0:T(128)S(1)}, f32[2]{0:T(128)S(1)}, u32[]{:S(2)}, u32[]{:S(2)}) collective-permute-start(f32[2]{0:T(128)S(1)} %fusion.170), channel_id=1, source_target_pairs={{0,4},{1,5},{2,6},{3,7},{4,0},{5,1},{6,2},{7,3},{8,12},{9,13},{10,... | collective-permute-start | bytes 32 | tf_op jit(solution)/shard_map/ppermute | solution.py:111
  75.4 1.5 %collective-permute-done.10 = f32[2]{0:T(128)S(1)} collective-permute-done((f32[2]{0:T(128)S(1)}, f32[2]{0:T(128)S(1)}, u32[]{:S(2)}, u32[]{:S(2)}) %collective-permute-start.10) | collective-permute-done | bytes 40 | tf_op jit(solution)/shard_map/ppermute | solution.py:111
  76.9 3.5 %collective-permute-start.12 = (f32[2]{0:T(128)S(1)}, f32[2]{0:T(128)S(1)}, u32[]{:S(2)}, u32[]{:S(2)}) collective-permute-start(f32[2]{0:T(128)S(1)} %add.703), channel_id=1, source_target_pairs={{0,8},{1,9},{2,10},{3,11},{4,12},{5,13},{6,14},{7,15},{8,16},{9,17... | collective-permute-start | bytes 32 | tf_op jit(solution)/shard_map/ppermute | solution.py:132
  80.4 3.3 %collective-permute-start.11 = (f32[2]{0:T(128)S(1)}, f32[2]{0:T(128)S(1)}, u32[]{:S(2)}, u32[]{:S(2)}) collective-permute-start(f32[2]{0:T(128)S(1)} %add.703), channel_id=1, source_target_pairs={{0,16},{1,17},{2,18},{3,19},{4,20},{5,21},{6,22},{7,23},{8,0},{9,1... | collective-permute-start | bytes 32 | tf_op jit(solution)/shard_map/ppermute | solution.py:132
  83.7 2.2 %collective-permute-done.11 = f32[2]{0:T(128)S(1)} collective-permute-done((f32[2]{0:T(128)S(1)}, f32[2]{0:T(128)S(1)}, u32[]{:S(2)}, u32[]{:S(2)}) %collective-permute-start.11) | collective-permute-done | bytes 40 | tf_op jit(solution)/shard_map/ppermute | solution.py:132
  89.4 1.4 and_select_fusion
  90.8 1.3 collective-permute-start.23
  92.1 3.7 %collective-permute-start.22 = (f32[128,512]{1,0:T(8,128)}, f32[128,512]{1,0:T(8,128)}, u32[]{:S(2)}, u32[]{:S(2)}) collective-permute-start(f32[128,512]{1,0:T(8,128)} %bitcast.50), channel_id=1, source_target_pairs={{0,1},{1,2},{2,3},{3,4},{4,5},{5,6},{6,7},{8,9},{9,10},{10,11},{11... | collective-permute-start | bytes 786440 | tf_op jit(solution)/shard_map/ppermute | solution.py:62
  98.9 1.2 multiply_reduce_fusion
  101.7 1.3 collective-permute-start.16
  107.2 19.0 %collective-permute-start.13 = (f32[32,512]{1,0:T(8,128)S(1)}, f32[32,512]{1,0:T(8,128)S(1)}, u32[]{:S(2)}, u32[]{:S(2)}) collective-permute-start(f32[32,512]{1,0:T(8,128)S(1)} %pad_maximum_fusion.10), channel_id=1, source_target_pairs={{0,24},{1,25},{2,26},{3,27},{4,28},{5,29},{6,30},{7,31}} | collective-permute-start | bytes 196616 | tf_op jit(solution)/shard_map/ppermute | solution.py:274
  135.3 1.2 pad_maximum_fusion.3
  136.5 7.8 %conditional.3 = (f32[1,8,60,512]{3,2,1,0:T(8,128)S(1)}) conditional(s32[]{:T(128)} %convert_element_type.32, (pred[8,1,1]{0,2,1:T(4,128)(4,1)S(1)}, f32[10,64,512]{2,0,1:T(8,128)}, pred[10,1,1]{0,2,1:T(4,128)(4,1)S(1)}, f32[12,64,512]{2,1,0:T(8,128)S(1)}, f32[10,64,512]{2,0,1:T(8,128)}) %tuple.124, () %tuple.43), branch_computations={%region_19.20_spmd, %region_20.21_spmd} | conditional | flops 5193728 | bytes 48509976 | solution.py:248
  137.5 4.8 %divide_select_fusion = (f32[10,64,512]{2,1,0:T(8,128)S(1)}, f32[10,64,512]{2,1,0:T(8,128)S(1)}, f32[10,64,512]{2,1,0:T(8,128)S(1)}) fusion(f32[10,64,511]{2,1,0:T(8,128)S(1)} %get-tuple-element.160, f32[10,64,511]{2,1,0:T(8,128)S(1)} %get-tuple-element.159, f32[10,63,512]{2,1,0:T(8,128)S(1)} %get-tuple-element.158, ...), kind=kLoop, calls=%fused_computation.17 | loop fusion | flops 2949120 | bytes 14371850 | tf_op jit(solution)/shard_map/cond/branch_0_fun/jit(_where)/select_n | solution.py:86
  (224 shorter events, 38.7 us)
Async XLA Ops:
  0.6 4.2 %copy-start.6 = (f32[1,8,64,512]{3,2,1,0:T(8,128)S(1)}, f32[1,8,64,512]{3,2,1,0:T(8,128)}, u32[]{:S(2)}) copy-start(f32[1,8,64,512]{3,2,1,0:T(8,128)} %param.22) | copy-start | bytes 3145732
  5.5 14.8 %copy-start.2 = (f32[1,8,64,512]{3,1,2,0:T(8,128)}, f32[1,8,64,512]{3,1,2,0:T(8,128)S(1)}, u32[]{:S(2)}) copy-start(f32[1,8,64,512]{3,1,2,0:T(8,128)S(1)} %copy.89) | copy-start | bytes 3145732
  6.7 6.8 %copy-start.11 = (s32[8]{0:T(128)S(1)}, s32[8]{0:T(128)}, u32[]{:S(2)}) copy-start(s32[8]{0:T(128)} %param.29) | copy-start | bytes 100
  6.7 6.9 %copy-start.10 = (s32[8]{0:T(128)S(1)}, s32[8]{0:T(128)}, u32[]{:S(2)}) copy-start(s32[8]{0:T(128)} %param.27) | copy-start | bytes 100
  7.7 8.8 %collective-permute-start.1 = (f32[100,512]{1,0:T(8,128)S(1)}, f32[100,512]{1,0:T(8,128)}, u32[]{:S(2)}, u32[]{:S(2)}) collective-permute-start(f32[100,512]{1,0:T(8,128)S(1)} %pad_maximum_fusion.9), channel_id=1, source_target_pairs={{1,0},{2,1},{3,2},{4,3},{5,4},{6,5},{7,6},{9,8},{10,9},{11,10},{12... | collective-permute-start | bytes 614408 | tf_op jit(solution)/shard_map/ppermute | solution.py:63
  9.0 5.8 %collective-permute-start = (f32[100,512]{1,0:T(8,128)S(1)}, f32[100,512]{1,0:T(8,128)}, u32[]{:S(2)}, u32[]{:S(2)}) collective-permute-start(f32[100,512]{1,0:T(8,128)S(1)} %pad_maximum_fusion.8), channel_id=1, source_target_pairs={{0,1},{1,2},{2,3},{3,4},{4,5},{5,6},{6,7},{8,9},{9,10},{10,11},{11... | collective-permute-start | bytes 614408 | tf_op jit(solution)/shard_map/ppermute | solution.py:62
  19.8 4.6 %slice-start = ((s8[8388608]{0:T(1024)(128)(4,1)}), s8[4194304]{0:T(1024)(128)(4,1)S(1)}, s32[]{:S(2)}) async-start(s8[8388608]{0:T(1024)(128)(4,1)} %bitcast.93), calls=%async_computation | async-start | bytes 8388608
  22.7 16.2 %collective-permute-start.3 = (f32[224,512]{1,0:T(8,128)S(1)}, f32[224,512]{1,0:T(8,128)S(1)}, u32[]{:S(2)}, u32[]{:S(2)}) collective-permute-start(f32[224,512]{1,0:T(8,128)S(1)} %pad_maximum_fusion.6), channel_id=1, source_target_pairs={{1,0},{2,1},{3,2},{4,3},{5,4},{6,5},{7,6},{9,8},{10,9},{11,10},{12... | collective-permute-start | bytes 1376264 | tf_op jit(solution)/shard_map/ppermute | solution.py:63
  25.3 11.6 %collective-permute-start.4 = (f32[4,512]{1,0:T(4,128)S(1)}, f32[4,512]{1,0:T(4,128)S(1)}, u32[]{:S(2)}, u32[]{:S(2)}) collective-permute-start(f32[4,512]{1,0:T(4,128)S(1)} %get-tuple-element.225), channel_id=1, source_target_pairs={{0,1},{1,2},{2,3},{3,4},{4,5},{5,6},{6,7},{8,9},{9,10},{10,11},{11... | collective-permute-start | bytes 24584 | tf_op jit(solution)/shard_map/ppermute | solution.py:62
  30.4 6.5 %collective-permute-start.5 = (f32[4,512]{1,0:T(4,128)S(1)}, f32[4,512]{1,0:T(4,128)S(1)}, u32[]{:S(2)}, u32[]{:S(2)}) collective-permute-start(f32[4,512]{1,0:T(4,128)S(1)} %get-tuple-element.226), channel_id=1, source_target_pairs={{1,0},{2,1},{3,2},{4,3},{5,4},{6,5},{7,6},{9,8},{10,9},{11,10},{12... | collective-permute-start | bytes 24584 | tf_op jit(solution)/shard_map/ppermute | solution.py:63
  31.8 7.5 %collective-permute-start.2 = (f32[224,512]{1,0:T(8,128)S(1)}, f32[224,512]{1,0:T(8,128)S(1)}, u32[]{:S(2)}, u32[]{:S(2)}) collective-permute-start(f32[224,512]{1,0:T(8,128)S(1)} %pad_maximum_fusion.5), channel_id=1, source_target_pairs={{0,1},{1,2},{2,3},{3,4},{4,5},{5,6},{6,7},{8,9},{9,10},{10,11},{11... | collective-permute-start | bytes 1376264 | tf_op jit(solution)/shard_map/ppermute | solution.py:62
  42.0 21.4 %collective-permute-start.8 = (f32[2]{0:T(128)S(1)}, f32[2]{0:T(128)S(1)}, u32[]{:S(2)}, u32[]{:S(2)}) collective-permute-start(f32[2]{0:T(128)S(1)} %pad_maximum_fusion.15), channel_id=1, source_target_pairs={{0,1},{1,0},{2,3},{3,2},{4,5},{5,4},{6,7},{7,6},{8,9},{9,8},{10,11... | collective-permute-start | bytes 32 | tf_op jit(solution)/shard_map/ppermute | solution.py:111
  47.0 48.9 %collective-permute-start.7 = (f32[8,512]{1,0:T(8,128)S(1)}, f32[8,512]{1,0:T(8,128)S(1)}, u32[]{:S(2)}, u32[]{:S(2)}) collective-permute-start(f32[8,512]{1,0:T(8,128)S(1)} %pad_maximum_fusion.14), channel_id=1, source_target_pairs={{1,0},{2,1},{3,2},{4,3},{5,4},{6,5},{7,6},{9,8},{10,9},{11,10},{12... | collective-permute-start | bytes 49160 | tf_op jit(solution)/shard_map/ppermute | solution.py:63
  48.3 47.6 %collective-permute-start.6 = (f32[8,512]{1,0:T(8,128)S(1)}, f32[8,512]{1,0:T(8,128)S(1)}, u32[]{:S(2)}, u32[]{:S(2)}) collective-permute-start(f32[8,512]{1,0:T(8,128)S(1)} %pad_maximum_fusion.13), channel_id=1, source_target_pairs={{0,1},{1,2},{2,3},{3,4},{4,5},{5,6},{6,7},{8,9},{9,10},{10,11},{11... | collective-permute-start | bytes 49160 | tf_op jit(solution)/shard_map/ppermute | solution.py:62
  64.6 5.7 %collective-permute-start.9 = (f32[2]{0:T(128)S(1)}, f32[2]{0:T(128)S(1)}, u32[]{:S(2)}, u32[]{:S(2)}) collective-permute-start(f32[2]{0:T(128)S(1)} %fusion.169), channel_id=1, source_target_pairs={{0,2},{1,3},{2,0},{3,1},{4,6},{5,7},{6,4},{7,5},{8,10},{9,11},{10,... | collective-permute-start | bytes 32 | tf_op jit(solution)/shard_map/ppermute | solution.py:111
  71.6 5.4 %collective-permute-start.10 = (f32[2]{0:T(128)S(1)}, f32[2]{0:T(128)S(1)}, u32[]{:S(2)}, u32[]{:S(2)}) collective-permute-start(f32[2]{0:T(128)S(1)} %fusion.170), channel_id=1, source_target_pairs={{0,4},{1,5},{2,6},{3,7},{4,0},{5,1},{6,2},{7,3},{8,12},{9,13},{10,... | collective-permute-start | bytes 32 | tf_op jit(solution)/shard_map/ppermute | solution.py:111
  76.9 6.7 %collective-permute-start.12 = (f32[2]{0:T(128)S(1)}, f32[2]{0:T(128)S(1)}, u32[]{:S(2)}, u32[]{:S(2)}) collective-permute-start(f32[2]{0:T(128)S(1)} %add.703), channel_id=1, source_target_pairs={{0,8},{1,9},{2,10},{3,11},{4,12},{5,13},{6,14},{7,15},{8,16},{9,17... | collective-permute-start | bytes 32 | tf_op jit(solution)/shard_map/ppermute | solution.py:132
  80.4 5.4 %collective-permute-start.11 = (f32[2]{0:T(128)S(1)}, f32[2]{0:T(128)S(1)}, u32[]{:S(2)}, u32[]{:S(2)}) collective-permute-start(f32[2]{0:T(128)S(1)} %add.703), channel_id=1, source_target_pairs={{0,16},{1,17},{2,18},{3,19},{4,20},{5,21},{6,22},{7,23},{8,0},{9,1... | collective-permute-start | bytes 32 | tf_op jit(solution)/shard_map/ppermute | solution.py:132
  88.4 10.4 %slice-start.2 = ((s8[8388608]{0:T(1024)(128)(4,1)}), s8[4194304]{0:T(1024)(128)(4,1)S(1)}, s32[]{:S(2)}) async-start(s8[8388608]{0:T(1024)(128)(4,1)} %bitcast.95), calls=%async_computation.2 | async-start | bytes 8388608
  88.5 7.6 %copy-start = (f32[8,64,512]{2,1,0:T(8,128)}, f32[8,64,512]{2,1,0:T(8,128)S(1)}, u32[]{:S(2)}) copy-start(f32[8,64,512]{2,1,0:T(8,128)S(1)} %broadcast_add_fusion) | copy-start | bytes 3145732
  90.8 44.5 %collective-permute-start.23 = (f32[128,512]{1,0:T(8,128)}, f32[128,512]{1,0:T(8,128)}, u32[]{:S(2)}, u32[]{:S(2)}) collective-permute-start(f32[128,512]{1,0:T(8,128)} %bitcast.52), channel_id=1, source_target_pairs={{1,0},{2,1},{3,2},{4,3},{5,4},{6,5},{7,6},{9,8},{10,9},{11,10},{12... | collective-permute-start | bytes 786440 | tf_op jit(solution)/shard_map/ppermute | solution.py:63
  92.1 43.2 %collective-permute-start.22 = (f32[128,512]{1,0:T(8,128)}, f32[128,512]{1,0:T(8,128)}, u32[]{:S(2)}, u32[]{:S(2)}) collective-permute-start(f32[128,512]{1,0:T(8,128)} %bitcast.50), channel_id=1, source_target_pairs={{0,1},{1,2},{2,3},{3,4},{4,5},{5,6},{6,7},{8,9},{9,10},{10,11},{11... | collective-permute-start | bytes 786440 | tf_op jit(solution)/shard_map/ppermute | solution.py:62
  100.1 35.2 %copy-start.1 = (f32[8,64,512]{2,1,0:T(8,128)S(1)}, f32[8,64,512]{2,1,0:T(8,128)}, u32[]{:S(2)}) copy-start(f32[8,64,512]{2,1,0:T(8,128)} %copy-done) | copy-start | bytes 3145732
  100.2 2.8 %collective-permute-start.18 = (f32[5,512]{1,0:T(8,128)S(1)}, f32[5,512]{1,0:T(8,128)S(1)}, u32[]{:S(2)}, u32[]{:S(2)}) collective-permute-start(f32[5,512]{1,0:T(8,128)S(1)} %concatenate.313), channel_id=1, source_target_pairs={{16,24},{17,25},{18,26},{19,27},{20,28},{21,29},{22,30},{23,31}} | collective-permute-start | bytes 30728 | tf_op jit(solution)/shard_map/ppermute | solution.py:272
  101.0 2.7 %collective-permute-start.17 = (f32[5,512]{1,0:T(8,128)S(1)}, f32[5,512]{1,0:T(8,128)S(1)}, u32[]{:S(2)}, u32[]{:S(2)}) collective-permute-start(f32[5,512]{1,0:T(8,128)S(1)} %concatenate.313), channel_id=1, source_target_pairs={{8,24},{9,25},{10,26},{11,27},{12,28},{13,29},{14,30},{15,31}} | collective-permute-start | bytes 30728 | tf_op jit(solution)/shard_map/ppermute | solution.py:272
  101.7 2.7 %collective-permute-start.16 = (f32[5,512]{1,0:T(8,128)S(1)}, f32[5,512]{1,0:T(8,128)S(1)}, u32[]{:S(2)}, u32[]{:S(2)}) collective-permute-start(f32[5,512]{1,0:T(8,128)S(1)} %concatenate.313), channel_id=1, source_target_pairs={{0,24},{1,25},{2,26},{3,27},{4,28},{5,29},{6,30},{7,31}} | collective-permute-start | bytes 30728 | tf_op jit(solution)/shard_map/ppermute | solution.py:272
  103.0 31.6 %collective-permute-start.14 = (f32[32,512]{1,0:T(8,128)S(1)}, f32[32,512]{1,0:T(8,128)S(1)}, u32[]{:S(2)}, u32[]{:S(2)}) collective-permute-start(f32[32,512]{1,0:T(8,128)S(1)} %pad_maximum_fusion.10), channel_id=1, source_target_pairs={{8,24},{9,25},{10,26},{11,27},{12,28},{13,29},{14,30},{15,31}} | collective-permute-start | bytes 196616 | tf_op jit(solution)/shard_map/ppermute | solution.py:274
  103.7 30.9 %collective-permute-start.15 = (f32[32,512]{1,0:T(8,128)S(1)}, f32[32,512]{1,0:T(8,128)S(1)}, u32[]{:S(2)}, u32[]{:S(2)}) collective-permute-start(f32[32,512]{1,0:T(8,128)S(1)} %pad_maximum_fusion.10), channel_id=1, source_target_pairs={{16,24},{17,25},{18,26},{19,27},{20,28},{21,29},{22,30},{23,31}} | collective-permute-start | bytes 196616 | tf_op jit(solution)/shard_map/ppermute | solution.py:274
  105.1 0.7 collective-permute-start.19
  105.8 0.7 collective-permute-start.20
  106.5 0.7 collective-permute-start.21
  107.2 27.5 %collective-permute-start.13 = (f32[32,512]{1,0:T(8,128)S(1)}, f32[32,512]{1,0:T(8,128)S(1)}, u32[]{:S(2)}, u32[]{:S(2)}) collective-permute-start(f32[32,512]{1,0:T(8,128)S(1)} %pad_maximum_fusion.10), channel_id=1, source_target_pairs={{0,24},{1,25},{2,26},{3,27},{4,28},{5,29},{6,30},{7,31}} | collective-permute-start | bytes 196616 | tf_op jit(solution)/shard_map/ppermute | solution.py:274
  (9 other events, 15.1 us)

commit v20 on v16

--- a/solution.py
+++ b/solution.py
@@ -171,23 +171,11 @@
             (plane_zero, HALO),
         ]
     )
-    after_band = 0.0 * packed[0, 0, 0]
-    init_deep, fc_deep = exchange(
-        [
-            (start_here[:, BAND:] + after_band, 2),
-            (jnp.concatenate([force_here[:, BAND:], coef_here[:, BAND:]], axis=1) + after_band, 1),
-        ]
-    )
     init_band, force_band, coef_band = (
         packed[:, :BAND],
         packed[:, BAND : 2 * BAND],
         packed[:, 2 * BAND :],
     )
-    init_deep = jnp.concatenate([init_band[HALO - 2 : HALO + slab_rows + 2], init_deep], axis=1)
-    force_deep = jnp.concatenate(
-        [force_band[HALO - 1 : HALO + slab_rows + 1], fc_deep[:, :deep_planes]], axis=1
-    )
-    coef_deep = jnp.concatenate([coef_band[HALO - 1 : HALO + slab_rows + 1], fc_deep[:, deep_planes:]], axis=1)
     global_row = slab_id * slab_rows + jnp.arange(slab_rows + 2 * HALO) - HALO
     total_rows = slab_rows * lax.axis_size("slab")
     row_ok = ((global_row >= 0) & (global_row < total_rows))[:, None, None]
@@ -212,7 +200,18 @@
     tilde_zero, unused, unused_extra = evaluate(disp_zero, plane_zero_rims)
     resid_zero = tilde_zero - disp_zero
     disp_one = disp_zero + RELAX * resid_zero
-    tilde_one, unused, unused_extra = evaluate(disp_one)
+    tilde_one, unused, (init_deep, fc_deep) = evaluate(
+        disp_one,
+        extra=[
+            (start_here[:, BAND:], 2),
+            (jnp.concatenate([force_here[:, BAND:], coef_here[:, BAND:]], axis=1), 1),
+        ],
+    )
+    init_deep = jnp.concatenate([init_band[HALO - 2 : HALO + slab_rows + 2], init_deep], axis=1)
+    force_deep = jnp.concatenate(
+        [force_band[HALO - 1 : HALO + slab_rows + 1], fc_deep[:, :deep_planes]], axis=1
+    )
+    coef_deep = jnp.concatenate([coef_band[HALO - 1 : HALO + slab_rows + 1], fc_deep[:, deep_planes:]], axis=1)
     init_deep, tilde_one = lax.optimization_barrier((init_deep, tilde_one))
     deep = lax.cond(
         shell_flag,

time: 128 us -> 145 us (1.13)
  other arithmetic: 22.5 us -> 37.8 us
  local copies, waits for them, and re-layouts: 18.6 us -> 32 us
  waiting for transfers between devices: 34.9 us -> 27.4 us
  starting transfers between devices: 38.2 us -> 34.2 us
    ppermute x5 -> x4, waiting for transfers between devices: 10.4 us -> 1.89 us  [exchange(): low = lax.ppermute(up, 'slab', forward)]
    select_n x9 -> x11, other arithmetic: 1.6 us -> 6.19 us  [band_solve(): q = jnp.where(row_ok[k:rows - k], new, 0.0)]
    reduce_sum x2, other arithmetic: 1.29 us -> 4.71 us  [evaluate(): tilde = own_live * jnp.sum(compliance * loaded[:, None, :], axis=-1)]
    reduce_sum x1, other arithmetic: 1.22 us -> 4.59 us  [body(): jnp.sum(compliance[None] * loaded[:, :, None, :], axis=-1)]
    ppermute x5 -> x4, starting transfers between devices: 11.1 us -> 7.82 us  [exchange(): low = lax.ppermute(up, 'slab', forward)]
    ppermute x5 -> x4, waiting for transfers between devices: 0.01 us -> 2.61 us  [exchange(): high = lax.ppermute(down, 'slab', backward)]
    scatter-add x0 -> x3, local copies, waits for them, and re-layouts: none -> 2.23 us  [the longest x2 1.9 us: evaluate(): rhs = force_band.at[:, 0, :].add(plane_rims)]
    ppermute x3, waiting for transfers between devices: 12.8 us -> 10.9 us  [body(): lax.ppermute(outgoing, 'side', [(source, side_count - 1)])]
  transfers between devices with their start and end apart: 21 -> 19, of which waited for: 9 -> 9; matrix products, arithmetic and copies ran while one was open for 15% -> 14% of each run, Pallas kernels for 0% -> 0%
where the time goes in v20:
time: 145 us; the launch traced here: 143 us
  other arithmetic  37.8 us (26%)
  starting transfers between devices  34.2 us (24%)
  local copies, waits for them, and re-layouts  32 us (22%)
  waiting for transfers between devices  27.4 us (19%)
  between operations  11.7 us (8%)
    ppermute x4, starting transfers between devices, exchange(): high = lax.ppermute(down, 'slab', backward)  12.2 us
    ppermute x3, waiting for transfers between devices, body(): lax.ppermute(outgoing, 'side', [(source, side_count - 1)])  10.9 us
    ppermute x4, starting transfers between devices, exchange(): low = lax.ppermute(up, 'slab', forward)  7.82 us
    ppermute x3, starting transfers between devices, shell_sum(): v = v + lax.ppermute(v, ('side', 'slab'), pairs)  7.37 us
    ppermute x3, waiting for transfers between devices, shell_sum(): v = v + lax.ppermute(v, ('side', 'slab'), pairs)  6.46 us
    select_n x11, other arithmetic, band_solve(): q = jnp.where(row_ok[k:rows - k], new, 0.0)  6.19 us
    unnamed x106, local copies, waits for them, and re-layouts  5.94 us
    ppermute x3, waiting for transfers between devices, allsum_axis(): v = v + lax.ppermute(v, axis, [(i, i ^ step) for i in range(count)])  5.48 us
  transfers between devices with their start and end apart: 19, of which 9 were waited for; matrix products, arithmetic and copies ran while one was open for 14% of the time, Pallas kernels for 0%

profile of v20, /device:TPU:28, one launch (start us, length us, event | category | flops | bytes accessed | tf_op | source)
XLA Modules:
  0.0 143.2 jit_solution(1120373881363453399)
XLA Ops:
  5.8 1.9 %collective-permute-start = (f32[100,512]{1,0:T(8,128)S(1)}, f32[100,512]{1,0:T(8,128)S(1)}, u32[]{:S(2)}, u32[]{:S(2)}) collective-permute-start(f32[100,512]{1,0:T(8,128)S(1)} %pad_maximum_fusion.9), channel_id=1, source_target_pairs={{0,1},{1,2},{2,3},{3,4},{4,5},{5,6},{6,7},{8,9},{9,10},{10,11},{11... | collective-permute-start | bytes 614408 | tf_op jit(solution)/shard_map/ppermute | solution.py:62
  7.7 4.5 %collective-permute-start.1 = (f32[100,512]{1,0:T(8,128)S(1)}, f32[100,512]{1,0:T(8,128)}, u32[]{:S(2)}, u32[]{:S(2)}) collective-permute-start(f32[100,512]{1,0:T(8,128)S(1)} %pad_maximum_fusion.10), channel_id=1, source_target_pairs={{1,0},{2,1},{3,2},{4,3},{5,4},{6,5},{7,6},{9,8},{10,9},{11,10},{12... | collective-permute-start | bytes 614408 | tf_op jit(solution)/shard_map/ppermute | solution.py:63
  13.7 2.0 %fusion.129 = (f32[2,56,512]{2,1,0:T(8,128)}, f32[2,56,512]{2,1,0:T(8,128)}) fusion(f32[8,64,512]{2,1,0:T(8,128)} %bitcast.85), kind=kLoop, calls=%fused_computation.253 | loop fusion | bytes 917504 | tf_op jit(solution)/shard_map/slice | solution.py:60
  22.8 2.0 %fusion.22 = (f32[14,7,512]{2,1,0:T(8,128)S(1)}, f32[14,7,512]{2,1,0:T(8,128)}) fusion(f32[16,8,512]{2,1,0:T(8,128)S(1)} %scatter-add.10, f32[16,24,512]{2,1,0:T(8,128)S(1)} %pad_maximum_fusion.4, pred[14]{0:T(512)(128)(4,1)S(1)} %slice.813, f32[14,7,511]{2,1,0:T(8,128)} %get-tuple-element.144, f32[14,7,511]{2,1,0:T(8,128)} %get-tuple-element.143, ...), kind=kLoop, calls=%fused_computation.60 | loop fusion | flops 451584 | bytes 1977598 | tf_op jit(solution)/shard_map/jit(_where)/select_n | solution.py:38
  26.9 4.1 %multiply_reduce_fusion.2 = f32[8,512]{1,0:T(8,128)S(1)} fusion(f32[8,512,512]{2,1,0:T(8,128)} %param.24, f32[8,512]{1,0:T(8,128)S(1)} %subtract_select_fusion.1), kind=kLoop, calls=%fused_computation.22 | loop fusion | flops 4190208 | bytes 8421376 | tf_op jit(solution)/shard_map/reduce_sum | solution.py:197
  32.6 2.6 %collective-permute-start.3 = (f32[228,512]{1,0:T(8,128)}, f32[228,512]{1,0:T(8,128)}, u32[]{:S(2)}, u32[]{:S(2)}) collective-permute-start(f32[228,512]{1,0:T(8,128)} %pad_maximum_fusion.6), channel_id=1, source_target_pairs={{1,0},{2,1},{3,2},{4,3},{5,4},{6,5},{7,6},{9,8},{10,9},{11,10},{12... | collective-permute-start | bytes 1400840 | tf_op jit(solution)/shard_map/ppermute | solution.py:63
  36.1 1.9 %collective-permute-start.2 = (f32[228,512]{1,0:T(8,128)}, f32[228,512]{1,0:T(8,128)}, u32[]{:S(2)}, u32[]{:S(2)}) collective-permute-start(f32[228,512]{1,0:T(8,128)} %pad_maximum_fusion.5), channel_id=1, source_target_pairs={{0,1},{1,2},{2,3},{3,4},{4,5},{5,6},{6,7},{8,9},{9,10},{10,11},{11... | collective-permute-start | bytes 1400840 | tf_op jit(solution)/shard_map/ppermute | solution.py:62
  39.3 1.3 fusion.99
  42.0 2.6 %collective-permute-done.3 = f32[228,512]{1,0:T(8,128)} collective-permute-done((f32[228,512]{1,0:T(8,128)}, f32[228,512]{1,0:T(8,128)}, u32[]{:S(2)}, u32[]{:S(2)}) %collective-permute-start.3) | collective-permute-done | bytes 466976 | tf_op jit(solution)/shard_map/ppermute | solution.py:63
  45.4 1.9 %collective-permute-done.2 = f32[228,512]{1,0:T(8,128)} collective-permute-done((f32[228,512]{1,0:T(8,128)}, f32[228,512]{1,0:T(8,128)}, u32[]{:S(2)}, u32[]{:S(2)}) %collective-permute-start.2) | collective-permute-done | bytes 466976 | tf_op jit(solution)/shard_map/ppermute | solution.py:62
  49.4 1.8 %scatter-add.11 = f32[16,8,512]{2,1,0:T(8,128)} dynamic-update-slice(f32[16,8,512]{2,1,0:T(8,128)} %copy.33, f32[16,1,512]{2,1,0:T(1,128)} %copy.19, s32[]{:T(128)} %constant.155.clone.1, s32[]{:T(128)} %constant.155.clone.1, s32[]{:T(128)} %constant.155.clone.1) | dynamic-update-slice | bytes 65540 | tf_op jit(solution)/shard_map/scatter-add | solution.py:193
  54.4 1.5 %slice_bitcast_fusion = (f32[1,112,512]{2,1,0:T(8,128)S(1)}, f32[112,512]{1,0:T(8,128)S(1)}) fusion(f32[228,512]{1,0:T(8,128)} %collective-permute-done.3), kind=kLoop, calls=%fused_computation.41 | loop fusion | bytes 917504 | tf_op jit(solution)/shard_map/reshape | solution.py:68
  61.8 1.9 %pad_maximum_fusion.16 = f32[2]{0:T(128)} fusion(f32[1]{0:T(128)} %bitcast.26, f32[1]{0:T(128)} %bitcast.25), kind=kLoop, calls=%fused_computation.239 | loop fusion | flops 2 | bytes 16 | tf_op jit(solution)/shard_map/stack | solution.py:226
  63.9 2.8 %collective-permute-start.5 = (f32[8,512]{1,0:T(8,128)S(1)}, f32[8,512]{1,0:T(8,128)S(1)}, u32[]{:S(2)}, u32[]{:S(2)}) collective-permute-start(f32[8,512]{1,0:T(8,128)S(1)} %pad_maximum_fusion.15), channel_id=1, source_target_pairs={{1,0},{2,1},{3,2},{4,3},{5,4},{6,5},{7,6},{9,8},{10,9},{11,10},{12... | collective-permute-start | bytes 49160 | tf_op jit(solution)/shard_map/ppermute | solution.py:63
  67.4 1.9 %collective-permute-start.4 = (f32[8,512]{1,0:T(8,128)}, f32[8,512]{1,0:T(8,128)}, u32[]{:S(2)}, u32[]{:S(2)}) collective-permute-start(f32[8,512]{1,0:T(8,128)} %pad_maximum_fusion.14), channel_id=1, source_target_pairs={{0,1},{1,2},{2,3},{3,4},{4,5},{5,6},{6,7},{8,9},{9,10},{10,11},{11... | collective-permute-start | bytes 49160 | tf_op jit(solution)/shard_map/ppermute | solution.py:62
  71.6 2.1 %fusion.153 = f32[2]{0:T(128)S(1)} fusion(f32[2]{0:T(128)} %collective-permute-done.6, f32[1]{0:T(128)} %bitcast.26, f32[1]{0:T(128)} %bitcast.25), kind=kLoop, calls=%fused_computation.277 | loop fusion | flops 4 | bytes 24 | tf_op jit(solution)/shard_map/add | solution.py:111
  73.7 1.6 %collective-permute-start.7 = (f32[2]{0:T(128)S(1)}, f32[2]{0:T(128)S(1)}, u32[]{:S(2)}, u32[]{:S(2)}) collective-permute-start(f32[2]{0:T(128)S(1)} %fusion.153), channel_id=1, source_target_pairs={{0,2},{1,3},{2,0},{3,1},{4,6},{5,7},{6,4},{7,5},{8,10},{9,11},{10,... | collective-permute-start | bytes 32 | tf_op jit(solution)/shard_map/ppermute | solution.py:111
  75.3 1.9 %collective-permute-done.7 = f32[2]{0:T(128)S(1)} collective-permute-done((f32[2]{0:T(128)S(1)}, f32[2]{0:T(128)S(1)}, u32[]{:S(2)}, u32[]{:S(2)}) %collective-permute-start.7) | collective-permute-done | bytes 40 | tf_op jit(solution)/shard_map/ppermute | solution.py:111
  77.2 2.0 %fusion.154 = f32[2]{0:T(128)S(1)} fusion(f32[2]{0:T(128)S(1)} %collective-permute-done.7, f32[2]{0:T(128)} %collective-permute-done.6, f32[1]{0:T(128)} %bitcast.26, f32[1]{0:T(128)} %bitcast.25), kind=kLoop, calls=%fused_computation.278 | loop fusion | flops 6 | bytes 32 | tf_op jit(solution)/shard_map/add | solution.py:111
  79.2 3.5 %collective-permute-done.8 = f32[2]{0:T(128)S(1)} collective-permute-done((f32[2]{0:T(128)S(1)}, f32[2]{0:T(128)S(1)}, u32[]{:S(2)}, u32[]{:S(2)}) %collective-permute-start.8) | collective-permute-done | bytes 40 | tf_op jit(solution)/shard_map/ppermute | solution.py:111
  93.1 4.6 %multiply_reduce_fusion = f32[2,8,512]{2,1,0:T(8,128)S(1)} fusion(f32[2,8,512]{2,1,0:T(8,128)S(1)} %subtract_multiply_fusion, f32[8,512,512]{2,1,0:T(8,128)} %param.24), kind=kLoop, calls=%fused_computation.20 | loop fusion | flops 8380416 | bytes 8454144 | tf_op jit(solution)/shard_map/reduce_sum | solution.py:239
  97.8 1.3 collective-permute-start.13
  99.1 1.3 collective-permute-start.12
  101.8 2.2 %collective-permute-start.18 = (f32[128,512]{1,0:T(8,128)S(1)}, f32[128,512]{1,0:T(8,128)S(1)}, u32[]{:S(2)}, u32[]{:S(2)}) collective-permute-start(f32[128,512]{1,0:T(8,128)S(1)} %bitcast.106), channel_id=1, source_target_pairs={{1,0},{2,1},{3,2},{4,3},{5,4},{6,5},{7,6},{9,8},{10,9},{11,10},{12... | collective-permute-start | bytes 786440 | tf_op jit(solution)/shard_map/ppermute | solution.py:63
  104.0 2.1 %collective-permute-start.17 = (f32[128,512]{1,0:T(8,128)S(1)}, f32[128,512]{1,0:T(8,128)S(1)}, u32[]{:S(2)}, u32[]{:S(2)}) collective-permute-start(f32[128,512]{1,0:T(8,128)S(1)} %bitcast.105), channel_id=1, source_target_pairs={{0,1},{1,2},{2,3},{3,4},{4,5},{5,6},{6,7},{8,9},{9,10},{10,11},{11... | collective-permute-start | bytes 786440 | tf_op jit(solution)/shard_map/ppermute | solution.py:62
  106.1 9.1 %collective-permute-done.13 = f32[37,512]{1,0:T(8,128)S(1)} collective-permute-done((f32[37,512]{1,0:T(8,128)S(1)}, f32[37,512]{1,0:T(8,128)S(1)}, u32[]{:S(2)}, u32[]{:S(2)}) %collective-permute-start.13) | collective-permute-done | bytes 75808 | tf_op jit(solution)/shard_map/ppermute | solution.py:278
  115.3 1.8 %collective-permute-done.12 = f32[37,512]{1,0:T(8,128)S(1)} collective-permute-done((f32[37,512]{1,0:T(8,128)S(1)}, f32[37,512]{1,0:T(8,128)S(1)}, u32[]{:S(2)}, u32[]{:S(2)}) %collective-permute-start.12) | collective-permute-done | bytes 75808 | tf_op jit(solution)/shard_map/ppermute | solution.py:278
  117.7 1.9 %collective-permute-start.14 = (f32[4]{0:T(128)S(1)}, f32[4]{0:T(128)S(1)}, u32[]{:S(2)}, u32[]{:S(2)}) collective-permute-start(f32[4]{0:T(128)S(1)} %slice_reduce_fusion), channel_id=1, source_target_pairs={{24,25},{25,24},{26,27},{27,26},{28,29},{29,28},{30,31},{31,30}} | collective-permute-start | bytes 56 | tf_op jit(solution)/shard_map/ppermute | solution.py:122
  120.7 3.5 %collective-permute-start.15 = (f32[4]{0:T(128)S(1)}, f32[4]{0:T(128)S(1)}, u32[]{:S(2)}, u32[]{:S(2)}) collective-permute-start(f32[4]{0:T(128)S(1)} %add.689), channel_id=1, source_target_pairs={{24,26},{25,27},{26,24},{27,25},{28,30},{29,31},{30,28},{31,29}} | collective-permute-start | bytes 56 | tf_op jit(solution)/shard_map/ppermute | solution.py:122
  124.2 1.9 %collective-permute-done.15 = f32[4]{0:T(128)S(1)} collective-permute-done((f32[4]{0:T(128)S(1)}, f32[4]{0:T(128)S(1)}, u32[]{:S(2)}, u32[]{:S(2)}) %collective-permute-start.15) | collective-permute-done | bytes 48 | tf_op jit(solution)/shard_map/ppermute | solution.py:122
  126.2 2.0 %collective-permute-start.16 = (f32[4]{0:T(128)S(1)}, f32[4]{0:T(128)S(1)}, u32[]{:S(2)}, u32[]{:S(2)}) collective-permute-start(f32[4]{0:T(128)S(1)} %add.690), channel_id=1, source_target_pairs={{24,28},{25,29},{26,30},{27,31},{28,24},{29,25},{30,26},{31,27}} | collective-permute-start | bytes 56 | tf_op jit(solution)/shard_map/ppermute | solution.py:122
  128.1 3.5 %collective-permute-done.16 = f32[4]{0:T(128)S(1)} collective-permute-done((f32[4]{0:T(128)S(1)}, f32[4]{0:T(128)S(1)}, u32[]{:S(2)}, u32[]{:S(2)}) %collective-permute-start.16) | collective-permute-done | bytes 48 | tf_op jit(solution)/shard_map/ppermute | solution.py:122
  (262 shorter events, 50.7 us)
Async XLA Ops:
  4.7 8.3 %copy-start.46 = (s32[8]{0:T(128)S(1)}, s32[8]{0:T(128)}, u32[]{:S(2)}) copy-start(s32[8]{0:T(128)} %param.29) | copy-start | bytes 100
  5.8 12.0 %collective-permute-start = (f32[100,512]{1,0:T(8,128)S(1)}, f32[100,512]{1,0:T(8,128)S(1)}, u32[]{:S(2)}, u32[]{:S(2)}) collective-permute-start(f32[100,512]{1,0:T(8,128)S(1)} %pad_maximum_fusion.9), channel_id=1, source_target_pairs={{0,1},{1,2},{2,3},{3,4},{4,5},{5,6},{6,7},{8,9},{9,10},{10,11},{11... | collective-permute-start | bytes 614408 | tf_op jit(solution)/shard_map/ppermute | solution.py:62
  7.7 10.0 %collective-permute-start.1 = (f32[100,512]{1,0:T(8,128)S(1)}, f32[100,512]{1,0:T(8,128)}, u32[]{:S(2)}, u32[]{:S(2)}) collective-permute-start(f32[100,512]{1,0:T(8,128)S(1)} %pad_maximum_fusion.10), channel_id=1, source_target_pairs={{1,0},{2,1},{3,2},{4,3},{5,4},{6,5},{7,6},{9,8},{10,9},{11,10},{12... | collective-permute-start | bytes 614408 | tf_op jit(solution)/shard_map/ppermute | solution.py:63
  12.4 10.4 %copy-start.40 = (pred[14]{0:T(512)(128)(4,1)}, pred[14]{0:T(512)(128)(4,1)S(1)}, u32[]{:S(2)}) copy-start(pred[14]{0:T(512)(128)(4,1)S(1)} %slice.813) | copy-start | bytes 46
  12.4 12.5 %copy-start.41 = (pred[12]{0:T(512)(128)(4,1)}, pred[12]{0:T(512)(128)(4,1)S(1)}, u32[]{:S(2)}) copy-start(pred[12]{0:T(512)(128)(4,1)S(1)} %slice.811) | copy-start | bytes 40
  17.7 7.6 %copy-start.37 = (pred[10]{0:T(512)(128)(4,1)}, pred[10]{0:T(512)(128)(4,1)S(1)}, u32[]{:S(2)}) copy-start(pred[10]{0:T(512)(128)(4,1)S(1)} %get-tuple-element.193) | copy-start | bytes 34
  26.9 4.8 %copy-start.23 = (f32[8,8]{1,0:T(8,128)S(1)}, f32[8,8]{1,0:T(8,128)}, u32[]{:S(2)}) copy-start(f32[8,8]{1,0:T(8,128)} %copy-done.22) | copy-start | bytes 772
  26.9 4.9 %copy-start.7 = (f32[2,56,512]{2,1,0:T(8,128)S(1)}, f32[2,56,512]{2,1,0:T(8,128)}, u32[]{:S(2)}) copy-start(f32[2,56,512]{2,1,0:T(8,128)} %get-tuple-element.134) | copy-start | bytes 688132
  26.9 8.4 %copy-start.6 = (f32[2,56,512]{2,1,0:T(8,128)S(1)}, f32[2,56,512]{2,1,0:T(8,128)}, u32[]{:S(2)}) copy-start(f32[2,56,512]{2,1,0:T(8,128)} %get-tuple-element.133) | copy-start | bytes 688132
  31.8 6.2 %copy-start.19 = (f32[8,512]{1,0:T(8,128)}, f32[8,512]{1,0:T(8,128)S(1)}, u32[]{:S(2)}) copy-start(f32[8,512]{1,0:T(8,128)S(1)} %multiply_reduce_fusion.7) | copy-start | bytes 49156
  32.6 12.0 %collective-permute-start.3 = (f32[228,512]{1,0:T(8,128)}, f32[228,512]{1,0:T(8,128)}, u32[]{:S(2)}, u32[]{:S(2)}) collective-permute-start(f32[228,512]{1,0:T(8,128)} %pad_maximum_fusion.6), channel_id=1, source_target_pairs={{1,0},{2,1},{3,2},{4,3},{5,4},{6,5},{7,6},{9,8},{10,9},{11,10},{12... | collective-permute-start | bytes 1400840 | tf_op jit(solution)/shard_map/ppermute | solution.py:63
  36.1 11.2 %collective-permute-start.2 = (f32[228,512]{1,0:T(8,128)}, f32[228,512]{1,0:T(8,128)}, u32[]{:S(2)}, u32[]{:S(2)}) collective-permute-start(f32[228,512]{1,0:T(8,128)} %pad_maximum_fusion.5), channel_id=1, source_target_pairs={{0,1},{1,2},{2,3},{3,4},{4,5},{5,6},{6,7},{8,9},{9,10},{10,11},{11... | collective-permute-start | bytes 1400840 | tf_op jit(solution)/shard_map/ppermute | solution.py:62
  53.5 6.0 %slice-start = ((s8[8388608]{0:T(1024)(128)(4,1)}), s8[4194304]{0:T(1024)(128)(4,1)S(1)}, s32[]{:S(2)}) async-start(s8[8388608]{0:T(1024)(128)(4,1)} %bitcast.82), calls=%async_computation | async-start | bytes 8388608
  60.4 8.9 %copy-start.10 = (f32[10,8,512]{2,1,0:T(8,128)S(1)}, f32[10,8,512]{2,1,0:T(8,128)}, u32[]{:S(2)}) copy-start(f32[10,8,512]{2,1,0:T(8,128)} %get-tuple-element.141) | copy-start | bytes 491524
  63.7 7.9 %collective-permute-start.6 = (f32[2]{0:T(128)}, f32[2]{0:T(128)}, u32[]{:S(2)}, u32[]{:S(2)}) collective-permute-start(f32[2]{0:T(128)} %pad_maximum_fusion.16), channel_id=1, source_target_pairs={{0,1},{1,0},{2,3},{3,2},{4,5},{5,4},{6,7},{7,6},{8,9},{9,8},{10,11... | collective-permute-start | bytes 32 | tf_op jit(solution)/shard_map/ppermute | solution.py:111
  63.9 23.6 %collective-permute-start.5 = (f32[8,512]{1,0:T(8,128)S(1)}, f32[8,512]{1,0:T(8,128)S(1)}, u32[]{:S(2)}, u32[]{:S(2)}) collective-permute-start(f32[8,512]{1,0:T(8,128)S(1)} %pad_maximum_fusion.15), channel_id=1, source_target_pairs={{1,0},{2,1},{3,2},{4,3},{5,4},{6,5},{7,6},{9,8},{10,9},{11,10},{12... | collective-permute-start | bytes 49160 | tf_op jit(solution)/shard_map/ppermute | solution.py:63
  67.4 20.2 %collective-permute-start.4 = (f32[8,512]{1,0:T(8,128)}, f32[8,512]{1,0:T(8,128)}, u32[]{:S(2)}, u32[]{:S(2)}) collective-permute-start(f32[8,512]{1,0:T(8,128)} %pad_maximum_fusion.14), channel_id=1, source_target_pairs={{0,1},{1,2},{2,3},{3,4},{4,5},{5,6},{6,7},{8,9},{9,10},{10,11},{11... | collective-permute-start | bytes 49160 | tf_op jit(solution)/shard_map/ppermute | solution.py:62
  71.6 16.9 %copy-start.12 = (f32[16,1,512]{2,1,0:T(1,128)S(1)}, f32[16,1,512]{2,1,0:T(1,128)}, u32[]{:S(2)}) copy-start(f32[16,1,512]{2,1,0:T(1,128)} %copy-done.11) | copy-start | bytes 98308
  71.6 16.9 %copy-start.3 = (f32[16,8,512]{2,1,0:T(8,128)S(1)}, f32[16,8,512]{2,1,0:T(8,128)}, u32[]{:S(2)}) copy-start(f32[16,8,512]{2,1,0:T(8,128)} %copy.34) | copy-start | bytes 786436
  71.6 17.3 %copy-start.4 = (f32[14,7,512]{2,1,0:T(8,128)S(1)}, f32[14,7,512]{2,1,0:T(8,128)}, u32[]{:S(2)}) copy-start(f32[14,7,512]{2,1,0:T(8,128)} %get-tuple-element.110) | copy-start | bytes 602116
  73.7 3.5 %collective-permute-start.7 = (f32[2]{0:T(128)S(1)}, f32[2]{0:T(128)S(1)}, u32[]{:S(2)}, u32[]{:S(2)}) collective-permute-start(f32[2]{0:T(128)S(1)} %fusion.153), channel_id=1, source_target_pairs={{0,2},{1,3},{2,0},{3,1},{4,6},{5,7},{6,4},{7,5},{8,10},{9,11},{10,... | collective-permute-start | bytes 32 | tf_op jit(solution)/shard_map/ppermute | solution.py:111
  79.2 3.5 %collective-permute-start.8 = (f32[2]{0:T(128)S(1)}, f32[2]{0:T(128)S(1)}, u32[]{:S(2)}, u32[]{:S(2)}) collective-permute-start(f32[2]{0:T(128)S(1)} %fusion.154), channel_id=1, source_target_pairs={{0,4},{1,5},{2,6},{3,7},{4,0},{5,1},{6,2},{7,3},{8,12},{9,13},{10,... | collective-permute-start | bytes 32 | tf_op jit(solution)/shard_map/ppermute | solution.py:111
  82.8 1.3 collective-permute-start.10
  83.4 0.7 collective-permute-start.9
  97.8 17.4 %collective-permute-start.13 = (f32[37,512]{1,0:T(8,128)S(1)}, f32[37,512]{1,0:T(8,128)S(1)}, u32[]{:S(2)}, u32[]{:S(2)}) collective-permute-start(f32[37,512]{1,0:T(8,128)S(1)} %concatenate.309), channel_id=1, source_target_pairs={{16,24},{17,25},{18,26},{19,27},{20,28},{21,29},{22,30},{23,31}} | collective-permute-start | bytes 227336 | tf_op jit(solution)/shard_map/ppermute | solution.py:278
  99.1 17.9 %collective-permute-start.12 = (f32[37,512]{1,0:T(8,128)S(1)}, f32[37,512]{1,0:T(8,128)S(1)}, u32[]{:S(2)}, u32[]{:S(2)}) collective-permute-start(f32[37,512]{1,0:T(8,128)S(1)} %concatenate.309), channel_id=1, source_target_pairs={{8,24},{9,25},{10,26},{11,27},{12,28},{13,29},{14,30},{15,31}} | collective-permute-start | bytes 227336 | tf_op jit(solution)/shard_map/ppermute | solution.py:278
  100.4 16.6 %collective-permute-start.11 = (f32[37,512]{1,0:T(8,128)S(1)}, f32[37,512]{1,0:T(8,128)S(1)}, u32[]{:S(2)}, u32[]{:S(2)}) collective-permute-start(f32[37,512]{1,0:T(8,128)S(1)} %concatenate.309), channel_id=1, source_target_pairs={{0,24},{1,25},{2,26},{3,27},{4,28},{5,29},{6,30},{7,31}} | collective-permute-start | bytes 227336 | tf_op jit(solution)/shard_map/ppermute | solution.py:278
  101.8 38.8 %collective-permute-start.18 = (f32[128,512]{1,0:T(8,128)S(1)}, f32[128,512]{1,0:T(8,128)S(1)}, u32[]{:S(2)}, u32[]{:S(2)}) collective-permute-start(f32[128,512]{1,0:T(8,128)S(1)} %bitcast.106), channel_id=1, source_target_pairs={{1,0},{2,1},{3,2},{4,3},{5,4},{6,5},{7,6},{9,8},{10,9},{11,10},{12... | collective-permute-start | bytes 786440 | tf_op jit(solution)/shard_map/ppermute | solution.py:63
  104.0 36.6 %collective-permute-start.17 = (f32[128,512]{1,0:T(8,128)S(1)}, f32[128,512]{1,0:T(8,128)S(1)}, u32[]{:S(2)}, u32[]{:S(2)}) collective-permute-start(f32[128,512]{1,0:T(8,128)S(1)} %bitcast.105), channel_id=1, source_target_pairs={{0,1},{1,2},{2,3},{3,4},{4,5},{5,6},{6,7},{8,9},{9,10},{10,11},{11... | collective-permute-start | bytes 786440 | tf_op jit(solution)/shard_map/ppermute | solution.py:62
  117.7 3.0 %collective-permute-start.14 = (f32[4]{0:T(128)S(1)}, f32[4]{0:T(128)S(1)}, u32[]{:S(2)}, u32[]{:S(2)}) collective-permute-start(f32[4]{0:T(128)S(1)} %slice_reduce_fusion), channel_id=1, source_target_pairs={{24,25},{25,24},{26,27},{27,26},{28,29},{29,28},{30,31},{31,30}} | collective-permute-start | bytes 56 | tf_op jit(solution)/shard_map/ppermute | solution.py:122
  120.7 5.4 %collective-permute-start.15 = (f32[4]{0:T(128)S(1)}, f32[4]{0:T(128)S(1)}, u32[]{:S(2)}, u32[]{:S(2)}) collective-permute-start(f32[4]{0:T(128)S(1)} %add.689), channel_id=1, source_target_pairs={{24,26},{25,27},{26,24},{27,25},{28,30},{29,31},{30,28},{31,29}} | collective-permute-start | bytes 56 | tf_op jit(solution)/shard_map/ppermute | solution.py:122
  126.2 5.4 %collective-permute-start.16 = (f32[4]{0:T(128)S(1)}, f32[4]{0:T(128)S(1)}, u32[]{:S(2)}, u32[]{:S(2)}) collective-permute-start(f32[4]{0:T(128)S(1)} %add.690), channel_id=1, source_target_pairs={{24,28},{25,29},{26,30},{27,31},{28,24},{29,25},{30,26},{31,27}} | collective-permute-start | bytes 56 | tf_op jit(solution)/shard_map/ppermute | solution.py:122
  (39 other events, 75.6 us)
